TPU v7x, 32 devices: a whole 2x2x4 slice. The times are simulated.
32 devices in a mesh: dom: 4 (over y, x), st: 8 (over z, core).
Axes of the slice: x: 2, y: 2, z: 4, core: 2. Of those that a mesh axis runs over, the one named last changes fastest.
Arguments:
- states: bfloat16 [6912, 1024], P('dom', 'st'), may hold values from -6 to 6
- inv_mass: float32 [6912], P('dom'), may hold values from 0.4 to 1
- potential: float32 [6912], P('dom'), may hold values from -1 to 0.5
- cell_matrix: bfloat16 [343, 343], replicated, may hold values from -0.21 to 2, as said below
- connect: int32 [32, 343], P('dom'), may hold values from 0 to 1871, as said below
- face_rows: int32 [576], P('dom'), may hold values from 0 to 1727, as said below
- rotation: bfloat16 [512, 1024], P(None, 'st'), may hold values from -0.25 to 0.25
Outputs:
- rotated: float32 [6912, 1024], P('dom', 'st')
Inputs may be any that keep to these rules, and one draw needn't show every extreme that they name: Row c of a device's block of connect lists the nodes of one of its 8 cells, in the order of cell_matrix's rows; each number below 1728 appears somewhere in the block. `face_rows`: A device's block holds 144 different node rows of that device. `cell_matrix`: Symmetric.
All inputs are finite; a program needn't handle non-finite values.
Results may differ from a plain program's by a relative error of at most 0.0031.
Values may be sent and summed in bfloat16 or wider, within the bound.
No kernel may reach another device: no remote copies, remote signals or barrier semaphores. Data moves between devices by JAX's collectives and lax.ppermute only.
A program may use at most 64 MiB of HBM per device.

v0:
```python
import jax
import jax.numpy as jnp
from jax import lax
from jax.sharding import PartitionSpec as P

POLY = 3


centre = 10.0
half_span = 10.0


def ring(block, axis, step):
    count = lax.axis_size(axis)
    route = [(i, (i + step) % count) for i in range(count)]
    return lax.ppermute(block, axis, route)


def from_partner(block, axis, distance):
    count = lax.axis_size(axis)
    route = []
    for low in range(count):
        high = low | 1 << distance
        if high != low and high < count:
            route += [(low, high), (high, low)]
    return lax.ppermute(block, axis, route)


def high_low(value):
    high = lax.reduce_precision(value, exponent_bits=8, mantissa_bits=7)
    low = value - high
    return jnp.concatenate([high.astype(jnp.bfloat16), low.astype(jnp.bfloat16)], 1)


def summed_halves(both):
    width = both.shape[1] // 2
    return both[:, :width] + both[:, width:]


def body(states, inv_mass, potential, cell_matrix, connect, face_rows, rotation):
    node_count, state_count = states.shape
    cell_count, cell_size = connect.shape
    face_count = face_rows.shape[0]
    wide_count = node_count + face_count
    pad = (-cell_size) % 16
    padded_size = cell_size + pad
    cell_rows = jnp.pad(connect, ((0, 0), (0, pad)), constant_values=-1).reshape(-1)
    padded_matrix = jnp.pad(cell_matrix, ((0, pad), (0, pad)))
    wide_ids = lax.broadcasted_iota(jnp.int32, (wide_count, 1), 0)
    gather_sel = (cell_rows[:, None] == wide_ids[:, 0][None, :]).astype(jnp.bfloat16)
    scatter_sel = (wide_ids == cell_rows[None, :]).astype(jnp.bfloat16)
    rim_ids = jnp.concatenate([face_rows, wide_ids[node_count:, 0]], 0)
    rim_sel = (rim_ids[:, None] == cell_rows[None, :]).astype(jnp.bfloat16)
    face_put = (wide_ids[:node_count] == face_rows[None, :]).astype(jnp.bfloat16)
    face_take = (face_rows[:, None] == wide_ids[:node_count, 0][None, :]).astype(jnp.bfloat16)

    face_states = jnp.dot(face_take, states, preferred_element_type=jnp.float32)
    mass_potential = jnp.stack([inv_mass, potential], 1)[face_rows]
    ghost = ring(jnp.concatenate([face_states, mass_potential], 1), "dom", -1)
    field_start = jnp.concatenate([states.astype(jnp.float32), ghost[:, :state_count]], 0)
    wide_mass = jnp.concatenate([inv_mass, ghost[:, state_count]], 0)
    wide_potential = jnp.concatenate([potential, ghost[:, state_count + 1]], 0)

    def operate(field_in):
        weighted = (wide_mass[:, None] * field_in).astype(jnp.bfloat16)
        values = jnp.dot(gather_sel, weighted, preferred_element_type=jnp.float32)
        values = values.astype(jnp.bfloat16).reshape(cell_count, padded_size, state_count)
        products = jnp.einsum(
            "ij,cjb->cib", padded_matrix, values, preferred_element_type=jnp.float32
        ).reshape(-1, state_count)
        both = high_low(products)
        rim = summed_halves(jnp.dot(rim_sel, both, preferred_element_type=jnp.float32))
        from_prev = ring(rim[face_count:], "dom", 1)
        from_next = ring(rim[:face_count], "dom", -1)
        main = summed_halves(jnp.dot(scatter_sel, both, preferred_element_type=jnp.float32))
        own = main[:node_count] + summed_halves(
            jnp.dot(face_put, high_low(from_prev), preferred_element_type=jnp.float32)
        )
        summed = jnp.concatenate([own, main[node_count:] + from_next], 0)
        return wide_mass[:, None] * summed + wide_potential[:, None] * field_in

    def chebyshev_step(step, carry):
        previous, current = carry
        scaled = (operate(current) - centre * current) / half_span
        first = step == 0
        gain = jnp.where(first, 1.0, 2.0).astype(jnp.float32)
        keep = jnp.where(first, 0.0, 1.0).astype(jnp.float32)
        return current, gain * scaled - keep * previous

    previous, current = lax.fori_loop(0, POLY, chebyshev_step, (field_start, field_start))
    filtered = current[:node_count].astype(jnp.bfloat16)
    position = lax.axis_index("st") % 4

    def rows_for(member):
        return lax.dynamic_slice_in_dim(rotation, member * state_count, state_count, 0)

    across = from_partner(filtered, "st", 1)
    beside = from_partner(filtered, "st", 0)
    diagonal = from_partner(across, "st", 0)
    rotated = jnp.dot(filtered, rows_for(position), preferred_element_type=jnp.float32)
    rotated = rotated + jnp.dot(beside, rows_for(position ^ 1), preferred_element_type=jnp.float32)
    rotated = rotated + jnp.dot(across, rows_for(position ^ 2), preferred_element_type=jnp.float32)
    rotated = rotated + jnp.dot(
        diagonal, rows_for(position ^ 3), preferred_element_type=jnp.float32
    )
    return rotated


def solution(mesh):
    return jax.shard_map(
        body,
        mesh=mesh,
        in_specs=(P("dom", "st"), P("dom"), P("dom"), P(), P("dom", None), P("dom"), P(None, "st")),
        out_specs=P("dom", "st"),
        check_vma=False,
    )
```

profile of v0, /device:TPU:0, one launch (start us, length us, event | category | flops | bytes accessed | tf_op | source)
XLA Modules:
  0.0 72.3 jit_solution(1198371347643267996)
XLA Ops:
  3.3 1.4 %fusion.47 = f32[144,128]{1,0:T(8,128)S(1)} fusion(bf16[1728,128]{1,0:T(8,128)(2,1)} %param.9, s32[1728]{0:T(1024)S(1)} %add_reduce_fusion, s32[144]{0:T(256)} %param.14), kind=kOutput, calls=%fused_computation.55 | convolution fusion | flops 63949824 | bytes 523584 | tf_op jit(solution)/shard_map/dot_general | solution.py:57
  4.7 3.9 %collective-permute-start.2 = (f32[144,130]{1,0:T(8,128)S(1)}, f32[144,130]{1,0:T(8,128)S(1)}, u32[]{:S(2)}, u32[]{:S(2)}) collective-permute-start(f32[144,130]{1,0:T(8,128)S(1)} %pad_maximum_fusion.4), channel_id=1, source_target_pairs={{0,24},{8,0},{16,8},{24,16},{1,25},{9,1},{17,9},{25,17},{2,26},{10... | collective-permute-start | bytes 224648 | tf_op jit(solution)/shard_map/ppermute | solution.py:16
  9.7 2.1 %collective-permute-done.2 = f32[144,130]{1,0:T(8,128)S(1)} collective-permute-done((f32[144,130]{1,0:T(8,128)S(1)}, f32[144,130]{1,0:T(8,128)S(1)}, u32[]{:S(2)}, u32[]{:S(2)}) %collective-permute-start.2) | collective-permute-done | bytes 74912 | tf_op jit(solution)/shard_map/ppermute | solution.py:16
  12.6 48.2 %while.17 = (s32[]{:T(128)}, f32[1872,128]{1,0:T(8,128)S(1)}, f32[1872,128]{1,0:T(8,128)S(1)}, f32[1872]{0:T(1024)S(1)}, bf16[352,352]{1,0:T(8,128)(2,1)}, /*ind...) while((s32[]{:T(128)}, f32[1872,128]{1,0:T(8,128)S(1)}, ...), condition=%wide.region_1.2_spmd.clone.clone, body=%wide.region_0.1_spmd.clone.clone.sunk | while | flops 4879314944 | bytes 31196832 | solution.py:90
  12.6 4.2 %fusion.84 = bf16[2816,128]{0,1:T(8,128)(2,1)S(1)} fusion(s32[2816]{0:T(1024)S(1)} %get-tuple-element.377, f32[1872,128]{1,0:T(8,128)S(1)} %get-tuple-element.357, f32[1872]{0:T(1024)S(1)} %get-tuple-element.374), kind=kOutput, calls=%fused_computation.14.clone.1 | convolution fusion | flops 1360900096 | bytes 1698112 | tf_op jit(solution)/shard_map/while/body/eval_jaxpr/dot_general | solution.py:66
  17.1 1.5 %fusion.85 = f32[8,128,352]{1,2,0:T(8,128)S(1)} fusion(bf16[8,352,128]{2,1,0:T(8,128)(2,1)S(1)} %bitcast.39, bf16[352,352]{1,0:T(8,128)(2,1)} %get-tuple-element.375), kind=kOutput, calls=%fused_computation.39.clone.1 | convolution fusion | flops 253755392 | bytes 2410496 | tf_op jit(solution)/shard_map/while/body/eval_jaxpr/ij,cjb->cib/dot_general | solution.py:68
  19.5 3.4 %collective-permute-start = (f32[144,128]{1,0:T(8,128)S(1)}, f32[144,128]{1,0:T(8,128)S(1)}, u32[]{:S(2)}, u32[]{:S(2)}) collective-permute-start(f32[144,128]{1,0:T(8,128)S(1)} %get-tuple-element.335), channel_id=1, source_target_pairs={{0,24},{8,0},{16,8},{24,16},{1,25},{9,1},{17,9},{25,17},{2,26},{10... | collective-permute-start | bytes 221192 | tf_op jit(solution)/shard_map/while/body/eval_jaxpr/ppermute | solution.py:16
  22.9 3.0 %fusion.88 = f32[1872,256]{1,0:T(8,128)S(1)} fusion(s32[2816]{0:T(1024)S(1)} %get-tuple-element.377, bf16[2816,128]{1,0:T(8,128)(2,1)S(1)} %get-tuple-element.333, bf16[2816,128]{1,0:T(8,128)(2,1)S(1)} %get-tuple-element.334), kind=kOutput, calls=%fused_computation.17.clone.1 | convolution fusion | flops 2712461312 | bytes 3369984 | tf_op jit(solution)/shard_map/while/body/eval_jaxpr/dot_general | solution.py:75
  26.1 2.1 %collective-permute-done.1 = f32[144,128]{1,0:T(8,128)S(1)} collective-permute-done((f32[144,128]{1,0:T(8,128)S(1)}, f32[144,128]{1,0:T(8,128)S(1)}, u32[]{:S(2)}, u32[]{:S(2)}) %collective-permute-start.1) | collective-permute-done | bytes 73760 | tf_op jit(solution)/shard_map/while/body/eval_jaxpr/ppermute | solution.py:16
  28.9 1.3 %fusion.90 = f32[1872,128]{1,0:T(8,128)S(1)} fusion(f32[144,128]{1,0:T(8,128)S(1)} %slice_add_fusion.9, f32[1728,128]{1,0:T(8,128)S(1)} %fusion.89, f32[1872,128]{1,0:T(8,128)S(1)} %get-tuple-element.356, f32[1872,128]{1,0:T(8,128)S(1)} %get-tuple-element.357, f32[]{:T(128)S(6)} %select_n.50, f32[]{:T(128)S(6)} %mul.171, ...), kind=kLoop, calls=%fused_computation.32.clone.1 | loop fusion | flops 2156544 | bytes 3848840 | tf_op jit(solution)/shard_map/while/body/eval_jaxpr/sub | solution.py:88
  30.3 4.2 %fusion.84 = bf16[2816,128]{0,1:T(8,128)(2,1)S(1)} fusion(s32[2816]{0:T(1024)S(1)} %get-tuple-element.377, f32[1872,128]{1,0:T(8,128)S(1)} %get-tuple-element.357, f32[1872]{0:T(1024)S(1)} %get-tuple-element.374), kind=kOutput, calls=%fused_computation.14.clone.1 | convolution fusion | flops 1360900096 | bytes 1698112 | tf_op jit(solution)/shard_map/while/body/eval_jaxpr/dot_general | solution.py:66
  34.8 1.5 %fusion.85 = f32[8,128,352]{1,2,0:T(8,128)S(1)} fusion(bf16[8,352,128]{2,1,0:T(8,128)(2,1)S(1)} %bitcast.39, bf16[352,352]{1,0:T(8,128)(2,1)} %get-tuple-element.375), kind=kOutput, calls=%fused_computation.39.clone.1 | convolution fusion | flops 253755392 | bytes 2410496 | tf_op jit(solution)/shard_map/while/body/eval_jaxpr/ij,cjb->cib/dot_general | solution.py:68
  38.1 1.2 %collective-permute-start.1 = (f32[144,128]{1,0:T(8,128)S(1)}, f32[144,128]{1,0:T(8,128)S(1)}, u32[]{:S(2)}, u32[]{:S(2)}) collective-permute-start(f32[144,128]{1,0:T(8,128)S(1)} %get-tuple-element.336), channel_id=1, source_target_pairs={{0,8},{8,16},{16,24},{24,0},{1,9},{9,17},{17,25},{25,1},{2,10},{10... | collective-permute-start | bytes 221192 | tf_op jit(solution)/shard_map/while/body/eval_jaxpr/ppermute | solution.py:16
  39.3 3.0 %fusion.88 = f32[1872,256]{1,0:T(8,128)S(1)} fusion(s32[2816]{0:T(1024)S(1)} %get-tuple-element.377, bf16[2816,128]{1,0:T(8,128)(2,1)S(1)} %get-tuple-element.333, bf16[2816,128]{1,0:T(8,128)(2,1)S(1)} %get-tuple-element.334), kind=kOutput, calls=%fused_computation.17.clone.1 | convolution fusion | flops 2712461312 | bytes 3369984 | tf_op jit(solution)/shard_map/while/body/eval_jaxpr/dot_general | solution.py:75
  44.1 1.3 %fusion.90 = f32[1872,128]{1,0:T(8,128)S(1)} fusion(f32[144,128]{1,0:T(8,128)S(1)} %slice_add_fusion.9, f32[1728,128]{1,0:T(8,128)S(1)} %fusion.89, f32[1872,128]{1,0:T(8,128)S(1)} %get-tuple-element.356, f32[1872,128]{1,0:T(8,128)S(1)} %get-tuple-element.357, f32[]{:T(128)S(6)} %select_n.50, f32[]{:T(128)S(6)} %mul.171, ...), kind=kLoop, calls=%fused_computation.32.clone.1 | loop fusion | flops 2156544 | bytes 3848840 | tf_op jit(solution)/shard_map/while/body/eval_jaxpr/sub | solution.py:88
  45.5 4.2 %fusion.84 = bf16[2816,128]{0,1:T(8,128)(2,1)S(1)} fusion(s32[2816]{0:T(1024)S(1)} %get-tuple-element.377, f32[1872,128]{1,0:T(8,128)S(1)} %get-tuple-element.357, f32[1872]{0:T(1024)S(1)} %get-tuple-element.374), kind=kOutput, calls=%fused_computation.14.clone.1 | convolution fusion | flops 1360900096 | bytes 1698112 | tf_op jit(solution)/shard_map/while/body/eval_jaxpr/dot_general | solution.py:66
  50.1 1.5 %fusion.85 = f32[8,128,352]{1,2,0:T(8,128)S(1)} fusion(bf16[8,352,128]{2,1,0:T(8,128)(2,1)S(1)} %bitcast.39, bf16[352,352]{1,0:T(8,128)(2,1)} %get-tuple-element.375), kind=kOutput, calls=%fused_computation.39.clone.1 | convolution fusion | flops 253755392 | bytes 2410496 | tf_op jit(solution)/shard_map/while/body/eval_jaxpr/ij,cjb->cib/dot_general | solution.py:68
  53.4 1.2 %collective-permute-start.1 = (f32[144,128]{1,0:T(8,128)S(1)}, f32[144,128]{1,0:T(8,128)S(1)}, u32[]{:S(2)}, u32[]{:S(2)}) collective-permute-start(f32[144,128]{1,0:T(8,128)S(1)} %get-tuple-element.336), channel_id=1, source_target_pairs={{0,8},{8,16},{16,24},{24,0},{1,9},{9,17},{17,25},{25,1},{2,10},{10... | collective-permute-start | bytes 221192 | tf_op jit(solution)/shard_map/while/body/eval_jaxpr/ppermute | solution.py:16
  54.6 3.0 %fusion.88 = f32[1872,256]{1,0:T(8,128)S(1)} fusion(s32[2816]{0:T(1024)S(1)} %get-tuple-element.377, bf16[2816,128]{1,0:T(8,128)(2,1)S(1)} %get-tuple-element.333, bf16[2816,128]{1,0:T(8,128)(2,1)S(1)} %get-tuple-element.334), kind=kOutput, calls=%fused_computation.17.clone.1 | convolution fusion | flops 2712461312 | bytes 3369984 | tf_op jit(solution)/shard_map/while/body/eval_jaxpr/dot_general | solution.py:75
  59.3 1.3 %fusion.90 = f32[1872,128]{1,0:T(8,128)S(1)} fusion(f32[144,128]{1,0:T(8,128)S(1)} %slice_add_fusion.9, f32[1728,128]{1,0:T(8,128)S(1)} %fusion.89, f32[1872,128]{1,0:T(8,128)S(1)} %get-tuple-element.356, f32[1872,128]{1,0:T(8,128)S(1)} %get-tuple-element.357, f32[]{:T(128)S(6)} %select_n.50, f32[]{:T(128)S(6)} %mul.171, ...), kind=kLoop, calls=%fused_computation.32.clone.1 | loop fusion | flops 2156544 | bytes 3848840 | tf_op jit(solution)/shard_map/while/body/eval_jaxpr/sub | solution.py:88
  60.8 1.6 %collective-permute-start.4 = (bf16[1728,128]{1,0:T(8,128)(2,1)S(1)}, bf16[1728,128]{1,0:T(8,128)(2,1)S(1)}, u32[]{:S(2)}, u32[]{:S(2)}) collective-permute-start(bf16[1728,128]{1,0:T(8,128)(2,1)S(1)} %slice.147), channel_id=1, source_target_pairs={{0,2},{2,0},{1,3},{3,1},{4,6},{6,4},{5,7},{7,5},{8,10},{10,8},{9,1... | collective-permute-start | bytes 1327112 | tf_op jit(solution)/shard_map/ppermute | solution.py:26
  62.7 6.6 %collective-permute-done.4 = bf16[1728,128]{1,0:T(8,128)(2,1)S(1)} collective-permute-done((bf16[1728,128]{1,0:T(8,128)(2,1)S(1)}, bf16[1728,128]{1,0:T(8,128)(2,1)S(1)}, u32[]{:S(2)}, u32[]{:S(2)}) %collective-permute-start.4) | collective-permute-done | bytes 442400 | tf_op jit(solution)/shard_map/ppermute | solution.py:26
  69.9 1.2 %collective-permute-done.5 = bf16[1728,128]{1,0:T(8,128)(2,1)S(1)} collective-permute-done((bf16[1728,128]{1,0:T(8,128)(2,1)S(1)}, bf16[1728,128]{1,0:T(8,128)(2,1)S(1)}, u32[]{:S(2)}, u32[]{:S(2)}) %collective-permute-start.5) | collective-permute-done | bytes 442400 | tf_op jit(solution)/shard_map/ppermute | solution.py:26
  71.1 1.2 %convolution_add_fusion = f32[1728,128]{1,0:T(8,128)} fusion(f32[1728,128]{1,0:T(8,128)S(1)} %convolution_add_fusion.1, bf16[1728,128]{1,0:T(8,128)(2,1)S(1)} %collective-permute-done.5, bf16[512,128]{1,0:T(8,128)(2,1)S(1)} %copy-done, s32[]{:T(128)S(6)} %select_n.42), kind=kOutput, calls=%fused_computation.52 | convolution fusion | flops 56844288 | bytes 2244612 | tf_op jit(solution)/shard_map/dot_general | solution.py:103
  (85 shorter events, 15.8 us)
Async XLA Ops:
  0.0 62.4 %copy-start = (bf16[512,128]{1,0:T(8,128)(2,1)S(1)}, bf16[512,128]{1,0:T(8,128)(2,1)}, u32[]{:S(2)}) copy-start(bf16[512,128]{1,0:T(8,128)(2,1)} %param.15) | copy-start | bytes 393220
  0.0 8.7 %copy-start.1 = (bf16[1728,128]{1,0:T(8,128)(2,1)S(1)}, bf16[1728,128]{1,0:T(8,128)(2,1)}, u32[]{:S(2)}) copy-start(bf16[1728,128]{1,0:T(8,128)(2,1)} %param.9) | copy-start | bytes 1327108
  1.5 7.2 %copy-start.6 = (s32[8,343]{1,0:T(8,128)S(1)}, s32[8,343]{1,0:T(8,128)}, u32[]{:S(2)}) copy-start(s32[8,343]{1,0:T(8,128)} %param.13) | copy-start | bytes 32932
  1.5 7.3 %copy-start.2 = (bf16[343,343]{1,0:T(8,128)(2,1)S(1)}, bf16[343,343]{1,0:T(8,128)(2,1)}, u32[]{:S(2)}) copy-start(bf16[343,343]{1,0:T(8,128)(2,1)} %param.12) | copy-start | bytes 705898
  1.9 7.7 %copy-start.3 = (s32[144]{0:T(256)S(1)}, s32[144]{0:T(256)}, u32[]{:S(2)}) copy-start(s32[144]{0:T(256)} %param.14) | copy-start | bytes 1732
  4.7 7.1 %collective-permute-start.2 = (f32[144,130]{1,0:T(8,128)S(1)}, f32[144,130]{1,0:T(8,128)S(1)}, u32[]{:S(2)}, u32[]{:S(2)}) collective-permute-start(f32[144,130]{1,0:T(8,128)S(1)} %pad_maximum_fusion.4), channel_id=1, source_target_pairs={{0,24},{8,0},{16,8},{24,16},{1,25},{9,1},{17,9},{25,17},{2,26},{10... | collective-permute-start | bytes 224648 | tf_op jit(solution)/shard_map/ppermute | solution.py:16
  11.8 0.7 copy-start.4
  11.8 0.7 copy-start.5
  19.5 9.3 %collective-permute-start = (f32[144,128]{1,0:T(8,128)S(1)}, f32[144,128]{1,0:T(8,128)S(1)}, u32[]{:S(2)}, u32[]{:S(2)}) collective-permute-start(f32[144,128]{1,0:T(8,128)S(1)} %get-tuple-element.335), channel_id=1, source_target_pairs={{0,24},{8,0},{16,8},{24,16},{1,25},{9,1},{17,9},{25,17},{2,26},{10... | collective-permute-start | bytes 221192 | tf_op jit(solution)/shard_map/while/body/eval_jaxpr/ppermute | solution.py:16
  22.9 5.3 %collective-permute-start.1 = (f32[144,128]{1,0:T(8,128)S(1)}, f32[144,128]{1,0:T(8,128)S(1)}, u32[]{:S(2)}, u32[]{:S(2)}) collective-permute-start(f32[144,128]{1,0:T(8,128)S(1)} %get-tuple-element.336), channel_id=1, source_target_pairs={{0,8},{8,16},{16,24},{24,0},{1,9},{9,17},{17,25},{25,1},{2,10},{10... | collective-permute-start | bytes 221192 | tf_op jit(solution)/shard_map/while/body/eval_jaxpr/ppermute | solution.py:16
  37.3 6.8 %collective-permute-start = (f32[144,128]{1,0:T(8,128)S(1)}, f32[144,128]{1,0:T(8,128)S(1)}, u32[]{:S(2)}, u32[]{:S(2)}) collective-permute-start(f32[144,128]{1,0:T(8,128)S(1)} %get-tuple-element.335), channel_id=1, source_target_pairs={{0,24},{8,0},{16,8},{24,16},{1,25},{9,1},{17,9},{25,17},{2,26},{10... | collective-permute-start | bytes 221192 | tf_op jit(solution)/shard_map/while/body/eval_jaxpr/ppermute | solution.py:16
  38.1 5.3 %collective-permute-start.1 = (f32[144,128]{1,0:T(8,128)S(1)}, f32[144,128]{1,0:T(8,128)S(1)}, u32[]{:S(2)}, u32[]{:S(2)}) collective-permute-start(f32[144,128]{1,0:T(8,128)S(1)} %get-tuple-element.336), channel_id=1, source_target_pairs={{0,8},{8,16},{16,24},{24,0},{1,9},{9,17},{17,25},{25,1},{2,10},{10... | collective-permute-start | bytes 221192 | tf_op jit(solution)/shard_map/while/body/eval_jaxpr/ppermute | solution.py:16
  52.5 6.8 %collective-permute-start = (f32[144,128]{1,0:T(8,128)S(1)}, f32[144,128]{1,0:T(8,128)S(1)}, u32[]{:S(2)}, u32[]{:S(2)}) collective-permute-start(f32[144,128]{1,0:T(8,128)S(1)} %get-tuple-element.335), channel_id=1, source_target_pairs={{0,24},{8,0},{16,8},{24,16},{1,25},{9,1},{17,9},{25,17},{2,26},{10... | collective-permute-start | bytes 221192 | tf_op jit(solution)/shard_map/while/body/eval_jaxpr/ppermute | solution.py:16
  53.4 5.3 %collective-permute-start.1 = (f32[144,128]{1,0:T(8,128)S(1)}, f32[144,128]{1,0:T(8,128)S(1)}, u32[]{:S(2)}, u32[]{:S(2)}) collective-permute-start(f32[144,128]{1,0:T(8,128)S(1)} %get-tuple-element.336), channel_id=1, source_target_pairs={{0,8},{8,16},{16,24},{24,0},{1,9},{9,17},{17,25},{25,1},{2,10},{10... | collective-permute-start | bytes 221192 | tf_op jit(solution)/shard_map/while/body/eval_jaxpr/ppermute | solution.py:16
  60.8 8.5 %collective-permute-start.4 = (bf16[1728,128]{1,0:T(8,128)(2,1)S(1)}, bf16[1728,128]{1,0:T(8,128)(2,1)S(1)}, u32[]{:S(2)}, u32[]{:S(2)}) collective-permute-start(bf16[1728,128]{1,0:T(8,128)(2,1)S(1)} %slice.147), channel_id=1, source_target_pairs={{0,2},{2,0},{1,3},{3,1},{4,6},{6,4},{5,7},{7,5},{8,10},{10,8},{9,1... | collective-permute-start | bytes 1327112 | tf_op jit(solution)/shard_map/ppermute | solution.py:26
  62.4 6.9 %collective-permute-start.3 = (bf16[1728,128]{1,0:T(8,128)(2,1)S(1)}, bf16[1728,128]{1,0:T(8,128)(2,1)S(1)}, u32[]{:S(2)}, u32[]{:S(2)}) collective-permute-start(bf16[1728,128]{1,0:T(8,128)(2,1)S(1)} %slice.147), channel_id=1, source_target_pairs={{0,1},{1,0},{2,3},{3,2},{4,5},{5,4},{6,7},{7,6},{8,9},{9,8},{10,11... | collective-permute-start | bytes 1327112 | tf_op jit(solution)/shard_map/ppermute | solution.py:26
  69.3 1.8 %collective-permute-start.5 = (bf16[1728,128]{1,0:T(8,128)(2,1)S(1)}, bf16[1728,128]{1,0:T(8,128)(2,1)S(1)}, u32[]{:S(2)}, u32[]{:S(2)}) collective-permute-start(bf16[1728,128]{1,0:T(8,128)(2,1)S(1)} %collective-permute-done.4), channel_id=1, source_target_pairs={{0,1},{1,0},{2,3},{3,2},{4,5},{5,4},{6,7},{7,6},{8,9},{9,8},{10,11... | collective-permute-start | bytes 1327112 | tf_op jit(solution)/shard_map/ppermute | solution.py:26
where the time goes:
time: 72.8 us; the launch traced here: 72.3 us
  matrix products  32.6 us (45%)
  waiting for transfers between devices  13.9 us (19%)
  starting transfers between devices  13.2 us (18%)
  other arithmetic  6.6 us (9%)
  local copies, waits for them, and re-layouts  5.43 us (7%)
    dot_general x3, matrix products, operate(): values = jnp.dot(gather_sel, weighted, preferred_element_type=jnp.float32)  12.5 us
    ppermute x7, starting transfers between devices, ring(): return lax.ppermute(block, axis, route)  11.5 us
    dot_general x3, matrix products, operate(): jnp.dot(scatter_sel, both, preferred_element_type=jnp.float32)  9.05 us
    ppermute x3, waiting for transfers between devices, from_partner(): return lax.ppermute(block, axis, route)  7.87 us
    ppermute x7, waiting for transfers between devices, ring(): return lax.ppermute(block, axis, route)  6.06 us
    dot_general x3, matrix products, operate(): jnp.einsum('ij,cjb->cib', padded_matrix, values, preferred_element_type=j...  4.47 us
    sub x3, other arithmetic, chebyshev_step(): return (current, gain * scaled - keep * previous)  3.86 us
    dot_general x3, matrix products, operate(): jnp.dot(rim_sel, both, preferred_element_type=jnp.float32)  1.89 us
  transfers between devices with their start and end apart: 10, of which 6 were waited for; matrix products, arithmetic and copies ran while one was open for 18% of the time, Pallas kernels for 0%

commit v1 on v0

--- a/solution.py
+++ b/solution.py
@@ -87,23 +87,58 @@
         keep = jnp.where(first, 0.0, 1.0).astype(jnp.float32)
         return current, gain * scaled - keep * previous
 
-    previous, current = lax.fori_loop(0, POLY, chebyshev_step, (field_start, field_start))
-    filtered = current[:node_count].astype(jnp.bfloat16)
+    previous, current = lax.fori_loop(
+        0, POLY - 1, chebyshev_step, (field_start, field_start)
+    )
+
+    weighted = (wide_mass[:, None] * current).astype(jnp.bfloat16)
+    values = jnp.dot(gather_sel, weighted, preferred_element_type=jnp.float32)
+    values = values.astype(jnp.bfloat16).reshape(cell_count, padded_size, state_count)
+    products = jnp.einsum(
+        "ij,cjb->cib", padded_matrix, values, preferred_element_type=jnp.float32
+    ).reshape(-1, state_count)
+    both = high_low(products)
+    ghost_part = summed_halves(
+        jnp.dot(rim_sel[face_count:], both, preferred_element_type=jnp.float32)
+    )
+    from_prev = high_low(ring(ghost_part, "dom", 1))
+    chunks = 2 if node_count % 32 == 0 else 1
+    chunk = node_count // chunks
     position = lax.axis_index("st") % 4
 
     def rows_for(member):
         return lax.dynamic_slice_in_dim(rotation, member * state_count, state_count, 0)
 
-    across = from_partner(filtered, "st", 1)
-    beside = from_partner(filtered, "st", 0)
-    diagonal = from_partner(across, "st", 0)
-    rotated = jnp.dot(filtered, rows_for(position), preferred_element_type=jnp.float32)
-    rotated = rotated + jnp.dot(beside, rows_for(position ^ 1), preferred_element_type=jnp.float32)
-    rotated = rotated + jnp.dot(across, rows_for(position ^ 2), preferred_element_type=jnp.float32)
-    rotated = rotated + jnp.dot(
-        diagonal, rows_for(position ^ 3), preferred_element_type=jnp.float32
-    )
-    return rotated
+    pieces = []
+    chunk_both = both
+    for part in range(chunks):
+        rows = slice(part * chunk, (part + 1) * chunk)
+        main = summed_halves(
+            jnp.dot(scatter_sel[rows], chunk_both, preferred_element_type=jnp.float32)
+        )
+        own = main + summed_halves(
+            jnp.dot(face_put[rows], from_prev, preferred_element_type=jnp.float32)
+        )
+        field = current[rows]
+        applied = wide_mass[rows, None] * own + wide_potential[rows, None] * field
+        scaled = (applied - centre * field) / half_span
+        filtered = (2.0 * scaled - previous[rows]).astype(jnp.bfloat16)
+        filtered, chunk_both = lax.optimization_barrier((filtered, both))
+        across = from_partner(filtered, "st", 1)
+        beside = from_partner(filtered, "st", 0)
+        diagonal = from_partner(across, "st", 0)
+        rotated = jnp.dot(filtered, rows_for(position), preferred_element_type=jnp.float32)
+        rotated = rotated + jnp.dot(
+            beside, rows_for(position ^ 1), preferred_element_type=jnp.float32
+        )
+        rotated = rotated + jnp.dot(
+            across, rows_for(position ^ 2), preferred_element_type=jnp.float32
+        )
+        rotated = rotated + jnp.dot(
+            diagonal, rows_for(position ^ 3), preferred_element_type=jnp.float32
+        )
+        pieces.append(rotated)
+    return jnp.concatenate(pieces, 0)
 
 
 def solution(mesh):

time: 72.8 us -> 74.9 us (1.029)
  other arithmetic: 6.6 us -> 13.8 us
  waiting for transfers between devices: 13.9 us -> 10 us
  matrix products: 32.6 us -> 31 us
    dot_general x0 -> x7, matrix products: none -> 8.44 us  [the longest x1 4.06 us: body(): values = jnp.dot(gather_sel, weighted, preferred_element_type=jnp.float32)]
    eq x0 -> x2, other arithmetic: none -> 6.98 us  [the longest x1 5.91 us: body(): scatter_sel = (wide_ids == cell_rows[None, :]).astype(jnp.bfloat16)]
    dot_general x3 -> x2, matrix products: 12.5 us -> 8.35 us  [operate(): values = jnp.dot(gather_sel, weighted, preferred_element_type=jnp.float32)]
    ppermute x7 -> x6, waiting for transfers between devices: 6.06 us -> 1.9 us  [ring(): return lax.ppermute(block, axis, route)]
    dot_general x3 -> x2, matrix products: 9.05 us -> 6.04 us  [operate(): jnp.dot(scatter_sel, both, preferred_element_type=jnp.float32)]
    dot_general x3 -> x2, matrix products: 4.47 us -> 2.98 us  [operate(): jnp.einsum('ij,cjb->cib', padded_matrix, values, preferred_element_type=j...]
    sub x3 -> x2, other arithmetic: 3.86 us -> 2.58 us  [chebyshev_step(): return (current, gain * scaled - keep * previous)]
    concatenate x0 -> x2, other arithmetic: none -> 1.13 us  [the longest x1 0.97 us: body(): return jnp.concatenate(pieces, 0)]
  transfers between devices with their start and end apart: 10 -> 12, of which waited for: 6 -> 4; matrix products, arithmetic and copies ran while one was open for 18% -> 28% of each run, Pallas kernels for 0% -> 0%
where the time goes in v1:
time: 74.9 us; the launch traced here: 74.6 us
  matrix products  31 us (41%)
  other arithmetic  13.8 us (18%)
  starting transfers between devices  12.8 us (17%)
  waiting for transfers between devices  10 us (13%)
  local copies, waits for them, and re-layouts  6 us (8%)
    ppermute x6, starting transfers between devices, ring(): return lax.ppermute(block, axis, route)  10.4 us
    dot_general x2, matrix products, operate(): values = jnp.dot(gather_sel, weighted, preferred_element_type=jnp.float32)  8.35 us
    ppermute x6, waiting for transfers between devices, from_partner(): return lax.ppermute(block, axis, route)  8.13 us
    dot_general x2, matrix products, operate(): jnp.dot(scatter_sel, both, preferred_element_type=jnp.float32)  6.04 us
    eq x1, other arithmetic, body(): scatter_sel = (wide_ids == cell_rows[None, :]).astype(jnp.bfloat16)  5.91 us
    dot_general x1, matrix products, body(): values = jnp.dot(gather_sel, weighted, preferred_element_type=jnp.float32)  4.06 us
    dot_general x2, matrix products, operate(): jnp.einsum('ij,cjb->cib', padded_matrix, values, preferred_element_type=j...  2.98 us
    dot_general x2, matrix products, body(): jnp.dot(scatter_sel[rows], chunk_both, preferred_element_type=jnp.float32)  2.87 us
  transfers between devices with their start and end apart: 12, of which 4 were waited for; matrix products, arithmetic and copies ran while one was open for 28% of the time, Pallas kernels for 0%

profile of v1, /device:TPU:0, one launch (start us, length us, event | category | flops | bytes accessed | tf_op | source)
XLA Modules:
  0.0 74.6 jit_solution(3566971828076703504)
XLA Ops:
  2.6 1.4 %fusion.57 = f32[144,128]{1,0:T(8,128)S(1)} fusion(bf16[1728,128]{1,0:T(8,128)(2,1)} %param.9, s32[1728]{0:T(1024)S(1)} %add_reduce_fusion, s32[144]{0:T(256)} %param.14), kind=kOutput, calls=%fused_computation.73 | convolution fusion | flops 63949824 | bytes 523584 | tf_op jit(solution)/shard_map/dot_general | solution.py:57
  4.7 3.9 %collective-permute-start.2 = (f32[144,130]{1,0:T(8,128)S(1)}, f32[144,130]{1,0:T(8,128)S(1)}, u32[]{:S(2)}, u32[]{:S(2)}) collective-permute-start(f32[144,130]{1,0:T(8,128)S(1)} %pad_maximum_fusion.6), channel_id=1, source_target_pairs={{0,24},{8,0},{16,8},{24,16},{1,25},{9,1},{17,9},{25,17},{2,26},{10... | collective-permute-start | bytes 224648 | tf_op jit(solution)/shard_map/ppermute | solution.py:16
  8.7 1.1 %broadcast_compare_fusion = pred[1728,144]{1,0:T(32,128)(4,1)} fusion(s32[144]{0:T(256)S(1)} %copy-done.8, s32[1728]{0:T(1024)S(1)} %add_reduce_fusion), kind=kLoop, calls=%fused_computation.78 | loop fusion | flops 248832 | bytes 256320 | tf_op jit(solution)/shard_map/eq | solution.py:54
  9.9 5.9 %iota_compare_fusion.4 = pred[1872,2816]{1,0:T(8,128)(4,1)} fusion(s32[2816]{0:T(1024)S(1)} %eq.81), kind=kLoop, calls=%fused_computation.54 | loop fusion | flops 5271552 | bytes 5282816 | tf_op jit(solution)/shard_map/eq | solution.py:51
  17.2 30.8 %while.17 = (s32[]{:T(128)}, f32[1872,128]{1,0:T(8,128)S(1)}, f32[1872,128]{1,0:T(8,128)S(1)}, f32[1872]{0:T(1024)S(1)}, bf16[352,352]{1,0:T(8,128)(2,1)}, /*ind...) while((s32[]{:T(128)}, f32[1872,128]{1,0:T(8,128)S(1)}, ...), condition=%wide.region_1.2_spmd.clone.clone, body=%wide.region_0.1_spmd.clone.clone.sunk | while | flops 4879314944 | bytes 31196824 | solution.py:90
  17.3 4.2 %fusion.139 = bf16[2816,128]{0,1:T(8,128)(2,1)S(1)} fusion(s32[2816]{0:T(1024)S(1)} %get-tuple-element.395, f32[1872,128]{1,0:T(8,128)S(1)} %get-tuple-element.375, f32[1872]{0:T(1024)S(1)} %get-tuple-element.392), kind=kOutput, calls=%fused_computation.14.clone.1 | convolution fusion | flops 1360900096 | bytes 1698112 | tf_op jit(solution)/shard_map/while/body/eval_jaxpr/dot_general | solution.py:66
  21.9 1.5 %fusion.140 = f32[8,128,352]{1,2,0:T(8,128)S(1)} fusion(bf16[8,352,128]{2,1,0:T(8,128)(2,1)S(1)} %bitcast.55, bf16[352,352]{1,0:T(8,128)(2,1)} %get-tuple-element.393), kind=kOutput, calls=%fused_computation.39.clone.1 | convolution fusion | flops 253755392 | bytes 2410496 | tf_op jit(solution)/shard_map/while/body/eval_jaxpr/ij,cjb->cib/dot_general | solution.py:68
  24.4 2.9 %collective-permute-start = (f32[144,128]{1,0:T(8,128)S(1)}, f32[144,128]{1,0:T(8,128)S(1)}, u32[]{:S(2)}, u32[]{:S(2)}) collective-permute-start(f32[144,128]{1,0:T(8,128)S(1)} %get-tuple-element.353), channel_id=1, source_target_pairs={{0,24},{8,0},{16,8},{24,16},{1,25},{9,1},{17,9},{25,17},{2,26},{10... | collective-permute-start | bytes 221192 | tf_op jit(solution)/shard_map/while/body/eval_jaxpr/ppermute | solution.py:16
  27.3 3.0 %fusion.143 = f32[1872,256]{1,0:T(8,128)S(1)} fusion(s32[2816]{0:T(1024)S(1)} %get-tuple-element.395, bf16[2816,128]{1,0:T(8,128)(2,1)S(1)} %get-tuple-element.351, bf16[2816,128]{1,0:T(8,128)(2,1)S(1)} %get-tuple-element.352), kind=kOutput, calls=%fused_computation.17.clone.1 | convolution fusion | flops 2712461312 | bytes 3369984 | tf_op jit(solution)/shard_map/while/body/eval_jaxpr/dot_general | solution.py:75
  31.1 1.3 %fusion.145 = f32[1872,128]{1,0:T(8,128)S(1)} fusion(f32[144,128]{1,0:T(8,128)S(1)} %slice_add_fusion.14, f32[1728,128]{1,0:T(8,128)S(1)} %fusion.144, f32[1872,128]{1,0:T(8,128)S(1)} %get-tuple-element.374, f32[1872,128]{1,0:T(8,128)S(1)} %get-tuple-element.375, f32[]{:T(128)S(6)} %select_n.54, f32[]{:T(128)S(6)} %mul.292, ...), kind=kLoop, calls=%fused_computation.32.clone.1 | loop fusion | flops 2156544 | bytes 3848840 | tf_op jit(solution)/shard_map/while/body/eval_jaxpr/sub | solution.py:88
  32.6 4.2 %fusion.139 = bf16[2816,128]{0,1:T(8,128)(2,1)S(1)} fusion(s32[2816]{0:T(1024)S(1)} %get-tuple-element.395, f32[1872,128]{1,0:T(8,128)S(1)} %get-tuple-element.375, f32[1872]{0:T(1024)S(1)} %get-tuple-element.392), kind=kOutput, calls=%fused_computation.14.clone.1 | convolution fusion | flops 1360900096 | bytes 1698112 | tf_op jit(solution)/shard_map/while/body/eval_jaxpr/dot_general | solution.py:66
  37.1 1.5 %fusion.140 = f32[8,128,352]{1,2,0:T(8,128)S(1)} fusion(bf16[8,352,128]{2,1,0:T(8,128)(2,1)S(1)} %bitcast.55, bf16[352,352]{1,0:T(8,128)(2,1)} %get-tuple-element.393), kind=kOutput, calls=%fused_computation.39.clone.1 | convolution fusion | flops 253755392 | bytes 2410496 | tf_op jit(solution)/shard_map/while/body/eval_jaxpr/ij,cjb->cib/dot_general | solution.py:68
  40.0 2.5 %collective-permute-start = (f32[144,128]{1,0:T(8,128)S(1)}, f32[144,128]{1,0:T(8,128)S(1)}, u32[]{:S(2)}, u32[]{:S(2)}) collective-permute-start(f32[144,128]{1,0:T(8,128)S(1)} %get-tuple-element.353), channel_id=1, source_target_pairs={{0,24},{8,0},{16,8},{24,16},{1,25},{9,1},{17,9},{25,17},{2,26},{10... | collective-permute-start | bytes 221192 | tf_op jit(solution)/shard_map/while/body/eval_jaxpr/ppermute | solution.py:16
  42.5 3.0 %fusion.143 = f32[1872,256]{1,0:T(8,128)S(1)} fusion(s32[2816]{0:T(1024)S(1)} %get-tuple-element.395, bf16[2816,128]{1,0:T(8,128)(2,1)S(1)} %get-tuple-element.351, bf16[2816,128]{1,0:T(8,128)(2,1)S(1)} %get-tuple-element.352), kind=kOutput, calls=%fused_computation.17.clone.1 | convolution fusion | flops 2712461312 | bytes 3369984 | tf_op jit(solution)/shard_map/while/body/eval_jaxpr/dot_general | solution.py:75
  46.3 1.3 %fusion.145 = f32[1872,128]{1,0:T(8,128)S(1)} fusion(f32[144,128]{1,0:T(8,128)S(1)} %slice_add_fusion.14, f32[1728,128]{1,0:T(8,128)S(1)} %fusion.144, f32[1872,128]{1,0:T(8,128)S(1)} %get-tuple-element.374, f32[1872,128]{1,0:T(8,128)S(1)} %get-tuple-element.375, f32[]{:T(128)S(6)} %select_n.54, f32[]{:T(128)S(6)} %mul.292, ...), kind=kLoop, calls=%fused_computation.32.clone.1 | loop fusion | flops 2156544 | bytes 3848840 | tf_op jit(solution)/shard_map/while/body/eval_jaxpr/sub | solution.py:88
  48.0 4.1 %fusion.53 = bf16[2816,128]{1,0:T(8,128)(2,1)S(1)} fusion(s32[2816]{0:T(1024)S(1)} %get-tuple-element.426, f32[1872,128]{1,0:T(8,128)S(1)} %get-tuple-element.178, f32[1872]{0:T(1024)S(1)} %get-tuple-element.414), kind=kOutput, calls=%fused_computation.60 | convolution fusion | flops 1355628544 | bytes 1698112 | tf_op jit(solution)/shard_map/dot_general | solution.py:95
  53.8 1.3 %copy-done.1 = pred[1872,2816]{1,0:T(8,128)(4,1)S(1)} copy-done((pred[1872,2816]{1,0:T(8,128)(4,1)S(1)}, pred[1872,2816]{1,0:T(8,128)(4,1)}, u32[]{:S(2)}) %copy-start.1) | copy-done | bytes 5271576
  55.1 1.4 %fusion.51 = f32[864,256]{1,0:T(8,128)S(1)} fusion(pred[1872,2816]{1,0:T(8,128)(4,1)S(1)} %copy-done.1, bf16[2816,128]{1,0:T(8,128)(2,1)S(1)} %get-tuple-element.273, bf16[2816,128]{1,0:T(8,128)(2,1)S(1)} %get-tuple-element.272), kind=kOutput, calls=%fused_computation.58 | convolution fusion | flops 1248591872 | bytes 4759552 | tf_op jit(solution)/shard_map/dot_general | solution.py:117
  56.7 1.9 %collective-permute-done.3 = f32[144,128]{1,0:T(8,128)S(1)} collective-permute-done((f32[144,128]{1,0:T(8,128)S(1)}, f32[144,128]{1,0:T(8,128)S(1)}, u32[]{:S(2)}, u32[]{:S(2)}) %collective-permute-start.3) | collective-permute-done | bytes 73760 | tf_op jit(solution)/shard_map/ppermute | solution.py:16
  59.3 1.6 %collective-permute-start.5 = (bf16[864,128]{1,0:T(8,128)(2,1)S(1)}, bf16[864,128]{1,0:T(8,128)(2,1)S(1)}, u32[]{:S(2)}, u32[]{:S(2)}) collective-permute-start(bf16[864,128]{1,0:T(8,128)(2,1)S(1)} %fusion.81), channel_id=1, source_target_pairs={{0,2},{2,0},{1,3},{3,1},{4,6},{6,4},{5,7},{7,5},{8,10},{10,8},{9,1... | collective-permute-start | bytes 663560 | tf_op jit(solution)/shard_map/ppermute | solution.py:26
  61.2 1.4 %fusion.49 = f32[864,256]{1,0:T(8,128)S(1)} fusion(bf16[2816,256]{1,0:T(8,128)(2,1)S(1)} %pad_maximum_fusion.3, pred[1872,2816]{1,0:T(8,128)(4,1)S(1)} %copy-done.1), kind=kOutput, calls=%fused_computation.56 | convolution fusion | flops 1245708288 | bytes 4759552 | tf_op jit(solution)/shard_map/dot_general | solution.py:117
  64.2 3.5 %collective-permute-done.5 = bf16[864,128]{1,0:T(8,128)(2,1)S(1)} collective-permute-done((bf16[864,128]{1,0:T(8,128)(2,1)S(1)}, bf16[864,128]{1,0:T(8,128)(2,1)S(1)}, u32[]{:S(2)}, u32[]{:S(2)}) %collective-permute-start.5) | collective-permute-done | bytes 221216 | tf_op jit(solution)/shard_map/ppermute | solution.py:26
  67.6 4.3 %collective-permute-done.8 = bf16[864,128]{1,0:T(8,128)(2,1)S(1)} collective-permute-done((bf16[864,128]{1,0:T(8,128)(2,1)S(1)}, bf16[864,128]{1,0:T(8,128)(2,1)S(1)}, u32[]{:S(2)}, u32[]{:S(2)}) %collective-permute-start.8) | collective-permute-done | bytes 221216 | tf_op jit(solution)/shard_map/ppermute | solution.py:26
  73.6 1.0 %pad_maximum_fusion.5 = f32[1728,128]{1,0:T(8,128)} fusion(f32[864,128]{1,0:T(8,128)S(1)} %convolution_add_fusion, f32[864,128]{1,0:T(8,128)S(1)} %convolution_add_fusion.3), kind=kLoop, calls=%fused_computation.77 | loop fusion | flops 221184 | bytes 1769472 | tf_op jit(solution)/shard_map/concatenate | solution.py:141
  (100 shorter events, 15.5 us)
Async XLA Ops:
  0.0 63.7 %copy-start = (bf16[512,128]{1,0:T(8,128)(2,1)S(1)}, bf16[512,128]{1,0:T(8,128)(2,1)}, u32[]{:S(2)}) copy-start(bf16[512,128]{1,0:T(8,128)(2,1)} %param.15) | copy-start | bytes 393220
  0.0 8.6 %copy-start.5 = (bf16[1728,128]{1,0:T(8,128)(2,1)S(1)}, bf16[1728,128]{1,0:T(8,128)(2,1)}, u32[]{:S(2)}) copy-start(bf16[1728,128]{1,0:T(8,128)(2,1)} %param.9) | copy-start | bytes 1327108
  1.5 7.2 %copy-start.8 = (s32[144]{0:T(256)S(1)}, s32[144]{0:T(256)}, u32[]{:S(2)}) copy-start(s32[144]{0:T(256)} %param.14) | copy-start | bytes 1732
  1.9 7.9 %copy-start.6 = (f32[1728]{0:T(1024)S(1)}, f32[1728]{0:T(1024)}, u32[]{:S(2)}) copy-start(f32[1728]{0:T(1024)} %param.11) | copy-start | bytes 20740
  1.9 7.9 %copy-start.7 = (f32[1728]{0:T(1024)S(1)}, f32[1728]{0:T(1024)}, u32[]{:S(2)}) copy-start(f32[1728]{0:T(1024)} %param.10) | copy-start | bytes 20740
  1.9 8.0 %copy-start.9 = (s32[8,343]{1,0:T(8,128)S(1)}, s32[8,343]{1,0:T(8,128)}, u32[]{:S(2)}) copy-start(s32[8,343]{1,0:T(8,128)} %param.13) | copy-start | bytes 32932
  4.7 12.1 %collective-permute-start.2 = (f32[144,130]{1,0:T(8,128)S(1)}, f32[144,130]{1,0:T(8,128)S(1)}, u32[]{:S(2)}, u32[]{:S(2)}) collective-permute-start(f32[144,130]{1,0:T(8,128)S(1)} %pad_maximum_fusion.6), channel_id=1, source_target_pairs={{0,24},{8,0},{16,8},{24,16},{1,25},{9,1},{17,9},{25,17},{2,26},{10... | collective-permute-start | bytes 224648 | tf_op jit(solution)/shard_map/ppermute | solution.py:16
  9.9 6.1 %copy-start.3 = (bf16[343,343]{1,0:T(8,128)(2,1)S(1)}, bf16[343,343]{1,0:T(8,128)(2,1)}, u32[]{:S(2)}) copy-start(bf16[343,343]{1,0:T(8,128)(2,1)} %param.12) | copy-start | bytes 705898
  24.3 6.1 %collective-permute-start.1 = (f32[144,128]{1,0:T(8,128)S(1)}, f32[144,128]{1,0:T(8,128)S(1)}, u32[]{:S(2)}, u32[]{:S(2)}) collective-permute-start(f32[144,128]{1,0:T(8,128)S(1)} %get-tuple-element.354), channel_id=1, source_target_pairs={{0,8},{8,16},{16,24},{24,0},{1,9},{9,17},{17,25},{25,1},{2,10},{10... | collective-permute-start | bytes 221192 | tf_op jit(solution)/shard_map/while/body/eval_jaxpr/ppermute | solution.py:16
  24.4 6.7 %collective-permute-start = (f32[144,128]{1,0:T(8,128)S(1)}, f32[144,128]{1,0:T(8,128)S(1)}, u32[]{:S(2)}, u32[]{:S(2)}) collective-permute-start(f32[144,128]{1,0:T(8,128)S(1)} %get-tuple-element.353), channel_id=1, source_target_pairs={{0,24},{8,0},{16,8},{24,16},{1,25},{9,1},{17,9},{25,17},{2,26},{10... | collective-permute-start | bytes 221192 | tf_op jit(solution)/shard_map/while/body/eval_jaxpr/ppermute | solution.py:16
  39.5 6.1 %collective-permute-start.1 = (f32[144,128]{1,0:T(8,128)S(1)}, f32[144,128]{1,0:T(8,128)S(1)}, u32[]{:S(2)}, u32[]{:S(2)}) collective-permute-start(f32[144,128]{1,0:T(8,128)S(1)} %get-tuple-element.354), channel_id=1, source_target_pairs={{0,8},{8,16},{16,24},{24,0},{1,9},{9,17},{17,25},{25,1},{2,10},{10... | collective-permute-start | bytes 221192 | tf_op jit(solution)/shard_map/while/body/eval_jaxpr/ppermute | solution.py:16
  40.0 6.3 %collective-permute-start = (f32[144,128]{1,0:T(8,128)S(1)}, f32[144,128]{1,0:T(8,128)S(1)}, u32[]{:S(2)}, u32[]{:S(2)}) collective-permute-start(f32[144,128]{1,0:T(8,128)S(1)} %get-tuple-element.353), channel_id=1, source_target_pairs={{0,24},{8,0},{16,8},{24,16},{1,25},{9,1},{17,9},{25,17},{2,26},{10... | collective-permute-start | bytes 221192 | tf_op jit(solution)/shard_map/while/body/eval_jaxpr/ppermute | solution.py:16
  48.0 4.1 %copy-start.4 = (bf16[343,343]{1,0:T(8,128)(2,1)S(1)}, bf16[343,343]{1,0:T(8,128)(2,1)}, u32[]{:S(2)}) copy-start(bf16[343,343]{1,0:T(8,128)(2,1)} %param.12) | copy-start | bytes 705898
  52.6 2.5 %copy-start.1 = (pred[1872,2816]{1,0:T(8,128)(4,1)S(1)}, pred[1872,2816]{1,0:T(8,128)(4,1)}, u32[]{:S(2)}) copy-start(pred[1872,2816]{1,0:T(8,128)(4,1)} %iota_compare_fusion.4) | copy-start | bytes 15814660
  53.3 5.3 %collective-permute-start.3 = (f32[144,128]{1,0:T(8,128)S(1)}, f32[144,128]{1,0:T(8,128)S(1)}, u32[]{:S(2)}, u32[]{:S(2)}) collective-permute-start(f32[144,128]{1,0:T(8,128)S(1)} %slice_add_fusion.8), channel_id=1, source_target_pairs={{0,8},{8,16},{16,24},{24,0},{1,9},{9,17},{17,25},{25,1},{2,10},{10... | collective-permute-start | bytes 221192 | tf_op jit(solution)/shard_map/ppermute | solution.py:16
  56.5 2.1 %copy-start.2 = (pred[1728,144]{1,0:T(32,128)(4,1)S(1)}, pred[1728,144]{1,0:T(32,128)(4,1)}, u32[]{:S(2)}) copy-start(pred[1728,144]{1,0:T(32,128)(4,1)} %broadcast_compare_fusion) | copy-start | bytes 746500
  59.2 12.7 %collective-permute-start.4 = (bf16[864,128]{1,0:T(8,128)(2,1)S(1)}, bf16[864,128]{1,0:T(8,128)(2,1)S(1)}, u32[]{:S(2)}, u32[]{:S(2)}) collective-permute-start(bf16[864,128]{1,0:T(8,128)(2,1)S(1)} %fusion.81), channel_id=1, source_target_pairs={{0,1},{1,0},{2,3},{3,2},{4,5},{5,4},{6,7},{7,6},{8,9},{9,8},{10,11... | collective-permute-start | bytes 663560 | tf_op jit(solution)/shard_map/ppermute | solution.py:26
  59.3 8.3 %collective-permute-start.5 = (bf16[864,128]{1,0:T(8,128)(2,1)S(1)}, bf16[864,128]{1,0:T(8,128)(2,1)S(1)}, u32[]{:S(2)}, u32[]{:S(2)}) collective-permute-start(bf16[864,128]{1,0:T(8,128)(2,1)S(1)} %fusion.81), channel_id=1, source_target_pairs={{0,2},{2,0},{1,3},{3,1},{4,6},{6,4},{5,7},{7,5},{8,10},{10,8},{9,1... | collective-permute-start | bytes 663560 | tf_op jit(solution)/shard_map/ppermute | solution.py:26
  63.0 9.3 %collective-permute-start.7 = (bf16[864,128]{1,0:T(8,128)(2,1)S(1)}, bf16[864,128]{1,0:T(8,128)(2,1)S(1)}, u32[]{:S(2)}, u32[]{:S(2)}) collective-permute-start(bf16[864,128]{1,0:T(8,128)(2,1)S(1)} %fusion.74), channel_id=1, source_target_pairs={{0,1},{1,0},{2,3},{3,2},{4,5},{5,4},{6,7},{7,6},{8,9},{9,8},{10,11... | collective-permute-start | bytes 663560 | tf_op jit(solution)/shard_map/ppermute | solution.py:26
  63.3 8.6 %collective-permute-start.8 = (bf16[864,128]{1,0:T(8,128)(2,1)S(1)}, bf16[864,128]{1,0:T(8,128)(2,1)S(1)}, u32[]{:S(2)}, u32[]{:S(2)}) collective-permute-start(bf16[864,128]{1,0:T(8,128)(2,1)S(1)} %fusion.74), channel_id=1, source_target_pairs={{0,2},{2,0},{1,3},{3,1},{4,6},{6,4},{5,7},{7,5},{8,10},{10,8},{9,1... | collective-permute-start | bytes 663560 | tf_op jit(solution)/shard_map/ppermute | solution.py:26
  67.6 5.2 %collective-permute-start.6 = (bf16[864,128]{1,0:T(8,128)(2,1)S(1)}, bf16[864,128]{1,0:T(8,128)(2,1)S(1)}, u32[]{:S(2)}, u32[]{:S(2)}) collective-permute-start(bf16[864,128]{1,0:T(8,128)(2,1)S(1)} %collective-permute-done.5), channel_id=1, source_target_pairs={{0,1},{1,0},{2,3},{3,2},{4,5},{5,4},{6,7},{7,6},{8,9},{9,8},{10,11... | collective-permute-start | bytes 663560 | tf_op jit(solution)/shard_map/ppermute | solution.py:26
  71.9 1.5 %collective-permute-start.9 = (bf16[864,128]{1,0:T(8,128)(2,1)S(1)}, bf16[864,128]{1,0:T(8,128)(2,1)S(1)}, u32[]{:S(2)}, u32[]{:S(2)}) collective-permute-start(bf16[864,128]{1,0:T(8,128)(2,1)S(1)} %collective-permute-done.8), channel_id=1, source_target_pairs={{0,1},{1,0},{2,3},{3,2},{4,5},{5,4},{6,7},{7,6},{8,9},{9,8},{10,11... | collective-permute-start | bytes 663560 | tf_op jit(solution)/shard_map/ppermute | solution.py:26

commit v2 on v0

--- a/solution.py
+++ b/solution.py
@@ -55,15 +55,16 @@
     face_take = (face_rows[:, None] == wide_ids[:node_count, 0][None, :]).astype(jnp.bfloat16)
 
     face_states = jnp.dot(face_take, states, preferred_element_type=jnp.float32)
-    mass_potential = jnp.stack([inv_mass, potential], 1)[face_rows]
-    ghost = ring(jnp.concatenate([face_states, mass_potential], 1), "dom", -1)
-    field_start = jnp.concatenate([states.astype(jnp.float32), ghost[:, :state_count]], 0)
-    wide_mass = jnp.concatenate([inv_mass, ghost[:, state_count]], 0)
-    wide_potential = jnp.concatenate([potential, ghost[:, state_count + 1]], 0)
+    face_mass_potential = jnp.stack([inv_mass, potential], 0)[:, face_rows]
+    ghost_states, ghost_mass_potential = ring((face_states, face_mass_potential), "dom", -1)
+    field_start = jnp.concatenate([states.astype(jnp.float32), ghost_states], 0)
+    wide_mass = jnp.concatenate([inv_mass, ghost_mass_potential[0]], 0)
+    wide_potential = jnp.concatenate([potential, ghost_mass_potential[1]], 0)
 
-    def operate(field_in):
-        weighted = (wide_mass[:, None] * field_in).astype(jnp.bfloat16)
-        values = jnp.dot(gather_sel, weighted, preferred_element_type=jnp.float32)
+    def operate(field_in, values=None):
+        if values is None:
+            weighted = (wide_mass[:, None] * field_in).astype(jnp.bfloat16)
+            values = jnp.dot(gather_sel, weighted, preferred_element_type=jnp.float32)
         values = values.astype(jnp.bfloat16).reshape(cell_count, padded_size, state_count)
         products = jnp.einsum(
             "ij,cjb->cib", padded_matrix, values, preferred_element_type=jnp.float32
@@ -87,7 +88,13 @@
         keep = jnp.where(first, 0.0, 1.0).astype(jnp.float32)
         return current, gain * scaled - keep * previous
 
-    previous, current = lax.fori_loop(0, POLY, chebyshev_step, (field_start, field_start))
+    local_weighted = (inv_mass[:, None] * states.astype(jnp.float32)).astype(jnp.bfloat16)
+    ghost_weighted = (ghost_mass_potential[0][:, None] * ghost_states).astype(jnp.bfloat16)
+    first_values = jnp.dot(
+        gather_sel[:, :node_count], local_weighted, preferred_element_type=jnp.float32
+    ) + jnp.dot(gather_sel[:, node_count:], ghost_weighted, preferred_element_type=jnp.float32)
+    first = (operate(field_start, first_values) - centre * field_start) / half_span
+    previous, current = lax.fori_loop(1, POLY, chebyshev_step, (field_start, first))
     filtered = current[:node_count].astype(jnp.bfloat16)
     position = lax.axis_index("st") % 4
 
@@ -99,6 +106,7 @@
     diagonal = from_partner(across, "st", 0)
     rotated = jnp.dot(filtered, rows_for(position), preferred_element_type=jnp.float32)
     rotated = rotated + jnp.dot(beside, rows_for(position ^ 1), preferred_element_type=jnp.float32)
+    rotated = lax.optimization_barrier(rotated)
     rotated = rotated + jnp.dot(across, rows_for(position ^ 2), preferred_element_type=jnp.float32)
     rotated = rotated + jnp.dot(
         diagonal, rows_for(position ^ 3), preferred_element_type=jnp.float32

time: 72.8 us -> 78 us (1.071)
  matrix products: 32.6 us -> 35.9 us
  other arithmetic: 6.6 us -> 9.46 us
  waiting for transfers between devices: 13.9 us -> 11.4 us
  starting transfers between devices: 13.2 us -> 15.2 us
    dot_general x0 -> x2, matrix products: none -> 7.32 us  [the longest x1 4.64 us: body(): jnp.dot(gather_sel[:, :node_count], local_weighted, preferred_element_typ...]
    dot_general x3 -> x2, matrix products: 12.5 us -> 8.35 us  [operate(): values = jnp.dot(gather_sel, weighted, preferred_element_type=jnp.float32)]
    ppermute x7 -> x8, waiting for transfers between devices: 6.06 us -> 2.29 us  [ring(): return lax.ppermute(block, axis, route)]
    eq x0 -> x1, other arithmetic: none -> 3.08 us  [body(): cell_rows[:, None] == wide_ids[:, 0][None, :]]
    ppermute x7 -> x8, starting transfers between devices: 11.5 us -> 13.5 us  [ring(): return lax.ppermute(block, axis, route)]
    div x0 -> x1, other arithmetic: none -> 1.3 us  [body(): (operate(field_start, first_values) - centre * field_start) / half_span]
    sub x3 -> x2, other arithmetic: 3.86 us -> 2.58 us  [chebyshev_step(): return (current, gain * scaled - keep * previous)]
    ppermute x3, waiting for transfers between devices: 7.87 us -> 9.07 us  [from_partner(): return lax.ppermute(block, axis, route)]
  transfers between devices with their start and end apart: 10 -> 11, of which waited for: 6 -> 4; matrix products, arithmetic and copies ran while one was open for 18% -> 28% of each run, Pallas kernels for 0% -> 0%
where the time goes in v2:
time: 78 us; the launch traced here: 77.6 us
  matrix products  35.9 us (46%)
  starting transfers between devices  15.2 us (19%)
  waiting for transfers between devices  11.4 us (15%)
  other arithmetic  9.46 us (12%)
  local copies, waits for them, and re-layouts  5.19 us (7%)
    ppermute x8, starting transfers between devices, ring(): return lax.ppermute(block, axis, route)  13.5 us
    dot_general x3, matrix products, operate(): jnp.dot(scatter_sel, both, preferred_element_type=jnp.float32)  10.1 us
    ppermute x3, waiting for transfers between devices, from_partner(): return lax.ppermute(block, axis, route)  9.07 us
    dot_general x2, matrix products, operate(): values = jnp.dot(gather_sel, weighted, preferred_element_type=jnp.float32)  8.35 us
    dot_general x1, matrix products, body(): jnp.dot(gather_sel[:, :node_count], local_weighted, preferred_element_typ...  4.64 us
    dot_general x3, matrix products, operate(): jnp.einsum('ij,cjb->cib', padded_matrix, values, preferred_element_type=j...  3.51 us
    eq x1, other arithmetic, body(): cell_rows[:, None] == wide_ids[:, 0][None, :]  3.08 us
    dot_general x1, matrix products, body(): jnp.dot(gather_sel[:, node_count:], ghost_weighted, preferred_element_typ...  2.68 us
  transfers between devices with their start and end apart: 11, of which 4 were waited for; matrix products, arithmetic and copies ran while one was open for 28% of the time, Pallas kernels for 0%

profile of v2, /device:TPU:0, one launch (start us, length us, event | category | flops | bytes accessed | tf_op | source)
XLA Modules:
  0.0 77.6 jit_solution(8098359614692310177)
XLA Ops:
  0.0 1.4 %fusion.60 = f32[144,128]{1,0:T(8,128)S(1)} fusion(bf16[1728,128]{1,0:T(8,128)(2,1)} %param.9, s32[1728]{0:T(1024)S(1)} %add_reduce_fusion, s32[144]{0:T(256)} %param.14), kind=kOutput, calls=%fused_computation.74 | convolution fusion | flops 63949824 | bytes 523584 | tf_op jit(solution)/shard_map/dot_general | solution.py:57
  1.5 3.9 %collective-permute-start.2 = (f32[144,128]{1,0:T(8,128)S(1)}, f32[144,128]{1,0:T(8,128)S(1)}, u32[]{:S(2)}, u32[]{:S(2)}) collective-permute-start(f32[144,128]{1,0:T(8,128)S(1)} %fusion.60), channel_id=1, source_target_pairs={{0,24},{8,0},{16,8},{24,16},{1,25},{9,1},{17,9},{25,17},{2,26},{10... | collective-permute-start | bytes 221192 | tf_op jit(solution)/shard_map/ppermute | solution.py:16
  9.9 3.1 %iota_compare_fusion.2 = pred[2816,1872]{1,0:T(32,128)(4,1)S(1)} fusion(s32[2816]{0:T(1024)S(1)} %eq.85), kind=kLoop, calls=%fused_computation.52 | loop fusion | flops 5271552 | bytes 5282816 | tf_op jit(solution)/shard_map/eq | solution.py:50
  13.0 4.6 %fusion.48 = f32[2816,128]{1,0:T(8,128)} fusion(pred[2816,1872]{1,0:T(32,128)(4,1)S(1)} %iota_compare_fusion.2, f32[1728]{0:T(1024)S(1)} %copy-done.5, bf16[1728,128]{1,0:T(8,128)(2,1)S(1)} %copy-done.3), kind=kOutput, calls=%fused_computation.55 | convolution fusion | flops 1246371840 | bytes 6938624 | tf_op jit(solution)/shard_map/dot_general | solution.py:93
  18.9 2.7 %fusion.51 = bf16[2816,128]{1,0:T(8,128)(2,1)S(1)} fusion(f32[2816,128]{1,0:T(8,128)} %fusion.48, pred[2816,1872]{1,0:T(32,128)(4,1)} %copy-done.1, f32[144,128]{1,0:T(8,128)S(1)} %collective-permute-done.2, f32[144]{0:T(256)S(1)} %get-tuple-element.237), kind=kOutput, calls=%fused_computation.59 | convolution fusion | flops 104566784 | bytes 2957888 | tf_op jit(solution)/shard_map/dot_general | solution.py:95
  22.4 4.1 %fusion.47 = f32[1872,256]{1,0:T(8,128)S(1)} fusion(s32[2816]{0:T(1024)S(1)} %eq.85, bf16[2816,128]{1,0:T(8,128)(2,1)S(1)} %get-tuple-element.265, bf16[2816,128]{1,0:T(8,128)(2,1)S(1)} %get-tuple-element.264), kind=kOutput, calls=%fused_computation.54 | convolution fusion | flops 2707189760 | bytes 3369984 | tf_op jit(solution)/shard_map/dot_general | solution.py:76
  27.1 1.5 %collective-permute-start.4 = (f32[144,128]{1,0:T(8,128)S(1)}, f32[144,128]{1,0:T(8,128)S(1)}, u32[]{:S(2)}, u32[]{:S(2)}) collective-permute-start(f32[144,128]{1,0:T(8,128)S(1)} %get-tuple-element.268), channel_id=1, source_target_pairs={{0,8},{8,16},{16,24},{24,0},{1,9},{9,17},{17,25},{25,1},{2,10},{10... | collective-permute-start | bytes 221192 | tf_op jit(solution)/shard_map/ppermute | solution.py:16
  28.8 1.5 %collective-permute-start.5 = (f32[144,128]{1,0:T(8,128)S(1)}, f32[144,128]{1,0:T(8,128)S(1)}, u32[]{:S(2)}, u32[]{:S(2)}) collective-permute-start(f32[144,128]{1,0:T(8,128)S(1)} %get-tuple-element.269), channel_id=1, source_target_pairs={{0,24},{8,0},{16,8},{24,16},{1,25},{9,1},{17,9},{25,17},{2,26},{10... | collective-permute-start | bytes 221192 | tf_op jit(solution)/shard_map/ppermute | solution.py:16
  30.2 2.2 %collective-permute-done.4 = f32[144,128]{1,0:T(8,128)S(1)} collective-permute-done((f32[144,128]{1,0:T(8,128)S(1)}, f32[144,128]{1,0:T(8,128)S(1)}, u32[]{:S(2)}, u32[]{:S(2)}) %collective-permute-start.4) | collective-permute-done | bytes 73760 | tf_op jit(solution)/shard_map/ppermute | solution.py:16
  33.2 1.3 %fusion.64 = (f32[1872,128]{1,0:T(8,128)S(1)}, f32[1872,128]{1,0:T(8,128)S(1)}) fusion(f32[144,128]{1,0:T(8,128)S(1)} %slice_add_fusion.7, f32[1728,128]{1,0:T(8,128)S(1)} %fusion.65, f32[1872]{0:T(1024)S(1)} %get-tuple-element.352, f32[1872]{0:T(1024)S(1)} %get-tuple-element.350, f32[144,128]{1,0:T(8,128)S(1)} %collective-permute-done.2, ...), kind=kLoop, calls=%fused_computation.81 | loop fusion | flops 1916928 | bytes 3848832 | tf_op jit(solution)/shard_map/div | solution.py:96
  34.5 30.4 %while.17 = (s32[]{:T(128)}, f32[1872,128]{1,0:T(8,128)S(1)}, f32[1872,128]{1,0:T(8,128)S(1)}, f32[1872]{0:T(1024)S(1)}, bf16[352,352]{1,0:T(8,128)(2,1)}, /*ind...) while((s32[]{:T(128)}, f32[1872,128]{1,0:T(8,128)S(1)}, ...), condition=%wide.region_1.2_spmd.clone.clone, body=%wide.region_0.1_spmd.clone.clone.sunk | while | flops 4879314944 | bytes 31196824 | solution.py:97
  34.5 4.2 %fusion.119 = bf16[2816,128]{0,1:T(8,128)(2,1)S(1)} fusion(s32[2816]{0:T(1024)S(1)} %get-tuple-element.385, f32[1872,128]{1,0:T(8,128)S(1)} %get-tuple-element.365, f32[1872]{0:T(1024)S(1)} %get-tuple-element.382), kind=kOutput, calls=%fused_computation.14.clone.1 | convolution fusion | flops 1360900096 | bytes 1698112 | tf_op jit(solution)/shard_map/while/body/eval_jaxpr/dot_general | solution.py:67
  39.0 1.5 %fusion.120 = f32[8,128,352]{1,2,0:T(8,128)S(1)} fusion(bf16[8,352,128]{2,1,0:T(8,128)(2,1)S(1)} %bitcast.50, bf16[352,352]{1,0:T(8,128)(2,1)} %get-tuple-element.383), kind=kOutput, calls=%fused_computation.39.clone.1 | convolution fusion | flops 253755392 | bytes 2410496 | tf_op jit(solution)/shard_map/while/body/eval_jaxpr/ij,cjb->cib/dot_general | solution.py:69
  42.4 2.0 %collective-permute-start = (f32[144,128]{1,0:T(8,128)S(1)}, f32[144,128]{1,0:T(8,128)S(1)}, u32[]{:S(2)}, u32[]{:S(2)}) collective-permute-start(f32[144,128]{1,0:T(8,128)S(1)} %get-tuple-element.343), channel_id=1, source_target_pairs={{0,24},{8,0},{16,8},{24,16},{1,25},{9,1},{17,9},{25,17},{2,26},{10... | collective-permute-start | bytes 221192 | tf_op jit(solution)/shard_map/while/body/eval_jaxpr/ppermute | solution.py:16
  44.4 3.0 %fusion.123 = f32[1872,256]{1,0:T(8,128)S(1)} fusion(s32[2816]{0:T(1024)S(1)} %get-tuple-element.385, bf16[2816,128]{1,0:T(8,128)(2,1)S(1)} %get-tuple-element.341, bf16[2816,128]{1,0:T(8,128)(2,1)S(1)} %get-tuple-element.342), kind=kOutput, calls=%fused_computation.17.clone.1 | convolution fusion | flops 2712461312 | bytes 3369984 | tf_op jit(solution)/shard_map/while/body/eval_jaxpr/dot_general | solution.py:76
  48.2 1.3 %fusion.125 = f32[1872,128]{1,0:T(8,128)S(1)} fusion(f32[144,128]{1,0:T(8,128)S(1)} %slice_add_fusion.13, f32[1728,128]{1,0:T(8,128)S(1)} %fusion.124, f32[1872,128]{1,0:T(8,128)S(1)} %get-tuple-element.364, f32[1872,128]{1,0:T(8,128)S(1)} %get-tuple-element.365, f32[]{:T(128)S(6)} %select_n.50, f32[]{:T(128)S(6)} %mul.238, ...), kind=kLoop, calls=%fused_computation.32.clone.1 | loop fusion | flops 2156544 | bytes 3848840 | tf_op jit(solution)/shard_map/while/body/eval_jaxpr/sub | solution.py:89
  49.7 4.2 %fusion.119 = bf16[2816,128]{0,1:T(8,128)(2,1)S(1)} fusion(s32[2816]{0:T(1024)S(1)} %get-tuple-element.385, f32[1872,128]{1,0:T(8,128)S(1)} %get-tuple-element.365, f32[1872]{0:T(1024)S(1)} %get-tuple-element.382), kind=kOutput, calls=%fused_computation.14.clone.1 | convolution fusion | flops 1360900096 | bytes 1698112 | tf_op jit(solution)/shard_map/while/body/eval_jaxpr/dot_general | solution.py:67
  54.2 1.5 %fusion.120 = f32[8,128,352]{1,2,0:T(8,128)S(1)} fusion(bf16[8,352,128]{2,1,0:T(8,128)(2,1)S(1)} %bitcast.50, bf16[352,352]{1,0:T(8,128)(2,1)} %get-tuple-element.383), kind=kOutput, calls=%fused_computation.39.clone.1 | convolution fusion | flops 253755392 | bytes 2410496 | tf_op jit(solution)/shard_map/while/body/eval_jaxpr/ij,cjb->cib/dot_general | solution.py:69
  57.4 2.2 %collective-permute-start = (f32[144,128]{1,0:T(8,128)S(1)}, f32[144,128]{1,0:T(8,128)S(1)}, u32[]{:S(2)}, u32[]{:S(2)}) collective-permute-start(f32[144,128]{1,0:T(8,128)S(1)} %get-tuple-element.343), channel_id=1, source_target_pairs={{0,24},{8,0},{16,8},{24,16},{1,25},{9,1},{17,9},{25,17},{2,26},{10... | collective-permute-start | bytes 221192 | tf_op jit(solution)/shard_map/while/body/eval_jaxpr/ppermute | solution.py:16
  59.6 3.0 %fusion.123 = f32[1872,256]{1,0:T(8,128)S(1)} fusion(s32[2816]{0:T(1024)S(1)} %get-tuple-element.385, bf16[2816,128]{1,0:T(8,128)(2,1)S(1)} %get-tuple-element.341, bf16[2816,128]{1,0:T(8,128)(2,1)S(1)} %get-tuple-element.342), kind=kOutput, calls=%fused_computation.17.clone.1 | convolution fusion | flops 2712461312 | bytes 3369984 | tf_op jit(solution)/shard_map/while/body/eval_jaxpr/dot_general | solution.py:76
  63.4 1.3 %fusion.125 = f32[1872,128]{1,0:T(8,128)S(1)} fusion(f32[144,128]{1,0:T(8,128)S(1)} %slice_add_fusion.13, f32[1728,128]{1,0:T(8,128)S(1)} %fusion.124, f32[1872,128]{1,0:T(8,128)S(1)} %get-tuple-element.364, f32[1872,128]{1,0:T(8,128)S(1)} %get-tuple-element.365, f32[]{:T(128)S(6)} %select_n.50, f32[]{:T(128)S(6)} %mul.238, ...), kind=kLoop, calls=%fused_computation.32.clone.1 | loop fusion | flops 2156544 | bytes 3848840 | tf_op jit(solution)/shard_map/while/body/eval_jaxpr/sub | solution.py:89
  64.9 1.6 %collective-permute-start.7 = (bf16[1728,128]{1,0:T(8,128)(2,1)S(1)}, bf16[1728,128]{1,0:T(8,128)(2,1)S(1)}, u32[]{:S(2)}, u32[]{:S(2)}) collective-permute-start(bf16[1728,128]{1,0:T(8,128)(2,1)S(1)} %slice.217), channel_id=1, source_target_pairs={{0,2},{2,0},{1,3},{3,1},{4,6},{6,4},{5,7},{7,5},{8,10},{10,8},{9,1... | collective-permute-start | bytes 1327112 | tf_op jit(solution)/shard_map/ppermute | solution.py:26
  66.8 7.8 %collective-permute-done.7 = bf16[1728,128]{1,0:T(8,128)(2,1)S(1)} collective-permute-done((bf16[1728,128]{1,0:T(8,128)(2,1)S(1)}, bf16[1728,128]{1,0:T(8,128)(2,1)S(1)}, u32[]{:S(2)}, u32[]{:S(2)}) %collective-permute-start.7) | collective-permute-done | bytes 442400 | tf_op jit(solution)/shard_map/ppermute | solution.py:26
  75.2 1.2 %collective-permute-done.8 = bf16[1728,128]{1,0:T(8,128)(2,1)S(1)} collective-permute-done((bf16[1728,128]{1,0:T(8,128)(2,1)S(1)}, bf16[1728,128]{1,0:T(8,128)(2,1)S(1)}, u32[]{:S(2)}, u32[]{:S(2)}) %collective-permute-start.8) | collective-permute-done | bytes 442400 | tf_op jit(solution)/shard_map/ppermute | solution.py:26
  (82 shorter events, 16.0 us)
Async XLA Ops:
  0.0 66.6 %copy-start = (bf16[512,128]{1,0:T(8,128)(2,1)S(1)}, bf16[512,128]{1,0:T(8,128)(2,1)}, u32[]{:S(2)}) copy-start(bf16[512,128]{1,0:T(8,128)(2,1)} %param.15) | copy-start | bytes 393220
  1.5 17.4 %collective-permute-start.2 = (f32[144,128]{1,0:T(8,128)S(1)}, f32[144,128]{1,0:T(8,128)S(1)}, u32[]{:S(2)}, u32[]{:S(2)}) collective-permute-start(f32[144,128]{1,0:T(8,128)S(1)} %fusion.60), channel_id=1, source_target_pairs={{0,24},{8,0},{16,8},{24,16},{1,25},{9,1},{17,9},{25,17},{2,26},{10... | collective-permute-start | bytes 221192 | tf_op jit(solution)/shard_map/ppermute | solution.py:16
  8.5 10.1 %collective-permute-start.3 = (f32[2,144]{0,1:T(8,128)S(1)}, f32[2,144]{0,1:T(8,128)S(1)}, u32[]{:S(2)}, u32[]{:S(2)}) collective-permute-start(f32[2,144]{0,1:T(8,128)S(1)} %bitcast.53), channel_id=1, source_target_pairs={{0,24},{8,0},{16,8},{24,16},{1,25},{9,1},{17,9},{25,17},{2,26},{10... | collective-permute-start | bytes 3464 | tf_op jit(solution)/shard_map/ppermute | solution.py:16
  9.9 3.1 %copy-start.3 = (bf16[1728,128]{1,0:T(8,128)(2,1)S(1)}, bf16[1728,128]{1,0:T(8,128)(2,1)}, u32[]{:S(2)}) copy-start(bf16[1728,128]{1,0:T(8,128)(2,1)} %param.9) | copy-start | bytes 1327108
  9.9 3.1 %copy-start.5 = (f32[1728]{0:T(1024)S(1)}, f32[1728]{0:T(1024)}, u32[]{:S(2)}) copy-start(f32[1728]{0:T(1024)} %param.10) | copy-start | bytes 20740
  13.0 4.7 %copy-start.1 = (pred[2816,1872]{1,0:T(32,128)(4,1)}, pred[2816,1872]{1,0:T(32,128)(4,1)S(1)}, u32[]{:S(2)}) copy-start(pred[2816,1872]{1,0:T(32,128)(4,1)S(1)} %iota_compare_fusion.2) | copy-start | bytes 15814660
  13.0 4.7 %copy-start.4 = (s32[144]{0:T(256)S(1)}, s32[144]{0:T(256)}, u32[]{:S(2)}) copy-start(s32[144]{0:T(256)} %param.14) | copy-start | bytes 1732
  13.0 4.8 %copy-start.2 = (bf16[343,343]{1,0:T(8,128)(2,1)S(1)}, bf16[343,343]{1,0:T(8,128)(2,1)}, u32[]{:S(2)}) copy-start(bf16[343,343]{1,0:T(8,128)(2,1)} %param.12) | copy-start | bytes 705898
  17.7 1.1 %copy-start.6 = (f32[1728]{0:T(1024)S(1)}, f32[1728]{0:T(1024)}, u32[]{:S(2)}) copy-start(f32[1728]{0:T(1024)} %param.11) | copy-start | bytes 20740
  27.1 5.3 %collective-permute-start.4 = (f32[144,128]{1,0:T(8,128)S(1)}, f32[144,128]{1,0:T(8,128)S(1)}, u32[]{:S(2)}, u32[]{:S(2)}) collective-permute-start(f32[144,128]{1,0:T(8,128)S(1)} %get-tuple-element.268), channel_id=1, source_target_pairs={{0,8},{8,16},{16,24},{24,0},{1,9},{9,17},{17,25},{25,1},{2,10},{10... | collective-permute-start | bytes 221192 | tf_op jit(solution)/shard_map/ppermute | solution.py:16
  28.8 4.4 %collective-permute-start.5 = (f32[144,128]{1,0:T(8,128)S(1)}, f32[144,128]{1,0:T(8,128)S(1)}, u32[]{:S(2)}, u32[]{:S(2)}) collective-permute-start(f32[144,128]{1,0:T(8,128)S(1)} %get-tuple-element.269), channel_id=1, source_target_pairs={{0,24},{8,0},{16,8},{24,16},{1,25},{9,1},{17,9},{25,17},{2,26},{10... | collective-permute-start | bytes 221192 | tf_op jit(solution)/shard_map/ppermute | solution.py:16
  41.4 6.1 %collective-permute-start.1 = (f32[144,128]{1,0:T(8,128)S(1)}, f32[144,128]{1,0:T(8,128)S(1)}, u32[]{:S(2)}, u32[]{:S(2)}) collective-permute-start(f32[144,128]{1,0:T(8,128)S(1)} %get-tuple-element.344), channel_id=1, source_target_pairs={{0,8},{8,16},{16,24},{24,0},{1,9},{9,17},{17,25},{25,1},{2,10},{10... | collective-permute-start | bytes 221192 | tf_op jit(solution)/shard_map/while/body/eval_jaxpr/ppermute | solution.py:16
  42.4 5.8 %collective-permute-start = (f32[144,128]{1,0:T(8,128)S(1)}, f32[144,128]{1,0:T(8,128)S(1)}, u32[]{:S(2)}, u32[]{:S(2)}) collective-permute-start(f32[144,128]{1,0:T(8,128)S(1)} %get-tuple-element.343), channel_id=1, source_target_pairs={{0,24},{8,0},{16,8},{24,16},{1,25},{9,1},{17,9},{25,17},{2,26},{10... | collective-permute-start | bytes 221192 | tf_op jit(solution)/shard_map/while/body/eval_jaxpr/ppermute | solution.py:16
  56.6 6.1 %collective-permute-start.1 = (f32[144,128]{1,0:T(8,128)S(1)}, f32[144,128]{1,0:T(8,128)S(1)}, u32[]{:S(2)}, u32[]{:S(2)}) collective-permute-start(f32[144,128]{1,0:T(8,128)S(1)} %get-tuple-element.344), channel_id=1, source_target_pairs={{0,8},{8,16},{16,24},{24,0},{1,9},{9,17},{17,25},{25,1},{2,10},{10... | collective-permute-start | bytes 221192 | tf_op jit(solution)/shard_map/while/body/eval_jaxpr/ppermute | solution.py:16
  57.4 5.9 %collective-permute-start = (f32[144,128]{1,0:T(8,128)S(1)}, f32[144,128]{1,0:T(8,128)S(1)}, u32[]{:S(2)}, u32[]{:S(2)}) collective-permute-start(f32[144,128]{1,0:T(8,128)S(1)} %get-tuple-element.343), channel_id=1, source_target_pairs={{0,24},{8,0},{16,8},{24,16},{1,25},{9,1},{17,9},{25,17},{2,26},{10... | collective-permute-start | bytes 221192 | tf_op jit(solution)/shard_map/while/body/eval_jaxpr/ppermute | solution.py:16
  64.9 9.7 %collective-permute-start.7 = (bf16[1728,128]{1,0:T(8,128)(2,1)S(1)}, bf16[1728,128]{1,0:T(8,128)(2,1)S(1)}, u32[]{:S(2)}, u32[]{:S(2)}) collective-permute-start(bf16[1728,128]{1,0:T(8,128)(2,1)S(1)} %slice.217), channel_id=1, source_target_pairs={{0,2},{2,0},{1,3},{3,1},{4,6},{6,4},{5,7},{7,5},{8,10},{10,8},{9,1... | collective-permute-start | bytes 1327112 | tf_op jit(solution)/shard_map/ppermute | solution.py:26
  66.6 8.1 %collective-permute-start.6 = (bf16[1728,128]{1,0:T(8,128)(2,1)S(1)}, bf16[1728,128]{1,0:T(8,128)(2,1)S(1)}, u32[]{:S(2)}, u32[]{:S(2)}) collective-permute-start(bf16[1728,128]{1,0:T(8,128)(2,1)S(1)} %slice.217), channel_id=1, source_target_pairs={{0,1},{1,0},{2,3},{3,2},{4,5},{5,4},{6,7},{7,6},{8,9},{9,8},{10,11... | collective-permute-start | bytes 1327112 | tf_op jit(solution)/shard_map/ppermute | solution.py:26
  74.6 1.8 %collective-permute-start.8 = (bf16[1728,128]{1,0:T(8,128)(2,1)S(1)}, bf16[1728,128]{1,0:T(8,128)(2,1)S(1)}, u32[]{:S(2)}, u32[]{:S(2)}) collective-permute-start(bf16[1728,128]{1,0:T(8,128)(2,1)S(1)} %collective-permute-done.7), channel_id=1, source_target_pairs={{0,1},{1,0},{2,3},{3,2},{4,5},{5,4},{6,7},{7,6},{8,9},{9,8},{10,11... | collective-permute-start | bytes 1327112 | tf_op jit(solution)/shard_map/ppermute | solution.py:26

commit v3 on v0

--- a/solution.py
+++ b/solution.py
@@ -63,7 +63,9 @@
 
     def operate(field_in):
         weighted = (wide_mass[:, None] * field_in).astype(jnp.bfloat16)
-        values = jnp.dot(gather_sel, weighted, preferred_element_type=jnp.float32)
+        values = lax.dot_general(
+            scatter_sel, weighted, (((0,), (0,)), ((), ())), preferred_element_type=jnp.float32
+        )
         values = values.astype(jnp.bfloat16).reshape(cell_count, padded_size, state_count)
         products = jnp.einsum(
             "ij,cjb->cib", padded_matrix, values, preferred_element_type=jnp.float32

time: 72.8 us -> 67.3 us (0.924)
  matrix products: 32.6 us -> 27.2 us
    dot_general x3, matrix products: 12.5 us -> 7.04 us  [operate(): lax.dot_general(scatter_sel, weighted, (((0,), (0,)), ((), ())), preferre...]
  transfers between devices with their start and end apart: 10 -> 10, of which waited for: 6 -> 6; matrix products, arithmetic and copies ran while one was open for 18% -> 19% of each run, Pallas kernels for 0% -> 0%
where the time goes in v3:
time: 67.3 us; the launch traced here: 66.8 us
  matrix products  27.2 us (40%)
  waiting for transfers between devices  13.9 us (21%)
  starting transfers between devices  13.2 us (20%)
  other arithmetic  6.6 us (10%)
  local copies, waits for them, and re-layouts  5.43 us (8%)
    ppermute x7, starting transfers between devices, ring(): return lax.ppermute(block, axis, route)  11.5 us
    dot_general x3, matrix products, operate(): jnp.dot(scatter_sel, both, preferred_element_type=jnp.float32)  9.05 us
    ppermute x3, waiting for transfers between devices, from_partner(): return lax.ppermute(block, axis, route)  7.89 us
    dot_general x3, matrix products, operate(): lax.dot_general(scatter_sel, weighted, (((0,), (0,)), ((), ())), preferre...  7.04 us
    ppermute x7, waiting for transfers between devices, ring(): return lax.ppermute(block, axis, route)  6.05 us
    dot_general x3, matrix products, operate(): jnp.einsum('ij,cjb->cib', padded_matrix, values, preferred_element_type=j...  4.46 us
    sub x3, other arithmetic, chebyshev_step(): return (current, gain * scaled - keep * previous)  3.86 us
    dot_general x3, matrix products, operate(): jnp.dot(rim_sel, both, preferred_element_type=jnp.float32)  1.89 us
  transfers between devices with their start and end apart: 10, of which 6 were waited for; matrix products, arithmetic and copies ran while one was open for 19% of the time, Pallas kernels for 0%

profile of v3, /device:TPU:0, one launch (start us, length us, event | category | flops | bytes accessed | tf_op | source)
XLA Modules:
  0.0 66.8 jit_solution(6741719476691798375)
XLA Ops:
  3.3 1.4 %fusion.44 = f32[144,128]{1,0:T(8,128)S(1)} fusion(bf16[1728,128]{1,0:T(8,128)(2,1)} %param.9, s32[1728]{0:T(1024)S(1)} %add_reduce_fusion, s32[144]{0:T(256)} %param.14), kind=kOutput, calls=%fused_computation.52 | convolution fusion | flops 63949824 | bytes 523584 | tf_op jit(solution)/shard_map/dot_general | solution.py:57
  4.7 3.9 %collective-permute-start.2 = (f32[144,130]{1,0:T(8,128)S(1)}, f32[144,130]{1,0:T(8,128)S(1)}, u32[]{:S(2)}, u32[]{:S(2)}) collective-permute-start(f32[144,130]{1,0:T(8,128)S(1)} %pad_maximum_fusion.4), channel_id=1, source_target_pairs={{0,24},{8,0},{16,8},{24,16},{1,25},{9,1},{17,9},{25,17},{2,26},{10... | collective-permute-start | bytes 224648 | tf_op jit(solution)/shard_map/ppermute | solution.py:16
  9.7 2.1 %collective-permute-done.2 = f32[144,130]{1,0:T(8,128)S(1)} collective-permute-done((f32[144,130]{1,0:T(8,128)S(1)}, f32[144,130]{1,0:T(8,128)S(1)}, u32[]{:S(2)}, u32[]{:S(2)}) %collective-permute-start.2) | collective-permute-done | bytes 74912 | tf_op jit(solution)/shard_map/ppermute | solution.py:16
  12.6 42.7 %while.17 = (s32[]{:T(128)}, f32[1872,128]{1,0:T(8,128)S(1)}, f32[1872,128]{1,0:T(8,128)S(1)}, f32[1872]{0:T(1024)S(1)}, bf16[352,352]{1,0:T(8,128)(2,1)}, /*ind...) while((s32[]{:T(128)}, f32[1872,128]{1,0:T(8,128)S(1)}, ...), condition=%wide.region_1.2_spmd.clone.clone, body=%wide.region_0.1_spmd.clone.clone.sunk | while | flops 4879314944 | bytes 31196832 | solution.py:92
  12.6 2.4 %fusion.81 = bf16[2816,128]{0,1:T(8,128)(2,1)S(1)} fusion(s32[2816]{0:T(1024)S(1)} %get-tuple-element.358, f32[1872,128]{1,0:T(8,128)S(1)} %get-tuple-element.338, f32[1872]{0:T(1024)S(1)} %get-tuple-element.355), kind=kOutput, calls=%fused_computation.11.clone.1 | convolution fusion | flops 1360900096 | bytes 1698112 | tf_op jit(solution)/shard_map/while/body/eval_jaxpr/dot_general | solution.py:66
  15.3 1.5 %fusion.82 = f32[8,128,352]{1,2,0:T(8,128)S(1)} fusion(bf16[8,352,128]{2,1,0:T(8,128)(2,1)S(1)} %bitcast.39, bf16[352,352]{1,0:T(8,128)(2,1)} %get-tuple-element.356), kind=kOutput, calls=%fused_computation.36.clone.1 | convolution fusion | flops 253755392 | bytes 2410496 | tf_op jit(solution)/shard_map/while/body/eval_jaxpr/ij,cjb->cib/dot_general | solution.py:70
  17.7 3.4 %collective-permute-start = (f32[144,128]{1,0:T(8,128)S(1)}, f32[144,128]{1,0:T(8,128)S(1)}, u32[]{:S(2)}, u32[]{:S(2)}) collective-permute-start(f32[144,128]{1,0:T(8,128)S(1)} %get-tuple-element.316), channel_id=1, source_target_pairs={{0,24},{8,0},{16,8},{24,16},{1,25},{9,1},{17,9},{25,17},{2,26},{10... | collective-permute-start | bytes 221192 | tf_op jit(solution)/shard_map/while/body/eval_jaxpr/ppermute | solution.py:16
  21.1 3.0 %fusion.85 = f32[1872,256]{1,0:T(8,128)S(1)} fusion(s32[2816]{0:T(1024)S(1)} %get-tuple-element.358, bf16[2816,128]{1,0:T(8,128)(2,1)S(1)} %get-tuple-element.314, bf16[2816,128]{1,0:T(8,128)(2,1)S(1)} %get-tuple-element.315), kind=kOutput, calls=%fused_computation.14.clone.1 | convolution fusion | flops 2712461312 | bytes 3369984 | tf_op jit(solution)/shard_map/while/body/eval_jaxpr/dot_general | solution.py:77
  24.3 2.1 %collective-permute-done.1 = f32[144,128]{1,0:T(8,128)S(1)} collective-permute-done((f32[144,128]{1,0:T(8,128)S(1)}, f32[144,128]{1,0:T(8,128)S(1)}, u32[]{:S(2)}, u32[]{:S(2)}) %collective-permute-start.1) | collective-permute-done | bytes 73760 | tf_op jit(solution)/shard_map/while/body/eval_jaxpr/ppermute | solution.py:16
  27.1 1.3 %fusion.87 = f32[1872,128]{1,0:T(8,128)S(1)} fusion(f32[144,128]{1,0:T(8,128)S(1)} %slice_add_fusion.9, f32[1728,128]{1,0:T(8,128)S(1)} %fusion.86, f32[1872,128]{1,0:T(8,128)S(1)} %get-tuple-element.337, f32[1872,128]{1,0:T(8,128)S(1)} %get-tuple-element.338, f32[]{:T(128)S(6)} %select_n.50, f32[]{:T(128)S(6)} %mul.171, ...), kind=kLoop, calls=%fused_computation.29.clone.1 | loop fusion | flops 2156544 | bytes 3848840 | tf_op jit(solution)/shard_map/while/body/eval_jaxpr/sub | solution.py:90
  28.5 2.3 %fusion.81 = bf16[2816,128]{0,1:T(8,128)(2,1)S(1)} fusion(s32[2816]{0:T(1024)S(1)} %get-tuple-element.358, f32[1872,128]{1,0:T(8,128)S(1)} %get-tuple-element.338, f32[1872]{0:T(1024)S(1)} %get-tuple-element.355), kind=kOutput, calls=%fused_computation.11.clone.1 | convolution fusion | flops 1360900096 | bytes 1698112 | tf_op jit(solution)/shard_map/while/body/eval_jaxpr/dot_general | solution.py:66
  31.2 1.5 %fusion.82 = f32[8,128,352]{1,2,0:T(8,128)S(1)} fusion(bf16[8,352,128]{2,1,0:T(8,128)(2,1)S(1)} %bitcast.39, bf16[352,352]{1,0:T(8,128)(2,1)} %get-tuple-element.356), kind=kOutput, calls=%fused_computation.36.clone.1 | convolution fusion | flops 253755392 | bytes 2410496 | tf_op jit(solution)/shard_map/while/body/eval_jaxpr/ij,cjb->cib/dot_general | solution.py:70
  34.5 1.2 %collective-permute-start.1 = (f32[144,128]{1,0:T(8,128)S(1)}, f32[144,128]{1,0:T(8,128)S(1)}, u32[]{:S(2)}, u32[]{:S(2)}) collective-permute-start(f32[144,128]{1,0:T(8,128)S(1)} %get-tuple-element.317), channel_id=1, source_target_pairs={{0,8},{8,16},{16,24},{24,0},{1,9},{9,17},{17,25},{25,1},{2,10},{10... | collective-permute-start | bytes 221192 | tf_op jit(solution)/shard_map/while/body/eval_jaxpr/ppermute | solution.py:16
  35.7 3.0 %fusion.85 = f32[1872,256]{1,0:T(8,128)S(1)} fusion(s32[2816]{0:T(1024)S(1)} %get-tuple-element.358, bf16[2816,128]{1,0:T(8,128)(2,1)S(1)} %get-tuple-element.314, bf16[2816,128]{1,0:T(8,128)(2,1)S(1)} %get-tuple-element.315), kind=kOutput, calls=%fused_computation.14.clone.1 | convolution fusion | flops 2712461312 | bytes 3369984 | tf_op jit(solution)/shard_map/while/body/eval_jaxpr/dot_general | solution.py:77
  40.4 1.3 %fusion.87 = f32[1872,128]{1,0:T(8,128)S(1)} fusion(f32[144,128]{1,0:T(8,128)S(1)} %slice_add_fusion.9, f32[1728,128]{1,0:T(8,128)S(1)} %fusion.86, f32[1872,128]{1,0:T(8,128)S(1)} %get-tuple-element.337, f32[1872,128]{1,0:T(8,128)S(1)} %get-tuple-element.338, f32[]{:T(128)S(6)} %select_n.50, f32[]{:T(128)S(6)} %mul.171, ...), kind=kLoop, calls=%fused_computation.29.clone.1 | loop fusion | flops 2156544 | bytes 3848840 | tf_op jit(solution)/shard_map/while/body/eval_jaxpr/sub | solution.py:90
  41.9 2.3 %fusion.81 = bf16[2816,128]{0,1:T(8,128)(2,1)S(1)} fusion(s32[2816]{0:T(1024)S(1)} %get-tuple-element.358, f32[1872,128]{1,0:T(8,128)S(1)} %get-tuple-element.338, f32[1872]{0:T(1024)S(1)} %get-tuple-element.355), kind=kOutput, calls=%fused_computation.11.clone.1 | convolution fusion | flops 1360900096 | bytes 1698112 | tf_op jit(solution)/shard_map/while/body/eval_jaxpr/dot_general | solution.py:66
  44.6 1.5 %fusion.82 = f32[8,128,352]{1,2,0:T(8,128)S(1)} fusion(bf16[8,352,128]{2,1,0:T(8,128)(2,1)S(1)} %bitcast.39, bf16[352,352]{1,0:T(8,128)(2,1)} %get-tuple-element.356), kind=kOutput, calls=%fused_computation.36.clone.1 | convolution fusion | flops 253755392 | bytes 2410496 | tf_op jit(solution)/shard_map/while/body/eval_jaxpr/ij,cjb->cib/dot_general | solution.py:70
  47.9 1.2 %collective-permute-start.1 = (f32[144,128]{1,0:T(8,128)S(1)}, f32[144,128]{1,0:T(8,128)S(1)}, u32[]{:S(2)}, u32[]{:S(2)}) collective-permute-start(f32[144,128]{1,0:T(8,128)S(1)} %get-tuple-element.317), channel_id=1, source_target_pairs={{0,8},{8,16},{16,24},{24,0},{1,9},{9,17},{17,25},{25,1},{2,10},{10... | collective-permute-start | bytes 221192 | tf_op jit(solution)/shard_map/while/body/eval_jaxpr/ppermute | solution.py:16
  49.1 3.0 %fusion.85 = f32[1872,256]{1,0:T(8,128)S(1)} fusion(s32[2816]{0:T(1024)S(1)} %get-tuple-element.358, bf16[2816,128]{1,0:T(8,128)(2,1)S(1)} %get-tuple-element.314, bf16[2816,128]{1,0:T(8,128)(2,1)S(1)} %get-tuple-element.315), kind=kOutput, calls=%fused_computation.14.clone.1 | convolution fusion | flops 2712461312 | bytes 3369984 | tf_op jit(solution)/shard_map/while/body/eval_jaxpr/dot_general | solution.py:77
  53.8 1.3 %fusion.87 = f32[1872,128]{1,0:T(8,128)S(1)} fusion(f32[144,128]{1,0:T(8,128)S(1)} %slice_add_fusion.9, f32[1728,128]{1,0:T(8,128)S(1)} %fusion.86, f32[1872,128]{1,0:T(8,128)S(1)} %get-tuple-element.337, f32[1872,128]{1,0:T(8,128)S(1)} %get-tuple-element.338, f32[]{:T(128)S(6)} %select_n.50, f32[]{:T(128)S(6)} %mul.171, ...), kind=kLoop, calls=%fused_computation.29.clone.1 | loop fusion | flops 2156544 | bytes 3848840 | tf_op jit(solution)/shard_map/while/body/eval_jaxpr/sub | solution.py:90
  55.3 1.6 %collective-permute-start.4 = (bf16[1728,128]{1,0:T(8,128)(2,1)S(1)}, bf16[1728,128]{1,0:T(8,128)(2,1)S(1)}, u32[]{:S(2)}, u32[]{:S(2)}) collective-permute-start(bf16[1728,128]{1,0:T(8,128)(2,1)S(1)} %slice.147), channel_id=1, source_target_pairs={{0,2},{2,0},{1,3},{3,1},{4,6},{6,4},{5,7},{7,5},{8,10},{10,8},{9,1... | collective-permute-start | bytes 1327112 | tf_op jit(solution)/shard_map/ppermute | solution.py:26
  57.2 6.6 %collective-permute-done.4 = bf16[1728,128]{1,0:T(8,128)(2,1)S(1)} collective-permute-done((bf16[1728,128]{1,0:T(8,128)(2,1)S(1)}, bf16[1728,128]{1,0:T(8,128)(2,1)S(1)}, u32[]{:S(2)}, u32[]{:S(2)}) %collective-permute-start.4) | collective-permute-done | bytes 442400 | tf_op jit(solution)/shard_map/ppermute | solution.py:26
  64.4 1.2 %collective-permute-done.5 = bf16[1728,128]{1,0:T(8,128)(2,1)S(1)} collective-permute-done((bf16[1728,128]{1,0:T(8,128)(2,1)S(1)}, bf16[1728,128]{1,0:T(8,128)(2,1)S(1)}, u32[]{:S(2)}, u32[]{:S(2)}) %collective-permute-start.5) | collective-permute-done | bytes 442400 | tf_op jit(solution)/shard_map/ppermute | solution.py:26
  65.7 1.2 %convolution_add_fusion = f32[1728,128]{1,0:T(8,128)} fusion(f32[1728,128]{1,0:T(8,128)S(1)} %convolution_add_fusion.1, bf16[1728,128]{1,0:T(8,128)(2,1)S(1)} %collective-permute-done.5, bf16[512,128]{1,0:T(8,128)(2,1)S(1)} %copy-done, s32[]{:T(128)S(6)} %select_n.42), kind=kOutput, calls=%fused_computation.49 | convolution fusion | flops 56844288 | bytes 2244612 | tf_op jit(solution)/shard_map/dot_general | solution.py:105
  (85 shorter events, 15.8 us)
Async XLA Ops:
  0.0 57.0 %copy-start = (bf16[512,128]{1,0:T(8,128)(2,1)S(1)}, bf16[512,128]{1,0:T(8,128)(2,1)}, u32[]{:S(2)}) copy-start(bf16[512,128]{1,0:T(8,128)(2,1)} %param.15) | copy-start | bytes 393220
  0.0 8.7 %copy-start.1 = (bf16[1728,128]{1,0:T(8,128)(2,1)S(1)}, bf16[1728,128]{1,0:T(8,128)(2,1)}, u32[]{:S(2)}) copy-start(bf16[1728,128]{1,0:T(8,128)(2,1)} %param.9) | copy-start | bytes 1327108
  1.5 7.2 %copy-start.6 = (s32[8,343]{1,0:T(8,128)S(1)}, s32[8,343]{1,0:T(8,128)}, u32[]{:S(2)}) copy-start(s32[8,343]{1,0:T(8,128)} %param.13) | copy-start | bytes 32932
  1.5 7.3 %copy-start.2 = (bf16[343,343]{1,0:T(8,128)(2,1)S(1)}, bf16[343,343]{1,0:T(8,128)(2,1)}, u32[]{:S(2)}) copy-start(bf16[343,343]{1,0:T(8,128)(2,1)} %param.12) | copy-start | bytes 705898
  1.9 7.7 %copy-start.3 = (s32[144]{0:T(256)S(1)}, s32[144]{0:T(256)}, u32[]{:S(2)}) copy-start(s32[144]{0:T(256)} %param.14) | copy-start | bytes 1732
  4.7 7.1 %collective-permute-start.2 = (f32[144,130]{1,0:T(8,128)S(1)}, f32[144,130]{1,0:T(8,128)S(1)}, u32[]{:S(2)}, u32[]{:S(2)}) collective-permute-start(f32[144,130]{1,0:T(8,128)S(1)} %pad_maximum_fusion.4), channel_id=1, source_target_pairs={{0,24},{8,0},{16,8},{24,16},{1,25},{9,1},{17,9},{25,17},{2,26},{10... | collective-permute-start | bytes 224648 | tf_op jit(solution)/shard_map/ppermute | solution.py:16
  11.8 0.7 %copy-start.4 = (f32[1728]{0:T(1024)S(1)}, f32[1728]{0:T(1024)}, u32[]{:S(2)}) copy-start(f32[1728]{0:T(1024)} %param.11) | copy-start | bytes 20740
  11.8 0.7 %copy-start.5 = (f32[1728]{0:T(1024)S(1)}, f32[1728]{0:T(1024)}, u32[]{:S(2)}) copy-start(f32[1728]{0:T(1024)} %param.10) | copy-start | bytes 20740
  17.7 9.3 %collective-permute-start = (f32[144,128]{1,0:T(8,128)S(1)}, f32[144,128]{1,0:T(8,128)S(1)}, u32[]{:S(2)}, u32[]{:S(2)}) collective-permute-start(f32[144,128]{1,0:T(8,128)S(1)} %get-tuple-element.316), channel_id=1, source_target_pairs={{0,24},{8,0},{16,8},{24,16},{1,25},{9,1},{17,9},{25,17},{2,26},{10... | collective-permute-start | bytes 221192 | tf_op jit(solution)/shard_map/while/body/eval_jaxpr/ppermute | solution.py:16
  21.1 5.3 %collective-permute-start.1 = (f32[144,128]{1,0:T(8,128)S(1)}, f32[144,128]{1,0:T(8,128)S(1)}, u32[]{:S(2)}, u32[]{:S(2)}) collective-permute-start(f32[144,128]{1,0:T(8,128)S(1)} %get-tuple-element.317), channel_id=1, source_target_pairs={{0,8},{8,16},{16,24},{24,0},{1,9},{9,17},{17,25},{25,1},{2,10},{10... | collective-permute-start | bytes 221192 | tf_op jit(solution)/shard_map/while/body/eval_jaxpr/ppermute | solution.py:16
  33.6 6.8 %collective-permute-start = (f32[144,128]{1,0:T(8,128)S(1)}, f32[144,128]{1,0:T(8,128)S(1)}, u32[]{:S(2)}, u32[]{:S(2)}) collective-permute-start(f32[144,128]{1,0:T(8,128)S(1)} %get-tuple-element.316), channel_id=1, source_target_pairs={{0,24},{8,0},{16,8},{24,16},{1,25},{9,1},{17,9},{25,17},{2,26},{10... | collective-permute-start | bytes 221192 | tf_op jit(solution)/shard_map/while/body/eval_jaxpr/ppermute | solution.py:16
  34.5 5.3 %collective-permute-start.1 = (f32[144,128]{1,0:T(8,128)S(1)}, f32[144,128]{1,0:T(8,128)S(1)}, u32[]{:S(2)}, u32[]{:S(2)}) collective-permute-start(f32[144,128]{1,0:T(8,128)S(1)} %get-tuple-element.317), channel_id=1, source_target_pairs={{0,8},{8,16},{16,24},{24,0},{1,9},{9,17},{17,25},{25,1},{2,10},{10... | collective-permute-start | bytes 221192 | tf_op jit(solution)/shard_map/while/body/eval_jaxpr/ppermute | solution.py:16
  47.0 6.8 %collective-permute-start = (f32[144,128]{1,0:T(8,128)S(1)}, f32[144,128]{1,0:T(8,128)S(1)}, u32[]{:S(2)}, u32[]{:S(2)}) collective-permute-start(f32[144,128]{1,0:T(8,128)S(1)} %get-tuple-element.316), channel_id=1, source_target_pairs={{0,24},{8,0},{16,8},{24,16},{1,25},{9,1},{17,9},{25,17},{2,26},{10... | collective-permute-start | bytes 221192 | tf_op jit(solution)/shard_map/while/body/eval_jaxpr/ppermute | solution.py:16
  47.9 5.3 %collective-permute-start.1 = (f32[144,128]{1,0:T(8,128)S(1)}, f32[144,128]{1,0:T(8,128)S(1)}, u32[]{:S(2)}, u32[]{:S(2)}) collective-permute-start(f32[144,128]{1,0:T(8,128)S(1)} %get-tuple-element.317), channel_id=1, source_target_pairs={{0,8},{8,16},{16,24},{24,0},{1,9},{9,17},{17,25},{25,1},{2,10},{10... | collective-permute-start | bytes 221192 | tf_op jit(solution)/shard_map/while/body/eval_jaxpr/ppermute | solution.py:16
  55.3 8.6 %collective-permute-start.4 = (bf16[1728,128]{1,0:T(8,128)(2,1)S(1)}, bf16[1728,128]{1,0:T(8,128)(2,1)S(1)}, u32[]{:S(2)}, u32[]{:S(2)}) collective-permute-start(bf16[1728,128]{1,0:T(8,128)(2,1)S(1)} %slice.147), channel_id=1, source_target_pairs={{0,2},{2,0},{1,3},{3,1},{4,6},{6,4},{5,7},{7,5},{8,10},{10,8},{9,1... | collective-permute-start | bytes 1327112 | tf_op jit(solution)/shard_map/ppermute | solution.py:26
  57.0 6.9 %collective-permute-start.3 = (bf16[1728,128]{1,0:T(8,128)(2,1)S(1)}, bf16[1728,128]{1,0:T(8,128)(2,1)S(1)}, u32[]{:S(2)}, u32[]{:S(2)}) collective-permute-start(bf16[1728,128]{1,0:T(8,128)(2,1)S(1)} %slice.147), channel_id=1, source_target_pairs={{0,1},{1,0},{2,3},{3,2},{4,5},{5,4},{6,7},{7,6},{8,9},{9,8},{10,11... | collective-permute-start | bytes 1327112 | tf_op jit(solution)/shard_map/ppermute | solution.py:26
  63.9 1.8 %collective-permute-start.5 = (bf16[1728,128]{1,0:T(8,128)(2,1)S(1)}, bf16[1728,128]{1,0:T(8,128)(2,1)S(1)}, u32[]{:S(2)}, u32[]{:S(2)}) collective-permute-start(bf16[1728,128]{1,0:T(8,128)(2,1)S(1)} %collective-permute-done.4), channel_id=1, source_target_pairs={{0,1},{1,0},{2,3},{3,2},{4,5},{5,4},{6,7},{7,6},{8,9},{9,8},{10,11... | collective-permute-start | bytes 1327112 | tf_op jit(solution)/shard_map/ppermute | solution.py:26

commit v4 on v3

--- a/solution.py
+++ b/solution.py
@@ -52,10 +52,21 @@
     rim_ids = jnp.concatenate([face_rows, wide_ids[node_count:, 0]], 0)
     rim_sel = (rim_ids[:, None] == cell_rows[None, :]).astype(jnp.bfloat16)
     face_put = (wide_ids[:node_count] == face_rows[None, :]).astype(jnp.bfloat16)
-    face_take = (face_rows[:, None] == wide_ids[:node_count, 0][None, :]).astype(jnp.bfloat16)
 
-    face_states = jnp.dot(face_take, states, preferred_element_type=jnp.float32)
-    mass_potential = jnp.stack([inv_mass, potential], 1)[face_rows]
+    face_states = lax.dot_general(
+        face_put, states, (((0,), (0,)), ((), ())), preferred_element_type=jnp.float32
+    )
+    mass_potential = jnp.stack([inv_mass, potential], 1).at[face_rows].get(
+        mode="promise_in_bounds"
+    )
+    rim_cells = rim_sel.reshape(2 * face_count, cell_count, padded_size)
+    rim_matrix = jnp.einsum(
+        "rci,ij->rcj", rim_cells, padded_matrix, preferred_element_type=jnp.float32
+    ).reshape(2 * face_count, -1)
+    rim_high = lax.reduce_precision(rim_matrix, exponent_bits=8, mantissa_bits=7)
+    rim_both = jnp.concatenate(
+        [rim_high.astype(jnp.bfloat16), (rim_matrix - rim_high).astype(jnp.bfloat16)], 0
+    )
     ghost = ring(jnp.concatenate([face_states, mass_potential], 1), "dom", -1)
     field_start = jnp.concatenate([states.astype(jnp.float32), ghost[:, :state_count]], 0)
     wide_mass = jnp.concatenate([inv_mass, ghost[:, state_count]], 0)
@@ -71,7 +82,8 @@
             "ij,cjb->cib", padded_matrix, values, preferred_element_type=jnp.float32
         ).reshape(-1, state_count)
         both = high_low(products)
-        rim = summed_halves(jnp.dot(rim_sel, both, preferred_element_type=jnp.float32))
+        rim_two = jnp.dot(rim_both, values.reshape(-1, state_count), preferred_element_type=jnp.float32)
+        rim = rim_two[: 2 * face_count] + rim_two[2 * face_count :]
         from_prev = ring(rim[face_count:], "dom", 1)
         from_next = ring(rim[:face_count], "dom", -1)
         main = summed_halves(jnp.dot(scatter_sel, both, preferred_element_type=jnp.float32))

time: 67.3 us -> 85.1 us (1.26)
  other arithmetic: 6.6 us -> 15.5 us
  local copies, waits for them, and re-layouts: 5.43 us -> 12.8 us
  matrix products: 27.2 us -> 33.8 us
  waiting for transfers between devices: 13.9 us -> 9.64 us
  starting transfers between devices: 13.2 us -> 11.9 us
    ppermute x7, waiting for transfers between devices: 6.05 us -> 0.02 us  [ring(): return lax.ppermute(block, axis, route)]
    dot_general x4 -> x5, matrix products: 3.27 us -> 7.92 us  [the longest x1 3.01 us: body(): jnp.einsum('rci,ij->rcj', rim_cells, padded_matrix, preferred_element_typ...]
    reshape x0 -> x1, local copies, waits for them, and re-layouts: none -> 3.26 us  [body(): rim_matrix = jnp.einsum('rci,ij->rcj', rim_cells, padded_matrix, preferre...]
    convert_element_type x6, other arithmetic: 0.73 us -> 3.38 us  [high_low(): high.astype(jnp.bfloat16)]
    add x3, other arithmetic: 0.04 us -> 2.68 us  [operate(): summed = jnp.concatenate([own, main[node_count:] + from_next], 0)]
    dot_general x3, matrix products: 9.05 us -> 11.1 us  [operate(): jnp.dot(scatter_sel, both, preferred_element_type=jnp.float32)]
    slice x3, local copies, waits for them, and re-layouts: 0.04 us -> 2.07 us  [operate(): from_prev = ring(rim[face_count:], 'dom', 1)]
    concatenate x0 -> x1, other arithmetic: none -> 1.89 us  [body(): jnp.concatenate([rim_high.astype(jnp.bfloat16), (rim_matrix - rim_high).a...]
  transfers between devices with their start and end apart: 10 -> 10, of which waited for: 6 -> 2; matrix products, arithmetic and copies ran while one was open for 19% -> 40% of each run, Pallas kernels for 0% -> 0%
where the time goes in v4:
time: 85.1 us; the launch traced here: 84.1 us
  matrix products  33.8 us (40%)
  other arithmetic  15.5 us (18%)
  local copies, waits for them, and re-layouts  12.8 us (15%)
  starting transfers between devices  11.9 us (14%)
  waiting for transfers between devices  9.64 us (11%)
    dot_general x3, matrix products, operate(): jnp.dot(scatter_sel, both, preferred_element_type=jnp.float32)  11.1 us
    ppermute x7, starting transfers between devices, ring(): return lax.ppermute(block, axis, route)  10.3 us
    ppermute x3, waiting for transfers between devices, from_partner(): return lax.ppermute(block, axis, route)  9.62 us
    dot_general x3, matrix products, operate(): lax.dot_general(scatter_sel, weighted, (((0,), (0,)), ((), ())), preferre...  7.01 us
    dot_general x3, matrix products, operate(): jnp.einsum('ij,cjb->cib', padded_matrix, values, preferred_element_type=j...  4.46 us
    sub x3, other arithmetic, chebyshev_step(): return (current, gain * scaled - keep * previous)  3.86 us
    convert_element_type x6, other arithmetic, high_low(): high.astype(jnp.bfloat16)  3.38 us
    reshape x1, local copies, waits for them, and re-layouts, body(): rim_matrix = jnp.einsum('rci,ij->rcj', rim_cells, padded_matrix, preferre...  3.26 us
  transfers between devices with their start and end apart: 10, of which 2 were waited for; matrix products, arithmetic and copies ran while one was open for 40% of the time, Pallas kernels for 0%

profile of v4, /device:TPU:0, one launch (start us, length us, event | category | flops | bytes accessed | tf_op | source)
XLA Modules:
  0.0 84.1 jit_solution(13902397348641994033)
XLA Ops:
  3.2 1.9 %fusion.42 = f32[144,128]{1,0:T(8,128)S(1)} fusion(bf16[1728,128]{1,0:T(8,128)(2,1)} %param.9, s32[144]{0:T(256)} %param.14, s32[1728]{0:T(1024)S(1)} %add_reduce_fusion), kind=kOutput, calls=%fused_computation.55 | convolution fusion | flops 63949824 | bytes 523584 | tf_op jit(solution)/shard_map/dot_general | solution.py:56
  5.8 3.9 %collective-permute-start.2 = (f32[144,130]{1,0:T(8,128)}, f32[144,130]{1,0:T(8,128)S(1)}, u32[]{:S(2)}, u32[]{:S(2)}) collective-permute-start(f32[144,130]{1,0:T(8,128)} %pad_maximum_fusion.2), channel_id=1, source_target_pairs={{0,24},{8,0},{16,8},{24,16},{1,25},{9,1},{17,9},{25,17},{2,26},{10... | collective-permute-start | bytes 224648 | tf_op jit(solution)/shard_map/ppermute | solution.py:16
  11.2 3.0 %fusion.37 = f32[288,8,352]{2,1,0:T(8,128)} fusion(s32[8,352]{1,0:T(8,128)S(1)} %pad.8, s32[288]{0:T(512)S(1)} %pad_add_fusion, bf16[343,343]{1,0:T(8,128)(2,1)S(1)} %copy-done.2), kind=kOutput, calls=%fused_computation.46 | convolution fusion | flops 571760640 | bytes 3491746 | tf_op jit(solution)/shard_map/rci,ij->rcj/dot_general | solution.py:63
  14.2 3.3 %reshape.33 = f32[288,2816]{1,0:T(8,128)S(1)} reshape(f32[288,8,352]{2,1,0:T(8,128)} %fusion.37) | data formatting | bytes 6488064 | tf_op jit(solution)/shard_map/reshape | solution.py:65
  17.9 1.9 %pad_maximum_fusion = bf16[576,2816]{1,0:T(8,128)(2,1)} fusion(bf16[288,2816]{1,0:T(8,128)(2,1)S(1)} %get-tuple-element.215, bf16[288,2816]{1,0:T(8,128)(2,1)S(1)} %get-tuple-element.214), kind=kLoop, calls=%fused_computation.49 | loop fusion | flops 6488064 | bytes 6488064 | tf_op jit(solution)/shard_map/concatenate | solution.py:67
  21.1 49.7 %while.16 = (s32[]{:T(128)}, f32[1872,128]{1,0:T(8,128)S(1)}, f32[1872,128]{1,0:T(8,128)S(1)}, f32[1872]{0:T(1024)S(1)}, bf16[352,352]{1,0:T(8,128)(2,1)}, /*ind...) while((s32[]{:T(128)}, f32[1872,128]{1,0:T(8,128)S(1)}, ...), condition=%wide.region_1.2_spmd.clone, body=%wide.region_0.1_spmd.clone.sunk | while | flops 4874809344 | bytes 46773876 | solution.py:104
  21.1 2.3 %fusion.89 = bf16[128,2816]{1,0:T(8,128)(2,1)S(1)} fusion(s32[2816]{0:T(1024)S(1)} %get-tuple-element.330, f32[1872,128]{1,0:T(8,128)S(1)} %get-tuple-element.309, f32[1872]{0:T(1024)S(1)} %get-tuple-element.326), kind=kOutput, calls=%fused_computation.9.clone.1 | convolution fusion | flops 1360900096 | bytes 1698112 | tf_op jit(solution)/shard_map/while/body/eval_jaxpr/dot_general | solution.py:77
  25.7 1.5 %collective-permute-start.1 = (f32[144,128]{1,0:T(8,128)}, f32[144,128]{1,0:T(8,128)}, u32[]{:S(2)}, u32[]{:S(2)}) collective-permute-start(f32[144,128]{1,0:T(8,128)} %get-tuple-element.288), channel_id=1, source_target_pairs={{0,8},{8,16},{16,24},{24,0},{1,9},{9,17},{17,25},{25,1},{2,10},{10... | collective-permute-start | bytes 221192 | tf_op jit(solution)/shard_map/while/body/eval_jaxpr/ppermute | solution.py:16
  27.6 1.5 %fusion.91 = f32[8,128,352]{1,2,0:T(8,128)S(1)} fusion(bf16[8,352,128]{2,1,0:T(8,128)(2,1)S(1)} %bitcast.47, bf16[352,352]{1,0:T(8,128)(2,1)} %get-tuple-element.327), kind=kOutput, calls=%fused_computation.32.clone.1 | convolution fusion | flops 253755392 | bytes 2410496 | tf_op jit(solution)/shard_map/while/body/eval_jaxpr/ij,cjb->cib/dot_general | solution.py:81
  29.3 3.7 %fusion.92 = f32[1872,256]{1,0:T(8,128)S(1)} fusion(s32[2816]{0:T(1024)} %copy-done.8, bf16[2816,128]{1,0:T(8,128)(2,1)S(1)} %get-tuple-element.286, bf16[2816,128]{1,0:T(8,128)(2,1)S(1)} %get-tuple-element.287), kind=kOutput, calls=%fused_computation.11.clone.1 | convolution fusion | flops 2712461312 | bytes 3369984 | tf_op jit(solution)/shard_map/while/body/eval_jaxpr/dot_general | solution.py:89
  35.6 1.3 %fusion.94 = f32[1872,128]{1,0:T(8,128)S(1)} fusion(f32[144,128]{1,0:T(8,128)S(1)} %slice_add_fusion.9, f32[1728,128]{1,0:T(8,128)S(1)} %fusion.93, f32[1872,128]{1,0:T(8,128)S(1)} %get-tuple-element.308, f32[1872,128]{1,0:T(8,128)S(1)} %get-tuple-element.309, f32[]{:T(128)S(6)} %select_n.48, f32[]{:T(128)S(6)} %mul.160, ...), kind=kLoop, calls=%fused_computation.25.clone.1 | loop fusion | flops 2156544 | bytes 3848840 | tf_op jit(solution)/shard_map/while/body/eval_jaxpr/sub | solution.py:102
  37.6 2.3 %fusion.89 = bf16[128,2816]{1,0:T(8,128)(2,1)S(1)} fusion(s32[2816]{0:T(1024)S(1)} %get-tuple-element.330, f32[1872,128]{1,0:T(8,128)S(1)} %get-tuple-element.309, f32[1872]{0:T(1024)S(1)} %get-tuple-element.326), kind=kOutput, calls=%fused_computation.9.clone.1 | convolution fusion | flops 1360900096 | bytes 1698112 | tf_op jit(solution)/shard_map/while/body/eval_jaxpr/dot_general | solution.py:77
  41.7 1.4 %collective-permute-start = (f32[144,128]{1,0:T(8,128)}, f32[144,128]{1,0:T(8,128)}, u32[]{:S(2)}, u32[]{:S(2)}) collective-permute-start(f32[144,128]{1,0:T(8,128)} %get-tuple-element.285), channel_id=1, source_target_pairs={{0,24},{8,0},{16,8},{24,16},{1,25},{9,1},{17,9},{25,17},{2,26},{10... | collective-permute-start | bytes 221192 | tf_op jit(solution)/shard_map/while/body/eval_jaxpr/ppermute | solution.py:16
  44.1 1.5 %fusion.91 = f32[8,128,352]{1,2,0:T(8,128)S(1)} fusion(bf16[8,352,128]{2,1,0:T(8,128)(2,1)S(1)} %bitcast.47, bf16[352,352]{1,0:T(8,128)(2,1)} %get-tuple-element.327), kind=kOutput, calls=%fused_computation.32.clone.1 | convolution fusion | flops 253755392 | bytes 2410496 | tf_op jit(solution)/shard_map/while/body/eval_jaxpr/ij,cjb->cib/dot_general | solution.py:81
  45.8 3.7 %fusion.92 = f32[1872,256]{1,0:T(8,128)S(1)} fusion(s32[2816]{0:T(1024)} %copy-done.8, bf16[2816,128]{1,0:T(8,128)(2,1)S(1)} %get-tuple-element.286, bf16[2816,128]{1,0:T(8,128)(2,1)S(1)} %get-tuple-element.287), kind=kOutput, calls=%fused_computation.11.clone.1 | convolution fusion | flops 2712461312 | bytes 3369984 | tf_op jit(solution)/shard_map/while/body/eval_jaxpr/dot_general | solution.py:89
  52.1 1.3 %fusion.94 = f32[1872,128]{1,0:T(8,128)S(1)} fusion(f32[144,128]{1,0:T(8,128)S(1)} %slice_add_fusion.9, f32[1728,128]{1,0:T(8,128)S(1)} %fusion.93, f32[1872,128]{1,0:T(8,128)S(1)} %get-tuple-element.308, f32[1872,128]{1,0:T(8,128)S(1)} %get-tuple-element.309, f32[]{:T(128)S(6)} %select_n.48, f32[]{:T(128)S(6)} %mul.160, ...), kind=kLoop, calls=%fused_computation.25.clone.1 | loop fusion | flops 2156544 | bytes 3848840 | tf_op jit(solution)/shard_map/while/body/eval_jaxpr/sub | solution.py:102
  54.1 2.3 %fusion.89 = bf16[128,2816]{1,0:T(8,128)(2,1)S(1)} fusion(s32[2816]{0:T(1024)S(1)} %get-tuple-element.330, f32[1872,128]{1,0:T(8,128)S(1)} %get-tuple-element.309, f32[1872]{0:T(1024)S(1)} %get-tuple-element.326), kind=kOutput, calls=%fused_computation.9.clone.1 | convolution fusion | flops 1360900096 | bytes 1698112 | tf_op jit(solution)/shard_map/while/body/eval_jaxpr/dot_general | solution.py:77
  58.2 2.3 %collective-permute-start = (f32[144,128]{1,0:T(8,128)}, f32[144,128]{1,0:T(8,128)}, u32[]{:S(2)}, u32[]{:S(2)}) collective-permute-start(f32[144,128]{1,0:T(8,128)} %get-tuple-element.285), channel_id=1, source_target_pairs={{0,24},{8,0},{16,8},{24,16},{1,25},{9,1},{17,9},{25,17},{2,26},{10... | collective-permute-start | bytes 221192 | tf_op jit(solution)/shard_map/while/body/eval_jaxpr/ppermute | solution.py:16
  60.8 1.5 %fusion.91 = f32[8,128,352]{1,2,0:T(8,128)S(1)} fusion(bf16[8,352,128]{2,1,0:T(8,128)(2,1)S(1)} %bitcast.47, bf16[352,352]{1,0:T(8,128)(2,1)} %get-tuple-element.327), kind=kOutput, calls=%fused_computation.32.clone.1 | convolution fusion | flops 253755392 | bytes 2410496 | tf_op jit(solution)/shard_map/while/body/eval_jaxpr/ij,cjb->cib/dot_general | solution.py:81
  62.6 3.7 %fusion.92 = f32[1872,256]{1,0:T(8,128)S(1)} fusion(s32[2816]{0:T(1024)} %copy-done.8, bf16[2816,128]{1,0:T(8,128)(2,1)S(1)} %get-tuple-element.286, bf16[2816,128]{1,0:T(8,128)(2,1)S(1)} %get-tuple-element.287), kind=kOutput, calls=%fused_computation.11.clone.1 | convolution fusion | flops 2712461312 | bytes 3369984 | tf_op jit(solution)/shard_map/while/body/eval_jaxpr/dot_general | solution.py:89
  68.8 1.3 %fusion.94 = f32[1872,128]{1,0:T(8,128)S(1)} fusion(f32[144,128]{1,0:T(8,128)S(1)} %slice_add_fusion.9, f32[1728,128]{1,0:T(8,128)S(1)} %fusion.93, f32[1872,128]{1,0:T(8,128)S(1)} %get-tuple-element.308, f32[1872,128]{1,0:T(8,128)S(1)} %get-tuple-element.309, f32[]{:T(128)S(6)} %select_n.48, f32[]{:T(128)S(6)} %mul.160, ...), kind=kLoop, calls=%fused_computation.25.clone.1 | loop fusion | flops 2156544 | bytes 3848840 | tf_op jit(solution)/shard_map/while/body/eval_jaxpr/sub | solution.py:102
  70.9 1.7 %collective-permute-start.4 = (bf16[1728,128]{1,0:T(8,128)(2,1)S(1)}, bf16[1728,128]{1,0:T(8,128)(2,1)S(1)}, u32[]{:S(2)}, u32[]{:S(2)}) collective-permute-start(bf16[1728,128]{1,0:T(8,128)(2,1)S(1)} %slice.134), channel_id=1, source_target_pairs={{0,2},{2,0},{1,3},{3,1},{4,6},{6,4},{5,7},{7,5},{8,10},{10,8},{9,1... | collective-permute-start | bytes 1327112 | tf_op jit(solution)/shard_map/ppermute | solution.py:26
  72.8 8.4 %collective-permute-done.4 = bf16[1728,128]{1,0:T(8,128)(2,1)S(1)} collective-permute-done((bf16[1728,128]{1,0:T(8,128)(2,1)S(1)}, bf16[1728,128]{1,0:T(8,128)(2,1)S(1)}, u32[]{:S(2)}, u32[]{:S(2)}) %collective-permute-start.4) | collective-permute-done | bytes 442400 | tf_op jit(solution)/shard_map/ppermute | solution.py:26
  81.7 1.3 %collective-permute-done.5 = bf16[1728,128]{1,0:T(8,128)(2,1)S(1)} collective-permute-done((bf16[1728,128]{1,0:T(8,128)(2,1)S(1)}, bf16[1728,128]{1,0:T(8,128)(2,1)S(1)}, u32[]{:S(2)}, u32[]{:S(2)}) %collective-permute-start.5) | collective-permute-done | bytes 442400 | tf_op jit(solution)/shard_map/ppermute | solution.py:26
  (107 shorter events, 26.7 us)
Async XLA Ops:
  0.0 72.6 %copy-start = (bf16[512,128]{1,0:T(8,128)(2,1)S(1)}, bf16[512,128]{1,0:T(8,128)(2,1)}, u32[]{:S(2)}) copy-start(bf16[512,128]{1,0:T(8,128)(2,1)} %param.15) | copy-start | bytes 393220
  0.0 11.2 %copy-start.2 = (bf16[343,343]{1,0:T(8,128)(2,1)S(1)}, bf16[343,343]{1,0:T(8,128)(2,1)}, u32[]{:S(2)}) copy-start(bf16[343,343]{1,0:T(8,128)(2,1)} %param.12) | copy-start | bytes 705898
  5.8 14.9 %collective-permute-start.2 = (f32[144,130]{1,0:T(8,128)}, f32[144,130]{1,0:T(8,128)S(1)}, u32[]{:S(2)}, u32[]{:S(2)}) collective-permute-start(f32[144,130]{1,0:T(8,128)} %pad_maximum_fusion.2), channel_id=1, source_target_pairs={{0,24},{8,0},{16,8},{24,16},{1,25},{9,1},{17,9},{25,17},{2,26},{10... | collective-permute-start | bytes 224648 | tf_op jit(solution)/shard_map/ppermute | solution.py:16
  17.8 1.9 %copy-start.4 = (bf16[1728,128]{1,0:T(8,128)(2,1)S(1)}, bf16[1728,128]{1,0:T(8,128)(2,1)}, u32[]{:S(2)}) copy-start(bf16[1728,128]{1,0:T(8,128)(2,1)} %param.9) | copy-start | bytes 1327108
  17.8 2.1 %copy-start.3 = (bf16[343,343]{1,0:T(8,128)(2,1)S(1)}, bf16[343,343]{1,0:T(8,128)(2,1)}, u32[]{:S(2)}) copy-start(bf16[343,343]{1,0:T(8,128)(2,1)} %param.12) | copy-start | bytes 705898
  19.8 1.3 %copy-start.6 = (f32[1728]{0:T(1024)S(1)}, f32[1728]{0:T(1024)}, u32[]{:S(2)}) copy-start(f32[1728]{0:T(1024)} %param.11) | copy-start | bytes 20740
  19.8 1.3 %copy-start.7 = (f32[1728]{0:T(1024)S(1)}, f32[1728]{0:T(1024)}, u32[]{:S(2)}) copy-start(f32[1728]{0:T(1024)} %param.10) | copy-start | bytes 20740
  19.8 1.4 %copy-start.5 = (s32[144]{0:T(256)S(1)}, s32[144]{0:T(256)}, u32[]{:S(2)}) copy-start(s32[144]{0:T(256)} %param.14) | copy-start | bytes 1732
  21.1 6.1 %copy-start.8 = (s32[2816]{0:T(1024)}, s32[2816]{0:T(1024)S(1)}, u32[]{:S(2)}) copy-start(s32[2816]{0:T(1024)S(1)} %get-tuple-element.330) | copy-start | bytes 33796 | tf_op jit(solution)/shard_map/while
  21.1 2.4 %copy-start.1 = (bf16[576,2816]{1,0:T(8,128)(2,1)S(1)}, bf16[576,2816]{1,0:T(8,128)(2,1)}, u32[]{:S(2)}) copy-start(bf16[576,2816]{1,0:T(8,128)(2,1)} %get-tuple-element.328) | copy-start | bytes 9732100 | tf_op jit(solution)/shard_map/while
  25.2 9.5 %collective-permute-start = (f32[144,128]{1,0:T(8,128)}, f32[144,128]{1,0:T(8,128)}, u32[]{:S(2)}, u32[]{:S(2)}) collective-permute-start(f32[144,128]{1,0:T(8,128)} %get-tuple-element.285), channel_id=1, source_target_pairs={{0,24},{8,0},{16,8},{24,16},{1,25},{9,1},{17,9},{25,17},{2,26},{10... | collective-permute-start | bytes 221192 | tf_op jit(solution)/shard_map/while/body/eval_jaxpr/ppermute | solution.py:16
  25.7 7.4 %collective-permute-start.1 = (f32[144,128]{1,0:T(8,128)}, f32[144,128]{1,0:T(8,128)}, u32[]{:S(2)}, u32[]{:S(2)}) collective-permute-start(f32[144,128]{1,0:T(8,128)} %get-tuple-element.288), channel_id=1, source_target_pairs={{0,8},{8,16},{16,24},{24,0},{1,9},{9,17},{17,25},{25,1},{2,10},{10... | collective-permute-start | bytes 221192 | tf_op jit(solution)/shard_map/while/body/eval_jaxpr/ppermute | solution.py:16
  36.9 0.7 copy-start.9
  37.6 6.1 %copy-start.8 = (s32[2816]{0:T(1024)}, s32[2816]{0:T(1024)S(1)}, u32[]{:S(2)}) copy-start(s32[2816]{0:T(1024)S(1)} %get-tuple-element.330) | copy-start | bytes 33796 | tf_op jit(solution)/shard_map/while
  37.6 2.3 %copy-start.1 = (bf16[576,2816]{1,0:T(8,128)(2,1)S(1)}, bf16[576,2816]{1,0:T(8,128)(2,1)}, u32[]{:S(2)}) copy-start(bf16[576,2816]{1,0:T(8,128)(2,1)} %get-tuple-element.328) | copy-start | bytes 9732100 | tf_op jit(solution)/shard_map/while
  41.7 9.5 %collective-permute-start = (f32[144,128]{1,0:T(8,128)}, f32[144,128]{1,0:T(8,128)}, u32[]{:S(2)}, u32[]{:S(2)}) collective-permute-start(f32[144,128]{1,0:T(8,128)} %get-tuple-element.285), channel_id=1, source_target_pairs={{0,24},{8,0},{16,8},{24,16},{1,25},{9,1},{17,9},{25,17},{2,26},{10... | collective-permute-start | bytes 221192 | tf_op jit(solution)/shard_map/while/body/eval_jaxpr/ppermute | solution.py:16
  43.1 6.5 %collective-permute-start.1 = (f32[144,128]{1,0:T(8,128)}, f32[144,128]{1,0:T(8,128)}, u32[]{:S(2)}, u32[]{:S(2)}) collective-permute-start(f32[144,128]{1,0:T(8,128)} %get-tuple-element.288), channel_id=1, source_target_pairs={{0,8},{8,16},{16,24},{24,0},{1,9},{9,17},{17,25},{25,1},{2,10},{10... | collective-permute-start | bytes 221192 | tf_op jit(solution)/shard_map/while/body/eval_jaxpr/ppermute | solution.py:16
  54.1 6.4 %copy-start.8 = (s32[2816]{0:T(1024)}, s32[2816]{0:T(1024)S(1)}, u32[]{:S(2)}) copy-start(s32[2816]{0:T(1024)S(1)} %get-tuple-element.330) | copy-start | bytes 33796 | tf_op jit(solution)/shard_map/while
  54.1 2.3 %copy-start.1 = (bf16[576,2816]{1,0:T(8,128)(2,1)S(1)}, bf16[576,2816]{1,0:T(8,128)(2,1)}, u32[]{:S(2)}) copy-start(bf16[576,2816]{1,0:T(8,128)(2,1)} %get-tuple-element.328) | copy-start | bytes 9732100 | tf_op jit(solution)/shard_map/while
  58.2 9.8 %collective-permute-start = (f32[144,128]{1,0:T(8,128)}, f32[144,128]{1,0:T(8,128)}, u32[]{:S(2)}, u32[]{:S(2)}) collective-permute-start(f32[144,128]{1,0:T(8,128)} %get-tuple-element.285), channel_id=1, source_target_pairs={{0,24},{8,0},{16,8},{24,16},{1,25},{9,1},{17,9},{25,17},{2,26},{10... | collective-permute-start | bytes 221192 | tf_op jit(solution)/shard_map/while/body/eval_jaxpr/ppermute | solution.py:16
  60.5 5.9 %collective-permute-start.1 = (f32[144,128]{1,0:T(8,128)}, f32[144,128]{1,0:T(8,128)}, u32[]{:S(2)}, u32[]{:S(2)}) collective-permute-start(f32[144,128]{1,0:T(8,128)} %get-tuple-element.288), channel_id=1, source_target_pairs={{0,8},{8,16},{16,24},{24,0},{1,9},{9,17},{17,25},{25,1},{2,10},{10... | collective-permute-start | bytes 221192 | tf_op jit(solution)/shard_map/while/body/eval_jaxpr/ppermute | solution.py:16
  70.9 10.3 %collective-permute-start.4 = (bf16[1728,128]{1,0:T(8,128)(2,1)S(1)}, bf16[1728,128]{1,0:T(8,128)(2,1)S(1)}, u32[]{:S(2)}, u32[]{:S(2)}) collective-permute-start(bf16[1728,128]{1,0:T(8,128)(2,1)S(1)} %slice.134), channel_id=1, source_target_pairs={{0,2},{2,0},{1,3},{3,1},{4,6},{6,4},{5,7},{7,5},{8,10},{10,8},{9,1... | collective-permute-start | bytes 1327112 | tf_op jit(solution)/shard_map/ppermute | solution.py:26
  72.5 8.6 %collective-permute-start.3 = (bf16[1728,128]{1,0:T(8,128)(2,1)S(1)}, bf16[1728,128]{1,0:T(8,128)(2,1)S(1)}, u32[]{:S(2)}, u32[]{:S(2)}) collective-permute-start(bf16[1728,128]{1,0:T(8,128)(2,1)S(1)} %slice.134), channel_id=1, source_target_pairs={{0,1},{1,0},{2,3},{3,2},{4,5},{5,4},{6,7},{7,6},{8,9},{9,8},{10,11... | collective-permute-start | bytes 1327112 | tf_op jit(solution)/shard_map/ppermute | solution.py:26
  81.2 1.8 %collective-permute-start.5 = (bf16[1728,128]{1,0:T(8,128)(2,1)S(1)}, bf16[1728,128]{1,0:T(8,128)(2,1)S(1)}, u32[]{:S(2)}, u32[]{:S(2)}) collective-permute-start(bf16[1728,128]{1,0:T(8,128)(2,1)S(1)} %collective-permute-done.4), channel_id=1, source_target_pairs={{0,1},{1,0},{2,3},{3,2},{4,5},{5,4},{6,7},{7,6},{8,9},{9,8},{10,11... | collective-permute-start | bytes 1327112 | tf_op jit(solution)/shard_map/ppermute | solution.py:26
  (2 other events, 1.4 us)

commit v5 on v3

--- a/solution.py
+++ b/solution.py
@@ -55,11 +55,17 @@
     face_take = (face_rows[:, None] == wide_ids[:node_count, 0][None, :]).astype(jnp.bfloat16)
 
     face_states = jnp.dot(face_take, states, preferred_element_type=jnp.float32)
-    mass_potential = jnp.stack([inv_mass, potential], 1)[face_rows]
-    ghost = ring(jnp.concatenate([face_states, mass_potential], 1), "dom", -1)
-    field_start = jnp.concatenate([states.astype(jnp.float32), ghost[:, :state_count]], 0)
-    wide_mass = jnp.concatenate([inv_mass, ghost[:, state_count]], 0)
-    wide_potential = jnp.concatenate([potential, ghost[:, state_count + 1]], 0)
+    face_mass_potential = lax.dot_general(
+        jnp.stack([inv_mass, potential], 0),
+        face_put.astype(jnp.float32),
+        (((1,), (0,)), ((), ())),
+        precision=lax.Precision.HIGHEST,
+        preferred_element_type=jnp.float32,
+    )
+    ghost_states, ghost_mass_potential = ring((face_states, face_mass_potential), "dom", -1)
+    field_start = jnp.concatenate([states.astype(jnp.float32), ghost_states], 0)
+    wide_mass = jnp.concatenate([inv_mass, ghost_mass_potential[0]], 0)
+    wide_potential = jnp.concatenate([potential, ghost_mass_potential[1]], 0)
 
     def operate(field_in):
         weighted = (wide_mass[:, None] * field_in).astype(jnp.bfloat16)

time: 67.3 us -> 65.2 us (0.969)
  waiting for transfers between devices: 13.9 us -> 11.6 us
  matrix products: 27.2 us -> 28.6 us
  local copies, waits for them, and re-layouts: 5.43 us -> 4.35 us
  other arithmetic: 6.6 us -> 7.43 us
  starting transfers between devices: 13.2 us -> 12.4 us
    ppermute x7 -> x8, waiting for transfers between devices: 6.05 us -> 3.85 us  [ring(): return lax.ppermute(block, axis, route)]
    dot_general x0 -> x1, matrix products: none -> 1.36 us  [body(): lax.dot_general(jnp.stack([inv_mass, potential], 0), face_put.astype(jnp....]
    convert_element_type x1, other arithmetic: 0.06 us -> 1.07 us  [body(): field_start = jnp.concatenate([states.astype(jnp.float32), ghost_states], 0)]
    ppermute x7 -> x8, starting transfers between devices: 11.5 us -> 10.7 us  [ring(): return lax.ppermute(block, axis, route)]
    select_n x1 -> x0, other arithmetic: 0.75 us -> none  [body(): mass_potential = jnp.stack([inv_mass, potential], 1)[face_rows]]
    concatenate x1, other arithmetic: 0.07 us -> 0.75 us  [body(): rim_ids = jnp.concatenate([face_rows, wide_ids[node_count:, 0]], 0)]
    another operation x3 -> x2, local copies, waits for them, and re-layouts: 1.78 us -> 1.4 us  [body(): jnp.stack([inv_mass, potential], 0)]
  transfers between devices with their start and end apart: 10 -> 11, of which waited for: 6 -> 6; matrix products, arithmetic and copies ran while one was open for 19% -> 27% of each run, Pallas kernels for 0% -> 0%
where the time goes in v5:
time: 65.2 us; the launch traced here: 64.8 us
  matrix products  28.6 us (44%)
  starting transfers between devices  12.4 us (19%)
  waiting for transfers between devices  11.6 us (18%)
  other arithmetic  7.43 us (11%)
  local copies, waits for them, and re-layouts  4.35 us (7%)
    ppermute x8, starting transfers between devices, ring(): return lax.ppermute(block, axis, route)  10.7 us
    dot_general x3, matrix products, operate(): jnp.dot(scatter_sel, both, preferred_element_type=jnp.float32)  8.99 us
    ppermute x3, waiting for transfers between devices, from_partner(): return lax.ppermute(block, axis, route)  7.72 us
    dot_general x3, matrix products, operate(): lax.dot_general(scatter_sel, weighted, (((0,), (0,)), ((), ())), preferre...  7.05 us
    dot_general x3, matrix products, operate(): jnp.einsum('ij,cjb->cib', padded_matrix, values, preferred_element_type=j...  4.46 us
    sub x3, other arithmetic, chebyshev_step(): return (current, gain * scaled - keep * previous)  3.86 us
    ppermute x8, waiting for transfers between devices, ring(): return lax.ppermute(block, axis, route)  3.85 us
    dot_general x3, matrix products, operate(): jnp.dot(rim_sel, both, preferred_element_type=jnp.float32)  1.89 us
  transfers between devices with their start and end apart: 11, of which 6 were waited for; matrix products, arithmetic and copies ran while one was open for 27% of the time, Pallas kernels for 0%

profile of v5, /device:TPU:0, one launch (start us, length us, event | category | flops | bytes accessed | tf_op | source)
XLA Modules:
  0.0 64.8 jit_solution(9469264238667536867)
XLA Ops:
  0.1 1.4 %fusion.46 = f32[144,128]{1,0:T(8,128)S(1)} fusion(bf16[1728,128]{1,0:T(8,128)(2,1)} %param.9, s32[1728]{0:T(1024)S(1)} %add_reduce_fusion, s32[144]{0:T(256)} %param.14), kind=kOutput, calls=%fused_computation.53 | convolution fusion | flops 63949824 | bytes 523584 | tf_op jit(solution)/shard_map/dot_general | solution.py:57
  1.5 4.0 %collective-permute-start.2 = (f32[144,128]{1,0:T(8,128)S(1)}, f32[144,128]{1,0:T(8,128)S(1)}, u32[]{:S(2)}, u32[]{:S(2)}) collective-permute-start(f32[144,128]{1,0:T(8,128)S(1)} %fusion.46), channel_id=1, source_target_pairs={{0,24},{8,0},{16,8},{24,16},{1,25},{9,1},{17,9},{25,17},{2,26},{10... | collective-permute-start | bytes 221192 | tf_op jit(solution)/shard_map/ppermute | solution.py:16
  6.9 1.4 %fusion.44 = f32[2,144]{1,0:T(2,128)S(1)} fusion(s32[144]{0:T(256)} %param.14, s32[1728]{0:T(1024)S(1)} %add_reduce_fusion, f32[1,1728]{1,0:T(1,128)S(1)} %stack.10, f32[1,1728]{1,0:T(1,128)S(1)} %stack.9), kind=kOutput, calls=%fused_computation.51 | convolution fusion | flops 6224256 | bytes 22464 | tf_op jit(solution)/shard_map/dot_general | solution.py:58
  12.6 40.7 %while.17 = (s32[]{:T(128)}, f32[1872,128]{1,0:T(8,128)S(1)}, f32[1872,128]{1,0:T(8,128)S(1)}, f32[1872]{0:T(1024)S(1)}, bf16[352,352]{1,0:T(8,128)(2,1)}, /*ind...) while((s32[]{:T(128)}, f32[1872,128]{1,0:T(8,128)S(1)}, ...), condition=%wide.region_1.2_spmd.clone.clone, body=%wide.region_0.1_spmd.clone.clone.sunk | while | flops 4879314944 | bytes 31196832 | solution.py:98
  12.6 2.4 %fusion.90 = bf16[2816,128]{0,1:T(8,128)(2,1)S(1)} fusion(s32[2816]{0:T(1024)S(1)} %get-tuple-element.358, f32[1872,128]{1,0:T(8,128)S(1)} %get-tuple-element.338, f32[1872]{0:T(1024)S(1)} %get-tuple-element.355), kind=kOutput, calls=%fused_computation.10.clone.1 | convolution fusion | flops 1360900096 | bytes 1698112 | tf_op jit(solution)/shard_map/while/body/eval_jaxpr/dot_general | solution.py:72
  15.3 1.5 %fusion.91 = f32[8,128,352]{1,2,0:T(8,128)S(1)} fusion(bf16[8,352,128]{2,1,0:T(8,128)(2,1)S(1)} %bitcast.41, bf16[352,352]{1,0:T(8,128)(2,1)} %get-tuple-element.356), kind=kOutput, calls=%fused_computation.35.clone.1 | convolution fusion | flops 253755392 | bytes 2410496 | tf_op jit(solution)/shard_map/while/body/eval_jaxpr/ij,cjb->cib/dot_general | solution.py:76
  17.7 1.5 %collective-permute-start = (f32[144,128]{1,0:T(8,128)S(1)}, f32[144,128]{1,0:T(8,128)S(1)}, u32[]{:S(2)}, u32[]{:S(2)}) collective-permute-start(f32[144,128]{1,0:T(8,128)S(1)} %get-tuple-element.316), channel_id=1, source_target_pairs={{0,24},{8,0},{16,8},{24,16},{1,25},{9,1},{17,9},{25,17},{2,26},{10... | collective-permute-start | bytes 221192 | tf_op jit(solution)/shard_map/while/body/eval_jaxpr/ppermute | solution.py:16
  19.8 3.0 %fusion.94 = f32[1872,256]{1,0:T(8,128)S(1)} fusion(s32[2816]{0:T(1024)S(1)} %get-tuple-element.358, bf16[2816,128]{1,0:T(8,128)(2,1)S(1)} %get-tuple-element.314, bf16[2816,128]{1,0:T(8,128)(2,1)S(1)} %get-tuple-element.315), kind=kOutput, calls=%fused_computation.13.clone.1 | convolution fusion | flops 2712461312 | bytes 3369984 | tf_op jit(solution)/shard_map/while/body/eval_jaxpr/dot_general | solution.py:83
  22.9 1.5 %collective-permute-done.1 = f32[144,128]{1,0:T(8,128)S(1)} collective-permute-done((f32[144,128]{1,0:T(8,128)S(1)}, f32[144,128]{1,0:T(8,128)S(1)}, u32[]{:S(2)}, u32[]{:S(2)}) %collective-permute-start.1) | collective-permute-done | bytes 73760 | tf_op jit(solution)/shard_map/while/body/eval_jaxpr/ppermute | solution.py:16
  25.1 1.3 %fusion.96 = f32[1872,128]{1,0:T(8,128)S(1)} fusion(f32[144,128]{1,0:T(8,128)S(1)} %slice_add_fusion.9, f32[1728,128]{1,0:T(8,128)S(1)} %fusion.95, f32[1872,128]{1,0:T(8,128)S(1)} %get-tuple-element.337, f32[1872,128]{1,0:T(8,128)S(1)} %get-tuple-element.338, f32[]{:T(128)S(6)} %select_n.45, f32[]{:T(128)S(6)} %mul.171, ...), kind=kLoop, calls=%fused_computation.28.clone.1 | loop fusion | flops 2156544 | bytes 3848840 | tf_op jit(solution)/shard_map/while/body/eval_jaxpr/sub | solution.py:96
  26.6 2.4 %fusion.90 = bf16[2816,128]{0,1:T(8,128)(2,1)S(1)} fusion(s32[2816]{0:T(1024)S(1)} %get-tuple-element.358, f32[1872,128]{1,0:T(8,128)S(1)} %get-tuple-element.338, f32[1872]{0:T(1024)S(1)} %get-tuple-element.355), kind=kOutput, calls=%fused_computation.10.clone.1 | convolution fusion | flops 1360900096 | bytes 1698112 | tf_op jit(solution)/shard_map/while/body/eval_jaxpr/dot_general | solution.py:72
  29.3 1.5 %fusion.91 = f32[8,128,352]{1,2,0:T(8,128)S(1)} fusion(bf16[8,352,128]{2,1,0:T(8,128)(2,1)S(1)} %bitcast.41, bf16[352,352]{1,0:T(8,128)(2,1)} %get-tuple-element.356), kind=kOutput, calls=%fused_computation.35.clone.1 | convolution fusion | flops 253755392 | bytes 2410496 | tf_op jit(solution)/shard_map/while/body/eval_jaxpr/ij,cjb->cib/dot_general | solution.py:76
  32.6 1.2 %collective-permute-start.1 = (f32[144,128]{1,0:T(8,128)S(1)}, f32[144,128]{1,0:T(8,128)S(1)}, u32[]{:S(2)}, u32[]{:S(2)}) collective-permute-start(f32[144,128]{1,0:T(8,128)S(1)} %get-tuple-element.317), channel_id=1, source_target_pairs={{0,8},{8,16},{16,24},{24,0},{1,9},{9,17},{17,25},{25,1},{2,10},{10... | collective-permute-start | bytes 221192 | tf_op jit(solution)/shard_map/while/body/eval_jaxpr/ppermute | solution.py:16
  33.8 3.0 %fusion.94 = f32[1872,256]{1,0:T(8,128)S(1)} fusion(s32[2816]{0:T(1024)S(1)} %get-tuple-element.358, bf16[2816,128]{1,0:T(8,128)(2,1)S(1)} %get-tuple-element.314, bf16[2816,128]{1,0:T(8,128)(2,1)S(1)} %get-tuple-element.315), kind=kOutput, calls=%fused_computation.13.clone.1 | convolution fusion | flops 2712461312 | bytes 3369984 | tf_op jit(solution)/shard_map/while/body/eval_jaxpr/dot_general | solution.py:83
  38.5 1.3 %fusion.96 = f32[1872,128]{1,0:T(8,128)S(1)} fusion(f32[144,128]{1,0:T(8,128)S(1)} %slice_add_fusion.9, f32[1728,128]{1,0:T(8,128)S(1)} %fusion.95, f32[1872,128]{1,0:T(8,128)S(1)} %get-tuple-element.337, f32[1872,128]{1,0:T(8,128)S(1)} %get-tuple-element.338, f32[]{:T(128)S(6)} %select_n.45, f32[]{:T(128)S(6)} %mul.171, ...), kind=kLoop, calls=%fused_computation.28.clone.1 | loop fusion | flops 2156544 | bytes 3848840 | tf_op jit(solution)/shard_map/while/body/eval_jaxpr/sub | solution.py:96
  39.9 2.4 %fusion.90 = bf16[2816,128]{0,1:T(8,128)(2,1)S(1)} fusion(s32[2816]{0:T(1024)S(1)} %get-tuple-element.358, f32[1872,128]{1,0:T(8,128)S(1)} %get-tuple-element.338, f32[1872]{0:T(1024)S(1)} %get-tuple-element.355), kind=kOutput, calls=%fused_computation.10.clone.1 | convolution fusion | flops 1360900096 | bytes 1698112 | tf_op jit(solution)/shard_map/while/body/eval_jaxpr/dot_general | solution.py:72
  42.6 1.5 %fusion.91 = f32[8,128,352]{1,2,0:T(8,128)S(1)} fusion(bf16[8,352,128]{2,1,0:T(8,128)(2,1)S(1)} %bitcast.41, bf16[352,352]{1,0:T(8,128)(2,1)} %get-tuple-element.356), kind=kOutput, calls=%fused_computation.35.clone.1 | convolution fusion | flops 253755392 | bytes 2410496 | tf_op jit(solution)/shard_map/while/body/eval_jaxpr/ij,cjb->cib/dot_general | solution.py:76
  46.0 1.1 %collective-permute-start.1 = (f32[144,128]{1,0:T(8,128)S(1)}, f32[144,128]{1,0:T(8,128)S(1)}, u32[]{:S(2)}, u32[]{:S(2)}) collective-permute-start(f32[144,128]{1,0:T(8,128)S(1)} %get-tuple-element.317), channel_id=1, source_target_pairs={{0,8},{8,16},{16,24},{24,0},{1,9},{9,17},{17,25},{25,1},{2,10},{10... | collective-permute-start | bytes 221192 | tf_op jit(solution)/shard_map/while/body/eval_jaxpr/ppermute | solution.py:16
  47.1 3.0 %fusion.94 = f32[1872,256]{1,0:T(8,128)S(1)} fusion(s32[2816]{0:T(1024)S(1)} %get-tuple-element.358, bf16[2816,128]{1,0:T(8,128)(2,1)S(1)} %get-tuple-element.314, bf16[2816,128]{1,0:T(8,128)(2,1)S(1)} %get-tuple-element.315), kind=kOutput, calls=%fused_computation.13.clone.1 | convolution fusion | flops 2712461312 | bytes 3369984 | tf_op jit(solution)/shard_map/while/body/eval_jaxpr/dot_general | solution.py:83
  51.9 1.3 %fusion.96 = f32[1872,128]{1,0:T(8,128)S(1)} fusion(f32[144,128]{1,0:T(8,128)S(1)} %slice_add_fusion.9, f32[1728,128]{1,0:T(8,128)S(1)} %fusion.95, f32[1872,128]{1,0:T(8,128)S(1)} %get-tuple-element.337, f32[1872,128]{1,0:T(8,128)S(1)} %get-tuple-element.338, f32[]{:T(128)S(6)} %select_n.45, f32[]{:T(128)S(6)} %mul.171, ...), kind=kLoop, calls=%fused_computation.28.clone.1 | loop fusion | flops 2156544 | bytes 3848840 | tf_op jit(solution)/shard_map/while/body/eval_jaxpr/sub | solution.py:96
  53.4 1.6 %collective-permute-start.5 = (bf16[1728,128]{1,0:T(8,128)(2,1)S(1)}, bf16[1728,128]{1,0:T(8,128)(2,1)S(1)}, u32[]{:S(2)}, u32[]{:S(2)}) collective-permute-start(bf16[1728,128]{1,0:T(8,128)(2,1)S(1)} %slice.138), channel_id=1, source_target_pairs={{0,2},{2,0},{1,3},{3,1},{4,6},{6,4},{5,7},{7,5},{8,10},{10,8},{9,1... | collective-permute-start | bytes 1327112 | tf_op jit(solution)/shard_map/ppermute | solution.py:26
  55.3 6.5 %collective-permute-done.5 = bf16[1728,128]{1,0:T(8,128)(2,1)S(1)} collective-permute-done((bf16[1728,128]{1,0:T(8,128)(2,1)S(1)}, bf16[1728,128]{1,0:T(8,128)(2,1)S(1)}, u32[]{:S(2)}, u32[]{:S(2)}) %collective-permute-start.5) | collective-permute-done | bytes 442400 | tf_op jit(solution)/shard_map/ppermute | solution.py:26
  62.3 1.2 %collective-permute-done.6 = bf16[1728,128]{1,0:T(8,128)(2,1)S(1)} collective-permute-done((bf16[1728,128]{1,0:T(8,128)(2,1)S(1)}, bf16[1728,128]{1,0:T(8,128)(2,1)S(1)}, u32[]{:S(2)}, u32[]{:S(2)}) %collective-permute-start.6) | collective-permute-done | bytes 442400 | tf_op jit(solution)/shard_map/ppermute | solution.py:26
  63.6 1.2 %convolution_add_fusion = f32[1728,128]{1,0:T(8,128)} fusion(f32[1728,128]{1,0:T(8,128)S(1)} %convolution_add_fusion.1, bf16[1728,128]{1,0:T(8,128)(2,1)S(1)} %collective-permute-done.6, bf16[512,128]{1,0:T(8,128)(2,1)S(1)} %copy-done, s32[]{:T(128)S(6)} %select_n.38), kind=kOutput, calls=%fused_computation.48 | convolution fusion | flops 56844288 | bytes 2244612 | tf_op jit(solution)/shard_map/dot_general | solution.py:111
  (79 shorter events, 17.3 us)
Async XLA Ops:
  0.0 55.0 %copy-start = (bf16[512,128]{1,0:T(8,128)(2,1)S(1)}, bf16[512,128]{1,0:T(8,128)(2,1)}, u32[]{:S(2)}) copy-start(bf16[512,128]{1,0:T(8,128)(2,1)} %param.15) | copy-start | bytes 393220
  0.0 11.8 %copy-start.3 = (f32[1728]{0:T(1024)S(1)}, f32[1728]{0:T(1024)}, u32[]{:S(2)}) copy-start(f32[1728]{0:T(1024)} %param.11) | copy-start | bytes 20740
  0.0 11.8 %copy-start.4 = (f32[1728]{0:T(1024)S(1)}, f32[1728]{0:T(1024)}, u32[]{:S(2)}) copy-start(f32[1728]{0:T(1024)} %param.10) | copy-start | bytes 20740
  0.0 10.6 %copy-start.5 = (s32[8,343]{1,0:T(8,128)S(1)}, s32[8,343]{1,0:T(8,128)}, u32[]{:S(2)}) copy-start(s32[8,343]{1,0:T(8,128)} %param.13) | copy-start | bytes 32932
  0.0 10.7 %copy-start.1 = (bf16[343,343]{1,0:T(8,128)(2,1)S(1)}, bf16[343,343]{1,0:T(8,128)(2,1)}, u32[]{:S(2)}) copy-start(bf16[343,343]{1,0:T(8,128)(2,1)} %param.12) | copy-start | bytes 705898
  1.5 10.4 %collective-permute-start.2 = (f32[144,128]{1,0:T(8,128)S(1)}, f32[144,128]{1,0:T(8,128)S(1)}, u32[]{:S(2)}, u32[]{:S(2)}) collective-permute-start(f32[144,128]{1,0:T(8,128)S(1)} %fusion.46), channel_id=1, source_target_pairs={{0,24},{8,0},{16,8},{24,16},{1,25},{9,1},{17,9},{25,17},{2,26},{10... | collective-permute-start | bytes 221192 | tf_op jit(solution)/shard_map/ppermute | solution.py:16
  8.2 3.6 %collective-permute-start.3 = (f32[2,144]{1,0:T(2,128)S(1)}, f32[2,144]{1,0:T(2,128)S(1)}, u32[]{:S(2)}, u32[]{:S(2)}) collective-permute-start(f32[2,144]{1,0:T(2,128)S(1)} %fusion.44), channel_id=1, source_target_pairs={{0,24},{8,0},{16,8},{24,16},{1,25},{9,1},{17,9},{25,17},{2,26},{10... | collective-permute-start | bytes 3464 | tf_op jit(solution)/shard_map/ppermute | solution.py:16
  11.9 0.7 %copy-start.2 = (s32[144]{0:T(256)S(1)}, s32[144]{0:T(256)}, u32[]{:S(2)}) copy-start(s32[144]{0:T(256)} %param.14) | copy-start | bytes 1732
  17.7 7.4 %collective-permute-start = (f32[144,128]{1,0:T(8,128)S(1)}, f32[144,128]{1,0:T(8,128)S(1)}, u32[]{:S(2)}, u32[]{:S(2)}) collective-permute-start(f32[144,128]{1,0:T(8,128)S(1)} %get-tuple-element.316), channel_id=1, source_target_pairs={{0,24},{8,0},{16,8},{24,16},{1,25},{9,1},{17,9},{25,17},{2,26},{10... | collective-permute-start | bytes 221192 | tf_op jit(solution)/shard_map/while/body/eval_jaxpr/ppermute | solution.py:16
  19.2 5.3 %collective-permute-start.1 = (f32[144,128]{1,0:T(8,128)S(1)}, f32[144,128]{1,0:T(8,128)S(1)}, u32[]{:S(2)}, u32[]{:S(2)}) collective-permute-start(f32[144,128]{1,0:T(8,128)S(1)} %get-tuple-element.317), channel_id=1, source_target_pairs={{0,8},{8,16},{16,24},{24,0},{1,9},{9,17},{17,25},{25,1},{2,10},{10... | collective-permute-start | bytes 221192 | tf_op jit(solution)/shard_map/while/body/eval_jaxpr/ppermute | solution.py:16
  31.7 6.7 %collective-permute-start = (f32[144,128]{1,0:T(8,128)S(1)}, f32[144,128]{1,0:T(8,128)S(1)}, u32[]{:S(2)}, u32[]{:S(2)}) collective-permute-start(f32[144,128]{1,0:T(8,128)S(1)} %get-tuple-element.316), channel_id=1, source_target_pairs={{0,24},{8,0},{16,8},{24,16},{1,25},{9,1},{17,9},{25,17},{2,26},{10... | collective-permute-start | bytes 221192 | tf_op jit(solution)/shard_map/while/body/eval_jaxpr/ppermute | solution.py:16
  32.6 5.3 %collective-permute-start.1 = (f32[144,128]{1,0:T(8,128)S(1)}, f32[144,128]{1,0:T(8,128)S(1)}, u32[]{:S(2)}, u32[]{:S(2)}) collective-permute-start(f32[144,128]{1,0:T(8,128)S(1)} %get-tuple-element.317), channel_id=1, source_target_pairs={{0,8},{8,16},{16,24},{24,0},{1,9},{9,17},{17,25},{25,1},{2,10},{10... | collective-permute-start | bytes 221192 | tf_op jit(solution)/shard_map/while/body/eval_jaxpr/ppermute | solution.py:16
  45.0 6.8 %collective-permute-start = (f32[144,128]{1,0:T(8,128)S(1)}, f32[144,128]{1,0:T(8,128)S(1)}, u32[]{:S(2)}, u32[]{:S(2)}) collective-permute-start(f32[144,128]{1,0:T(8,128)S(1)} %get-tuple-element.316), channel_id=1, source_target_pairs={{0,24},{8,0},{16,8},{24,16},{1,25},{9,1},{17,9},{25,17},{2,26},{10... | collective-permute-start | bytes 221192 | tf_op jit(solution)/shard_map/while/body/eval_jaxpr/ppermute | solution.py:16
  46.0 5.3 %collective-permute-start.1 = (f32[144,128]{1,0:T(8,128)S(1)}, f32[144,128]{1,0:T(8,128)S(1)}, u32[]{:S(2)}, u32[]{:S(2)}) collective-permute-start(f32[144,128]{1,0:T(8,128)S(1)} %get-tuple-element.317), channel_id=1, source_target_pairs={{0,8},{8,16},{16,24},{24,0},{1,9},{9,17},{17,25},{25,1},{2,10},{10... | collective-permute-start | bytes 221192 | tf_op jit(solution)/shard_map/while/body/eval_jaxpr/ppermute | solution.py:16
  53.4 8.4 %collective-permute-start.5 = (bf16[1728,128]{1,0:T(8,128)(2,1)S(1)}, bf16[1728,128]{1,0:T(8,128)(2,1)S(1)}, u32[]{:S(2)}, u32[]{:S(2)}) collective-permute-start(bf16[1728,128]{1,0:T(8,128)(2,1)S(1)} %slice.138), channel_id=1, source_target_pairs={{0,2},{2,0},{1,3},{3,1},{4,6},{6,4},{5,7},{7,5},{8,10},{10,8},{9,1... | collective-permute-start | bytes 1327112 | tf_op jit(solution)/shard_map/ppermute | solution.py:26
  55.0 6.8 %collective-permute-start.4 = (bf16[1728,128]{1,0:T(8,128)(2,1)S(1)}, bf16[1728,128]{1,0:T(8,128)(2,1)S(1)}, u32[]{:S(2)}, u32[]{:S(2)}) collective-permute-start(bf16[1728,128]{1,0:T(8,128)(2,1)S(1)} %slice.138), channel_id=1, source_target_pairs={{0,1},{1,0},{2,3},{3,2},{4,5},{5,4},{6,7},{7,6},{8,9},{9,8},{10,11... | collective-permute-start | bytes 1327112 | tf_op jit(solution)/shard_map/ppermute | solution.py:26
  61.8 1.8 %collective-permute-start.6 = (bf16[1728,128]{1,0:T(8,128)(2,1)S(1)}, bf16[1728,128]{1,0:T(8,128)(2,1)S(1)}, u32[]{:S(2)}, u32[]{:S(2)}) collective-permute-start(bf16[1728,128]{1,0:T(8,128)(2,1)S(1)} %collective-permute-done.5), channel_id=1, source_target_pairs={{0,1},{1,0},{2,3},{3,2},{4,5},{5,4},{6,7},{7,6},{8,9},{9,8},{10,11... | collective-permute-start | bytes 1327112 | tf_op jit(solution)/shard_map/ppermute | solution.py:26

commit v6 on v5

--- a/solution.py
+++ b/solution.py
@@ -62,8 +62,11 @@
         precision=lax.Precision.HIGHEST,
         preferred_element_type=jnp.float32,
     )
+    face_states, face_mass_potential, local_start, padded_matrix = lax.optimization_barrier(
+        (face_states, face_mass_potential, states.astype(jnp.float32), padded_matrix)
+    )
     ghost_states, ghost_mass_potential = ring((face_states, face_mass_potential), "dom", -1)
-    field_start = jnp.concatenate([states.astype(jnp.float32), ghost_states], 0)
+    field_start = jnp.concatenate([local_start, ghost_states], 0)
     wide_mass = jnp.concatenate([inv_mass, ghost_mass_potential[0]], 0)
     wide_potential = jnp.concatenate([potential, ghost_mass_potential[1]], 0)
 

time: 65.2 us -> 65.8 us (level)
  waiting for transfers between devices: 11.6 us -> 14.2 us
  matrix products: 28.6 us -> 27.8 us
  other arithmetic: 7.43 us -> 6.76 us
    ppermute x8, waiting for transfers between devices: 3.85 us -> 6.5 us  [ring(): return lax.ppermute(block, axis, route)]
    concatenate x1, other arithmetic: 0.75 us -> 0.08 us  [body(): rim_ids = jnp.concatenate([face_rows, wide_ids[node_count:, 0]], 0)]
    dot_general x1, matrix products: 1.36 us -> 0.68 us  [body(): lax.dot_general(jnp.stack([inv_mass, potential], 0), face_put.astype(jnp....]
  transfers between devices with their start and end apart: 11 -> 11, of which waited for: 6 -> 6; matrix products, arithmetic and copies ran while one was open for 27% -> 19% of each run, Pallas kernels for 0% -> 0%
where the time goes in v6:
time: 65.8 us; the launch traced here: 65.5 us
  matrix products  27.8 us (42%)
  waiting for transfers between devices  14.2 us (22%)
  starting transfers between devices  12.3 us (19%)
  other arithmetic  6.76 us (10%)
  local copies, waits for them, and re-layouts  3.94 us (6%)
    ppermute x8, starting transfers between devices, ring(): return lax.ppermute(block, axis, route)  10.7 us
    dot_general x3, matrix products, operate(): jnp.dot(scatter_sel, both, preferred_element_type=jnp.float32)  8.99 us
    ppermute x3, waiting for transfers between devices, from_partner(): return lax.ppermute(block, axis, route)  7.71 us
    dot_general x3, matrix products, operate(): lax.dot_general(scatter_sel, weighted, (((0,), (0,)), ((), ())), preferre...  7.05 us
    ppermute x8, waiting for transfers between devices, ring(): return lax.ppermute(block, axis, route)  6.5 us
    dot_general x3, matrix products, operate(): jnp.einsum('ij,cjb->cib', padded_matrix, values, preferred_element_type=j...  4.46 us
    sub x3, other arithmetic, chebyshev_step(): return (current, gain * scaled - keep * previous)  3.86 us
    dot_general x3, matrix products, operate(): jnp.dot(rim_sel, both, preferred_element_type=jnp.float32)  1.89 us
  transfers between devices with their start and end apart: 11, of which 6 were waited for; matrix products, arithmetic and copies ran while one was open for 19% of the time, Pallas kernels for 0%

profile of v6, /device:TPU:0, one launch (start us, length us, event | category | flops | bytes accessed | tf_op | source)
XLA Modules:
  0.0 65.5 jit_solution(12843647922313525441)
XLA Ops:
  2.7 1.4 %fusion.46 = f32[144,128]{1,0:T(8,128)S(1)} fusion(bf16[1728,128]{1,0:T(8,128)(2,1)} %param.9, s32[1728]{0:T(1024)S(1)} %add_reduce_fusion, s32[144]{0:T(256)} %param.14), kind=kOutput, calls=%fused_computation.53 | convolution fusion | flops 63949824 | bytes 523584 | tf_op jit(solution)/shard_map/dot_general | solution.py:57
  5.5 3.9 %collective-permute-start.2 = (f32[144,128]{1,0:T(8,128)S(1)}, f32[144,128]{1,0:T(8,128)S(1)}, u32[]{:S(2)}, u32[]{:S(2)}) collective-permute-start(f32[144,128]{1,0:T(8,128)S(1)} %fusion.46), channel_id=1, source_target_pairs={{0,24},{8,0},{16,8},{24,16},{1,25},{9,1},{17,9},{25,17},{2,26},{10... | collective-permute-start | bytes 221192 | tf_op jit(solution)/shard_map/ppermute | solution.py:16
  10.1 2.9 %collective-permute-done.3 = f32[2,144]{1,0:T(2,128)S(1)} collective-permute-done((f32[2,144]{1,0:T(2,128)S(1)}, f32[2,144]{1,0:T(2,128)S(1)}, u32[]{:S(2)}, u32[]{:S(2)}) %collective-permute-start.3) | collective-permute-done | bytes 1184 | tf_op jit(solution)/shard_map/ppermute | solution.py:16
  13.2 40.9 %while.17 = (s32[]{:T(128)}, f32[1872,128]{1,0:T(8,128)S(1)}, f32[1872,128]{1,0:T(8,128)S(1)}, f32[1872]{0:T(1024)S(1)}, bf16[352,352]{1,0:T(8,128)(2,1)}, /*ind...) while((s32[]{:T(128)}, f32[1872,128]{1,0:T(8,128)S(1)}, ...), condition=%wide.region_1.2_spmd.clone.clone, body=%wide.region_0.1_spmd.clone.clone.sunk | while | flops 4879314944 | bytes 31196832 | solution.py:101
  13.2 2.4 %fusion.90 = bf16[2816,128]{0,1:T(8,128)(2,1)S(1)} fusion(s32[2816]{0:T(1024)S(1)} %get-tuple-element.366, f32[1872,128]{1,0:T(8,128)S(1)} %get-tuple-element.346, f32[1872]{0:T(1024)S(1)} %get-tuple-element.363), kind=kOutput, calls=%fused_computation.10.clone.1 | convolution fusion | flops 1360900096 | bytes 1698112 | tf_op jit(solution)/shard_map/while/body/eval_jaxpr/dot_general | solution.py:75
  15.9 1.5 %fusion.91 = f32[8,128,352]{1,2,0:T(8,128)S(1)} fusion(bf16[8,352,128]{2,1,0:T(8,128)(2,1)S(1)} %bitcast.41, bf16[352,352]{1,0:T(8,128)(2,1)} %get-tuple-element.364), kind=kOutput, calls=%fused_computation.35.clone.1 | convolution fusion | flops 253755392 | bytes 2410496 | tf_op jit(solution)/shard_map/while/body/eval_jaxpr/ij,cjb->cib/dot_general | solution.py:79
  18.3 1.7 %collective-permute-start = (f32[144,128]{1,0:T(8,128)S(1)}, f32[144,128]{1,0:T(8,128)S(1)}, u32[]{:S(2)}, u32[]{:S(2)}) collective-permute-start(f32[144,128]{1,0:T(8,128)S(1)} %get-tuple-element.324), channel_id=1, source_target_pairs={{0,24},{8,0},{16,8},{24,16},{1,25},{9,1},{17,9},{25,17},{2,26},{10... | collective-permute-start | bytes 221192 | tf_op jit(solution)/shard_map/while/body/eval_jaxpr/ppermute | solution.py:16
  20.4 3.0 %fusion.94 = f32[1872,256]{1,0:T(8,128)S(1)} fusion(s32[2816]{0:T(1024)S(1)} %get-tuple-element.366, bf16[2816,128]{1,0:T(8,128)(2,1)S(1)} %get-tuple-element.322, bf16[2816,128]{1,0:T(8,128)(2,1)S(1)} %get-tuple-element.323), kind=kOutput, calls=%fused_computation.13.clone.1 | convolution fusion | flops 2712461312 | bytes 3369984 | tf_op jit(solution)/shard_map/while/body/eval_jaxpr/dot_general | solution.py:86
  23.5 1.8 %collective-permute-done.1 = f32[144,128]{1,0:T(8,128)S(1)} collective-permute-done((f32[144,128]{1,0:T(8,128)S(1)}, f32[144,128]{1,0:T(8,128)S(1)}, u32[]{:S(2)}, u32[]{:S(2)}) %collective-permute-start.1) | collective-permute-done | bytes 73760 | tf_op jit(solution)/shard_map/while/body/eval_jaxpr/ppermute | solution.py:16
  26.0 1.3 %fusion.96 = f32[1872,128]{1,0:T(8,128)S(1)} fusion(f32[144,128]{1,0:T(8,128)S(1)} %slice_add_fusion.9, f32[1728,128]{1,0:T(8,128)S(1)} %fusion.95, f32[1872,128]{1,0:T(8,128)S(1)} %get-tuple-element.345, f32[1872,128]{1,0:T(8,128)S(1)} %get-tuple-element.346, f32[]{:T(128)S(6)} %select_n.45, f32[]{:T(128)S(6)} %mul.171, ...), kind=kLoop, calls=%fused_computation.28.clone.1 | loop fusion | flops 2156544 | bytes 3848840 | tf_op jit(solution)/shard_map/while/body/eval_jaxpr/sub | solution.py:99
  27.4 2.4 %fusion.90 = bf16[2816,128]{0,1:T(8,128)(2,1)S(1)} fusion(s32[2816]{0:T(1024)S(1)} %get-tuple-element.366, f32[1872,128]{1,0:T(8,128)S(1)} %get-tuple-element.346, f32[1872]{0:T(1024)S(1)} %get-tuple-element.363), kind=kOutput, calls=%fused_computation.10.clone.1 | convolution fusion | flops 1360900096 | bytes 1698112 | tf_op jit(solution)/shard_map/while/body/eval_jaxpr/dot_general | solution.py:75
  30.2 1.5 %fusion.91 = f32[8,128,352]{1,2,0:T(8,128)S(1)} fusion(bf16[8,352,128]{2,1,0:T(8,128)(2,1)S(1)} %bitcast.41, bf16[352,352]{1,0:T(8,128)(2,1)} %get-tuple-element.364), kind=kOutput, calls=%fused_computation.35.clone.1 | convolution fusion | flops 253755392 | bytes 2410496 | tf_op jit(solution)/shard_map/while/body/eval_jaxpr/ij,cjb->cib/dot_general | solution.py:79
  33.4 1.2 %collective-permute-start.1 = (f32[144,128]{1,0:T(8,128)S(1)}, f32[144,128]{1,0:T(8,128)S(1)}, u32[]{:S(2)}, u32[]{:S(2)}) collective-permute-start(f32[144,128]{1,0:T(8,128)S(1)} %get-tuple-element.325), channel_id=1, source_target_pairs={{0,8},{8,16},{16,24},{24,0},{1,9},{9,17},{17,25},{25,1},{2,10},{10... | collective-permute-start | bytes 221192 | tf_op jit(solution)/shard_map/while/body/eval_jaxpr/ppermute | solution.py:16
  34.6 3.0 %fusion.94 = f32[1872,256]{1,0:T(8,128)S(1)} fusion(s32[2816]{0:T(1024)S(1)} %get-tuple-element.366, bf16[2816,128]{1,0:T(8,128)(2,1)S(1)} %get-tuple-element.322, bf16[2816,128]{1,0:T(8,128)(2,1)S(1)} %get-tuple-element.323), kind=kOutput, calls=%fused_computation.13.clone.1 | convolution fusion | flops 2712461312 | bytes 3369984 | tf_op jit(solution)/shard_map/while/body/eval_jaxpr/dot_general | solution.py:86
  39.3 1.3 %fusion.96 = f32[1872,128]{1,0:T(8,128)S(1)} fusion(f32[144,128]{1,0:T(8,128)S(1)} %slice_add_fusion.9, f32[1728,128]{1,0:T(8,128)S(1)} %fusion.95, f32[1872,128]{1,0:T(8,128)S(1)} %get-tuple-element.345, f32[1872,128]{1,0:T(8,128)S(1)} %get-tuple-element.346, f32[]{:T(128)S(6)} %select_n.45, f32[]{:T(128)S(6)} %mul.171, ...), kind=kLoop, calls=%fused_computation.28.clone.1 | loop fusion | flops 2156544 | bytes 3848840 | tf_op jit(solution)/shard_map/while/body/eval_jaxpr/sub | solution.py:99
  40.8 2.4 %fusion.90 = bf16[2816,128]{0,1:T(8,128)(2,1)S(1)} fusion(s32[2816]{0:T(1024)S(1)} %get-tuple-element.366, f32[1872,128]{1,0:T(8,128)S(1)} %get-tuple-element.346, f32[1872]{0:T(1024)S(1)} %get-tuple-element.363), kind=kOutput, calls=%fused_computation.10.clone.1 | convolution fusion | flops 1360900096 | bytes 1698112 | tf_op jit(solution)/shard_map/while/body/eval_jaxpr/dot_general | solution.py:75
  43.5 1.5 %fusion.91 = f32[8,128,352]{1,2,0:T(8,128)S(1)} fusion(bf16[8,352,128]{2,1,0:T(8,128)(2,1)S(1)} %bitcast.41, bf16[352,352]{1,0:T(8,128)(2,1)} %get-tuple-element.364), kind=kOutput, calls=%fused_computation.35.clone.1 | convolution fusion | flops 253755392 | bytes 2410496 | tf_op jit(solution)/shard_map/while/body/eval_jaxpr/ij,cjb->cib/dot_general | solution.py:79
  46.8 1.2 %collective-permute-start.1 = (f32[144,128]{1,0:T(8,128)S(1)}, f32[144,128]{1,0:T(8,128)S(1)}, u32[]{:S(2)}, u32[]{:S(2)}) collective-permute-start(f32[144,128]{1,0:T(8,128)S(1)} %get-tuple-element.325), channel_id=1, source_target_pairs={{0,8},{8,16},{16,24},{24,0},{1,9},{9,17},{17,25},{25,1},{2,10},{10... | collective-permute-start | bytes 221192 | tf_op jit(solution)/shard_map/while/body/eval_jaxpr/ppermute | solution.py:16
  48.0 3.0 %fusion.94 = f32[1872,256]{1,0:T(8,128)S(1)} fusion(s32[2816]{0:T(1024)S(1)} %get-tuple-element.366, bf16[2816,128]{1,0:T(8,128)(2,1)S(1)} %get-tuple-element.322, bf16[2816,128]{1,0:T(8,128)(2,1)S(1)} %get-tuple-element.323), kind=kOutput, calls=%fused_computation.13.clone.1 | convolution fusion | flops 2712461312 | bytes 3369984 | tf_op jit(solution)/shard_map/while/body/eval_jaxpr/dot_general | solution.py:86
  52.7 1.3 %fusion.96 = f32[1872,128]{1,0:T(8,128)S(1)} fusion(f32[144,128]{1,0:T(8,128)S(1)} %slice_add_fusion.9, f32[1728,128]{1,0:T(8,128)S(1)} %fusion.95, f32[1872,128]{1,0:T(8,128)S(1)} %get-tuple-element.345, f32[1872,128]{1,0:T(8,128)S(1)} %get-tuple-element.346, f32[]{:T(128)S(6)} %select_n.45, f32[]{:T(128)S(6)} %mul.171, ...), kind=kLoop, calls=%fused_computation.28.clone.1 | loop fusion | flops 2156544 | bytes 3848840 | tf_op jit(solution)/shard_map/while/body/eval_jaxpr/sub | solution.py:99
  54.2 1.6 %collective-permute-start.5 = (bf16[1728,128]{1,0:T(8,128)(2,1)S(1)}, bf16[1728,128]{1,0:T(8,128)(2,1)S(1)}, u32[]{:S(2)}, u32[]{:S(2)}) collective-permute-start(bf16[1728,128]{1,0:T(8,128)(2,1)S(1)} %slice.138), channel_id=1, source_target_pairs={{0,2},{2,0},{1,3},{3,1},{4,6},{6,4},{5,7},{7,5},{8,10},{10,8},{9,1... | collective-permute-start | bytes 1327112 | tf_op jit(solution)/shard_map/ppermute | solution.py:26
  56.1 6.5 %collective-permute-done.5 = bf16[1728,128]{1,0:T(8,128)(2,1)S(1)} collective-permute-done((bf16[1728,128]{1,0:T(8,128)(2,1)S(1)}, bf16[1728,128]{1,0:T(8,128)(2,1)S(1)}, u32[]{:S(2)}, u32[]{:S(2)}) %collective-permute-start.5) | collective-permute-done | bytes 442400 | tf_op jit(solution)/shard_map/ppermute | solution.py:26
  63.1 1.3 %collective-permute-done.6 = bf16[1728,128]{1,0:T(8,128)(2,1)S(1)} collective-permute-done((bf16[1728,128]{1,0:T(8,128)(2,1)S(1)}, bf16[1728,128]{1,0:T(8,128)(2,1)S(1)}, u32[]{:S(2)}, u32[]{:S(2)}) %collective-permute-start.6) | collective-permute-done | bytes 442400 | tf_op jit(solution)/shard_map/ppermute | solution.py:26
  64.3 1.2 %convolution_add_fusion = f32[1728,128]{1,0:T(8,128)} fusion(f32[1728,128]{1,0:T(8,128)S(1)} %convolution_add_fusion.1, bf16[1728,128]{1,0:T(8,128)(2,1)S(1)} %collective-permute-done.6, bf16[512,128]{1,0:T(8,128)(2,1)S(1)} %copy-done, s32[]{:T(128)S(6)} %select_n.38), kind=kOutput, calls=%fused_computation.48 | convolution fusion | flops 56844288 | bytes 2244612 | tf_op jit(solution)/shard_map/dot_general | solution.py:114
  (79 shorter events, 16.0 us)
Async XLA Ops:
  0.0 55.8 %copy-start = (bf16[512,128]{1,0:T(8,128)(2,1)S(1)}, bf16[512,128]{1,0:T(8,128)(2,1)}, u32[]{:S(2)}) copy-start(bf16[512,128]{1,0:T(8,128)(2,1)} %param.15) | copy-start | bytes 393220
  0.0 13.0 %copy-start.3 = (f32[1728]{0:T(1024)S(1)}, f32[1728]{0:T(1024)}, u32[]{:S(2)}) copy-start(f32[1728]{0:T(1024)} %param.11) | copy-start | bytes 20740
  0.0 13.0 %copy-start.4 = (f32[1728]{0:T(1024)S(1)}, f32[1728]{0:T(1024)}, u32[]{:S(2)}) copy-start(f32[1728]{0:T(1024)} %param.10) | copy-start | bytes 20740
  0.0 4.0 %copy-start.2 = (s32[144]{0:T(256)S(1)}, s32[144]{0:T(256)}, u32[]{:S(2)}) copy-start(s32[144]{0:T(256)} %param.14) | copy-start | bytes 1732
  0.0 4.7 %copy-start.1 = (bf16[343,343]{1,0:T(8,128)(2,1)S(1)}, bf16[343,343]{1,0:T(8,128)(2,1)}, u32[]{:S(2)}) copy-start(bf16[343,343]{1,0:T(8,128)(2,1)} %param.12) | copy-start | bytes 705898
  0.0 10.0 %copy-start.5 = (s32[8,343]{1,0:T(8,128)S(1)}, s32[8,343]{1,0:T(8,128)}, u32[]{:S(2)}) copy-start(s32[8,343]{1,0:T(8,128)} %param.13) | copy-start | bytes 32932
  5.5 7.6 %collective-permute-start.2 = (f32[144,128]{1,0:T(8,128)S(1)}, f32[144,128]{1,0:T(8,128)S(1)}, u32[]{:S(2)}, u32[]{:S(2)}) collective-permute-start(f32[144,128]{1,0:T(8,128)S(1)} %fusion.46), channel_id=1, source_target_pairs={{0,24},{8,0},{16,8},{24,16},{1,25},{9,1},{17,9},{25,17},{2,26},{10... | collective-permute-start | bytes 221192 | tf_op jit(solution)/shard_map/ppermute | solution.py:16
  9.4 3.6 %collective-permute-start.3 = (f32[2,144]{1,0:T(2,128)S(1)}, f32[2,144]{1,0:T(2,128)S(1)}, u32[]{:S(2)}, u32[]{:S(2)}) collective-permute-start(f32[2,144]{1,0:T(2,128)S(1)} %fusion.44), channel_id=1, source_target_pairs={{0,24},{8,0},{16,8},{24,16},{1,25},{9,1},{17,9},{25,17},{2,26},{10... | collective-permute-start | bytes 3464 | tf_op jit(solution)/shard_map/ppermute | solution.py:16
  18.3 7.6 %collective-permute-start = (f32[144,128]{1,0:T(8,128)S(1)}, f32[144,128]{1,0:T(8,128)S(1)}, u32[]{:S(2)}, u32[]{:S(2)}) collective-permute-start(f32[144,128]{1,0:T(8,128)S(1)} %get-tuple-element.324), channel_id=1, source_target_pairs={{0,24},{8,0},{16,8},{24,16},{1,25},{9,1},{17,9},{25,17},{2,26},{10... | collective-permute-start | bytes 221192 | tf_op jit(solution)/shard_map/while/body/eval_jaxpr/ppermute | solution.py:16
  20.1 5.3 %collective-permute-start.1 = (f32[144,128]{1,0:T(8,128)S(1)}, f32[144,128]{1,0:T(8,128)S(1)}, u32[]{:S(2)}, u32[]{:S(2)}) collective-permute-start(f32[144,128]{1,0:T(8,128)S(1)} %get-tuple-element.325), channel_id=1, source_target_pairs={{0,8},{8,16},{16,24},{24,0},{1,9},{9,17},{17,25},{25,1},{2,10},{10... | collective-permute-start | bytes 221192 | tf_op jit(solution)/shard_map/while/body/eval_jaxpr/ppermute | solution.py:16
  32.6 6.7 %collective-permute-start = (f32[144,128]{1,0:T(8,128)S(1)}, f32[144,128]{1,0:T(8,128)S(1)}, u32[]{:S(2)}, u32[]{:S(2)}) collective-permute-start(f32[144,128]{1,0:T(8,128)S(1)} %get-tuple-element.324), channel_id=1, source_target_pairs={{0,24},{8,0},{16,8},{24,16},{1,25},{9,1},{17,9},{25,17},{2,26},{10... | collective-permute-start | bytes 221192 | tf_op jit(solution)/shard_map/while/body/eval_jaxpr/ppermute | solution.py:16
  33.4 5.3 %collective-permute-start.1 = (f32[144,128]{1,0:T(8,128)S(1)}, f32[144,128]{1,0:T(8,128)S(1)}, u32[]{:S(2)}, u32[]{:S(2)}) collective-permute-start(f32[144,128]{1,0:T(8,128)S(1)} %get-tuple-element.325), channel_id=1, source_target_pairs={{0,8},{8,16},{16,24},{24,0},{1,9},{9,17},{17,25},{25,1},{2,10},{10... | collective-permute-start | bytes 221192 | tf_op jit(solution)/shard_map/while/body/eval_jaxpr/ppermute | solution.py:16
  45.9 6.7 %collective-permute-start = (f32[144,128]{1,0:T(8,128)S(1)}, f32[144,128]{1,0:T(8,128)S(1)}, u32[]{:S(2)}, u32[]{:S(2)}) collective-permute-start(f32[144,128]{1,0:T(8,128)S(1)} %get-tuple-element.324), channel_id=1, source_target_pairs={{0,24},{8,0},{16,8},{24,16},{1,25},{9,1},{17,9},{25,17},{2,26},{10... | collective-permute-start | bytes 221192 | tf_op jit(solution)/shard_map/while/body/eval_jaxpr/ppermute | solution.py:16
  46.8 5.3 %collective-permute-start.1 = (f32[144,128]{1,0:T(8,128)S(1)}, f32[144,128]{1,0:T(8,128)S(1)}, u32[]{:S(2)}, u32[]{:S(2)}) collective-permute-start(f32[144,128]{1,0:T(8,128)S(1)} %get-tuple-element.325), channel_id=1, source_target_pairs={{0,8},{8,16},{16,24},{24,0},{1,9},{9,17},{17,25},{25,1},{2,10},{10... | collective-permute-start | bytes 221192 | tf_op jit(solution)/shard_map/while/body/eval_jaxpr/ppermute | solution.py:16
  54.2 8.4 %collective-permute-start.5 = (bf16[1728,128]{1,0:T(8,128)(2,1)S(1)}, bf16[1728,128]{1,0:T(8,128)(2,1)S(1)}, u32[]{:S(2)}, u32[]{:S(2)}) collective-permute-start(bf16[1728,128]{1,0:T(8,128)(2,1)S(1)} %slice.138), channel_id=1, source_target_pairs={{0,2},{2,0},{1,3},{3,1},{4,6},{6,4},{5,7},{7,5},{8,10},{10,8},{9,1... | collective-permute-start | bytes 1327112 | tf_op jit(solution)/shard_map/ppermute | solution.py:26
  55.8 6.7 %collective-permute-start.4 = (bf16[1728,128]{1,0:T(8,128)(2,1)S(1)}, bf16[1728,128]{1,0:T(8,128)(2,1)S(1)}, u32[]{:S(2)}, u32[]{:S(2)}) collective-permute-start(bf16[1728,128]{1,0:T(8,128)(2,1)S(1)} %slice.138), channel_id=1, source_target_pairs={{0,1},{1,0},{2,3},{3,2},{4,5},{5,4},{6,7},{7,6},{8,9},{9,8},{10,11... | collective-permute-start | bytes 1327112 | tf_op jit(solution)/shard_map/ppermute | solution.py:26
  62.5 1.8 %collective-permute-start.6 = (bf16[1728,128]{1,0:T(8,128)(2,1)S(1)}, bf16[1728,128]{1,0:T(8,128)(2,1)S(1)}, u32[]{:S(2)}, u32[]{:S(2)}) collective-permute-start(bf16[1728,128]{1,0:T(8,128)(2,1)S(1)} %collective-permute-done.5), channel_id=1, source_target_pairs={{0,1},{1,0},{2,3},{3,2},{4,5},{5,4},{6,7},{7,6},{8,9},{9,8},{10,11... | collective-permute-start | bytes 1327112 | tf_op jit(solution)/shard_map/ppermute | solution.py:26

commit v7 on v5

--- a/solution.py
+++ b/solution.py
@@ -82,7 +82,10 @@
         from_next = ring(rim[:face_count], "dom", -1)
         main = summed_halves(jnp.dot(scatter_sel, both, preferred_element_type=jnp.float32))
         own = main[:node_count] + summed_halves(
-            jnp.dot(face_put, high_low(from_prev), preferred_element_type=jnp.float32)
+            lax.dot_general(
+                face_take, high_low(from_prev), (((0,), (0,)), ((), ())),
+                preferred_element_type=jnp.float32,
+            )
         )
         summed = jnp.concatenate([own, main[node_count:] + from_next], 0)
         return wide_mass[:, None] * summed + wide_potential[:, None] * field_in

time: 65.2 us -> 65.6 us (level)
  no operation moved by 1% of the time
where the time goes in v7:
time: 65.6 us; the launch traced here: 65.1 us
  matrix products  28.9 us (44%)
  starting transfers between devices  12.4 us (19%)
  waiting for transfers between devices  11.6 us (18%)
  other arithmetic  7.43 us (11%)
  local copies, waits for them, and re-layouts  4.35 us (7%)
    ppermute x8, starting transfers between devices, ring(): return lax.ppermute(block, axis, route)  10.7 us
    dot_general x3, matrix products, operate(): jnp.dot(scatter_sel, both, preferred_element_type=jnp.float32)  8.99 us
    ppermute x3, waiting for transfers between devices, from_partner(): return lax.ppermute(block, axis, route)  7.74 us
    dot_general x3, matrix products, operate(): lax.dot_general(scatter_sel, weighted, (((0,), (0,)), ((), ())), preferre...  7.05 us
    dot_general x3, matrix products, operate(): jnp.einsum('ij,cjb->cib', padded_matrix, values, preferred_element_type=j...  4.46 us
    sub x3, other arithmetic, chebyshev_step(): return (current, gain * scaled - keep * previous)  3.86 us
    ppermute x8, waiting for transfers between devices, ring(): return lax.ppermute(block, axis, route)  3.86 us
    dot_general x3, matrix products, operate(): jnp.dot(rim_sel, both, preferred_element_type=jnp.float32)  1.89 us
  transfers between devices with their start and end apart: 11, of which 6 were waited for; matrix products, arithmetic and copies ran while one was open for 27% of the time, Pallas kernels for 0%

profile of v7, /device:TPU:0, one launch (start us, length us, event | category | flops | bytes accessed | tf_op | source)
XLA Modules:
  0.0 65.1 jit_solution(13729710543341284874)
XLA Ops:
  0.1 1.4 %fusion.46 = f32[144,128]{1,0:T(8,128)S(1)} fusion(bf16[1728,128]{1,0:T(8,128)(2,1)} %param.9, s32[1728]{0:T(1024)S(1)} %add_reduce_fusion, s32[144]{0:T(256)} %param.14), kind=kOutput, calls=%fused_computation.53 | convolution fusion | flops 63949824 | bytes 523584 | tf_op jit(solution)/shard_map/dot_general | solution.py:57
  1.5 4.0 %collective-permute-start.2 = (f32[144,128]{1,0:T(8,128)S(1)}, f32[144,128]{1,0:T(8,128)S(1)}, u32[]{:S(2)}, u32[]{:S(2)}) collective-permute-start(f32[144,128]{1,0:T(8,128)S(1)} %fusion.46), channel_id=1, source_target_pairs={{0,24},{8,0},{16,8},{24,16},{1,25},{9,1},{17,9},{25,17},{2,26},{10... | collective-permute-start | bytes 221192 | tf_op jit(solution)/shard_map/ppermute | solution.py:16
  6.9 1.4 %fusion.44 = f32[2,144]{1,0:T(2,128)S(1)} fusion(s32[144]{0:T(256)} %param.14, s32[1728]{0:T(1024)S(1)} %add_reduce_fusion, f32[1,1728]{1,0:T(1,128)S(1)} %stack.10, f32[1,1728]{1,0:T(1,128)S(1)} %stack.9), kind=kOutput, calls=%fused_computation.51 | convolution fusion | flops 6224256 | bytes 22464 | tf_op jit(solution)/shard_map/dot_general | solution.py:58
  12.6 41.1 %while.17 = (s32[]{:T(128)}, f32[1872,128]{1,0:T(8,128)S(1)}, f32[1872,128]{1,0:T(8,128)S(1)}, f32[1872]{0:T(1024)S(1)}, bf16[352,352]{1,0:T(8,128)(2,1)}, /*ind...) while((s32[]{:T(128)}, f32[1872,128]{1,0:T(8,128)S(1)}, ...), condition=%wide.region_1.2_spmd.clone.clone, body=%wide.region_0.1_spmd.clone.clone.sunk | while | flops 4879314944 | bytes 31196832 | solution.py:101
  12.6 2.4 %fusion.90 = bf16[2816,128]{0,1:T(8,128)(2,1)S(1)} fusion(s32[2816]{0:T(1024)S(1)} %get-tuple-element.358, f32[1872,128]{1,0:T(8,128)S(1)} %get-tuple-element.338, f32[1872]{0:T(1024)S(1)} %get-tuple-element.355), kind=kOutput, calls=%fused_computation.10.clone.1 | convolution fusion | flops 1360900096 | bytes 1698112 | tf_op jit(solution)/shard_map/while/body/eval_jaxpr/dot_general | solution.py:72
  15.3 1.5 %fusion.91 = f32[8,128,352]{1,2,0:T(8,128)S(1)} fusion(bf16[8,352,128]{2,1,0:T(8,128)(2,1)S(1)} %bitcast.41, bf16[352,352]{1,0:T(8,128)(2,1)} %get-tuple-element.356), kind=kOutput, calls=%fused_computation.35.clone.1 | convolution fusion | flops 253755392 | bytes 2410496 | tf_op jit(solution)/shard_map/while/body/eval_jaxpr/ij,cjb->cib/dot_general | solution.py:76
  17.7 1.5 %collective-permute-start = (f32[144,128]{1,0:T(8,128)S(1)}, f32[144,128]{1,0:T(8,128)S(1)}, u32[]{:S(2)}, u32[]{:S(2)}) collective-permute-start(f32[144,128]{1,0:T(8,128)S(1)} %get-tuple-element.316), channel_id=1, source_target_pairs={{0,24},{8,0},{16,8},{24,16},{1,25},{9,1},{17,9},{25,17},{2,26},{10... | collective-permute-start | bytes 221192 | tf_op jit(solution)/shard_map/while/body/eval_jaxpr/ppermute | solution.py:16
  19.8 3.0 %fusion.94 = f32[1872,256]{1,0:T(8,128)S(1)} fusion(s32[2816]{0:T(1024)S(1)} %get-tuple-element.358, bf16[2816,128]{1,0:T(8,128)(2,1)S(1)} %get-tuple-element.314, bf16[2816,128]{1,0:T(8,128)(2,1)S(1)} %get-tuple-element.315), kind=kOutput, calls=%fused_computation.12.clone.1 | convolution fusion | flops 2712461312 | bytes 3369984 | tf_op jit(solution)/shard_map/while/body/eval_jaxpr/dot_general | solution.py:83
  22.9 1.5 %collective-permute-done.1 = f32[144,128]{1,0:T(8,128)S(1)} collective-permute-done((f32[144,128]{1,0:T(8,128)S(1)}, f32[144,128]{1,0:T(8,128)S(1)}, u32[]{:S(2)}, u32[]{:S(2)}) %collective-permute-start.1) | collective-permute-done | bytes 73760 | tf_op jit(solution)/shard_map/while/body/eval_jaxpr/ppermute | solution.py:16
  25.3 1.3 %fusion.96 = f32[1872,128]{1,0:T(8,128)S(1)} fusion(f32[144,128]{1,0:T(8,128)S(1)} %slice_add_fusion.9, f32[1728,128]{1,0:T(8,128)S(1)} %fusion.95, f32[1872,128]{1,0:T(8,128)S(1)} %get-tuple-element.337, f32[1872,128]{1,0:T(8,128)S(1)} %get-tuple-element.338, f32[]{:T(128)S(6)} %select_n.45, f32[]{:T(128)S(6)} %mul.171, ...), kind=kLoop, calls=%fused_computation.28.clone.1 | loop fusion | flops 2156544 | bytes 3848840 | tf_op jit(solution)/shard_map/while/body/eval_jaxpr/sub | solution.py:99
  26.7 2.3 %fusion.90 = bf16[2816,128]{0,1:T(8,128)(2,1)S(1)} fusion(s32[2816]{0:T(1024)S(1)} %get-tuple-element.358, f32[1872,128]{1,0:T(8,128)S(1)} %get-tuple-element.338, f32[1872]{0:T(1024)S(1)} %get-tuple-element.355), kind=kOutput, calls=%fused_computation.10.clone.1 | convolution fusion | flops 1360900096 | bytes 1698112 | tf_op jit(solution)/shard_map/while/body/eval_jaxpr/dot_general | solution.py:72
  29.4 1.5 %fusion.91 = f32[8,128,352]{1,2,0:T(8,128)S(1)} fusion(bf16[8,352,128]{2,1,0:T(8,128)(2,1)S(1)} %bitcast.41, bf16[352,352]{1,0:T(8,128)(2,1)} %get-tuple-element.356), kind=kOutput, calls=%fused_computation.35.clone.1 | convolution fusion | flops 253755392 | bytes 2410496 | tf_op jit(solution)/shard_map/while/body/eval_jaxpr/ij,cjb->cib/dot_general | solution.py:76
  32.7 1.2 %collective-permute-start.1 = (f32[144,128]{1,0:T(8,128)S(1)}, f32[144,128]{1,0:T(8,128)S(1)}, u32[]{:S(2)}, u32[]{:S(2)}) collective-permute-start(f32[144,128]{1,0:T(8,128)S(1)} %get-tuple-element.317), channel_id=1, source_target_pairs={{0,8},{8,16},{16,24},{24,0},{1,9},{9,17},{17,25},{25,1},{2,10},{10... | collective-permute-start | bytes 221192 | tf_op jit(solution)/shard_map/while/body/eval_jaxpr/ppermute | solution.py:16
  33.9 3.0 %fusion.94 = f32[1872,256]{1,0:T(8,128)S(1)} fusion(s32[2816]{0:T(1024)S(1)} %get-tuple-element.358, bf16[2816,128]{1,0:T(8,128)(2,1)S(1)} %get-tuple-element.314, bf16[2816,128]{1,0:T(8,128)(2,1)S(1)} %get-tuple-element.315), kind=kOutput, calls=%fused_computation.12.clone.1 | convolution fusion | flops 2712461312 | bytes 3369984 | tf_op jit(solution)/shard_map/while/body/eval_jaxpr/dot_general | solution.py:83
  38.7 1.3 %fusion.96 = f32[1872,128]{1,0:T(8,128)S(1)} fusion(f32[144,128]{1,0:T(8,128)S(1)} %slice_add_fusion.9, f32[1728,128]{1,0:T(8,128)S(1)} %fusion.95, f32[1872,128]{1,0:T(8,128)S(1)} %get-tuple-element.337, f32[1872,128]{1,0:T(8,128)S(1)} %get-tuple-element.338, f32[]{:T(128)S(6)} %select_n.45, f32[]{:T(128)S(6)} %mul.171, ...), kind=kLoop, calls=%fused_computation.28.clone.1 | loop fusion | flops 2156544 | bytes 3848840 | tf_op jit(solution)/shard_map/while/body/eval_jaxpr/sub | solution.py:99
  40.2 2.3 %fusion.90 = bf16[2816,128]{0,1:T(8,128)(2,1)S(1)} fusion(s32[2816]{0:T(1024)S(1)} %get-tuple-element.358, f32[1872,128]{1,0:T(8,128)S(1)} %get-tuple-element.338, f32[1872]{0:T(1024)S(1)} %get-tuple-element.355), kind=kOutput, calls=%fused_computation.10.clone.1 | convolution fusion | flops 1360900096 | bytes 1698112 | tf_op jit(solution)/shard_map/while/body/eval_jaxpr/dot_general | solution.py:72
  42.9 1.5 %fusion.91 = f32[8,128,352]{1,2,0:T(8,128)S(1)} fusion(bf16[8,352,128]{2,1,0:T(8,128)(2,1)S(1)} %bitcast.41, bf16[352,352]{1,0:T(8,128)(2,1)} %get-tuple-element.356), kind=kOutput, calls=%fused_computation.35.clone.1 | convolution fusion | flops 253755392 | bytes 2410496 | tf_op jit(solution)/shard_map/while/body/eval_jaxpr/ij,cjb->cib/dot_general | solution.py:76
  46.3 1.1 %collective-permute-start.1 = (f32[144,128]{1,0:T(8,128)S(1)}, f32[144,128]{1,0:T(8,128)S(1)}, u32[]{:S(2)}, u32[]{:S(2)}) collective-permute-start(f32[144,128]{1,0:T(8,128)S(1)} %get-tuple-element.317), channel_id=1, source_target_pairs={{0,8},{8,16},{16,24},{24,0},{1,9},{9,17},{17,25},{25,1},{2,10},{10... | collective-permute-start | bytes 221192 | tf_op jit(solution)/shard_map/while/body/eval_jaxpr/ppermute | solution.py:16
  47.4 3.0 %fusion.94 = f32[1872,256]{1,0:T(8,128)S(1)} fusion(s32[2816]{0:T(1024)S(1)} %get-tuple-element.358, bf16[2816,128]{1,0:T(8,128)(2,1)S(1)} %get-tuple-element.314, bf16[2816,128]{1,0:T(8,128)(2,1)S(1)} %get-tuple-element.315), kind=kOutput, calls=%fused_computation.12.clone.1 | convolution fusion | flops 2712461312 | bytes 3369984 | tf_op jit(solution)/shard_map/while/body/eval_jaxpr/dot_general | solution.py:83
  52.3 1.3 %fusion.96 = f32[1872,128]{1,0:T(8,128)S(1)} fusion(f32[144,128]{1,0:T(8,128)S(1)} %slice_add_fusion.9, f32[1728,128]{1,0:T(8,128)S(1)} %fusion.95, f32[1872,128]{1,0:T(8,128)S(1)} %get-tuple-element.337, f32[1872,128]{1,0:T(8,128)S(1)} %get-tuple-element.338, f32[]{:T(128)S(6)} %select_n.45, f32[]{:T(128)S(6)} %mul.171, ...), kind=kLoop, calls=%fused_computation.28.clone.1 | loop fusion | flops 2156544 | bytes 3848840 | tf_op jit(solution)/shard_map/while/body/eval_jaxpr/sub | solution.py:99
  53.8 1.6 %collective-permute-start.5 = (bf16[1728,128]{1,0:T(8,128)(2,1)S(1)}, bf16[1728,128]{1,0:T(8,128)(2,1)S(1)}, u32[]{:S(2)}, u32[]{:S(2)}) collective-permute-start(bf16[1728,128]{1,0:T(8,128)(2,1)S(1)} %slice.138), channel_id=1, source_target_pairs={{0,2},{2,0},{1,3},{3,1},{4,6},{6,4},{5,7},{7,5},{8,10},{10,8},{9,1... | collective-permute-start | bytes 1327112 | tf_op jit(solution)/shard_map/ppermute | solution.py:26
  55.7 6.5 %collective-permute-done.5 = bf16[1728,128]{1,0:T(8,128)(2,1)S(1)} collective-permute-done((bf16[1728,128]{1,0:T(8,128)(2,1)S(1)}, bf16[1728,128]{1,0:T(8,128)(2,1)S(1)}, u32[]{:S(2)}, u32[]{:S(2)}) %collective-permute-start.5) | collective-permute-done | bytes 442400 | tf_op jit(solution)/shard_map/ppermute | solution.py:26
  62.7 1.3 %collective-permute-done.6 = bf16[1728,128]{1,0:T(8,128)(2,1)S(1)} collective-permute-done((bf16[1728,128]{1,0:T(8,128)(2,1)S(1)}, bf16[1728,128]{1,0:T(8,128)(2,1)S(1)}, u32[]{:S(2)}, u32[]{:S(2)}) %collective-permute-start.6) | collective-permute-done | bytes 442400 | tf_op jit(solution)/shard_map/ppermute | solution.py:26
  64.0 1.2 %convolution_add_fusion = f32[1728,128]{1,0:T(8,128)} fusion(f32[1728,128]{1,0:T(8,128)S(1)} %convolution_add_fusion.1, bf16[1728,128]{1,0:T(8,128)(2,1)S(1)} %collective-permute-done.6, bf16[512,128]{1,0:T(8,128)(2,1)S(1)} %copy-done, s32[]{:T(128)S(6)} %select_n.38), kind=kOutput, calls=%fused_computation.48 | convolution fusion | flops 56844288 | bytes 2244612 | tf_op jit(solution)/shard_map/dot_general | solution.py:114
  (79 shorter events, 17.6 us)
Async XLA Ops:
  0.0 55.4 %copy-start = (bf16[512,128]{1,0:T(8,128)(2,1)S(1)}, bf16[512,128]{1,0:T(8,128)(2,1)}, u32[]{:S(2)}) copy-start(bf16[512,128]{1,0:T(8,128)(2,1)} %param.15) | copy-start | bytes 393220
  0.0 11.8 %copy-start.3 = (f32[1728]{0:T(1024)S(1)}, f32[1728]{0:T(1024)}, u32[]{:S(2)}) copy-start(f32[1728]{0:T(1024)} %param.11) | copy-start | bytes 20740
  0.0 11.8 %copy-start.4 = (f32[1728]{0:T(1024)S(1)}, f32[1728]{0:T(1024)}, u32[]{:S(2)}) copy-start(f32[1728]{0:T(1024)} %param.10) | copy-start | bytes 20740
  0.0 10.6 %copy-start.5 = (s32[8,343]{1,0:T(8,128)S(1)}, s32[8,343]{1,0:T(8,128)}, u32[]{:S(2)}) copy-start(s32[8,343]{1,0:T(8,128)} %param.13) | copy-start | bytes 32932
  0.0 10.7 %copy-start.1 = (bf16[343,343]{1,0:T(8,128)(2,1)S(1)}, bf16[343,343]{1,0:T(8,128)(2,1)}, u32[]{:S(2)}) copy-start(bf16[343,343]{1,0:T(8,128)(2,1)} %param.12) | copy-start | bytes 705898
  1.5 10.4 %collective-permute-start.2 = (f32[144,128]{1,0:T(8,128)S(1)}, f32[144,128]{1,0:T(8,128)S(1)}, u32[]{:S(2)}, u32[]{:S(2)}) collective-permute-start(f32[144,128]{1,0:T(8,128)S(1)} %fusion.46), channel_id=1, source_target_pairs={{0,24},{8,0},{16,8},{24,16},{1,25},{9,1},{17,9},{25,17},{2,26},{10... | collective-permute-start | bytes 221192 | tf_op jit(solution)/shard_map/ppermute | solution.py:16
  8.2 3.6 %collective-permute-start.3 = (f32[2,144]{1,0:T(2,128)S(1)}, f32[2,144]{1,0:T(2,128)S(1)}, u32[]{:S(2)}, u32[]{:S(2)}) collective-permute-start(f32[2,144]{1,0:T(2,128)S(1)} %fusion.44), channel_id=1, source_target_pairs={{0,24},{8,0},{16,8},{24,16},{1,25},{9,1},{17,9},{25,17},{2,26},{10... | collective-permute-start | bytes 3464 | tf_op jit(solution)/shard_map/ppermute | solution.py:16
  11.9 0.7 %copy-start.2 = (s32[144]{0:T(256)S(1)}, s32[144]{0:T(256)}, u32[]{:S(2)}) copy-start(s32[144]{0:T(256)} %param.14) | copy-start | bytes 1732
  17.7 7.5 %collective-permute-start = (f32[144,128]{1,0:T(8,128)S(1)}, f32[144,128]{1,0:T(8,128)S(1)}, u32[]{:S(2)}, u32[]{:S(2)}) collective-permute-start(f32[144,128]{1,0:T(8,128)S(1)} %get-tuple-element.316), channel_id=1, source_target_pairs={{0,24},{8,0},{16,8},{24,16},{1,25},{9,1},{17,9},{25,17},{2,26},{10... | collective-permute-start | bytes 221192 | tf_op jit(solution)/shard_map/while/body/eval_jaxpr/ppermute | solution.py:16
  19.2 5.3 %collective-permute-start.1 = (f32[144,128]{1,0:T(8,128)S(1)}, f32[144,128]{1,0:T(8,128)S(1)}, u32[]{:S(2)}, u32[]{:S(2)}) collective-permute-start(f32[144,128]{1,0:T(8,128)S(1)} %get-tuple-element.317), channel_id=1, source_target_pairs={{0,8},{8,16},{16,24},{24,0},{1,9},{9,17},{17,25},{25,1},{2,10},{10... | collective-permute-start | bytes 221192 | tf_op jit(solution)/shard_map/while/body/eval_jaxpr/ppermute | solution.py:16
  31.8 6.9 %collective-permute-start = (f32[144,128]{1,0:T(8,128)S(1)}, f32[144,128]{1,0:T(8,128)S(1)}, u32[]{:S(2)}, u32[]{:S(2)}) collective-permute-start(f32[144,128]{1,0:T(8,128)S(1)} %get-tuple-element.316), channel_id=1, source_target_pairs={{0,24},{8,0},{16,8},{24,16},{1,25},{9,1},{17,9},{25,17},{2,26},{10... | collective-permute-start | bytes 221192 | tf_op jit(solution)/shard_map/while/body/eval_jaxpr/ppermute | solution.py:16
  32.7 5.3 %collective-permute-start.1 = (f32[144,128]{1,0:T(8,128)S(1)}, f32[144,128]{1,0:T(8,128)S(1)}, u32[]{:S(2)}, u32[]{:S(2)}) collective-permute-start(f32[144,128]{1,0:T(8,128)S(1)} %get-tuple-element.317), channel_id=1, source_target_pairs={{0,8},{8,16},{16,24},{24,0},{1,9},{9,17},{17,25},{25,1},{2,10},{10... | collective-permute-start | bytes 221192 | tf_op jit(solution)/shard_map/while/body/eval_jaxpr/ppermute | solution.py:16
  45.3 7.0 %collective-permute-start = (f32[144,128]{1,0:T(8,128)S(1)}, f32[144,128]{1,0:T(8,128)S(1)}, u32[]{:S(2)}, u32[]{:S(2)}) collective-permute-start(f32[144,128]{1,0:T(8,128)S(1)} %get-tuple-element.316), channel_id=1, source_target_pairs={{0,24},{8,0},{16,8},{24,16},{1,25},{9,1},{17,9},{25,17},{2,26},{10... | collective-permute-start | bytes 221192 | tf_op jit(solution)/shard_map/while/body/eval_jaxpr/ppermute | solution.py:16
  46.3 5.3 %collective-permute-start.1 = (f32[144,128]{1,0:T(8,128)S(1)}, f32[144,128]{1,0:T(8,128)S(1)}, u32[]{:S(2)}, u32[]{:S(2)}) collective-permute-start(f32[144,128]{1,0:T(8,128)S(1)} %get-tuple-element.317), channel_id=1, source_target_pairs={{0,8},{8,16},{16,24},{24,0},{1,9},{9,17},{17,25},{25,1},{2,10},{10... | collective-permute-start | bytes 221192 | tf_op jit(solution)/shard_map/while/body/eval_jaxpr/ppermute | solution.py:16
  53.8 8.4 %collective-permute-start.5 = (bf16[1728,128]{1,0:T(8,128)(2,1)S(1)}, bf16[1728,128]{1,0:T(8,128)(2,1)S(1)}, u32[]{:S(2)}, u32[]{:S(2)}) collective-permute-start(bf16[1728,128]{1,0:T(8,128)(2,1)S(1)} %slice.138), channel_id=1, source_target_pairs={{0,2},{2,0},{1,3},{3,1},{4,6},{6,4},{5,7},{7,5},{8,10},{10,8},{9,1... | collective-permute-start | bytes 1327112 | tf_op jit(solution)/shard_map/ppermute | solution.py:26
  55.4 6.8 %collective-permute-start.4 = (bf16[1728,128]{1,0:T(8,128)(2,1)S(1)}, bf16[1728,128]{1,0:T(8,128)(2,1)S(1)}, u32[]{:S(2)}, u32[]{:S(2)}) collective-permute-start(bf16[1728,128]{1,0:T(8,128)(2,1)S(1)} %slice.138), channel_id=1, source_target_pairs={{0,1},{1,0},{2,3},{3,2},{4,5},{5,4},{6,7},{7,6},{8,9},{9,8},{10,11... | collective-permute-start | bytes 1327112 | tf_op jit(solution)/shard_map/ppermute | solution.py:26
  62.2 1.8 %collective-permute-start.6 = (bf16[1728,128]{1,0:T(8,128)(2,1)S(1)}, bf16[1728,128]{1,0:T(8,128)(2,1)S(1)}, u32[]{:S(2)}, u32[]{:S(2)}) collective-permute-start(bf16[1728,128]{1,0:T(8,128)(2,1)S(1)} %collective-permute-done.5), channel_id=1, source_target_pairs={{0,1},{1,0},{2,3},{3,2},{4,5},{5,4},{6,7},{7,6},{8,9},{9,8},{10,11... | collective-permute-start | bytes 1327112 | tf_op jit(solution)/shard_map/ppermute | solution.py:26

commit v8 on v5

--- a/solution.py
+++ b/solution.py
@@ -55,12 +55,12 @@
     face_take = (face_rows[:, None] == wide_ids[:node_count, 0][None, :]).astype(jnp.bfloat16)
 
     face_states = jnp.dot(face_take, states, preferred_element_type=jnp.float32)
-    face_mass_potential = lax.dot_general(
-        jnp.stack([inv_mass, potential], 0),
-        face_put.astype(jnp.float32),
-        (((1,), (0,)), ((), ())),
-        precision=lax.Precision.HIGHEST,
-        preferred_element_type=jnp.float32,
+    face_mass_potential = jnp.stack(
+        [
+            inv_mass.at[face_rows].get(mode="promise_in_bounds"),
+            potential.at[face_rows].get(mode="promise_in_bounds"),
+        ],
+        0,
     )
     ghost_states, ghost_mass_potential = ring((face_states, face_mass_potential), "dom", -1)
     field_start = jnp.concatenate([states.astype(jnp.float32), ghost_states], 0)

time: 65.2 us -> 65.9 us (1.011)
  local copies, waits for them, and re-layouts: 4.35 us -> 5.87 us
  waiting for transfers between devices: 11.6 us -> 13.1 us
  matrix products: 28.6 us -> 27.2 us
  other arithmetic: 7.43 us -> 6.44 us
    gather x0 -> x2, local copies, waits for them, and re-layouts: none -> 3.45 us  [the longest x1 2 us: body(): potential.at[face_rows].get(mode='promise_in_bounds')]
    ppermute x8, waiting for transfers between devices: 3.85 us -> 5.43 us  [ring(): return lax.ppermute(block, axis, route)]
    another operation x2 -> x0, local copies, waits for them, and re-layouts: 1.4 us -> none  [body(): jnp.stack([inv_mass, potential], 0)]
    dot_general x1 -> x0, matrix products: 1.36 us -> none  [body(): lax.dot_general(jnp.stack([inv_mass, potential], 0), face_put.astype(jnp....]
    convert_element_type x1, other arithmetic: 1.07 us -> 0.06 us  [body(): field_start = jnp.concatenate([states.astype(jnp.float32), ghost_states], 0)]
    select_n x0 -> x1, other arithmetic: none -> 0.68 us  [body(): inv_mass.at[face_rows].get(mode='promise_in_bounds')]
    concatenate x1, other arithmetic: 0.75 us -> 0.07 us  [body(): rim_ids = jnp.concatenate([face_rows, wide_ids[node_count:, 0]], 0)]
  transfers between devices with their start and end apart: 11 -> 11, of which waited for: 6 -> 6; matrix products, arithmetic and copies ran while one was open for 27% -> 26% of each run, Pallas kernels for 0% -> 0%
where the time goes in v8:
time: 65.9 us; the launch traced here: 65.6 us
  matrix products  27.2 us (41%)
  waiting for transfers between devices  13.1 us (20%)
  starting transfers between devices  12.4 us (19%)
  other arithmetic  6.44 us (10%)
  local copies, waits for them, and re-layouts  5.87 us (9%)
    ppermute x8, starting transfers between devices, ring(): return lax.ppermute(block, axis, route)  10.8 us
    dot_general x3, matrix products, operate(): jnp.dot(scatter_sel, both, preferred_element_type=jnp.float32)  8.99 us
    ppermute x3, waiting for transfers between devices, from_partner(): return lax.ppermute(block, axis, route)  7.71 us
    dot_general x3, matrix products, operate(): lax.dot_general(scatter_sel, weighted, (((0,), (0,)), ((), ())), preferre...  7.05 us
    ppermute x8, waiting for transfers between devices, ring(): return lax.ppermute(block, axis, route)  5.43 us
    dot_general x3, matrix products, operate(): jnp.einsum('ij,cjb->cib', padded_matrix, values, preferred_element_type=j...  4.46 us
    sub x3, other arithmetic, chebyshev_step(): return (current, gain * scaled - keep * previous)  3.86 us
    gather x1, local copies, waits for them, and re-layouts, body(): potential.at[face_rows].get(mode='promise_in_bounds')  2 us
  transfers between devices with their start and end apart: 11, of which 6 were waited for; matrix products, arithmetic and copies ran while one was open for 26% of the time, Pallas kernels for 0%

profile of v8, /device:TPU:0, one launch (start us, length us, event | category | flops | bytes accessed | tf_op | source)
XLA Modules:
  0.0 65.6 jit_solution(5652849662069007368)
XLA Ops:
  0.1 1.5 %fusion.44 = f32[144,128]{1,0:T(8,128)S(1)} fusion(bf16[1728,128]{1,0:T(8,128)(2,1)} %param.9, s32[1728]{0:T(1024)S(1)} %add_reduce_fusion, s32[144]{0:T(256)} %param.14), kind=kOutput, calls=%fused_computation.53 | convolution fusion | flops 63949824 | bytes 523584 | tf_op jit(solution)/shard_map/dot_general | solution.py:57
  1.6 4.0 %collective-permute-start.2 = (f32[144,128]{1,0:T(8,128)S(1)}, f32[144,128]{1,0:T(8,128)S(1)}, u32[]{:S(2)}, u32[]{:S(2)}) collective-permute-start(f32[144,128]{1,0:T(8,128)S(1)} %fusion.44), channel_id=1, source_target_pairs={{0,24},{8,0},{16,8},{24,16},{1,25},{9,1},{17,9},{25,17},{2,26},{10... | collective-permute-start | bytes 221192 | tf_op jit(solution)/shard_map/ppermute | solution.py:16
  6.2 2.0 %gather_fusion.1 = f32[144]{0:T(256)S(1)} fusion(f32[1728]{0:T(1024)} %param.11, s32[1024]{0:T(1024)S(1)} %pad_clamp_fusion), kind=kCustom, calls=%fused_computation.1 | custom fusion | bytes 1728 | tf_op jit(solution)/shard_map/gather | solution.py:61
  8.2 1.4 %gather_fusion = f32[144]{0:T(256)S(1)} fusion(f32[1728]{0:T(1024)S(1)} %copy-done.2, s32[1024]{0:T(1024)S(1)} %pad_clamp_fusion), kind=kCustom, calls=%fused_computation | custom fusion | bytes 1728 | tf_op jit(solution)/shard_map/gather | solution.py:60
  11.3 2.1 %collective-permute-done.3 = f32[2,144]{1,0:T(2,128)S(1)} collective-permute-done((f32[2,144]{1,0:T(2,128)S(1)}, f32[2,144]{1,0:T(2,128)S(1)}, u32[]{:S(2)}, u32[]{:S(2)}) %collective-permute-start.3) | collective-permute-done | bytes 1184 | tf_op jit(solution)/shard_map/ppermute | solution.py:16
  13.6 40.6 %while.17 = (s32[]{:T(128)}, f32[1872,128]{1,0:T(8,128)S(1)}, f32[1872,128]{1,0:T(8,128)S(1)}, f32[1872]{0:T(1024)S(1)}, bf16[352,352]{1,0:T(8,128)(2,1)}, /*ind...) while((s32[]{:T(128)}, f32[1872,128]{1,0:T(8,128)S(1)}, ...), condition=%wide.region_1.2_spmd.clone.clone, body=%wide.region_0.1_spmd.clone.clone.sunk | while | flops 4879314944 | bytes 31196832 | solution.py:98
  13.6 2.3 %fusion.82 = bf16[2816,128]{0,1:T(8,128)(2,1)S(1)} fusion(s32[2816]{0:T(1024)S(1)} %get-tuple-element.358, f32[1872,128]{1,0:T(8,128)S(1)} %get-tuple-element.338, f32[1872]{0:T(1024)S(1)} %get-tuple-element.355), kind=kOutput, calls=%fused_computation.12.clone.1 | convolution fusion | flops 1360900096 | bytes 1698112 | tf_op jit(solution)/shard_map/while/body/eval_jaxpr/dot_general | solution.py:72
  16.3 1.5 %fusion.83 = f32[8,128,352]{1,2,0:T(8,128)S(1)} fusion(bf16[8,352,128]{2,1,0:T(8,128)(2,1)S(1)} %bitcast.43, bf16[352,352]{1,0:T(8,128)(2,1)} %get-tuple-element.356), kind=kOutput, calls=%fused_computation.37.clone.1 | convolution fusion | flops 253755392 | bytes 2410496 | tf_op jit(solution)/shard_map/while/body/eval_jaxpr/ij,cjb->cib/dot_general | solution.py:76
  18.7 1.5 %collective-permute-start = (f32[144,128]{1,0:T(8,128)S(1)}, f32[144,128]{1,0:T(8,128)S(1)}, u32[]{:S(2)}, u32[]{:S(2)}) collective-permute-start(f32[144,128]{1,0:T(8,128)S(1)} %get-tuple-element.316), channel_id=1, source_target_pairs={{0,24},{8,0},{16,8},{24,16},{1,25},{9,1},{17,9},{25,17},{2,26},{10... | collective-permute-start | bytes 221192 | tf_op jit(solution)/shard_map/while/body/eval_jaxpr/ppermute | solution.py:16
  20.8 3.0 %fusion.86 = f32[1872,256]{1,0:T(8,128)S(1)} fusion(s32[2816]{0:T(1024)S(1)} %get-tuple-element.358, bf16[2816,128]{1,0:T(8,128)(2,1)S(1)} %get-tuple-element.314, bf16[2816,128]{1,0:T(8,128)(2,1)S(1)} %get-tuple-element.315), kind=kOutput, calls=%fused_computation.15.clone.1 | convolution fusion | flops 2712461312 | bytes 3369984 | tf_op jit(solution)/shard_map/while/body/eval_jaxpr/dot_general | solution.py:83
  23.9 1.5 %collective-permute-done.1 = f32[144,128]{1,0:T(8,128)S(1)} collective-permute-done((f32[144,128]{1,0:T(8,128)S(1)}, f32[144,128]{1,0:T(8,128)S(1)}, u32[]{:S(2)}, u32[]{:S(2)}) %collective-permute-start.1) | collective-permute-done | bytes 73760 | tf_op jit(solution)/shard_map/while/body/eval_jaxpr/ppermute | solution.py:16
  26.1 1.3 %fusion.88 = f32[1872,128]{1,0:T(8,128)S(1)} fusion(f32[144,128]{1,0:T(8,128)S(1)} %slice_add_fusion.9, f32[1728,128]{1,0:T(8,128)S(1)} %fusion.87, f32[1872,128]{1,0:T(8,128)S(1)} %get-tuple-element.337, f32[1872,128]{1,0:T(8,128)S(1)} %get-tuple-element.338, f32[]{:T(128)S(6)} %select_n.51, f32[]{:T(128)S(6)} %mul.171, ...), kind=kLoop, calls=%fused_computation.30.clone.1 | loop fusion | flops 2156544 | bytes 3848840 | tf_op jit(solution)/shard_map/while/body/eval_jaxpr/sub | solution.py:96
  27.5 2.4 %fusion.82 = bf16[2816,128]{0,1:T(8,128)(2,1)S(1)} fusion(s32[2816]{0:T(1024)S(1)} %get-tuple-element.358, f32[1872,128]{1,0:T(8,128)S(1)} %get-tuple-element.338, f32[1872]{0:T(1024)S(1)} %get-tuple-element.355), kind=kOutput, calls=%fused_computation.12.clone.1 | convolution fusion | flops 1360900096 | bytes 1698112 | tf_op jit(solution)/shard_map/while/body/eval_jaxpr/dot_general | solution.py:72
  30.2 1.5 %fusion.83 = f32[8,128,352]{1,2,0:T(8,128)S(1)} fusion(bf16[8,352,128]{2,1,0:T(8,128)(2,1)S(1)} %bitcast.43, bf16[352,352]{1,0:T(8,128)(2,1)} %get-tuple-element.356), kind=kOutput, calls=%fused_computation.37.clone.1 | convolution fusion | flops 253755392 | bytes 2410496 | tf_op jit(solution)/shard_map/while/body/eval_jaxpr/ij,cjb->cib/dot_general | solution.py:76
  33.5 1.2 %collective-permute-start.1 = (f32[144,128]{1,0:T(8,128)S(1)}, f32[144,128]{1,0:T(8,128)S(1)}, u32[]{:S(2)}, u32[]{:S(2)}) collective-permute-start(f32[144,128]{1,0:T(8,128)S(1)} %get-tuple-element.317), channel_id=1, source_target_pairs={{0,8},{8,16},{16,24},{24,0},{1,9},{9,17},{17,25},{25,1},{2,10},{10... | collective-permute-start | bytes 221192 | tf_op jit(solution)/shard_map/while/body/eval_jaxpr/ppermute | solution.py:16
  34.7 3.0 %fusion.86 = f32[1872,256]{1,0:T(8,128)S(1)} fusion(s32[2816]{0:T(1024)S(1)} %get-tuple-element.358, bf16[2816,128]{1,0:T(8,128)(2,1)S(1)} %get-tuple-element.314, bf16[2816,128]{1,0:T(8,128)(2,1)S(1)} %get-tuple-element.315), kind=kOutput, calls=%fused_computation.15.clone.1 | convolution fusion | flops 2712461312 | bytes 3369984 | tf_op jit(solution)/shard_map/while/body/eval_jaxpr/dot_general | solution.py:83
  39.4 1.3 %fusion.88 = f32[1872,128]{1,0:T(8,128)S(1)} fusion(f32[144,128]{1,0:T(8,128)S(1)} %slice_add_fusion.9, f32[1728,128]{1,0:T(8,128)S(1)} %fusion.87, f32[1872,128]{1,0:T(8,128)S(1)} %get-tuple-element.337, f32[1872,128]{1,0:T(8,128)S(1)} %get-tuple-element.338, f32[]{:T(128)S(6)} %select_n.51, f32[]{:T(128)S(6)} %mul.171, ...), kind=kLoop, calls=%fused_computation.30.clone.1 | loop fusion | flops 2156544 | bytes 3848840 | tf_op jit(solution)/shard_map/while/body/eval_jaxpr/sub | solution.py:96
  40.9 2.4 %fusion.82 = bf16[2816,128]{0,1:T(8,128)(2,1)S(1)} fusion(s32[2816]{0:T(1024)S(1)} %get-tuple-element.358, f32[1872,128]{1,0:T(8,128)S(1)} %get-tuple-element.338, f32[1872]{0:T(1024)S(1)} %get-tuple-element.355), kind=kOutput, calls=%fused_computation.12.clone.1 | convolution fusion | flops 1360900096 | bytes 1698112 | tf_op jit(solution)/shard_map/while/body/eval_jaxpr/dot_general | solution.py:72
  43.6 1.5 %fusion.83 = f32[8,128,352]{1,2,0:T(8,128)S(1)} fusion(bf16[8,352,128]{2,1,0:T(8,128)(2,1)S(1)} %bitcast.43, bf16[352,352]{1,0:T(8,128)(2,1)} %get-tuple-element.356), kind=kOutput, calls=%fused_computation.37.clone.1 | convolution fusion | flops 253755392 | bytes 2410496 | tf_op jit(solution)/shard_map/while/body/eval_jaxpr/ij,cjb->cib/dot_general | solution.py:76
  48.1 3.0 %fusion.86 = f32[1872,256]{1,0:T(8,128)S(1)} fusion(s32[2816]{0:T(1024)S(1)} %get-tuple-element.358, bf16[2816,128]{1,0:T(8,128)(2,1)S(1)} %get-tuple-element.314, bf16[2816,128]{1,0:T(8,128)(2,1)S(1)} %get-tuple-element.315), kind=kOutput, calls=%fused_computation.15.clone.1 | convolution fusion | flops 2712461312 | bytes 3369984 | tf_op jit(solution)/shard_map/while/body/eval_jaxpr/dot_general | solution.py:83
  52.8 1.3 %fusion.88 = f32[1872,128]{1,0:T(8,128)S(1)} fusion(f32[144,128]{1,0:T(8,128)S(1)} %slice_add_fusion.9, f32[1728,128]{1,0:T(8,128)S(1)} %fusion.87, f32[1872,128]{1,0:T(8,128)S(1)} %get-tuple-element.337, f32[1872,128]{1,0:T(8,128)S(1)} %get-tuple-element.338, f32[]{:T(128)S(6)} %select_n.51, f32[]{:T(128)S(6)} %mul.171, ...), kind=kLoop, calls=%fused_computation.30.clone.1 | loop fusion | flops 2156544 | bytes 3848840 | tf_op jit(solution)/shard_map/while/body/eval_jaxpr/sub | solution.py:96
  54.3 1.6 %collective-permute-start.5 = (bf16[1728,128]{1,0:T(8,128)(2,1)S(1)}, bf16[1728,128]{1,0:T(8,128)(2,1)S(1)}, u32[]{:S(2)}, u32[]{:S(2)}) collective-permute-start(bf16[1728,128]{1,0:T(8,128)(2,1)S(1)} %slice.142), channel_id=1, source_target_pairs={{0,2},{2,0},{1,3},{3,1},{4,6},{6,4},{5,7},{7,5},{8,10},{10,8},{9,1... | collective-permute-start | bytes 1327112 | tf_op jit(solution)/shard_map/ppermute | solution.py:26
  56.2 6.5 %collective-permute-done.5 = bf16[1728,128]{1,0:T(8,128)(2,1)S(1)} collective-permute-done((bf16[1728,128]{1,0:T(8,128)(2,1)S(1)}, bf16[1728,128]{1,0:T(8,128)(2,1)S(1)}, u32[]{:S(2)}, u32[]{:S(2)}) %collective-permute-start.5) | collective-permute-done | bytes 442400 | tf_op jit(solution)/shard_map/ppermute | solution.py:26
  63.2 1.3 %collective-permute-done.6 = bf16[1728,128]{1,0:T(8,128)(2,1)S(1)} collective-permute-done((bf16[1728,128]{1,0:T(8,128)(2,1)S(1)}, bf16[1728,128]{1,0:T(8,128)(2,1)S(1)}, u32[]{:S(2)}, u32[]{:S(2)}) %collective-permute-start.6) | collective-permute-done | bytes 442400 | tf_op jit(solution)/shard_map/ppermute | solution.py:26
  (83 shorter events, 16.2 us)
Async XLA Ops:
  0.0 55.9 %copy-start = (bf16[512,128]{1,0:T(8,128)(2,1)S(1)}, bf16[512,128]{1,0:T(8,128)(2,1)}, u32[]{:S(2)}) copy-start(bf16[512,128]{1,0:T(8,128)(2,1)} %param.15) | copy-start | bytes 393220
  0.0 10.4 %copy-start.3 = (bf16[1728,128]{1,0:T(8,128)(2,1)S(1)}, bf16[1728,128]{1,0:T(8,128)(2,1)}, u32[]{:S(2)}) copy-start(bf16[1728,128]{1,0:T(8,128)(2,1)} %param.9) | copy-start | bytes 1327108
  0.0 10.3 %copy-start.5 = (s32[144]{0:T(256)S(1)}, s32[144]{0:T(256)}, u32[]{:S(2)}) copy-start(s32[144]{0:T(256)} %param.14) | copy-start | bytes 1732
  0.0 8.2 %copy-start.2 = (f32[1728]{0:T(1024)S(1)}, f32[1728]{0:T(1024)}, u32[]{:S(2)}) copy-start(f32[1728]{0:T(1024)} %param.10) | copy-start | bytes 20740
  0.1 10.4 %copy-start.6 = (s32[8,343]{1,0:T(8,128)S(1)}, s32[8,343]{1,0:T(8,128)}, u32[]{:S(2)}) copy-start(s32[8,343]{1,0:T(8,128)} %param.13) | copy-start | bytes 32932
  1.5 9.0 %copy-start.4 = (bf16[343,343]{1,0:T(8,128)(2,1)S(1)}, bf16[343,343]{1,0:T(8,128)(2,1)}, u32[]{:S(2)}) copy-start(bf16[343,343]{1,0:T(8,128)(2,1)} %param.12) | copy-start | bytes 705898
  1.6 11.9 %collective-permute-start.2 = (f32[144,128]{1,0:T(8,128)S(1)}, f32[144,128]{1,0:T(8,128)S(1)}, u32[]{:S(2)}, u32[]{:S(2)}) collective-permute-start(f32[144,128]{1,0:T(8,128)S(1)} %fusion.44), channel_id=1, source_target_pairs={{0,24},{8,0},{16,8},{24,16},{1,25},{9,1},{17,9},{25,17},{2,26},{10... | collective-permute-start | bytes 221192 | tf_op jit(solution)/shard_map/ppermute | solution.py:16
  6.2 7.1 %copy-start.1 = (f32[1728]{0:T(1024)S(1)}, f32[1728]{0:T(1024)}, u32[]{:S(2)}) copy-start(f32[1728]{0:T(1024)} %param.11) | copy-start | bytes 20740
  9.7 3.6 %collective-permute-start.3 = (f32[2,144]{1,0:T(2,128)S(1)}, f32[2,144]{1,0:T(2,128)S(1)}, u32[]{:S(2)}, u32[]{:S(2)}) collective-permute-start(f32[2,144]{1,0:T(2,128)S(1)} %pad_maximum_fusion.6), channel_id=1, source_target_pairs={{0,24},{8,0},{16,8},{24,16},{1,25},{9,1},{17,9},{25,17},{2,26},{10... | collective-permute-start | bytes 3464 | tf_op jit(solution)/shard_map/ppermute | solution.py:16
  18.7 7.4 %collective-permute-start = (f32[144,128]{1,0:T(8,128)S(1)}, f32[144,128]{1,0:T(8,128)S(1)}, u32[]{:S(2)}, u32[]{:S(2)}) collective-permute-start(f32[144,128]{1,0:T(8,128)S(1)} %get-tuple-element.316), channel_id=1, source_target_pairs={{0,24},{8,0},{16,8},{24,16},{1,25},{9,1},{17,9},{25,17},{2,26},{10... | collective-permute-start | bytes 221192 | tf_op jit(solution)/shard_map/while/body/eval_jaxpr/ppermute | solution.py:16
  20.2 5.3 %collective-permute-start.1 = (f32[144,128]{1,0:T(8,128)S(1)}, f32[144,128]{1,0:T(8,128)S(1)}, u32[]{:S(2)}, u32[]{:S(2)}) collective-permute-start(f32[144,128]{1,0:T(8,128)S(1)} %get-tuple-element.317), channel_id=1, source_target_pairs={{0,8},{8,16},{16,24},{24,0},{1,9},{9,17},{17,25},{25,1},{2,10},{10... | collective-permute-start | bytes 221192 | tf_op jit(solution)/shard_map/while/body/eval_jaxpr/ppermute | solution.py:16
  32.7 6.7 %collective-permute-start = (f32[144,128]{1,0:T(8,128)S(1)}, f32[144,128]{1,0:T(8,128)S(1)}, u32[]{:S(2)}, u32[]{:S(2)}) collective-permute-start(f32[144,128]{1,0:T(8,128)S(1)} %get-tuple-element.316), channel_id=1, source_target_pairs={{0,24},{8,0},{16,8},{24,16},{1,25},{9,1},{17,9},{25,17},{2,26},{10... | collective-permute-start | bytes 221192 | tf_op jit(solution)/shard_map/while/body/eval_jaxpr/ppermute | solution.py:16
  33.5 5.3 %collective-permute-start.1 = (f32[144,128]{1,0:T(8,128)S(1)}, f32[144,128]{1,0:T(8,128)S(1)}, u32[]{:S(2)}, u32[]{:S(2)}) collective-permute-start(f32[144,128]{1,0:T(8,128)S(1)} %get-tuple-element.317), channel_id=1, source_target_pairs={{0,8},{8,16},{16,24},{24,0},{1,9},{9,17},{17,25},{25,1},{2,10},{10... | collective-permute-start | bytes 221192 | tf_op jit(solution)/shard_map/while/body/eval_jaxpr/ppermute | solution.py:16
  46.0 6.7 %collective-permute-start = (f32[144,128]{1,0:T(8,128)S(1)}, f32[144,128]{1,0:T(8,128)S(1)}, u32[]{:S(2)}, u32[]{:S(2)}) collective-permute-start(f32[144,128]{1,0:T(8,128)S(1)} %get-tuple-element.316), channel_id=1, source_target_pairs={{0,24},{8,0},{16,8},{24,16},{1,25},{9,1},{17,9},{25,17},{2,26},{10... | collective-permute-start | bytes 221192 | tf_op jit(solution)/shard_map/while/body/eval_jaxpr/ppermute | solution.py:16
  46.8 5.3 %collective-permute-start.1 = (f32[144,128]{1,0:T(8,128)S(1)}, f32[144,128]{1,0:T(8,128)S(1)}, u32[]{:S(2)}, u32[]{:S(2)}) collective-permute-start(f32[144,128]{1,0:T(8,128)S(1)} %get-tuple-element.317), channel_id=1, source_target_pairs={{0,8},{8,16},{16,24},{24,0},{1,9},{9,17},{17,25},{25,1},{2,10},{10... | collective-permute-start | bytes 221192 | tf_op jit(solution)/shard_map/while/body/eval_jaxpr/ppermute | solution.py:16
  54.3 8.4 %collective-permute-start.5 = (bf16[1728,128]{1,0:T(8,128)(2,1)S(1)}, bf16[1728,128]{1,0:T(8,128)(2,1)S(1)}, u32[]{:S(2)}, u32[]{:S(2)}) collective-permute-start(bf16[1728,128]{1,0:T(8,128)(2,1)S(1)} %slice.142), channel_id=1, source_target_pairs={{0,2},{2,0},{1,3},{3,1},{4,6},{6,4},{5,7},{7,5},{8,10},{10,8},{9,1... | collective-permute-start | bytes 1327112 | tf_op jit(solution)/shard_map/ppermute | solution.py:26
  55.9 6.7 %collective-permute-start.4 = (bf16[1728,128]{1,0:T(8,128)(2,1)S(1)}, bf16[1728,128]{1,0:T(8,128)(2,1)S(1)}, u32[]{:S(2)}, u32[]{:S(2)}) collective-permute-start(bf16[1728,128]{1,0:T(8,128)(2,1)S(1)} %slice.142), channel_id=1, source_target_pairs={{0,1},{1,0},{2,3},{3,2},{4,5},{5,4},{6,7},{7,6},{8,9},{9,8},{10,11... | collective-permute-start | bytes 1327112 | tf_op jit(solution)/shard_map/ppermute | solution.py:26
  62.6 1.8 %collective-permute-start.6 = (bf16[1728,128]{1,0:T(8,128)(2,1)S(1)}, bf16[1728,128]{1,0:T(8,128)(2,1)S(1)}, u32[]{:S(2)}, u32[]{:S(2)}) collective-permute-start(bf16[1728,128]{1,0:T(8,128)(2,1)S(1)} %collective-permute-done.5), channel_id=1, source_target_pairs={{0,1},{1,0},{2,3},{3,2},{4,5},{5,4},{6,7},{7,6},{8,9},{9,8},{10,11... | collective-permute-start | bytes 1327112 | tf_op jit(solution)/shard_map/ppermute | solution.py:26

commit v9 on v5

--- a/solution.py
+++ b/solution.py
@@ -42,7 +42,7 @@
     cell_count, cell_size = connect.shape
     face_count = face_rows.shape[0]
     wide_count = node_count + face_count
-    pad = (-cell_size) % 16
+    pad = (-cell_size) % 128
     padded_size = cell_size + pad
     cell_rows = jnp.pad(connect, ((0, 0), (0, pad)), constant_values=-1).reshape(-1)
     padded_matrix = jnp.pad(cell_matrix, ((0, pad), (0, pad)))

time: 65.2 us -> 74.5 us (1.14)
  local copies, waits for them, and re-layouts: 4.35 us -> 11.1 us
  matrix products: 28.6 us -> 30.5 us
    while x6 -> x36, local copies, waits for them, and re-layouts: 0.38 us -> 7.17 us
    dot_general x3, matrix products: 7.05 us -> 10.9 us  [operate(): lax.dot_general(scatter_sel, weighted, (((0,), (0,)), ((), ())), preferre...]
    dot_general x3, matrix products: 4.46 us -> 1.95 us  [operate(): jnp.einsum('ij,cjb->cib', padded_matrix, values, preferred_element_type=j...]
    transpose x0 -> x3, local copies, waits for them, and re-layouts: none -> 1.38 us  [operate(): jnp.einsum('ij,cjb->cib', padded_matrix, values, preferred_element_type=j...]
    convert_element_type x3 -> x0, local copies, waits for them, and re-layouts: 1.04 us -> none  [operate(): values.astype(jnp.bfloat16).reshape(cell_count, padded_size, state_count)]
  transfers between devices with their start and end apart: 11 -> 11, of which waited for: 6 -> 6; matrix products, arithmetic and copies ran while one was open for 27% -> 23% of each run, Pallas kernels for 0% -> 0%
where the time goes in v9:
time: 74.5 us; the launch traced here: 74 us
  matrix products  30.5 us (41%)
  starting transfers between devices  12.4 us (17%)
  waiting for transfers between devices  12 us (16%)
  local copies, waits for them, and re-layouts  11.1 us (15%)
  other arithmetic  7.41 us (10%)
    dot_general x3, matrix products, operate(): lax.dot_general(scatter_sel, weighted, (((0,), (0,)), ((), ())), preferre...  10.9 us
    ppermute x8, starting transfers between devices, ring(): return lax.ppermute(block, axis, route)  10.7 us
    dot_general x3, matrix products, operate(): jnp.dot(scatter_sel, both, preferred_element_type=jnp.float32)  9.6 us
    ppermute x3, waiting for transfers between devices, from_partner(): return lax.ppermute(block, axis, route)  7.71 us
    while x36, local copies, waits for them, and re-layouts  7.17 us
    ppermute x8, waiting for transfers between devices, ring(): return lax.ppermute(block, axis, route)  4.32 us
    sub x3, other arithmetic, chebyshev_step(): return (current, gain * scaled - keep * previous)  3.78 us
    dot_general x3, matrix products, operate(): jnp.dot(rim_sel, both, preferred_element_type=jnp.float32)  1.99 us
  transfers between devices with their start and end apart: 11, of which 6 were waited for; matrix products, arithmetic and copies ran while one was open for 23% of the time, Pallas kernels for 0%

profile of v9, /device:TPU:0, one launch (start us, length us, event | category | flops | bytes accessed | tf_op | source)
XLA Modules:
  0.0 74.0 jit_solution(14760019765506456355)
XLA Ops:
  0.1 1.4 %fusion.44 = f32[144,128]{1,0:T(8,128)S(1)} fusion(bf16[1728,128]{1,0:T(8,128)(2,1)} %param.9, s32[1728]{0:T(1024)S(1)} %add_reduce_fusion, s32[144]{0:T(256)} %param.14), kind=kOutput, calls=%fused_computation.54 | convolution fusion | flops 63949824 | bytes 523584 | tf_op jit(solution)/shard_map/dot_general | solution.py:57
  1.5 4.0 %collective-permute-start.2 = (f32[144,128]{1,0:T(8,128)S(1)}, f32[144,128]{1,0:T(8,128)S(1)}, u32[]{:S(2)}, u32[]{:S(2)}) collective-permute-start(f32[144,128]{1,0:T(8,128)S(1)} %fusion.44), channel_id=1, source_target_pairs={{0,24},{8,0},{16,8},{24,16},{1,25},{9,1},{17,9},{25,17},{2,26},{10... | collective-permute-start | bytes 221192 | tf_op jit(solution)/shard_map/ppermute | solution.py:16
  6.9 1.4 %fusion.42 = f32[2,144]{1,0:T(2,128)S(1)} fusion(s32[144]{0:T(256)} %param.14, s32[1728]{0:T(1024)S(1)} %add_reduce_fusion, f32[1,1728]{1,0:T(1,128)S(1)} %stack.10, f32[1,1728]{1,0:T(1,128)S(1)} %stack.9), kind=kOutput, calls=%fused_computation.52 | convolution fusion | flops 6224256 | bytes 22464 | tf_op jit(solution)/shard_map/dot_general | solution.py:58
  9.5 1.1 %convert_element_type.62 = f32[1728,128]{1,0:T(8,128)S(1)} convert(bf16[1728,128]{1,0:T(8,128)(2,1)} %param.9) | non-fusion elementwise | flops 221184 | bytes 1327104 | tf_op jit(solution)/shard_map/convert_element_type | solution.py:66
  10.7 1.1 %collective-permute-done.3 = f32[2,144]{1,0:T(2,128)S(1)} collective-permute-done((f32[2,144]{1,0:T(2,128)S(1)}, f32[2,144]{1,0:T(2,128)S(1)}, u32[]{:S(2)}, u32[]{:S(2)}) %collective-permute-start.3) | collective-permute-done | bytes 1184 | tf_op jit(solution)/shard_map/ppermute | solution.py:16
  13.0 49.6 %while.17 = (s32[]{:T(128)}, f32[1872,128]{1,0:T(8,128)}, f32[1872,128]{1,0:T(8,128)S(1)}, f32[1872]{0:T(1024)S(1)}, bf16[384,384]{1,0:T(8,128)(2,1)S(1)}, /*ind...) while((s32[]{:T(128)}, f32[1872,128]{1,0:T(8,128)}, ...), condition=%wide.region_1.2_spmd.clone.clone, body=%wide.region_0.1_spmd.clone.clone.sunk | while | flops 5336100864 | bytes 47598380 | solution.py:98
  13.0 3.6 %fusion.86 = bf16[128,3072]{1,0:T(8,128)(2,1)S(1)} fusion(s32[3072]{0:T(1024)S(1)} %get-tuple-element.358, f32[1872,128]{1,0:T(8,128)S(1)} %get-tuple-element.338, f32[1872]{0:T(1024)S(1)} %get-tuple-element.355), kind=kOutput, calls=%fused_computation.9.clone.1 | convolution fusion | flops 1484574720 | bytes 1764672 | tf_op jit(solution)/shard_map/while/body/eval_jaxpr/dot_general | solution.py:72
  18.7 1.5 %collective-permute-start = (f32[144,128]{1,0:T(8,128)S(1)}, f32[144,128]{1,0:T(8,128)S(1)}, u32[]{:S(2)}, u32[]{:S(2)}) collective-permute-start(f32[144,128]{1,0:T(8,128)S(1)} %get-tuple-element.316), channel_id=1, source_target_pairs={{0,24},{8,0},{16,8},{24,16},{1,25},{9,1},{17,9},{25,17},{2,26},{10... | collective-permute-start | bytes 221192 | tf_op jit(solution)/shard_map/while/body/eval_jaxpr/ppermute | solution.py:16
  20.8 3.2 %fusion.89 = f32[1872,256]{1,0:T(8,128)S(1)} fusion(s32[3072]{0:T(1024)S(1)} %get-tuple-element.358, bf16[3072,128]{1,0:T(8,128)(2,1)S(1)} %get-tuple-element.314, bf16[3072,128]{1,0:T(8,128)(2,1)S(1)} %get-tuple-element.315), kind=kOutput, calls=%fused_computation.12.clone.1 | convolution fusion | flops 2959048704 | bytes 3502080 | tf_op jit(solution)/shard_map/while/body/eval_jaxpr/dot_general | solution.py:83
  24.1 1.3 %collective-permute-done.1 = f32[144,128]{1,0:T(8,128)S(1)} collective-permute-done((f32[144,128]{1,0:T(8,128)S(1)}, f32[144,128]{1,0:T(8,128)S(1)}, u32[]{:S(2)}, u32[]{:S(2)}) %collective-permute-start.1) | collective-permute-done | bytes 73760 | tf_op jit(solution)/shard_map/while/body/eval_jaxpr/ppermute | solution.py:16
  27.4 1.3 %fusion.91 = f32[1872,128]{1,0:T(8,128)S(1)} fusion(f32[144,128]{1,0:T(8,128)S(1)} %slice_add_fusion.9, f32[1728,128]{1,0:T(8,128)S(1)} %fusion.90, f32[1872,128]{1,0:T(8,128)S(1)} %copy-done.4, f32[1872,128]{1,0:T(8,128)S(1)} %copy-done.2, f32[]{:T(128)S(6)} %select_n.45, f32[]{:T(128)S(6)} %mul.171, f32[1872]{0:T(1024)S(1)} %get-tuple-element.357, ...), kind=kLoop, calls=%fused_computation.28.clone.1 | loop fusion | flops 2156544 | bytes 3848840 | tf_op jit(solution)/shard_map/while/body/eval_jaxpr/sub | solution.py:96
  29.8 3.6 %fusion.86 = bf16[128,3072]{1,0:T(8,128)(2,1)S(1)} fusion(s32[3072]{0:T(1024)S(1)} %get-tuple-element.358, f32[1872,128]{1,0:T(8,128)S(1)} %get-tuple-element.338, f32[1872]{0:T(1024)S(1)} %get-tuple-element.355), kind=kOutput, calls=%fused_computation.9.clone.1 | convolution fusion | flops 1484574720 | bytes 1764672 | tf_op jit(solution)/shard_map/while/body/eval_jaxpr/dot_general | solution.py:72
  35.5 1.1 %collective-permute-start = (f32[144,128]{1,0:T(8,128)S(1)}, f32[144,128]{1,0:T(8,128)S(1)}, u32[]{:S(2)}, u32[]{:S(2)}) collective-permute-start(f32[144,128]{1,0:T(8,128)S(1)} %get-tuple-element.316), channel_id=1, source_target_pairs={{0,24},{8,0},{16,8},{24,16},{1,25},{9,1},{17,9},{25,17},{2,26},{10... | collective-permute-start | bytes 221192 | tf_op jit(solution)/shard_map/while/body/eval_jaxpr/ppermute | solution.py:16
  36.6 1.0 %collective-permute-start.1 = (f32[144,128]{1,0:T(8,128)S(1)}, f32[144,128]{1,0:T(8,128)S(1)}, u32[]{:S(2)}, u32[]{:S(2)}) collective-permute-start(f32[144,128]{1,0:T(8,128)S(1)} %get-tuple-element.317), channel_id=1, source_target_pairs={{0,8},{8,16},{16,24},{24,0},{1,9},{9,17},{17,25},{25,1},{2,10},{10... | collective-permute-start | bytes 221192 | tf_op jit(solution)/shard_map/while/body/eval_jaxpr/ppermute | solution.py:16
  37.6 3.2 %fusion.89 = f32[1872,256]{1,0:T(8,128)S(1)} fusion(s32[3072]{0:T(1024)S(1)} %get-tuple-element.358, bf16[3072,128]{1,0:T(8,128)(2,1)S(1)} %get-tuple-element.314, bf16[3072,128]{1,0:T(8,128)(2,1)S(1)} %get-tuple-element.315), kind=kOutput, calls=%fused_computation.12.clone.1 | convolution fusion | flops 2959048704 | bytes 3502080 | tf_op jit(solution)/shard_map/while/body/eval_jaxpr/dot_general | solution.py:83
  43.8 1.3 %fusion.91 = f32[1872,128]{1,0:T(8,128)S(1)} fusion(f32[144,128]{1,0:T(8,128)S(1)} %slice_add_fusion.9, f32[1728,128]{1,0:T(8,128)S(1)} %fusion.90, f32[1872,128]{1,0:T(8,128)S(1)} %copy-done.4, f32[1872,128]{1,0:T(8,128)S(1)} %copy-done.2, f32[]{:T(128)S(6)} %select_n.45, f32[]{:T(128)S(6)} %mul.171, f32[1872]{0:T(1024)S(1)} %get-tuple-element.357, ...), kind=kLoop, calls=%fused_computation.28.clone.1 | loop fusion | flops 2156544 | bytes 3848840 | tf_op jit(solution)/shard_map/while/body/eval_jaxpr/sub | solution.py:96
  46.2 3.6 %fusion.86 = bf16[128,3072]{1,0:T(8,128)(2,1)S(1)} fusion(s32[3072]{0:T(1024)S(1)} %get-tuple-element.358, f32[1872,128]{1,0:T(8,128)S(1)} %get-tuple-element.338, f32[1872]{0:T(1024)S(1)} %get-tuple-element.355), kind=kOutput, calls=%fused_computation.9.clone.1 | convolution fusion | flops 1484574720 | bytes 1764672 | tf_op jit(solution)/shard_map/while/body/eval_jaxpr/dot_general | solution.py:72
  51.9 1.1 %collective-permute-start = (f32[144,128]{1,0:T(8,128)S(1)}, f32[144,128]{1,0:T(8,128)S(1)}, u32[]{:S(2)}, u32[]{:S(2)}) collective-permute-start(f32[144,128]{1,0:T(8,128)S(1)} %get-tuple-element.316), channel_id=1, source_target_pairs={{0,24},{8,0},{16,8},{24,16},{1,25},{9,1},{17,9},{25,17},{2,26},{10... | collective-permute-start | bytes 221192 | tf_op jit(solution)/shard_map/while/body/eval_jaxpr/ppermute | solution.py:16
  54.0 3.2 %fusion.89 = f32[1872,256]{1,0:T(8,128)S(1)} fusion(s32[3072]{0:T(1024)S(1)} %get-tuple-element.358, bf16[3072,128]{1,0:T(8,128)(2,1)S(1)} %get-tuple-element.314, bf16[3072,128]{1,0:T(8,128)(2,1)S(1)} %get-tuple-element.315), kind=kOutput, calls=%fused_computation.12.clone.1 | convolution fusion | flops 2959048704 | bytes 3502080 | tf_op jit(solution)/shard_map/while/body/eval_jaxpr/dot_general | solution.py:83
  60.2 1.3 %fusion.91 = f32[1872,128]{1,0:T(8,128)S(1)} fusion(f32[144,128]{1,0:T(8,128)S(1)} %slice_add_fusion.9, f32[1728,128]{1,0:T(8,128)S(1)} %fusion.90, f32[1872,128]{1,0:T(8,128)S(1)} %copy-done.4, f32[1872,128]{1,0:T(8,128)S(1)} %copy-done.2, f32[]{:T(128)S(6)} %select_n.45, f32[]{:T(128)S(6)} %mul.171, f32[1872]{0:T(1024)S(1)} %get-tuple-element.357, ...), kind=kLoop, calls=%fused_computation.28.clone.1 | loop fusion | flops 2156544 | bytes 3848840 | tf_op jit(solution)/shard_map/while/body/eval_jaxpr/sub | solution.py:96
  62.6 1.6 %collective-permute-start.5 = (bf16[1728,128]{1,0:T(8,128)(2,1)S(1)}, bf16[1728,128]{1,0:T(8,128)(2,1)S(1)}, u32[]{:S(2)}, u32[]{:S(2)}) collective-permute-start(bf16[1728,128]{1,0:T(8,128)(2,1)S(1)} %slice.138), channel_id=1, source_target_pairs={{0,2},{2,0},{1,3},{3,1},{4,6},{6,4},{5,7},{7,5},{8,10},{10,8},{9,1... | collective-permute-start | bytes 1327112 | tf_op jit(solution)/shard_map/ppermute | solution.py:26
  64.5 6.5 %collective-permute-done.5 = bf16[1728,128]{1,0:T(8,128)(2,1)S(1)} collective-permute-done((bf16[1728,128]{1,0:T(8,128)(2,1)S(1)}, bf16[1728,128]{1,0:T(8,128)(2,1)S(1)}, u32[]{:S(2)}, u32[]{:S(2)}) %collective-permute-start.5) | collective-permute-done | bytes 442400 | tf_op jit(solution)/shard_map/ppermute | solution.py:26
  71.5 1.2 %collective-permute-done.6 = bf16[1728,128]{1,0:T(8,128)(2,1)S(1)} collective-permute-done((bf16[1728,128]{1,0:T(8,128)(2,1)S(1)}, bf16[1728,128]{1,0:T(8,128)(2,1)S(1)}, u32[]{:S(2)}, u32[]{:S(2)}) %collective-permute-start.6) | collective-permute-done | bytes 442400 | tf_op jit(solution)/shard_map/ppermute | solution.py:26
  72.8 1.2 %convolution_add_fusion = f32[1728,128]{1,0:T(8,128)} fusion(f32[1728,128]{1,0:T(8,128)S(1)} %convolution_add_fusion.1, bf16[1728,128]{1,0:T(8,128)(2,1)S(1)} %collective-permute-done.6, bf16[512,128]{1,0:T(8,128)(2,1)S(1)} %copy-done, s32[]{:T(128)S(6)} %select_n.38), kind=kOutput, calls=%fused_computation.49 | convolution fusion | flops 56844288 | bytes 2244612 | tf_op jit(solution)/shard_map/dot_general | solution.py:111
  (111 shorter events, 23.7 us)
Async XLA Ops:
  0.0 64.3 %copy-start = (bf16[512,128]{1,0:T(8,128)(2,1)S(1)}, bf16[512,128]{1,0:T(8,128)(2,1)}, u32[]{:S(2)}) copy-start(bf16[512,128]{1,0:T(8,128)(2,1)} %param.15) | copy-start | bytes 393220
  0.0 11.8 %copy-start.9 = (f32[1728]{0:T(1024)S(1)}, f32[1728]{0:T(1024)}, u32[]{:S(2)}) copy-start(f32[1728]{0:T(1024)} %param.11) | copy-start | bytes 20740
  0.0 11.8 %copy-start.10 = (f32[1728]{0:T(1024)S(1)}, f32[1728]{0:T(1024)}, u32[]{:S(2)}) copy-start(f32[1728]{0:T(1024)} %param.10) | copy-start | bytes 20740
  0.0 10.6 %copy-start.11 = (s32[8,343]{1,0:T(8,128)S(1)}, s32[8,343]{1,0:T(8,128)}, u32[]{:S(2)}) copy-start(s32[8,343]{1,0:T(8,128)} %param.13) | copy-start | bytes 32932
  0.0 10.6 %copy-start.7 = (bf16[343,343]{1,0:T(8,128)(2,1)S(1)}, bf16[343,343]{1,0:T(8,128)(2,1)}, u32[]{:S(2)}) copy-start(bf16[343,343]{1,0:T(8,128)(2,1)} %param.12) | copy-start | bytes 705898
  1.5 10.4 %collective-permute-start.2 = (f32[144,128]{1,0:T(8,128)S(1)}, f32[144,128]{1,0:T(8,128)S(1)}, u32[]{:S(2)}, u32[]{:S(2)}) collective-permute-start(f32[144,128]{1,0:T(8,128)S(1)} %fusion.44), channel_id=1, source_target_pairs={{0,24},{8,0},{16,8},{24,16},{1,25},{9,1},{17,9},{25,17},{2,26},{10... | collective-permute-start | bytes 221192 | tf_op jit(solution)/shard_map/ppermute | solution.py:16
  8.2 3.6 %collective-permute-start.3 = (f32[2,144]{1,0:T(2,128)S(1)}, f32[2,144]{1,0:T(2,128)S(1)}, u32[]{:S(2)}, u32[]{:S(2)}) collective-permute-start(f32[2,144]{1,0:T(2,128)S(1)} %fusion.42), channel_id=1, source_target_pairs={{0,24},{8,0},{16,8},{24,16},{1,25},{9,1},{17,9},{25,17},{2,26},{10... | collective-permute-start | bytes 3464 | tf_op jit(solution)/shard_map/ppermute | solution.py:16
  13.0 3.6 %copy-start.1 = (f32[1872,128]{1,0:T(8,128)}, f32[1872,128]{1,0:T(8,128)S(1)}, u32[]{:S(2)}) copy-start(f32[1872,128]{1,0:T(8,128)S(1)} %get-tuple-element.338) | copy-start | bytes 2875396 | tf_op jit(solution)/shard_map/while
  13.0 3.6 %copy-start.5 = (bf16[384,384]{1,0:T(8,128)(2,1)}, bf16[384,384]{1,0:T(8,128)(2,1)S(1)}, u32[]{:S(2)}) copy-start(bf16[384,384]{1,0:T(8,128)(2,1)S(1)} %get-tuple-element.356) | copy-start | bytes 884740 | tf_op jit(solution)/shard_map/while
  18.7 7.4 %collective-permute-start = (f32[144,128]{1,0:T(8,128)S(1)}, f32[144,128]{1,0:T(8,128)S(1)}, u32[]{:S(2)}, u32[]{:S(2)}) collective-permute-start(f32[144,128]{1,0:T(8,128)S(1)} %get-tuple-element.316), channel_id=1, source_target_pairs={{0,24},{8,0},{16,8},{24,16},{1,25},{9,1},{17,9},{25,17},{2,26},{10... | collective-permute-start | bytes 221192 | tf_op jit(solution)/shard_map/while/body/eval_jaxpr/ppermute | solution.py:16
  20.2 5.3 %collective-permute-start.1 = (f32[144,128]{1,0:T(8,128)S(1)}, f32[144,128]{1,0:T(8,128)S(1)}, u32[]{:S(2)}, u32[]{:S(2)}) collective-permute-start(f32[144,128]{1,0:T(8,128)S(1)} %get-tuple-element.317), channel_id=1, source_target_pairs={{0,8},{8,16},{16,24},{24,0},{1,9},{9,17},{17,25},{25,1},{2,10},{10... | collective-permute-start | bytes 221192 | tf_op jit(solution)/shard_map/while/body/eval_jaxpr/ppermute | solution.py:16
  25.9 1.5 %copy-start.4 = (f32[1872,128]{1,0:T(8,128)S(1)}, f32[1872,128]{1,0:T(8,128)}, u32[]{:S(2)}) copy-start(f32[1872,128]{1,0:T(8,128)} %get-tuple-element.337) | copy-start | bytes 2875396 | tf_op jit(solution)/shard_map/while
  29.8 3.6 %copy-start.1 = (f32[1872,128]{1,0:T(8,128)}, f32[1872,128]{1,0:T(8,128)S(1)}, u32[]{:S(2)}) copy-start(f32[1872,128]{1,0:T(8,128)S(1)} %get-tuple-element.338) | copy-start | bytes 2875396 | tf_op jit(solution)/shard_map/while
  29.8 3.6 %copy-start.5 = (bf16[384,384]{1,0:T(8,128)(2,1)}, bf16[384,384]{1,0:T(8,128)(2,1)S(1)}, u32[]{:S(2)}) copy-start(bf16[384,384]{1,0:T(8,128)(2,1)S(1)} %get-tuple-element.356) | copy-start | bytes 884740 | tf_op jit(solution)/shard_map/while
  35.5 7.0 %collective-permute-start = (f32[144,128]{1,0:T(8,128)S(1)}, f32[144,128]{1,0:T(8,128)S(1)}, u32[]{:S(2)}, u32[]{:S(2)}) collective-permute-start(f32[144,128]{1,0:T(8,128)S(1)} %get-tuple-element.316), channel_id=1, source_target_pairs={{0,24},{8,0},{16,8},{24,16},{1,25},{9,1},{17,9},{25,17},{2,26},{10... | collective-permute-start | bytes 221192 | tf_op jit(solution)/shard_map/while/body/eval_jaxpr/ppermute | solution.py:16
  36.6 5.3 %collective-permute-start.1 = (f32[144,128]{1,0:T(8,128)S(1)}, f32[144,128]{1,0:T(8,128)S(1)}, u32[]{:S(2)}, u32[]{:S(2)}) collective-permute-start(f32[144,128]{1,0:T(8,128)S(1)} %get-tuple-element.317), channel_id=1, source_target_pairs={{0,8},{8,16},{16,24},{24,0},{1,9},{9,17},{17,25},{25,1},{2,10},{10... | collective-permute-start | bytes 221192 | tf_op jit(solution)/shard_map/while/body/eval_jaxpr/ppermute | solution.py:16
  42.3 1.5 %copy-start.4 = (f32[1872,128]{1,0:T(8,128)S(1)}, f32[1872,128]{1,0:T(8,128)}, u32[]{:S(2)}) copy-start(f32[1872,128]{1,0:T(8,128)} %get-tuple-element.337) | copy-start | bytes 2875396 | tf_op jit(solution)/shard_map/while
  46.2 3.6 %copy-start.1 = (f32[1872,128]{1,0:T(8,128)}, f32[1872,128]{1,0:T(8,128)S(1)}, u32[]{:S(2)}) copy-start(f32[1872,128]{1,0:T(8,128)S(1)} %get-tuple-element.338) | copy-start | bytes 2875396 | tf_op jit(solution)/shard_map/while
  46.2 3.6 %copy-start.5 = (bf16[384,384]{1,0:T(8,128)(2,1)}, bf16[384,384]{1,0:T(8,128)(2,1)S(1)}, u32[]{:S(2)}) copy-start(bf16[384,384]{1,0:T(8,128)(2,1)S(1)} %get-tuple-element.356) | copy-start | bytes 884740 | tf_op jit(solution)/shard_map/while
  51.9 7.0 %collective-permute-start = (f32[144,128]{1,0:T(8,128)S(1)}, f32[144,128]{1,0:T(8,128)S(1)}, u32[]{:S(2)}, u32[]{:S(2)}) collective-permute-start(f32[144,128]{1,0:T(8,128)S(1)} %get-tuple-element.316), channel_id=1, source_target_pairs={{0,24},{8,0},{16,8},{24,16},{1,25},{9,1},{17,9},{25,17},{2,26},{10... | collective-permute-start | bytes 221192 | tf_op jit(solution)/shard_map/while/body/eval_jaxpr/ppermute | solution.py:16
  53.0 5.3 %collective-permute-start.1 = (f32[144,128]{1,0:T(8,128)S(1)}, f32[144,128]{1,0:T(8,128)S(1)}, u32[]{:S(2)}, u32[]{:S(2)}) collective-permute-start(f32[144,128]{1,0:T(8,128)S(1)} %get-tuple-element.317), channel_id=1, source_target_pairs={{0,8},{8,16},{16,24},{24,0},{1,9},{9,17},{17,25},{25,1},{2,10},{10... | collective-permute-start | bytes 221192 | tf_op jit(solution)/shard_map/while/body/eval_jaxpr/ppermute | solution.py:16
  62.6 8.4 %collective-permute-start.5 = (bf16[1728,128]{1,0:T(8,128)(2,1)S(1)}, bf16[1728,128]{1,0:T(8,128)(2,1)S(1)}, u32[]{:S(2)}, u32[]{:S(2)}) collective-permute-start(bf16[1728,128]{1,0:T(8,128)(2,1)S(1)} %slice.138), channel_id=1, source_target_pairs={{0,2},{2,0},{1,3},{3,1},{4,6},{6,4},{5,7},{7,5},{8,10},{10,8},{9,1... | collective-permute-start | bytes 1327112 | tf_op jit(solution)/shard_map/ppermute | solution.py:26
  64.3 6.7 %collective-permute-start.4 = (bf16[1728,128]{1,0:T(8,128)(2,1)S(1)}, bf16[1728,128]{1,0:T(8,128)(2,1)S(1)}, u32[]{:S(2)}, u32[]{:S(2)}) collective-permute-start(bf16[1728,128]{1,0:T(8,128)(2,1)S(1)} %slice.138), channel_id=1, source_target_pairs={{0,1},{1,0},{2,3},{3,2},{4,5},{5,4},{6,7},{7,6},{8,9},{9,8},{10,11... | collective-permute-start | bytes 1327112 | tf_op jit(solution)/shard_map/ppermute | solution.py:26
  71.0 1.8 %collective-permute-start.6 = (bf16[1728,128]{1,0:T(8,128)(2,1)S(1)}, bf16[1728,128]{1,0:T(8,128)(2,1)S(1)}, u32[]{:S(2)}, u32[]{:S(2)}) collective-permute-start(bf16[1728,128]{1,0:T(8,128)(2,1)S(1)} %collective-permute-done.5), channel_id=1, source_target_pairs={{0,1},{1,0},{2,3},{3,2},{4,5},{5,4},{6,7},{7,6},{8,9},{9,8},{10,11... | collective-permute-start | bytes 1327112 | tf_op jit(solution)/shard_map/ppermute | solution.py:26
  (9 other events, 10.4 us)

commit v10 on v5

--- a/solution.py
+++ b/solution.py
@@ -102,9 +102,13 @@
     def rows_for(member):
         return lax.dynamic_slice_in_dim(rotation, member * state_count, state_count, 0)
 
-    across = from_partner(filtered, "st", 1)
+    halves = 2 if node_count % 32 == 0 else 1
+    half = node_count // halves
+    parts = [filtered[part * half : (part + 1) * half] for part in range(halves)]
+    across = [from_partner(part, "st", 1) for part in parts]
     beside = from_partner(filtered, "st", 0)
-    diagonal = from_partner(across, "st", 0)
+    diagonal = jnp.concatenate([from_partner(piece, "st", 0) for piece in across], 0)
+    across = jnp.concatenate(across, 0)
     rotated = jnp.dot(filtered, rows_for(position), preferred_element_type=jnp.float32)
     rotated = rotated + jnp.dot(beside, rows_for(position ^ 1), preferred_element_type=jnp.float32)
     rotated = rotated + jnp.dot(across, rows_for(position ^ 2), preferred_element_type=jnp.float32)

time: 65.2 us -> 68.7 us (1.054)
  waiting for transfers between devices: 11.6 us -> 15.6 us
    ppermute x3 -> x5, waiting for transfers between devices: 7.72 us -> 11.2 us  [from_partner(): return lax.ppermute(block, axis, route)]
    ppermute x3 -> x5, starting transfers between devices: 1.64 us -> 2.17 us  [from_partner(): return lax.ppermute(block, axis, route)]
  transfers between devices with their start and end apart: 11 -> 13, of which waited for: 6 -> 7; matrix products, arithmetic and copies ran while one was open for 27% -> 25% of each run, Pallas kernels for 0% -> 0%
where the time goes in v10:
time: 68.7 us; the launch traced here: 68.4 us
  matrix products  28.6 us (42%)
  waiting for transfers between devices  15.6 us (23%)
  starting transfers between devices  12.9 us (19%)
  other arithmetic  6.88 us (10%)
  local copies, waits for them, and re-layouts  3.84 us (6%)
    ppermute x5, waiting for transfers between devices, from_partner(): return lax.ppermute(block, axis, route)  11.2 us
    ppermute x8, starting transfers between devices, ring(): return lax.ppermute(block, axis, route)  10.8 us
    dot_general x3, matrix products, operate(): jnp.dot(scatter_sel, both, preferred_element_type=jnp.float32)  9.05 us
    dot_general x3, matrix products, operate(): lax.dot_general(scatter_sel, weighted, (((0,), (0,)), ((), ())), preferre...  7.04 us
    dot_general x3, matrix products, operate(): jnp.einsum('ij,cjb->cib', padded_matrix, values, preferred_element_type=j...  4.46 us
    ppermute x8, waiting for transfers between devices, ring(): return lax.ppermute(block, axis, route)  4.39 us
    sub x3, other arithmetic, chebyshev_step(): return (current, gain * scaled - keep * previous)  3.86 us
    ppermute x5, starting transfers between devices, from_partner(): return lax.ppermute(block, axis, route)  2.17 us
  transfers between devices with their start and end apart: 13, of which 7 were waited for; matrix products, arithmetic and copies ran while one was open for 25% of the time, Pallas kernels for 0%

profile of v10, /device:TPU:0, one launch (start us, length us, event | category | flops | bytes accessed | tf_op | source)
XLA Modules:
  0.0 68.4 jit_solution(17004359100217962061)
XLA Ops:
  0.1 1.4 %fusion.46 = f32[144,128]{1,0:T(8,128)S(1)} fusion(bf16[1728,128]{1,0:T(8,128)(2,1)} %param.9, s32[1728]{0:T(1024)S(1)} %add_reduce_fusion, s32[144]{0:T(256)} %param.14), kind=kOutput, calls=%fused_computation.53 | convolution fusion | flops 63949824 | bytes 523584 | tf_op jit(solution)/shard_map/dot_general | solution.py:57
  1.5 4.0 %collective-permute-start.2 = (f32[144,128]{1,0:T(8,128)S(1)}, f32[144,128]{1,0:T(8,128)S(1)}, u32[]{:S(2)}, u32[]{:S(2)}) collective-permute-start(f32[144,128]{1,0:T(8,128)S(1)} %fusion.46), channel_id=1, source_target_pairs={{0,24},{8,0},{16,8},{24,16},{1,25},{9,1},{17,9},{25,17},{2,26},{10... | collective-permute-start | bytes 221192 | tf_op jit(solution)/shard_map/ppermute | solution.py:16
  6.9 1.4 %fusion.44 = f32[2,144]{1,0:T(2,128)S(1)} fusion(s32[144]{0:T(256)} %param.14, s32[1728]{0:T(1024)S(1)} %add_reduce_fusion, f32[1,1728]{1,0:T(1,128)S(1)} %stack.10, f32[1,1728]{1,0:T(1,128)S(1)} %stack.9), kind=kOutput, calls=%fused_computation.51 | convolution fusion | flops 6224256 | bytes 22464 | tf_op jit(solution)/shard_map/dot_general | solution.py:58
  12.1 40.8 %while.17 = (s32[]{:T(128)}, f32[1872,128]{1,0:T(8,128)S(1)}, f32[1872,128]{1,0:T(8,128)S(1)}, f32[1872]{0:T(1024)S(1)}, bf16[352,352]{1,0:T(8,128)(2,1)}, /*ind...) while((s32[]{:T(128)}, f32[1872,128]{1,0:T(8,128)S(1)}, ...), condition=%wide.region_1.2_spmd.clone.clone, body=%wide.region_0.1_spmd.clone.clone.sunk | while | flops 4879314944 | bytes 31196832 | solution.py:98
  12.1 2.4 %fusion.97 = bf16[2816,128]{0,1:T(8,128)(2,1)S(1)} fusion(s32[2816]{0:T(1024)S(1)} %get-tuple-element.360, f32[1872,128]{1,0:T(8,128)S(1)} %get-tuple-element.340, f32[1872]{0:T(1024)S(1)} %get-tuple-element.357), kind=kOutput, calls=%fused_computation.10.clone.1 | convolution fusion | flops 1360900096 | bytes 1698112 | tf_op jit(solution)/shard_map/while/body/eval_jaxpr/dot_general | solution.py:72
  14.8 1.5 %fusion.98 = f32[8,128,352]{1,2,0:T(8,128)S(1)} fusion(bf16[8,352,128]{2,1,0:T(8,128)(2,1)S(1)} %bitcast.39, bf16[352,352]{1,0:T(8,128)(2,1)} %get-tuple-element.358), kind=kOutput, calls=%fused_computation.35.clone.1 | convolution fusion | flops 253755392 | bytes 2410496 | tf_op jit(solution)/shard_map/while/body/eval_jaxpr/ij,cjb->cib/dot_general | solution.py:76
  17.2 1.5 %collective-permute-start = (f32[144,128]{1,0:T(8,128)S(1)}, f32[144,128]{1,0:T(8,128)S(1)}, u32[]{:S(2)}, u32[]{:S(2)}) collective-permute-start(f32[144,128]{1,0:T(8,128)S(1)} %get-tuple-element.318), channel_id=1, source_target_pairs={{0,24},{8,0},{16,8},{24,16},{1,25},{9,1},{17,9},{25,17},{2,26},{10... | collective-permute-start | bytes 221192 | tf_op jit(solution)/shard_map/while/body/eval_jaxpr/ppermute | solution.py:16
  19.3 3.0 %fusion.101 = f32[1872,256]{1,0:T(8,128)S(1)} fusion(s32[2816]{0:T(1024)S(1)} %get-tuple-element.360, bf16[2816,128]{1,0:T(8,128)(2,1)S(1)} %get-tuple-element.316, bf16[2816,128]{1,0:T(8,128)(2,1)S(1)} %get-tuple-element.317), kind=kOutput, calls=%fused_computation.13.clone.1 | convolution fusion | flops 2712461312 | bytes 3369984 | tf_op jit(solution)/shard_map/while/body/eval_jaxpr/dot_general | solution.py:83
  22.5 1.5 %collective-permute-done.1 = f32[144,128]{1,0:T(8,128)S(1)} collective-permute-done((f32[144,128]{1,0:T(8,128)S(1)}, f32[144,128]{1,0:T(8,128)S(1)}, u32[]{:S(2)}, u32[]{:S(2)}) %collective-permute-start.1) | collective-permute-done | bytes 73760 | tf_op jit(solution)/shard_map/while/body/eval_jaxpr/ppermute | solution.py:16
  24.7 1.3 %fusion.103 = f32[1872,128]{1,0:T(8,128)S(1)} fusion(f32[144,128]{1,0:T(8,128)S(1)} %slice_add_fusion.9, f32[1728,128]{1,0:T(8,128)S(1)} %fusion.102, f32[1872,128]{1,0:T(8,128)S(1)} %get-tuple-element.339, f32[1872,128]{1,0:T(8,128)S(1)} %get-tuple-element.340, f32[]{:T(128)S(6)} %select_n.45, f32[]{:T(128)S(6)} %mul.171, ...), kind=kLoop, calls=%fused_computation.28.clone.1 | loop fusion | flops 2156544 | bytes 3848840 | tf_op jit(solution)/shard_map/while/body/eval_jaxpr/sub | solution.py:96
  26.1 2.3 %fusion.97 = bf16[2816,128]{0,1:T(8,128)(2,1)S(1)} fusion(s32[2816]{0:T(1024)S(1)} %get-tuple-element.360, f32[1872,128]{1,0:T(8,128)S(1)} %get-tuple-element.340, f32[1872]{0:T(1024)S(1)} %get-tuple-element.357), kind=kOutput, calls=%fused_computation.10.clone.1 | convolution fusion | flops 1360900096 | bytes 1698112 | tf_op jit(solution)/shard_map/while/body/eval_jaxpr/dot_general | solution.py:72
  28.8 1.5 %fusion.98 = f32[8,128,352]{1,2,0:T(8,128)S(1)} fusion(bf16[8,352,128]{2,1,0:T(8,128)(2,1)S(1)} %bitcast.39, bf16[352,352]{1,0:T(8,128)(2,1)} %get-tuple-element.358), kind=kOutput, calls=%fused_computation.35.clone.1 | convolution fusion | flops 253755392 | bytes 2410496 | tf_op jit(solution)/shard_map/while/body/eval_jaxpr/ij,cjb->cib/dot_general | solution.py:76
  32.1 1.2 %collective-permute-start.1 = (f32[144,128]{1,0:T(8,128)S(1)}, f32[144,128]{1,0:T(8,128)S(1)}, u32[]{:S(2)}, u32[]{:S(2)}) collective-permute-start(f32[144,128]{1,0:T(8,128)S(1)} %get-tuple-element.319), channel_id=1, source_target_pairs={{0,8},{8,16},{16,24},{24,0},{1,9},{9,17},{17,25},{25,1},{2,10},{10... | collective-permute-start | bytes 221192 | tf_op jit(solution)/shard_map/while/body/eval_jaxpr/ppermute | solution.py:16
  33.3 3.0 %fusion.101 = f32[1872,256]{1,0:T(8,128)S(1)} fusion(s32[2816]{0:T(1024)S(1)} %get-tuple-element.360, bf16[2816,128]{1,0:T(8,128)(2,1)S(1)} %get-tuple-element.316, bf16[2816,128]{1,0:T(8,128)(2,1)S(1)} %get-tuple-element.317), kind=kOutput, calls=%fused_computation.13.clone.1 | convolution fusion | flops 2712461312 | bytes 3369984 | tf_op jit(solution)/shard_map/while/body/eval_jaxpr/dot_general | solution.py:83
  38.0 1.3 %fusion.103 = f32[1872,128]{1,0:T(8,128)S(1)} fusion(f32[144,128]{1,0:T(8,128)S(1)} %slice_add_fusion.9, f32[1728,128]{1,0:T(8,128)S(1)} %fusion.102, f32[1872,128]{1,0:T(8,128)S(1)} %get-tuple-element.339, f32[1872,128]{1,0:T(8,128)S(1)} %get-tuple-element.340, f32[]{:T(128)S(6)} %select_n.45, f32[]{:T(128)S(6)} %mul.171, ...), kind=kLoop, calls=%fused_computation.28.clone.1 | loop fusion | flops 2156544 | bytes 3848840 | tf_op jit(solution)/shard_map/while/body/eval_jaxpr/sub | solution.py:96
  39.5 2.3 %fusion.97 = bf16[2816,128]{0,1:T(8,128)(2,1)S(1)} fusion(s32[2816]{0:T(1024)S(1)} %get-tuple-element.360, f32[1872,128]{1,0:T(8,128)S(1)} %get-tuple-element.340, f32[1872]{0:T(1024)S(1)} %get-tuple-element.357), kind=kOutput, calls=%fused_computation.10.clone.1 | convolution fusion | flops 1360900096 | bytes 1698112 | tf_op jit(solution)/shard_map/while/body/eval_jaxpr/dot_general | solution.py:72
  42.2 1.5 %fusion.98 = f32[8,128,352]{1,2,0:T(8,128)S(1)} fusion(bf16[8,352,128]{2,1,0:T(8,128)(2,1)S(1)} %bitcast.39, bf16[352,352]{1,0:T(8,128)(2,1)} %get-tuple-element.358), kind=kOutput, calls=%fused_computation.35.clone.1 | convolution fusion | flops 253755392 | bytes 2410496 | tf_op jit(solution)/shard_map/while/body/eval_jaxpr/ij,cjb->cib/dot_general | solution.py:76
  45.5 1.2 %collective-permute-start.1 = (f32[144,128]{1,0:T(8,128)S(1)}, f32[144,128]{1,0:T(8,128)S(1)}, u32[]{:S(2)}, u32[]{:S(2)}) collective-permute-start(f32[144,128]{1,0:T(8,128)S(1)} %get-tuple-element.319), channel_id=1, source_target_pairs={{0,8},{8,16},{16,24},{24,0},{1,9},{9,17},{17,25},{25,1},{2,10},{10... | collective-permute-start | bytes 221192 | tf_op jit(solution)/shard_map/while/body/eval_jaxpr/ppermute | solution.py:16
  46.7 3.0 %fusion.101 = f32[1872,256]{1,0:T(8,128)S(1)} fusion(s32[2816]{0:T(1024)S(1)} %get-tuple-element.360, bf16[2816,128]{1,0:T(8,128)(2,1)S(1)} %get-tuple-element.316, bf16[2816,128]{1,0:T(8,128)(2,1)S(1)} %get-tuple-element.317), kind=kOutput, calls=%fused_computation.13.clone.1 | convolution fusion | flops 2712461312 | bytes 3369984 | tf_op jit(solution)/shard_map/while/body/eval_jaxpr/dot_general | solution.py:83
  51.4 1.3 %fusion.103 = f32[1872,128]{1,0:T(8,128)S(1)} fusion(f32[144,128]{1,0:T(8,128)S(1)} %slice_add_fusion.9, f32[1728,128]{1,0:T(8,128)S(1)} %fusion.102, f32[1872,128]{1,0:T(8,128)S(1)} %get-tuple-element.339, f32[1872,128]{1,0:T(8,128)S(1)} %get-tuple-element.340, f32[]{:T(128)S(6)} %select_n.45, f32[]{:T(128)S(6)} %mul.171, ...), kind=kLoop, calls=%fused_computation.28.clone.1 | loop fusion | flops 2156544 | bytes 3848840 | tf_op jit(solution)/shard_map/while/body/eval_jaxpr/sub | solution.py:96
  53.1 1.6 %collective-permute-start.6 = (bf16[864,128]{1,0:T(8,128)(2,1)S(1)}, bf16[864,128]{1,0:T(8,128)(2,1)S(1)}, u32[]{:S(2)}, u32[]{:S(2)}) collective-permute-start(bf16[864,128]{1,0:T(8,128)(2,1)S(1)} %get-tuple-element.244), channel_id=1, source_target_pairs={{0,2},{2,0},{1,3},{3,1},{4,6},{6,4},{5,7},{7,5},{8,10},{10,8},{9,1... | collective-permute-start | bytes 663560 | tf_op jit(solution)/shard_map/ppermute | solution.py:26
  55.4 5.9 %collective-permute-done.6 = bf16[864,128]{1,0:T(8,128)(2,1)S(1)} collective-permute-done((bf16[864,128]{1,0:T(8,128)(2,1)S(1)}, bf16[864,128]{1,0:T(8,128)(2,1)S(1)}, u32[]{:S(2)}, u32[]{:S(2)}) %collective-permute-start.6) | collective-permute-done | bytes 221216 | tf_op jit(solution)/shard_map/ppermute | solution.py:26
  61.4 4.3 %collective-permute-done.5 = bf16[864,128]{1,0:T(8,128)(2,1)S(1)} collective-permute-done((bf16[864,128]{1,0:T(8,128)(2,1)S(1)}, bf16[864,128]{1,0:T(8,128)(2,1)S(1)}, u32[]{:S(2)}, u32[]{:S(2)}) %collective-permute-start.5) | collective-permute-done | bytes 221216 | tf_op jit(solution)/shard_map/ppermute | solution.py:26
  67.2 1.2 %convolution_add_fusion = f32[1728,128]{1,0:T(8,128)} fusion(f32[1728,128]{1,0:T(8,128)S(1)} %convolution_add_fusion.1, bf16[864,128]{1,0:T(8,128)(2,1)S(1)} %collective-permute-done.8, bf16[864,128]{1,0:T(8,128)(2,1)S(1)} %collective-permute-done.7, bf16[512,128]{1,0:T(8,128)(2,1)S(1)} %copy-done, s32[]{:T(128)S(6)} %select_n.38), kind=kOutput, calls=%fused_computation.48 | convolution fusion | flops 57729024 | bytes 2244612 | tf_op jit(solution)/shard_map/dot_general | solution.py:115
  (85 shorter events, 18.1 us)
Async XLA Ops:
  0.0 55.2 %copy-start = (bf16[512,128]{1,0:T(8,128)(2,1)S(1)}, bf16[512,128]{1,0:T(8,128)(2,1)}, u32[]{:S(2)}) copy-start(bf16[512,128]{1,0:T(8,128)(2,1)} %param.15) | copy-start | bytes 393220
  0.0 9.9 %copy-start.2 = (s32[144]{0:T(256)S(1)}, s32[144]{0:T(256)}, u32[]{:S(2)}) copy-start(s32[144]{0:T(256)} %param.14) | copy-start | bytes 1732
  0.0 11.9 %copy-start.3 = (f32[1728]{0:T(1024)S(1)}, f32[1728]{0:T(1024)}, u32[]{:S(2)}) copy-start(f32[1728]{0:T(1024)} %param.11) | copy-start | bytes 20740
  0.0 11.9 %copy-start.4 = (f32[1728]{0:T(1024)S(1)}, f32[1728]{0:T(1024)}, u32[]{:S(2)}) copy-start(f32[1728]{0:T(1024)} %param.10) | copy-start | bytes 20740
  0.0 10.0 %copy-start.5 = (s32[8,343]{1,0:T(8,128)S(1)}, s32[8,343]{1,0:T(8,128)}, u32[]{:S(2)}) copy-start(s32[8,343]{1,0:T(8,128)} %param.13) | copy-start | bytes 32932
  0.0 10.1 %copy-start.1 = (bf16[343,343]{1,0:T(8,128)(2,1)S(1)}, bf16[343,343]{1,0:T(8,128)(2,1)}, u32[]{:S(2)}) copy-start(bf16[343,343]{1,0:T(8,128)(2,1)} %param.12) | copy-start | bytes 705898
  1.5 10.4 %collective-permute-start.2 = (f32[144,128]{1,0:T(8,128)S(1)}, f32[144,128]{1,0:T(8,128)S(1)}, u32[]{:S(2)}, u32[]{:S(2)}) collective-permute-start(f32[144,128]{1,0:T(8,128)S(1)} %fusion.46), channel_id=1, source_target_pairs={{0,24},{8,0},{16,8},{24,16},{1,25},{9,1},{17,9},{25,17},{2,26},{10... | collective-permute-start | bytes 221192 | tf_op jit(solution)/shard_map/ppermute | solution.py:16
  8.3 3.6 %collective-permute-start.3 = (f32[2,144]{1,0:T(2,128)S(1)}, f32[2,144]{1,0:T(2,128)S(1)}, u32[]{:S(2)}, u32[]{:S(2)}) collective-permute-start(f32[2,144]{1,0:T(2,128)S(1)} %fusion.44), channel_id=1, source_target_pairs={{0,24},{8,0},{16,8},{24,16},{1,25},{9,1},{17,9},{25,17},{2,26},{10... | collective-permute-start | bytes 3464 | tf_op jit(solution)/shard_map/ppermute | solution.py:16
  17.2 7.4 %collective-permute-start = (f32[144,128]{1,0:T(8,128)S(1)}, f32[144,128]{1,0:T(8,128)S(1)}, u32[]{:S(2)}, u32[]{:S(2)}) collective-permute-start(f32[144,128]{1,0:T(8,128)S(1)} %get-tuple-element.318), channel_id=1, source_target_pairs={{0,24},{8,0},{16,8},{24,16},{1,25},{9,1},{17,9},{25,17},{2,26},{10... | collective-permute-start | bytes 221192 | tf_op jit(solution)/shard_map/while/body/eval_jaxpr/ppermute | solution.py:16
  18.7 5.3 %collective-permute-start.1 = (f32[144,128]{1,0:T(8,128)S(1)}, f32[144,128]{1,0:T(8,128)S(1)}, u32[]{:S(2)}, u32[]{:S(2)}) collective-permute-start(f32[144,128]{1,0:T(8,128)S(1)} %get-tuple-element.319), channel_id=1, source_target_pairs={{0,8},{8,16},{16,24},{24,0},{1,9},{9,17},{17,25},{25,1},{2,10},{10... | collective-permute-start | bytes 221192 | tf_op jit(solution)/shard_map/while/body/eval_jaxpr/ppermute | solution.py:16
  31.2 6.8 %collective-permute-start = (f32[144,128]{1,0:T(8,128)S(1)}, f32[144,128]{1,0:T(8,128)S(1)}, u32[]{:S(2)}, u32[]{:S(2)}) collective-permute-start(f32[144,128]{1,0:T(8,128)S(1)} %get-tuple-element.318), channel_id=1, source_target_pairs={{0,24},{8,0},{16,8},{24,16},{1,25},{9,1},{17,9},{25,17},{2,26},{10... | collective-permute-start | bytes 221192 | tf_op jit(solution)/shard_map/while/body/eval_jaxpr/ppermute | solution.py:16
  32.1 5.3 %collective-permute-start.1 = (f32[144,128]{1,0:T(8,128)S(1)}, f32[144,128]{1,0:T(8,128)S(1)}, u32[]{:S(2)}, u32[]{:S(2)}) collective-permute-start(f32[144,128]{1,0:T(8,128)S(1)} %get-tuple-element.319), channel_id=1, source_target_pairs={{0,8},{8,16},{16,24},{24,0},{1,9},{9,17},{17,25},{25,1},{2,10},{10... | collective-permute-start | bytes 221192 | tf_op jit(solution)/shard_map/while/body/eval_jaxpr/ppermute | solution.py:16
  44.6 6.8 %collective-permute-start = (f32[144,128]{1,0:T(8,128)S(1)}, f32[144,128]{1,0:T(8,128)S(1)}, u32[]{:S(2)}, u32[]{:S(2)}) collective-permute-start(f32[144,128]{1,0:T(8,128)S(1)} %get-tuple-element.318), channel_id=1, source_target_pairs={{0,24},{8,0},{16,8},{24,16},{1,25},{9,1},{17,9},{25,17},{2,26},{10... | collective-permute-start | bytes 221192 | tf_op jit(solution)/shard_map/while/body/eval_jaxpr/ppermute | solution.py:16
  45.5 5.3 %collective-permute-start.1 = (f32[144,128]{1,0:T(8,128)S(1)}, f32[144,128]{1,0:T(8,128)S(1)}, u32[]{:S(2)}, u32[]{:S(2)}) collective-permute-start(f32[144,128]{1,0:T(8,128)S(1)} %get-tuple-element.319), channel_id=1, source_target_pairs={{0,8},{8,16},{16,24},{24,0},{1,9},{9,17},{17,25},{25,1},{2,10},{10... | collective-permute-start | bytes 221192 | tf_op jit(solution)/shard_map/while/body/eval_jaxpr/ppermute | solution.py:16
  53.0 12.8 %collective-permute-start.4 = (bf16[1728,128]{1,0:T(8,128)(2,1)S(1)}, bf16[1728,128]{1,0:T(8,128)(2,1)S(1)}, u32[]{:S(2)}, u32[]{:S(2)}) collective-permute-start(bf16[1728,128]{1,0:T(8,128)(2,1)S(1)} %slice.136), channel_id=1, source_target_pairs={{0,1},{1,0},{2,3},{3,2},{4,5},{5,4},{6,7},{7,6},{8,9},{9,8},{10,11... | collective-permute-start | bytes 1327112 | tf_op jit(solution)/shard_map/ppermute | solution.py:26
  53.1 8.3 %collective-permute-start.6 = (bf16[864,128]{1,0:T(8,128)(2,1)S(1)}, bf16[864,128]{1,0:T(8,128)(2,1)S(1)}, u32[]{:S(2)}, u32[]{:S(2)}) collective-permute-start(bf16[864,128]{1,0:T(8,128)(2,1)S(1)} %get-tuple-element.244), channel_id=1, source_target_pairs={{0,2},{2,0},{1,3},{3,1},{4,6},{6,4},{5,7},{7,5},{8,10},{10,8},{9,1... | collective-permute-start | bytes 663560 | tf_op jit(solution)/shard_map/ppermute | solution.py:26
  54.7 11.0 %collective-permute-start.5 = (bf16[864,128]{1,0:T(8,128)(2,1)S(1)}, bf16[864,128]{1,0:T(8,128)(2,1)S(1)}, u32[]{:S(2)}, u32[]{:S(2)}) collective-permute-start(bf16[864,128]{1,0:T(8,128)(2,1)S(1)} %get-tuple-element.243), channel_id=1, source_target_pairs={{0,2},{2,0},{1,3},{3,1},{4,6},{6,4},{5,7},{7,5},{8,10},{10,8},{9,1... | collective-permute-start | bytes 663560 | tf_op jit(solution)/shard_map/ppermute | solution.py:26
  61.4 4.9 %collective-permute-start.8 = (bf16[864,128]{1,0:T(8,128)(2,1)S(1)}, bf16[864,128]{1,0:T(8,128)(2,1)S(1)}, u32[]{:S(2)}, u32[]{:S(2)}) collective-permute-start(bf16[864,128]{1,0:T(8,128)(2,1)S(1)} %collective-permute-done.6), channel_id=1, source_target_pairs={{0,1},{1,0},{2,3},{3,2},{4,5},{5,4},{6,7},{7,6},{8,9},{9,8},{10,11... | collective-permute-start | bytes 663560 | tf_op jit(solution)/shard_map/ppermute | solution.py:26
  65.7 1.5 %collective-permute-start.7 = (bf16[864,128]{1,0:T(8,128)(2,1)S(1)}, bf16[864,128]{1,0:T(8,128)(2,1)S(1)}, u32[]{:S(2)}, u32[]{:S(2)}) collective-permute-start(bf16[864,128]{1,0:T(8,128)(2,1)S(1)} %collective-permute-done.5), channel_id=1, source_target_pairs={{0,1},{1,0},{2,3},{3,2},{4,5},{5,4},{6,7},{7,6},{8,9},{9,8},{10,11... | collective-permute-start | bytes 663560 | tf_op jit(solution)/shard_map/ppermute | solution.py:26

commit v11 on v3

--- a/solution.py
+++ b/solution.py
@@ -55,8 +55,14 @@
     face_take = (face_rows[:, None] == wide_ids[:node_count, 0][None, :]).astype(jnp.bfloat16)
 
     face_states = jnp.dot(face_take, states, preferred_element_type=jnp.float32)
-    mass_potential = jnp.stack([inv_mass, potential], 1)[face_rows]
-    ghost = ring(jnp.concatenate([face_states, mass_potential], 1), "dom", -1)
+    face_mass_potential = lax.dot_general(
+        face_put.astype(jnp.float32),
+        jnp.stack([inv_mass, potential], 0),
+        (((0,), (1,)), ((), ())),
+        precision=lax.Precision.HIGHEST,
+        preferred_element_type=jnp.float32,
+    )
+    ghost = ring(jnp.concatenate([face_states, face_mass_potential], 1), "dom", -1)
     field_start = jnp.concatenate([states.astype(jnp.float32), ghost[:, :state_count]], 0)
     wide_mass = jnp.concatenate([inv_mass, ghost[:, state_count]], 0)
     wide_potential = jnp.concatenate([potential, ghost[:, state_count + 1]], 0)

time: 67.3 us -> 67.4 us (level)
  matrix products: 27.2 us -> 29.2 us
  local copies, waits for them, and re-layouts: 5.43 us -> 4.45 us
  other arithmetic: 6.6 us -> 5.76 us
    dot_general x0 -> x1, matrix products: none -> 2.05 us  [body(): lax.dot_general(face_put.astype(jnp.float32), jnp.stack([inv_mass, potent...]
    select_n x1 -> x0, other arithmetic: 0.75 us -> none  [body(): mass_potential = jnp.stack([inv_mass, potential], 1)[face_rows]]
    another operation x3 -> x2, local copies, waits for them, and re-layouts: 1.78 us -> 1.47 us  [body(): jnp.stack([inv_mass, potential], 0)]
where the time goes in v11:
time: 67.4 us; the launch traced here: 67 us
  matrix products  29.2 us (43%)
  waiting for transfers between devices  13.9 us (21%)
  starting transfers between devices  13.2 us (20%)
  other arithmetic  5.76 us (9%)
  local copies, waits for them, and re-layouts  4.45 us (7%)
    ppermute x7, starting transfers between devices, ring(): return lax.ppermute(block, axis, route)  11.5 us
    dot_general x3, matrix products, operate(): jnp.dot(scatter_sel, both, preferred_element_type=jnp.float32)  8.99 us
    ppermute x3, waiting for transfers between devices, from_partner(): return lax.ppermute(block, axis, route)  7.86 us
    dot_general x3, matrix products, operate(): lax.dot_general(scatter_sel, weighted, (((0,), (0,)), ((), ())), preferre...  7.05 us
    ppermute x7, waiting for transfers between devices, ring(): return lax.ppermute(block, axis, route)  6.07 us
    dot_general x3, matrix products, operate(): jnp.einsum('ij,cjb->cib', padded_matrix, values, preferred_element_type=j...  4.46 us
    sub x3, other arithmetic, chebyshev_step(): return (current, gain * scaled - keep * previous)  3.86 us
    dot_general x1, matrix products, body(): lax.dot_general(face_put.astype(jnp.float32), jnp.stack([inv_mass, potent...  2.05 us
  transfers between devices with their start and end apart: 10, of which 6 were waited for; matrix products, arithmetic and copies ran while one was open for 19% of the time, Pallas kernels for 0%

profile of v11, /device:TPU:0, one launch (start us, length us, event | category | flops | bytes accessed | tf_op | source)
XLA Modules:
  0.0 67.0 jit_solution(9909795036154220049)
XLA Ops:
  1.5 1.4 %fusion.44 = f32[144,128]{1,0:T(8,128)S(1)} fusion(bf16[1728,128]{1,0:T(8,128)(2,1)} %param.9, s32[1728]{0:T(1024)S(1)} %add_reduce_fusion, s32[144]{0:T(256)} %param.14), kind=kOutput, calls=%fused_computation.52 | convolution fusion | flops 63949824 | bytes 523584 | tf_op jit(solution)/shard_map/dot_general | solution.py:57
  2.9 2.0 %fusion.46 = f32[144,2]{1,0:T(8,128)S(1)} fusion(s32[144]{0:T(256)} %param.14, s32[1728]{0:T(1024)S(1)} %add_reduce_fusion, f32[1,1728]{1,0:T(1,128)S(1)} %stack.10, f32[1,1728]{1,0:T(1,128)S(1)} %stack.9), kind=kOutput, calls=%fused_computation.55 | convolution fusion | flops 6473088 | bytes 22464 | tf_op jit(solution)/shard_map/dot_general | solution.py:58
  5.0 4.0 %collective-permute-start.2 = (f32[144,130]{1,0:T(8,128)S(1)}, f32[144,130]{1,0:T(8,128)S(1)}, u32[]{:S(2)}, u32[]{:S(2)}) collective-permute-start(f32[144,130]{1,0:T(8,128)S(1)} %pad_maximum_fusion.4), channel_id=1, source_target_pairs={{0,24},{8,0},{16,8},{24,16},{1,25},{9,1},{17,9},{25,17},{2,26},{10... | collective-permute-start | bytes 224648 | tf_op jit(solution)/shard_map/ppermute | solution.py:16
  10.0 2.1 %collective-permute-done.2 = f32[144,130]{1,0:T(8,128)S(1)} collective-permute-done((f32[144,130]{1,0:T(8,128)S(1)}, f32[144,130]{1,0:T(8,128)S(1)}, u32[]{:S(2)}, u32[]{:S(2)}) %collective-permute-start.2) | collective-permute-done | bytes 74912 | tf_op jit(solution)/shard_map/ppermute | solution.py:16
  12.9 42.6 %while.17 = (s32[]{:T(128)}, f32[1872,128]{1,0:T(8,128)S(1)}, f32[1872,128]{1,0:T(8,128)S(1)}, f32[1872]{0:T(1024)S(1)}, bf16[352,352]{1,0:T(8,128)(2,1)}, /*ind...) while((s32[]{:T(128)}, f32[1872,128]{1,0:T(8,128)S(1)}, ...), condition=%wide.region_1.2_spmd.clone.clone, body=%wide.region_0.1_spmd.clone.clone.sunk | while | flops 4879314944 | bytes 31196832 | solution.py:98
  12.9 2.4 %fusion.88 = bf16[2816,128]{0,1:T(8,128)(2,1)S(1)} fusion(s32[2816]{0:T(1024)S(1)} %get-tuple-element.358, f32[1872,128]{1,0:T(8,128)S(1)} %get-tuple-element.338, f32[1872]{0:T(1024)S(1)} %get-tuple-element.355), kind=kOutput, calls=%fused_computation.10.clone.1 | convolution fusion | flops 1360900096 | bytes 1698112 | tf_op jit(solution)/shard_map/while/body/eval_jaxpr/dot_general | solution.py:72
  15.6 1.5 %fusion.89 = f32[8,128,352]{1,2,0:T(8,128)S(1)} fusion(bf16[8,352,128]{2,1,0:T(8,128)(2,1)S(1)} %bitcast.39, bf16[352,352]{1,0:T(8,128)(2,1)} %get-tuple-element.356), kind=kOutput, calls=%fused_computation.35.clone.1 | convolution fusion | flops 253755392 | bytes 2410496 | tf_op jit(solution)/shard_map/while/body/eval_jaxpr/ij,cjb->cib/dot_general | solution.py:76
  18.0 3.4 %collective-permute-start = (f32[144,128]{1,0:T(8,128)S(1)}, f32[144,128]{1,0:T(8,128)S(1)}, u32[]{:S(2)}, u32[]{:S(2)}) collective-permute-start(f32[144,128]{1,0:T(8,128)S(1)} %get-tuple-element.316), channel_id=1, source_target_pairs={{0,24},{8,0},{16,8},{24,16},{1,25},{9,1},{17,9},{25,17},{2,26},{10... | collective-permute-start | bytes 221192 | tf_op jit(solution)/shard_map/while/body/eval_jaxpr/ppermute | solution.py:16
  21.4 3.0 %fusion.92 = f32[1872,256]{1,0:T(8,128)S(1)} fusion(s32[2816]{0:T(1024)S(1)} %get-tuple-element.358, bf16[2816,128]{1,0:T(8,128)(2,1)S(1)} %get-tuple-element.314, bf16[2816,128]{1,0:T(8,128)(2,1)S(1)} %get-tuple-element.315), kind=kOutput, calls=%fused_computation.13.clone.1 | convolution fusion | flops 2712461312 | bytes 3369984 | tf_op jit(solution)/shard_map/while/body/eval_jaxpr/dot_general | solution.py:83
  24.5 2.1 %collective-permute-done.1 = f32[144,128]{1,0:T(8,128)S(1)} collective-permute-done((f32[144,128]{1,0:T(8,128)S(1)}, f32[144,128]{1,0:T(8,128)S(1)}, u32[]{:S(2)}, u32[]{:S(2)}) %collective-permute-start.1) | collective-permute-done | bytes 73760 | tf_op jit(solution)/shard_map/while/body/eval_jaxpr/ppermute | solution.py:16
  27.3 1.3 %fusion.94 = f32[1872,128]{1,0:T(8,128)S(1)} fusion(f32[144,128]{1,0:T(8,128)S(1)} %slice_add_fusion.9, f32[1728,128]{1,0:T(8,128)S(1)} %fusion.93, f32[1872,128]{1,0:T(8,128)S(1)} %get-tuple-element.337, f32[1872,128]{1,0:T(8,128)S(1)} %get-tuple-element.338, f32[]{:T(128)S(6)} %select_n.45, f32[]{:T(128)S(6)} %mul.171, ...), kind=kLoop, calls=%fused_computation.28.clone.1 | loop fusion | flops 2156544 | bytes 3848840 | tf_op jit(solution)/shard_map/while/body/eval_jaxpr/sub | solution.py:96
  28.8 2.4 %fusion.88 = bf16[2816,128]{0,1:T(8,128)(2,1)S(1)} fusion(s32[2816]{0:T(1024)S(1)} %get-tuple-element.358, f32[1872,128]{1,0:T(8,128)S(1)} %get-tuple-element.338, f32[1872]{0:T(1024)S(1)} %get-tuple-element.355), kind=kOutput, calls=%fused_computation.10.clone.1 | convolution fusion | flops 1360900096 | bytes 1698112 | tf_op jit(solution)/shard_map/while/body/eval_jaxpr/dot_general | solution.py:72
  31.5 1.5 %fusion.89 = f32[8,128,352]{1,2,0:T(8,128)S(1)} fusion(bf16[8,352,128]{2,1,0:T(8,128)(2,1)S(1)} %bitcast.39, bf16[352,352]{1,0:T(8,128)(2,1)} %get-tuple-element.356), kind=kOutput, calls=%fused_computation.35.clone.1 | convolution fusion | flops 253755392 | bytes 2410496 | tf_op jit(solution)/shard_map/while/body/eval_jaxpr/ij,cjb->cib/dot_general | solution.py:76
  34.8 1.2 %collective-permute-start.1 = (f32[144,128]{1,0:T(8,128)S(1)}, f32[144,128]{1,0:T(8,128)S(1)}, u32[]{:S(2)}, u32[]{:S(2)}) collective-permute-start(f32[144,128]{1,0:T(8,128)S(1)} %get-tuple-element.317), channel_id=1, source_target_pairs={{0,8},{8,16},{16,24},{24,0},{1,9},{9,17},{17,25},{25,1},{2,10},{10... | collective-permute-start | bytes 221192 | tf_op jit(solution)/shard_map/while/body/eval_jaxpr/ppermute | solution.py:16
  36.0 3.0 %fusion.92 = f32[1872,256]{1,0:T(8,128)S(1)} fusion(s32[2816]{0:T(1024)S(1)} %get-tuple-element.358, bf16[2816,128]{1,0:T(8,128)(2,1)S(1)} %get-tuple-element.314, bf16[2816,128]{1,0:T(8,128)(2,1)S(1)} %get-tuple-element.315), kind=kOutput, calls=%fused_computation.13.clone.1 | convolution fusion | flops 2712461312 | bytes 3369984 | tf_op jit(solution)/shard_map/while/body/eval_jaxpr/dot_general | solution.py:83
  40.7 1.3 %fusion.94 = f32[1872,128]{1,0:T(8,128)S(1)} fusion(f32[144,128]{1,0:T(8,128)S(1)} %slice_add_fusion.9, f32[1728,128]{1,0:T(8,128)S(1)} %fusion.93, f32[1872,128]{1,0:T(8,128)S(1)} %get-tuple-element.337, f32[1872,128]{1,0:T(8,128)S(1)} %get-tuple-element.338, f32[]{:T(128)S(6)} %select_n.45, f32[]{:T(128)S(6)} %mul.171, ...), kind=kLoop, calls=%fused_computation.28.clone.1 | loop fusion | flops 2156544 | bytes 3848840 | tf_op jit(solution)/shard_map/while/body/eval_jaxpr/sub | solution.py:96
  42.1 2.4 %fusion.88 = bf16[2816,128]{0,1:T(8,128)(2,1)S(1)} fusion(s32[2816]{0:T(1024)S(1)} %get-tuple-element.358, f32[1872,128]{1,0:T(8,128)S(1)} %get-tuple-element.338, f32[1872]{0:T(1024)S(1)} %get-tuple-element.355), kind=kOutput, calls=%fused_computation.10.clone.1 | convolution fusion | flops 1360900096 | bytes 1698112 | tf_op jit(solution)/shard_map/while/body/eval_jaxpr/dot_general | solution.py:72
  44.8 1.5 %fusion.89 = f32[8,128,352]{1,2,0:T(8,128)S(1)} fusion(bf16[8,352,128]{2,1,0:T(8,128)(2,1)S(1)} %bitcast.39, bf16[352,352]{1,0:T(8,128)(2,1)} %get-tuple-element.356), kind=kOutput, calls=%fused_computation.35.clone.1 | convolution fusion | flops 253755392 | bytes 2410496 | tf_op jit(solution)/shard_map/while/body/eval_jaxpr/ij,cjb->cib/dot_general | solution.py:76
  48.1 1.2 %collective-permute-start.1 = (f32[144,128]{1,0:T(8,128)S(1)}, f32[144,128]{1,0:T(8,128)S(1)}, u32[]{:S(2)}, u32[]{:S(2)}) collective-permute-start(f32[144,128]{1,0:T(8,128)S(1)} %get-tuple-element.317), channel_id=1, source_target_pairs={{0,8},{8,16},{16,24},{24,0},{1,9},{9,17},{17,25},{25,1},{2,10},{10... | collective-permute-start | bytes 221192 | tf_op jit(solution)/shard_map/while/body/eval_jaxpr/ppermute | solution.py:16
  49.3 3.0 %fusion.92 = f32[1872,256]{1,0:T(8,128)S(1)} fusion(s32[2816]{0:T(1024)S(1)} %get-tuple-element.358, bf16[2816,128]{1,0:T(8,128)(2,1)S(1)} %get-tuple-element.314, bf16[2816,128]{1,0:T(8,128)(2,1)S(1)} %get-tuple-element.315), kind=kOutput, calls=%fused_computation.13.clone.1 | convolution fusion | flops 2712461312 | bytes 3369984 | tf_op jit(solution)/shard_map/while/body/eval_jaxpr/dot_general | solution.py:83
  54.0 1.3 %fusion.94 = f32[1872,128]{1,0:T(8,128)S(1)} fusion(f32[144,128]{1,0:T(8,128)S(1)} %slice_add_fusion.9, f32[1728,128]{1,0:T(8,128)S(1)} %fusion.93, f32[1872,128]{1,0:T(8,128)S(1)} %get-tuple-element.337, f32[1872,128]{1,0:T(8,128)S(1)} %get-tuple-element.338, f32[]{:T(128)S(6)} %select_n.45, f32[]{:T(128)S(6)} %mul.171, ...), kind=kLoop, calls=%fused_computation.28.clone.1 | loop fusion | flops 2156544 | bytes 3848840 | tf_op jit(solution)/shard_map/while/body/eval_jaxpr/sub | solution.py:96
  55.5 1.6 %collective-permute-start.4 = (bf16[1728,128]{1,0:T(8,128)(2,1)S(1)}, bf16[1728,128]{1,0:T(8,128)(2,1)S(1)}, u32[]{:S(2)}, u32[]{:S(2)}) collective-permute-start(bf16[1728,128]{1,0:T(8,128)(2,1)S(1)} %slice.145), channel_id=1, source_target_pairs={{0,2},{2,0},{1,3},{3,1},{4,6},{6,4},{5,7},{7,5},{8,10},{10,8},{9,1... | collective-permute-start | bytes 1327112 | tf_op jit(solution)/shard_map/ppermute | solution.py:26
  57.4 6.6 %collective-permute-done.4 = bf16[1728,128]{1,0:T(8,128)(2,1)S(1)} collective-permute-done((bf16[1728,128]{1,0:T(8,128)(2,1)S(1)}, bf16[1728,128]{1,0:T(8,128)(2,1)S(1)}, u32[]{:S(2)}, u32[]{:S(2)}) %collective-permute-start.4) | collective-permute-done | bytes 442400 | tf_op jit(solution)/shard_map/ppermute | solution.py:26
  64.6 1.2 %collective-permute-done.5 = bf16[1728,128]{1,0:T(8,128)(2,1)S(1)} collective-permute-done((bf16[1728,128]{1,0:T(8,128)(2,1)S(1)}, bf16[1728,128]{1,0:T(8,128)(2,1)S(1)}, u32[]{:S(2)}, u32[]{:S(2)}) %collective-permute-start.5) | collective-permute-done | bytes 442400 | tf_op jit(solution)/shard_map/ppermute | solution.py:26
  (81 shorter events, 15.1 us)
Async XLA Ops:
  0.0 57.2 %copy-start = (bf16[512,128]{1,0:T(8,128)(2,1)S(1)}, bf16[512,128]{1,0:T(8,128)(2,1)}, u32[]{:S(2)}) copy-start(bf16[512,128]{1,0:T(8,128)(2,1)} %param.15) | copy-start | bytes 393220
  0.0 9.0 %copy-start.1 = (bf16[1728,128]{1,0:T(8,128)(2,1)S(1)}, bf16[1728,128]{1,0:T(8,128)(2,1)}, u32[]{:S(2)}) copy-start(bf16[1728,128]{1,0:T(8,128)(2,1)} %param.9) | copy-start | bytes 1327108
  0.0 9.0 %copy-start.6 = (s32[8,343]{1,0:T(8,128)S(1)}, s32[8,343]{1,0:T(8,128)}, u32[]{:S(2)}) copy-start(s32[8,343]{1,0:T(8,128)} %param.13) | copy-start | bytes 32932
  0.0 9.1 %copy-start.2 = (bf16[343,343]{1,0:T(8,128)(2,1)S(1)}, bf16[343,343]{1,0:T(8,128)(2,1)}, u32[]{:S(2)}) copy-start(bf16[343,343]{1,0:T(8,128)(2,1)} %param.12) | copy-start | bytes 705898
  1.5 8.3 %copy-start.3 = (s32[144]{0:T(256)S(1)}, s32[144]{0:T(256)}, u32[]{:S(2)}) copy-start(s32[144]{0:T(256)} %param.14) | copy-start | bytes 1732
  5.0 7.1 %collective-permute-start.2 = (f32[144,130]{1,0:T(8,128)S(1)}, f32[144,130]{1,0:T(8,128)S(1)}, u32[]{:S(2)}, u32[]{:S(2)}) collective-permute-start(f32[144,130]{1,0:T(8,128)S(1)} %pad_maximum_fusion.4), channel_id=1, source_target_pairs={{0,24},{8,0},{16,8},{24,16},{1,25},{9,1},{17,9},{25,17},{2,26},{10... | collective-permute-start | bytes 224648 | tf_op jit(solution)/shard_map/ppermute | solution.py:16
  12.1 0.7 %copy-start.4 = (f32[1728]{0:T(1024)S(1)}, f32[1728]{0:T(1024)}, u32[]{:S(2)}) copy-start(f32[1728]{0:T(1024)} %param.11) | copy-start | bytes 20740
  12.1 0.7 %copy-start.5 = (f32[1728]{0:T(1024)S(1)}, f32[1728]{0:T(1024)}, u32[]{:S(2)}) copy-start(f32[1728]{0:T(1024)} %param.10) | copy-start | bytes 20740
  18.0 9.3 %collective-permute-start = (f32[144,128]{1,0:T(8,128)S(1)}, f32[144,128]{1,0:T(8,128)S(1)}, u32[]{:S(2)}, u32[]{:S(2)}) collective-permute-start(f32[144,128]{1,0:T(8,128)S(1)} %get-tuple-element.316), channel_id=1, source_target_pairs={{0,24},{8,0},{16,8},{24,16},{1,25},{9,1},{17,9},{25,17},{2,26},{10... | collective-permute-start | bytes 221192 | tf_op jit(solution)/shard_map/while/body/eval_jaxpr/ppermute | solution.py:16
  21.4 5.3 %collective-permute-start.1 = (f32[144,128]{1,0:T(8,128)S(1)}, f32[144,128]{1,0:T(8,128)S(1)}, u32[]{:S(2)}, u32[]{:S(2)}) collective-permute-start(f32[144,128]{1,0:T(8,128)S(1)} %get-tuple-element.317), channel_id=1, source_target_pairs={{0,8},{8,16},{16,24},{24,0},{1,9},{9,17},{17,25},{25,1},{2,10},{10... | collective-permute-start | bytes 221192 | tf_op jit(solution)/shard_map/while/body/eval_jaxpr/ppermute | solution.py:16
  33.9 6.7 %collective-permute-start = (f32[144,128]{1,0:T(8,128)S(1)}, f32[144,128]{1,0:T(8,128)S(1)}, u32[]{:S(2)}, u32[]{:S(2)}) collective-permute-start(f32[144,128]{1,0:T(8,128)S(1)} %get-tuple-element.316), channel_id=1, source_target_pairs={{0,24},{8,0},{16,8},{24,16},{1,25},{9,1},{17,9},{25,17},{2,26},{10... | collective-permute-start | bytes 221192 | tf_op jit(solution)/shard_map/while/body/eval_jaxpr/ppermute | solution.py:16
  34.8 5.3 %collective-permute-start.1 = (f32[144,128]{1,0:T(8,128)S(1)}, f32[144,128]{1,0:T(8,128)S(1)}, u32[]{:S(2)}, u32[]{:S(2)}) collective-permute-start(f32[144,128]{1,0:T(8,128)S(1)} %get-tuple-element.317), channel_id=1, source_target_pairs={{0,8},{8,16},{16,24},{24,0},{1,9},{9,17},{17,25},{25,1},{2,10},{10... | collective-permute-start | bytes 221192 | tf_op jit(solution)/shard_map/while/body/eval_jaxpr/ppermute | solution.py:16
  47.2 6.7 %collective-permute-start = (f32[144,128]{1,0:T(8,128)S(1)}, f32[144,128]{1,0:T(8,128)S(1)}, u32[]{:S(2)}, u32[]{:S(2)}) collective-permute-start(f32[144,128]{1,0:T(8,128)S(1)} %get-tuple-element.316), channel_id=1, source_target_pairs={{0,24},{8,0},{16,8},{24,16},{1,25},{9,1},{17,9},{25,17},{2,26},{10... | collective-permute-start | bytes 221192 | tf_op jit(solution)/shard_map/while/body/eval_jaxpr/ppermute | solution.py:16
  48.1 5.3 %collective-permute-start.1 = (f32[144,128]{1,0:T(8,128)S(1)}, f32[144,128]{1,0:T(8,128)S(1)}, u32[]{:S(2)}, u32[]{:S(2)}) collective-permute-start(f32[144,128]{1,0:T(8,128)S(1)} %get-tuple-element.317), channel_id=1, source_target_pairs={{0,8},{8,16},{16,24},{24,0},{1,9},{9,17},{17,25},{25,1},{2,10},{10... | collective-permute-start | bytes 221192 | tf_op jit(solution)/shard_map/while/body/eval_jaxpr/ppermute | solution.py:16
  55.5 8.5 %collective-permute-start.4 = (bf16[1728,128]{1,0:T(8,128)(2,1)S(1)}, bf16[1728,128]{1,0:T(8,128)(2,1)S(1)}, u32[]{:S(2)}, u32[]{:S(2)}) collective-permute-start(bf16[1728,128]{1,0:T(8,128)(2,1)S(1)} %slice.145), channel_id=1, source_target_pairs={{0,2},{2,0},{1,3},{3,1},{4,6},{6,4},{5,7},{7,5},{8,10},{10,8},{9,1... | collective-permute-start | bytes 1327112 | tf_op jit(solution)/shard_map/ppermute | solution.py:26
  57.2 6.9 %collective-permute-start.3 = (bf16[1728,128]{1,0:T(8,128)(2,1)S(1)}, bf16[1728,128]{1,0:T(8,128)(2,1)S(1)}, u32[]{:S(2)}, u32[]{:S(2)}) collective-permute-start(bf16[1728,128]{1,0:T(8,128)(2,1)S(1)} %slice.145), channel_id=1, source_target_pairs={{0,1},{1,0},{2,3},{3,2},{4,5},{5,4},{6,7},{7,6},{8,9},{9,8},{10,11... | collective-permute-start | bytes 1327112 | tf_op jit(solution)/shard_map/ppermute | solution.py:26
  64.0 1.8 %collective-permute-start.5 = (bf16[1728,128]{1,0:T(8,128)(2,1)S(1)}, bf16[1728,128]{1,0:T(8,128)(2,1)S(1)}, u32[]{:S(2)}, u32[]{:S(2)}) collective-permute-start(bf16[1728,128]{1,0:T(8,128)(2,1)S(1)} %collective-permute-done.4), channel_id=1, source_target_pairs={{0,1},{1,0},{2,3},{3,2},{4,5},{5,4},{6,7},{7,6},{8,9},{9,8},{10,11... | collective-permute-start | bytes 1327112 | tf_op jit(solution)/shard_map/ppermute | solution.py:26

commit v12 on v5

--- a/solution.py
+++ b/solution.py
@@ -81,11 +81,19 @@
         from_prev = ring(rim[face_count:], "dom", 1)
         from_next = ring(rim[:face_count], "dom", -1)
         main = summed_halves(jnp.dot(scatter_sel, both, preferred_element_type=jnp.float32))
-        own = main[:node_count] + summed_halves(
+        base = lax.optimization_barrier(
+            wide_mass[:node_count, None] * main[:node_count]
+            + wide_potential[:node_count, None] * field_in[:node_count]
+        )
+        face_add = summed_halves(
             jnp.dot(face_put, high_low(from_prev), preferred_element_type=jnp.float32)
         )
-        summed = jnp.concatenate([own, main[node_count:] + from_next], 0)
-        return wide_mass[:, None] * summed + wide_potential[:, None] * field_in
+        own = base + wide_mass[:node_count, None] * face_add
+        ghost_rows = slice(node_count, None)
+        ghost = wide_mass[ghost_rows, None] * (main[ghost_rows] + from_next) + wide_potential[
+            ghost_rows, None
+        ] * field_in[ghost_rows]
+        return jnp.concatenate([own, ghost], 0)
 
     def chebyshev_step(step, carry):
         previous, current = carry

time: 65.2 us -> 66.3 us (1.017)
  local copies, waits for them, and re-layouts: 4.35 us -> 8.99 us
  matrix products: 28.6 us -> 25.7 us
  other arithmetic: 7.43 us -> 6.65 us
    while x6 -> x24, local copies, waits for them, and re-layouts: 0.38 us -> 5.35 us
    sub x3, other arithmetic: 3.86 us -> 0.75 us  [chebyshev_step(): return (current, gain * scaled - keep * previous)]
    dot_general x3, matrix products: 4.46 us -> 1.62 us  [operate(): jnp.einsum('ij,cjb->cib', padded_matrix, values, preferred_element_type=j...]
    add x6 -> x9, other arithmetic: 0.49 us -> 2.82 us  [the longest x3 1.57 us: operate(): wide_mass[:node_count, None] * main[:node_count]]
    pad x1, local copies, waits for them, and re-layouts: 0.74 us -> 0.03 us  [body(): padded_matrix = jnp.pad(cell_matrix, ((0, pad), (0, pad)))]
  transfers between devices with their start and end apart: 11 -> 11, of which waited for: 6 -> 6; matrix products, arithmetic and copies ran while one was open for 27% -> 28% of each run, Pallas kernels for 0% -> 0%
where the time goes in v12:
time: 66.3 us; the launch traced here: 65.9 us
  matrix products  25.7 us (39%)
  starting transfers between devices  12.4 us (19%)
  waiting for transfers between devices  11.6 us (17%)
  local copies, waits for them, and re-layouts  8.99 us (14%)
  other arithmetic  6.65 us (10%)
    ppermute x8, starting transfers between devices, ring(): return lax.ppermute(block, axis, route)  10.7 us
    dot_general x3, matrix products, operate(): jnp.dot(scatter_sel, both, preferred_element_type=jnp.float32)  8.98 us
    ppermute x3, waiting for transfers between devices, from_partner(): return lax.ppermute(block, axis, route)  7.71 us
    dot_general x3, matrix products, operate(): lax.dot_general(scatter_sel, weighted, (((0,), (0,)), ((), ())), preferre...  7.05 us
    while x24, local copies, waits for them, and re-layouts  5.35 us
    ppermute x8, waiting for transfers between devices, ring(): return lax.ppermute(block, axis, route)  3.91 us
    dot_general x3, matrix products, operate(): jnp.dot(rim_sel, both, preferred_element_type=jnp.float32)  1.88 us
    ppermute x3, starting transfers between devices, from_partner(): return lax.ppermute(block, axis, route)  1.65 us
  transfers between devices with their start and end apart: 11, of which 6 were waited for; matrix products, arithmetic and copies ran while one was open for 28% of the time, Pallas kernels for 0%

profile of v12, /device:TPU:0, one launch (start us, length us, event | category | flops | bytes accessed | tf_op | source)
XLA Modules:
  0.0 65.9 jit_solution(14351653529845556541)
XLA Ops:
  0.1 1.5 %fusion.48 = f32[144,128]{1,0:T(8,128)S(1)} fusion(bf16[1728,128]{1,0:T(8,128)(2,1)} %param.9, s32[1728]{0:T(1024)S(1)} %add_reduce_fusion, s32[144]{0:T(256)} %param.14), kind=kOutput, calls=%fused_computation.56 | convolution fusion | flops 63949824 | bytes 523584 | tf_op jit(solution)/shard_map/dot_general | solution.py:57
  1.5 4.0 %collective-permute-start.2 = (f32[144,128]{1,0:T(8,128)S(1)}, f32[144,128]{1,0:T(8,128)S(1)}, u32[]{:S(2)}, u32[]{:S(2)}) collective-permute-start(f32[144,128]{1,0:T(8,128)S(1)} %fusion.48), channel_id=1, source_target_pairs={{0,24},{8,0},{16,8},{24,16},{1,25},{9,1},{17,9},{25,17},{2,26},{10... | collective-permute-start | bytes 221192 | tf_op jit(solution)/shard_map/ppermute | solution.py:16
  6.9 1.4 %fusion.46 = f32[2,144]{1,0:T(2,128)S(1)} fusion(s32[144]{0:T(256)} %param.14, s32[1728]{0:T(1024)S(1)} %add_reduce_fusion, f32[1,1728]{1,0:T(1,128)S(1)} %stack.10, f32[1,1728]{1,0:T(1,128)S(1)} %stack.9), kind=kOutput, calls=%fused_computation.54 | convolution fusion | flops 6224256 | bytes 22464 | tf_op jit(solution)/shard_map/dot_general | solution.py:58
  9.6 1.1 %convert_element_type.62 = f32[1728,128]{1,0:T(8,128)S(1)} convert(bf16[1728,128]{1,0:T(8,128)(2,1)} %param.9) | non-fusion elementwise | flops 221184 | bytes 1327104 | tf_op jit(solution)/shard_map/convert_element_type | solution.py:66
  10.8 1.1 %collective-permute-done.3 = f32[2,144]{1,0:T(2,128)S(1)} collective-permute-done((f32[2,144]{1,0:T(2,128)S(1)}, f32[2,144]{1,0:T(2,128)S(1)}, u32[]{:S(2)}, u32[]{:S(2)}) %collective-permute-start.3) | collective-permute-done | bytes 1184 | tf_op jit(solution)/shard_map/ppermute | solution.py:16
  13.0 41.5 %while.17 = (s32[]{:T(128)}, f32[1872,128]{1,0:T(8,128)}, f32[1872,128]{1,0:T(8,128)S(1)}, f32[1728]{0:T(1024)S(1)}, f32[1872]{0:T(1024)S(1)}, /*index=5*/bf16[3...) while((s32[]{:T(128)}, f32[1872,128]{1,0:T(8,128)}, ...), condition=%wide.region_1.2_spmd.clone.clone, body=%wide.region_0.1_spmd.clone.clone.sunk | while | flops 4879536128 | bytes 37774860 | solution.py:106
  13.0 2.3 %fusion.94 = bf16[2816,128]{0,1:T(8,128)(2,1)S(1)} fusion(s32[2816]{0:T(1024)S(1)} %get-tuple-element.446, f32[1872,128]{1,0:T(8,128)S(1)} %get-tuple-element.420, f32[1872]{0:T(1024)S(1)} %get-tuple-element.441), kind=kOutput, calls=%fused_computation.10.clone.1 | convolution fusion | flops 1360900096 | bytes 1698112 | tf_op jit(solution)/shard_map/while/body/eval_jaxpr/dot_general | solution.py:72
  17.1 1.5 %collective-permute-start = (f32[144,128]{1,0:T(8,128)S(1)}, f32[144,128]{1,0:T(8,128)S(1)}, u32[]{:S(2)}, u32[]{:S(2)}) collective-permute-start(f32[144,128]{1,0:T(8,128)S(1)} %get-tuple-element.395), channel_id=1, source_target_pairs={{0,24},{8,0},{16,8},{24,16},{1,25},{9,1},{17,9},{25,17},{2,26},{10... | collective-permute-start | bytes 221192 | tf_op jit(solution)/shard_map/while/body/eval_jaxpr/ppermute | solution.py:16
  19.2 3.0 %fusion.98 = f32[1872,256]{1,0:T(8,128)S(1)} fusion(s32[2816]{0:T(1024)S(1)} %get-tuple-element.446, bf16[2816,128]{1,0:T(8,128)(2,1)S(1)} %get-tuple-element.393, bf16[2816,128]{1,0:T(8,128)(2,1)S(1)} %get-tuple-element.394), kind=kOutput, calls=%fused_computation.13.clone.1 | convolution fusion | flops 2712461312 | bytes 3369984 | tf_op jit(solution)/shard_map/while/body/eval_jaxpr/dot_general | solution.py:83
  22.9 1.0 %collective-permute-done.1 = f32[144,128]{1,0:T(8,128)S(1)} collective-permute-done((f32[144,128]{1,0:T(8,128)S(1)}, f32[144,128]{1,0:T(8,128)S(1)}, u32[]{:S(2)}, u32[]{:S(2)}) %collective-permute-start.1) | collective-permute-done | bytes 73760 | tf_op jit(solution)/shard_map/while/body/eval_jaxpr/ppermute | solution.py:16
  25.8 1.0 %copy.19 = f32[1872,128]{1,0:T(8,128)} copy(f32[1872,128]{1,0:T(8,128)S(1)} %get-tuple-element.420) | data formatting | bytes 1916928 | tf_op jit(solution)/shard_map/while
  26.9 2.4 %fusion.94 = bf16[2816,128]{0,1:T(8,128)(2,1)S(1)} fusion(s32[2816]{0:T(1024)S(1)} %get-tuple-element.446, f32[1872,128]{1,0:T(8,128)S(1)} %get-tuple-element.420, f32[1872]{0:T(1024)S(1)} %get-tuple-element.441), kind=kOutput, calls=%fused_computation.10.clone.1 | convolution fusion | flops 1360900096 | bytes 1698112 | tf_op jit(solution)/shard_map/while/body/eval_jaxpr/dot_general | solution.py:72
  31.1 1.4 %collective-permute-start = (f32[144,128]{1,0:T(8,128)S(1)}, f32[144,128]{1,0:T(8,128)S(1)}, u32[]{:S(2)}, u32[]{:S(2)}) collective-permute-start(f32[144,128]{1,0:T(8,128)S(1)} %get-tuple-element.395), channel_id=1, source_target_pairs={{0,24},{8,0},{16,8},{24,16},{1,25},{9,1},{17,9},{25,17},{2,26},{10... | collective-permute-start | bytes 221192 | tf_op jit(solution)/shard_map/while/body/eval_jaxpr/ppermute | solution.py:16
  33.2 3.0 %fusion.98 = f32[1872,256]{1,0:T(8,128)S(1)} fusion(s32[2816]{0:T(1024)S(1)} %get-tuple-element.446, bf16[2816,128]{1,0:T(8,128)(2,1)S(1)} %get-tuple-element.393, bf16[2816,128]{1,0:T(8,128)(2,1)S(1)} %get-tuple-element.394), kind=kOutput, calls=%fused_computation.13.clone.1 | convolution fusion | flops 2712461312 | bytes 3369984 | tf_op jit(solution)/shard_map/while/body/eval_jaxpr/dot_general | solution.py:83
  36.8 0.9 %collective-permute-done.1 = f32[144,128]{1,0:T(8,128)S(1)} collective-permute-done((f32[144,128]{1,0:T(8,128)S(1)}, f32[144,128]{1,0:T(8,128)S(1)}, u32[]{:S(2)}, u32[]{:S(2)}) %collective-permute-start.1) | collective-permute-done | bytes 73760 | tf_op jit(solution)/shard_map/while/body/eval_jaxpr/ppermute | solution.py:16
  39.6 1.0 %copy.19 = f32[1872,128]{1,0:T(8,128)} copy(f32[1872,128]{1,0:T(8,128)S(1)} %get-tuple-element.420) | data formatting | bytes 1916928 | tf_op jit(solution)/shard_map/while
  40.7 2.4 %fusion.94 = bf16[2816,128]{0,1:T(8,128)(2,1)S(1)} fusion(s32[2816]{0:T(1024)S(1)} %get-tuple-element.446, f32[1872,128]{1,0:T(8,128)S(1)} %get-tuple-element.420, f32[1872]{0:T(1024)S(1)} %get-tuple-element.441), kind=kOutput, calls=%fused_computation.10.clone.1 | convolution fusion | flops 1360900096 | bytes 1698112 | tf_op jit(solution)/shard_map/while/body/eval_jaxpr/dot_general | solution.py:72
  44.9 1.4 %collective-permute-start = (f32[144,128]{1,0:T(8,128)S(1)}, f32[144,128]{1,0:T(8,128)S(1)}, u32[]{:S(2)}, u32[]{:S(2)}) collective-permute-start(f32[144,128]{1,0:T(8,128)S(1)} %get-tuple-element.395), channel_id=1, source_target_pairs={{0,24},{8,0},{16,8},{24,16},{1,25},{9,1},{17,9},{25,17},{2,26},{10... | collective-permute-start | bytes 221192 | tf_op jit(solution)/shard_map/while/body/eval_jaxpr/ppermute | solution.py:16
  47.0 3.0 %fusion.98 = f32[1872,256]{1,0:T(8,128)S(1)} fusion(s32[2816]{0:T(1024)S(1)} %get-tuple-element.446, bf16[2816,128]{1,0:T(8,128)(2,1)S(1)} %get-tuple-element.393, bf16[2816,128]{1,0:T(8,128)(2,1)S(1)} %get-tuple-element.394), kind=kOutput, calls=%fused_computation.13.clone.1 | convolution fusion | flops 2712461312 | bytes 3369984 | tf_op jit(solution)/shard_map/while/body/eval_jaxpr/dot_general | solution.py:83
  53.5 1.0 %copy.19 = f32[1872,128]{1,0:T(8,128)} copy(f32[1872,128]{1,0:T(8,128)S(1)} %get-tuple-element.420) | data formatting | bytes 1916928 | tf_op jit(solution)/shard_map/while
  54.6 1.6 %collective-permute-start.5 = (bf16[1728,128]{1,0:T(8,128)(2,1)S(1)}, bf16[1728,128]{1,0:T(8,128)(2,1)S(1)}, u32[]{:S(2)}, u32[]{:S(2)}) collective-permute-start(bf16[1728,128]{1,0:T(8,128)(2,1)S(1)} %slice.166), channel_id=1, source_target_pairs={{0,2},{2,0},{1,3},{3,1},{4,6},{6,4},{5,7},{7,5},{8,10},{10,8},{9,1... | collective-permute-start | bytes 1327112 | tf_op jit(solution)/shard_map/ppermute | solution.py:26
  56.5 6.5 %collective-permute-done.5 = bf16[1728,128]{1,0:T(8,128)(2,1)S(1)} collective-permute-done((bf16[1728,128]{1,0:T(8,128)(2,1)S(1)}, bf16[1728,128]{1,0:T(8,128)(2,1)S(1)}, u32[]{:S(2)}, u32[]{:S(2)}) %collective-permute-start.5) | collective-permute-done | bytes 442400 | tf_op jit(solution)/shard_map/ppermute | solution.py:26
  63.5 1.2 %collective-permute-done.6 = bf16[1728,128]{1,0:T(8,128)(2,1)S(1)} collective-permute-done((bf16[1728,128]{1,0:T(8,128)(2,1)S(1)}, bf16[1728,128]{1,0:T(8,128)(2,1)S(1)}, u32[]{:S(2)}, u32[]{:S(2)}) %collective-permute-start.6) | collective-permute-done | bytes 442400 | tf_op jit(solution)/shard_map/ppermute | solution.py:26
  64.7 1.2 %convolution_add_fusion = f32[1728,128]{1,0:T(8,128)} fusion(f32[1728,128]{1,0:T(8,128)S(1)} %convolution_add_fusion.1, bf16[1728,128]{1,0:T(8,128)(2,1)S(1)} %collective-permute-done.6, bf16[512,128]{1,0:T(8,128)(2,1)S(1)} %copy-done, s32[]{:T(128)S(6)} %select_n.38), kind=kOutput, calls=%fused_computation.51 | convolution fusion | flops 56844288 | bytes 2244612 | tf_op jit(solution)/shard_map/dot_general | solution.py:119
  (102 shorter events, 20.8 us)
Async XLA Ops:
  0.0 56.2 %copy-start = (bf16[512,128]{1,0:T(8,128)(2,1)S(1)}, bf16[512,128]{1,0:T(8,128)(2,1)}, u32[]{:S(2)}) copy-start(bf16[512,128]{1,0:T(8,128)(2,1)} %param.15) | copy-start | bytes 393220
  0.0 11.8 %copy-start.3 = (f32[1728]{0:T(1024)S(1)}, f32[1728]{0:T(1024)}, u32[]{:S(2)}) copy-start(f32[1728]{0:T(1024)} %param.10) | copy-start | bytes 20740
  0.0 10.6 %copy-start.7 = (s32[8,343]{1,0:T(8,128)S(1)}, s32[8,343]{1,0:T(8,128)}, u32[]{:S(2)}) copy-start(s32[8,343]{1,0:T(8,128)} %param.13) | copy-start | bytes 32932
  0.0 10.7 %copy-start.5 = (bf16[343,343]{1,0:T(8,128)(2,1)S(1)}, bf16[343,343]{1,0:T(8,128)(2,1)}, u32[]{:S(2)}) copy-start(bf16[343,343]{1,0:T(8,128)(2,1)} %param.12) | copy-start | bytes 705898
  1.5 10.4 %collective-permute-start.2 = (f32[144,128]{1,0:T(8,128)S(1)}, f32[144,128]{1,0:T(8,128)S(1)}, u32[]{:S(2)}, u32[]{:S(2)}) collective-permute-start(f32[144,128]{1,0:T(8,128)S(1)} %fusion.48), channel_id=1, source_target_pairs={{0,24},{8,0},{16,8},{24,16},{1,25},{9,1},{17,9},{25,17},{2,26},{10... | collective-permute-start | bytes 221192 | tf_op jit(solution)/shard_map/ppermute | solution.py:16
  8.2 3.6 %collective-permute-start.3 = (f32[2,144]{1,0:T(2,128)S(1)}, f32[2,144]{1,0:T(2,128)S(1)}, u32[]{:S(2)}, u32[]{:S(2)}) collective-permute-start(f32[2,144]{1,0:T(2,128)S(1)} %fusion.46), channel_id=1, source_target_pairs={{0,24},{8,0},{16,8},{24,16},{1,25},{9,1},{17,9},{25,17},{2,26},{10... | collective-permute-start | bytes 3464 | tf_op jit(solution)/shard_map/ppermute | solution.py:16
  13.0 3.5 %copy-start.8 = (s32[288]{0:T(512)}, s32[288]{0:T(512)S(1)}, u32[]{:S(2)}) copy-start(s32[288]{0:T(512)S(1)} %get-tuple-element.447) | copy-start | bytes 3460 | tf_op jit(solution)/shard_map/while
  17.1 7.5 %collective-permute-start = (f32[144,128]{1,0:T(8,128)S(1)}, f32[144,128]{1,0:T(8,128)S(1)}, u32[]{:S(2)}, u32[]{:S(2)}) collective-permute-start(f32[144,128]{1,0:T(8,128)S(1)} %get-tuple-element.395), channel_id=1, source_target_pairs={{0,24},{8,0},{16,8},{24,16},{1,25},{9,1},{17,9},{25,17},{2,26},{10... | collective-permute-start | bytes 221192 | tf_op jit(solution)/shard_map/while/body/eval_jaxpr/ppermute | solution.py:16
  18.6 5.3 %collective-permute-start.1 = (f32[144,128]{1,0:T(8,128)S(1)}, f32[144,128]{1,0:T(8,128)S(1)}, u32[]{:S(2)}, u32[]{:S(2)}) collective-permute-start(f32[144,128]{1,0:T(8,128)S(1)} %get-tuple-element.396), channel_id=1, source_target_pairs={{0,8},{8,16},{16,24},{24,0},{1,9},{9,17},{17,25},{25,1},{2,10},{10... | collective-permute-start | bytes 221192 | tf_op jit(solution)/shard_map/while/body/eval_jaxpr/ppermute | solution.py:16
  24.4 1.2 %copy-start.2 = (f32[1872,128]{1,0:T(8,128)S(1)}, f32[1872,128]{1,0:T(8,128)}, u32[]{:S(2)}) copy-start(f32[1872,128]{1,0:T(8,128)} %get-tuple-element.419) | copy-start | bytes 2875396 | tf_op jit(solution)/shard_map/while
  25.8 1.0 %copy-start.9 = (s32[288]{0:T(512)S(1)}, s32[288]{0:T(512)}, u32[]{:S(2)}) copy-start(s32[288]{0:T(512)} %copy-done.8) | copy-start | bytes 3460 | tf_op jit(solution)/shard_map/while
  26.9 3.5 %copy-start.8 = (s32[288]{0:T(512)}, s32[288]{0:T(512)S(1)}, u32[]{:S(2)}) copy-start(s32[288]{0:T(512)S(1)} %get-tuple-element.447) | copy-start | bytes 3460 | tf_op jit(solution)/shard_map/while
  31.1 7.4 %collective-permute-start = (f32[144,128]{1,0:T(8,128)S(1)}, f32[144,128]{1,0:T(8,128)S(1)}, u32[]{:S(2)}, u32[]{:S(2)}) collective-permute-start(f32[144,128]{1,0:T(8,128)S(1)} %get-tuple-element.395), channel_id=1, source_target_pairs={{0,24},{8,0},{16,8},{24,16},{1,25},{9,1},{17,9},{25,17},{2,26},{10... | collective-permute-start | bytes 221192 | tf_op jit(solution)/shard_map/while/body/eval_jaxpr/ppermute | solution.py:16
  32.5 5.3 %collective-permute-start.1 = (f32[144,128]{1,0:T(8,128)S(1)}, f32[144,128]{1,0:T(8,128)S(1)}, u32[]{:S(2)}, u32[]{:S(2)}) collective-permute-start(f32[144,128]{1,0:T(8,128)S(1)} %get-tuple-element.396), channel_id=1, source_target_pairs={{0,8},{8,16},{16,24},{24,0},{1,9},{9,17},{17,25},{25,1},{2,10},{10... | collective-permute-start | bytes 221192 | tf_op jit(solution)/shard_map/while/body/eval_jaxpr/ppermute | solution.py:16
  38.2 1.2 %copy-start.2 = (f32[1872,128]{1,0:T(8,128)S(1)}, f32[1872,128]{1,0:T(8,128)}, u32[]{:S(2)}) copy-start(f32[1872,128]{1,0:T(8,128)} %get-tuple-element.419) | copy-start | bytes 2875396 | tf_op jit(solution)/shard_map/while
  39.6 1.0 %copy-start.9 = (s32[288]{0:T(512)S(1)}, s32[288]{0:T(512)}, u32[]{:S(2)}) copy-start(s32[288]{0:T(512)} %copy-done.8) | copy-start | bytes 3460 | tf_op jit(solution)/shard_map/while
  40.7 3.5 %copy-start.8 = (s32[288]{0:T(512)}, s32[288]{0:T(512)S(1)}, u32[]{:S(2)}) copy-start(s32[288]{0:T(512)S(1)} %get-tuple-element.447) | copy-start | bytes 3460 | tf_op jit(solution)/shard_map/while
  44.9 7.4 %collective-permute-start = (f32[144,128]{1,0:T(8,128)S(1)}, f32[144,128]{1,0:T(8,128)S(1)}, u32[]{:S(2)}, u32[]{:S(2)}) collective-permute-start(f32[144,128]{1,0:T(8,128)S(1)} %get-tuple-element.395), channel_id=1, source_target_pairs={{0,24},{8,0},{16,8},{24,16},{1,25},{9,1},{17,9},{25,17},{2,26},{10... | collective-permute-start | bytes 221192 | tf_op jit(solution)/shard_map/while/body/eval_jaxpr/ppermute | solution.py:16
  46.3 5.3 %collective-permute-start.1 = (f32[144,128]{1,0:T(8,128)S(1)}, f32[144,128]{1,0:T(8,128)S(1)}, u32[]{:S(2)}, u32[]{:S(2)}) collective-permute-start(f32[144,128]{1,0:T(8,128)S(1)} %get-tuple-element.396), channel_id=1, source_target_pairs={{0,8},{8,16},{16,24},{24,0},{1,9},{9,17},{17,25},{25,1},{2,10},{10... | collective-permute-start | bytes 221192 | tf_op jit(solution)/shard_map/while/body/eval_jaxpr/ppermute | solution.py:16
  52.0 1.2 %copy-start.2 = (f32[1872,128]{1,0:T(8,128)S(1)}, f32[1872,128]{1,0:T(8,128)}, u32[]{:S(2)}) copy-start(f32[1872,128]{1,0:T(8,128)} %get-tuple-element.419) | copy-start | bytes 2875396 | tf_op jit(solution)/shard_map/while
  53.5 1.0 %copy-start.9 = (s32[288]{0:T(512)S(1)}, s32[288]{0:T(512)}, u32[]{:S(2)}) copy-start(s32[288]{0:T(512)} %copy-done.8) | copy-start | bytes 3460 | tf_op jit(solution)/shard_map/while
  54.6 8.4 %collective-permute-start.5 = (bf16[1728,128]{1,0:T(8,128)(2,1)S(1)}, bf16[1728,128]{1,0:T(8,128)(2,1)S(1)}, u32[]{:S(2)}, u32[]{:S(2)}) collective-permute-start(bf16[1728,128]{1,0:T(8,128)(2,1)S(1)} %slice.166), channel_id=1, source_target_pairs={{0,2},{2,0},{1,3},{3,1},{4,6},{6,4},{5,7},{7,5},{8,10},{10,8},{9,1... | collective-permute-start | bytes 1327112 | tf_op jit(solution)/shard_map/ppermute | solution.py:26
  56.2 6.7 %collective-permute-start.4 = (bf16[1728,128]{1,0:T(8,128)(2,1)S(1)}, bf16[1728,128]{1,0:T(8,128)(2,1)S(1)}, u32[]{:S(2)}, u32[]{:S(2)}) collective-permute-start(bf16[1728,128]{1,0:T(8,128)(2,1)S(1)} %slice.166), channel_id=1, source_target_pairs={{0,1},{1,0},{2,3},{3,2},{4,5},{5,4},{6,7},{7,6},{8,9},{9,8},{10,11... | collective-permute-start | bytes 1327112 | tf_op jit(solution)/shard_map/ppermute | solution.py:26
  62.9 1.8 %collective-permute-start.6 = (bf16[1728,128]{1,0:T(8,128)(2,1)S(1)}, bf16[1728,128]{1,0:T(8,128)(2,1)S(1)}, u32[]{:S(2)}, u32[]{:S(2)}) collective-permute-start(bf16[1728,128]{1,0:T(8,128)(2,1)S(1)} %collective-permute-done.5), channel_id=1, source_target_pairs={{0,1},{1,0},{2,3},{3,2},{4,5},{5,4},{6,7},{7,6},{8,9},{9,8},{10,11... | collective-permute-start | bytes 1327112 | tf_op jit(solution)/shard_map/ppermute | solution.py:26
  (3 other events, 3.0 us)

commit v13 on v5

--- a/solution.py
+++ b/solution.py
@@ -105,12 +105,9 @@
     across = from_partner(filtered, "st", 1)
     beside = from_partner(filtered, "st", 0)
     diagonal = from_partner(across, "st", 0)
-    rotated = jnp.dot(filtered, rows_for(position), preferred_element_type=jnp.float32)
-    rotated = rotated + jnp.dot(beside, rows_for(position ^ 1), preferred_element_type=jnp.float32)
-    rotated = rotated + jnp.dot(across, rows_for(position ^ 2), preferred_element_type=jnp.float32)
-    rotated = rotated + jnp.dot(
-        diagonal, rows_for(position ^ 3), preferred_element_type=jnp.float32
-    )
+    blocks = jnp.concatenate([filtered, beside, across, diagonal], 1)
+    turn = jnp.concatenate([rows_for(position ^ member) for member in range(4)], 0)
+    rotated = jnp.dot(blocks, turn, preferred_element_type=jnp.float32)
     return rotated
 
 

time: 65.2 us -> 65.6 us (level)
  waiting for transfers between devices: 11.6 us -> 12.4 us
    ppermute x3, waiting for transfers between devices: 7.72 us -> 8.54 us  [from_partner(): return lax.ppermute(block, axis, route)]
    dot_general x4 -> x1, matrix products: 1.99 us -> 1.54 us  [body(): rotated = jnp.dot(blocks, turn, preferred_element_type=jnp.float32)]
  transfers between devices with their start and end apart: 11 -> 11, of which waited for: 6 -> 6; matrix products, arithmetic and copies ran while one was open for 27% -> 26% of each run, Pallas kernels for 0% -> 0%
where the time goes in v13:
time: 65.6 us; the launch traced here: 65.2 us
  matrix products  28.2 us (43%)
  starting transfers between devices  12.4 us (19%)
  waiting for transfers between devices  12.4 us (19%)
  other arithmetic  7.5 us (11%)
  local copies, waits for them, and re-layouts  4.36 us (7%)
    ppermute x8, starting transfers between devices, ring(): return lax.ppermute(block, axis, route)  10.7 us
    dot_general x3, matrix products, operate(): jnp.dot(scatter_sel, both, preferred_element_type=jnp.float32)  9.05 us
    ppermute x3, waiting for transfers between devices, from_partner(): return lax.ppermute(block, axis, route)  8.54 us
    dot_general x3, matrix products, operate(): lax.dot_general(scatter_sel, weighted, (((0,), (0,)), ((), ())), preferre...  7.04 us
    dot_general x3, matrix products, operate(): jnp.einsum('ij,cjb->cib', padded_matrix, values, preferred_element_type=j...  4.46 us
    sub x3, other arithmetic, chebyshev_step(): return (current, gain * scaled - keep * previous)  3.86 us
    ppermute x8, waiting for transfers between devices, ring(): return lax.ppermute(block, axis, route)  3.81 us
    dot_general x3, matrix products, operate(): jnp.dot(rim_sel, both, preferred_element_type=jnp.float32)  1.89 us
  transfers between devices with their start and end apart: 11, of which 6 were waited for; matrix products, arithmetic and copies ran while one was open for 26% of the time, Pallas kernels for 0%

profile of v13, /device:TPU:0, one launch (start us, length us, event | category | flops | bytes accessed | tf_op | source)
XLA Modules:
  0.0 65.2 jit_solution(13359943295425881383)
XLA Ops:
  0.1 1.4 %fusion.54 = f32[144,128]{1,0:T(8,128)S(1)} fusion(bf16[1728,128]{1,0:T(8,128)(2,1)} %param.9, s32[1728]{0:T(1024)S(1)} %add_reduce_fusion, s32[144]{0:T(256)} %param.14), kind=kOutput, calls=%fused_computation.58 | convolution fusion | flops 63949824 | bytes 523584 | tf_op jit(solution)/shard_map/dot_general | solution.py:57
  1.5 4.0 %collective-permute-start.2 = (f32[144,128]{1,0:T(8,128)S(1)}, f32[144,128]{1,0:T(8,128)S(1)}, u32[]{:S(2)}, u32[]{:S(2)}) collective-permute-start(f32[144,128]{1,0:T(8,128)S(1)} %fusion.54), channel_id=1, source_target_pairs={{0,24},{8,0},{16,8},{24,16},{1,25},{9,1},{17,9},{25,17},{2,26},{10... | collective-permute-start | bytes 221192 | tf_op jit(solution)/shard_map/ppermute | solution.py:16
  6.9 1.4 %fusion.52 = f32[2,144]{1,0:T(2,128)S(1)} fusion(s32[144]{0:T(256)} %param.14, s32[1728]{0:T(1024)S(1)} %add_reduce_fusion, f32[1,1728]{1,0:T(1,128)S(1)} %stack.10, f32[1,1728]{1,0:T(1,128)S(1)} %stack.9), kind=kOutput, calls=%fused_computation.56 | convolution fusion | flops 6224256 | bytes 22464 | tf_op jit(solution)/shard_map/dot_general | solution.py:58
  12.6 40.8 %while.17 = (s32[]{:T(128)}, f32[1872,128]{1,0:T(8,128)S(1)}, f32[1872,128]{1,0:T(8,128)S(1)}, f32[1872]{0:T(1024)S(1)}, bf16[352,352]{1,0:T(8,128)(2,1)}, /*ind...) while((s32[]{:T(128)}, f32[1872,128]{1,0:T(8,128)S(1)}, ...), condition=%wide.region_1.2_spmd.clone.clone, body=%wide.region_0.1_spmd.clone.clone.sunk | while | flops 4879314944 | bytes 31196832 | solution.py:98
  12.6 2.3 %fusion.93 = bf16[2816,128]{0,1:T(8,128)(2,1)S(1)} fusion(s32[2816]{0:T(1024)S(1)} %get-tuple-element.362, f32[1872,128]{1,0:T(8,128)S(1)} %get-tuple-element.342, f32[1872]{0:T(1024)S(1)} %get-tuple-element.359), kind=kOutput, calls=%fused_computation.10.clone.1 | convolution fusion | flops 1360900096 | bytes 1698112 | tf_op jit(solution)/shard_map/while/body/eval_jaxpr/dot_general | solution.py:72
  15.3 1.5 %fusion.94 = f32[8,128,352]{1,2,0:T(8,128)S(1)} fusion(bf16[8,352,128]{2,1,0:T(8,128)(2,1)S(1)} %bitcast.38, bf16[352,352]{1,0:T(8,128)(2,1)} %get-tuple-element.360), kind=kOutput, calls=%fused_computation.35.clone.1 | convolution fusion | flops 253755392 | bytes 2410496 | tf_op jit(solution)/shard_map/while/body/eval_jaxpr/ij,cjb->cib/dot_general | solution.py:76
  17.7 1.5 %collective-permute-start = (f32[144,128]{1,0:T(8,128)S(1)}, f32[144,128]{1,0:T(8,128)S(1)}, u32[]{:S(2)}, u32[]{:S(2)}) collective-permute-start(f32[144,128]{1,0:T(8,128)S(1)} %get-tuple-element.320), channel_id=1, source_target_pairs={{0,24},{8,0},{16,8},{24,16},{1,25},{9,1},{17,9},{25,17},{2,26},{10... | collective-permute-start | bytes 221192 | tf_op jit(solution)/shard_map/while/body/eval_jaxpr/ppermute | solution.py:16
  19.8 3.0 %fusion.97 = f32[1872,256]{1,0:T(8,128)S(1)} fusion(s32[2816]{0:T(1024)S(1)} %get-tuple-element.362, bf16[2816,128]{1,0:T(8,128)(2,1)S(1)} %get-tuple-element.318, bf16[2816,128]{1,0:T(8,128)(2,1)S(1)} %get-tuple-element.319), kind=kOutput, calls=%fused_computation.13.clone.1 | convolution fusion | flops 2712461312 | bytes 3369984 | tf_op jit(solution)/shard_map/while/body/eval_jaxpr/dot_general | solution.py:83
  22.9 1.5 %collective-permute-done.1 = f32[144,128]{1,0:T(8,128)S(1)} collective-permute-done((f32[144,128]{1,0:T(8,128)S(1)}, f32[144,128]{1,0:T(8,128)S(1)}, u32[]{:S(2)}, u32[]{:S(2)}) %collective-permute-start.1) | collective-permute-done | bytes 73760 | tf_op jit(solution)/shard_map/while/body/eval_jaxpr/ppermute | solution.py:16
  25.1 1.3 %fusion.99 = f32[1872,128]{1,0:T(8,128)S(1)} fusion(f32[144,128]{1,0:T(8,128)S(1)} %slice_add_fusion.9, f32[1728,128]{1,0:T(8,128)S(1)} %fusion.98, f32[1872,128]{1,0:T(8,128)S(1)} %get-tuple-element.341, f32[1872,128]{1,0:T(8,128)S(1)} %get-tuple-element.342, f32[]{:T(128)S(6)} %select_n.45, f32[]{:T(128)S(6)} %mul.171, ...), kind=kLoop, calls=%fused_computation.28.clone.1 | loop fusion | flops 2156544 | bytes 3848840 | tf_op jit(solution)/shard_map/while/body/eval_jaxpr/sub | solution.py:96
  26.6 2.3 %fusion.93 = bf16[2816,128]{0,1:T(8,128)(2,1)S(1)} fusion(s32[2816]{0:T(1024)S(1)} %get-tuple-element.362, f32[1872,128]{1,0:T(8,128)S(1)} %get-tuple-element.342, f32[1872]{0:T(1024)S(1)} %get-tuple-element.359), kind=kOutput, calls=%fused_computation.10.clone.1 | convolution fusion | flops 1360900096 | bytes 1698112 | tf_op jit(solution)/shard_map/while/body/eval_jaxpr/dot_general | solution.py:72
  29.3 1.5 %fusion.94 = f32[8,128,352]{1,2,0:T(8,128)S(1)} fusion(bf16[8,352,128]{2,1,0:T(8,128)(2,1)S(1)} %bitcast.38, bf16[352,352]{1,0:T(8,128)(2,1)} %get-tuple-element.360), kind=kOutput, calls=%fused_computation.35.clone.1 | convolution fusion | flops 253755392 | bytes 2410496 | tf_op jit(solution)/shard_map/while/body/eval_jaxpr/ij,cjb->cib/dot_general | solution.py:76
  32.6 1.2 %collective-permute-start.1 = (f32[144,128]{1,0:T(8,128)S(1)}, f32[144,128]{1,0:T(8,128)S(1)}, u32[]{:S(2)}, u32[]{:S(2)}) collective-permute-start(f32[144,128]{1,0:T(8,128)S(1)} %get-tuple-element.321), channel_id=1, source_target_pairs={{0,8},{8,16},{16,24},{24,0},{1,9},{9,17},{17,25},{25,1},{2,10},{10... | collective-permute-start | bytes 221192 | tf_op jit(solution)/shard_map/while/body/eval_jaxpr/ppermute | solution.py:16
  33.8 3.0 %fusion.97 = f32[1872,256]{1,0:T(8,128)S(1)} fusion(s32[2816]{0:T(1024)S(1)} %get-tuple-element.362, bf16[2816,128]{1,0:T(8,128)(2,1)S(1)} %get-tuple-element.318, bf16[2816,128]{1,0:T(8,128)(2,1)S(1)} %get-tuple-element.319), kind=kOutput, calls=%fused_computation.13.clone.1 | convolution fusion | flops 2712461312 | bytes 3369984 | tf_op jit(solution)/shard_map/while/body/eval_jaxpr/dot_general | solution.py:83
  38.5 1.3 %fusion.99 = f32[1872,128]{1,0:T(8,128)S(1)} fusion(f32[144,128]{1,0:T(8,128)S(1)} %slice_add_fusion.9, f32[1728,128]{1,0:T(8,128)S(1)} %fusion.98, f32[1872,128]{1,0:T(8,128)S(1)} %get-tuple-element.341, f32[1872,128]{1,0:T(8,128)S(1)} %get-tuple-element.342, f32[]{:T(128)S(6)} %select_n.45, f32[]{:T(128)S(6)} %mul.171, ...), kind=kLoop, calls=%fused_computation.28.clone.1 | loop fusion | flops 2156544 | bytes 3848840 | tf_op jit(solution)/shard_map/while/body/eval_jaxpr/sub | solution.py:96
  40.0 2.3 %fusion.93 = bf16[2816,128]{0,1:T(8,128)(2,1)S(1)} fusion(s32[2816]{0:T(1024)S(1)} %get-tuple-element.362, f32[1872,128]{1,0:T(8,128)S(1)} %get-tuple-element.342, f32[1872]{0:T(1024)S(1)} %get-tuple-element.359), kind=kOutput, calls=%fused_computation.10.clone.1 | convolution fusion | flops 1360900096 | bytes 1698112 | tf_op jit(solution)/shard_map/while/body/eval_jaxpr/dot_general | solution.py:72
  42.7 1.5 %fusion.94 = f32[8,128,352]{1,2,0:T(8,128)S(1)} fusion(bf16[8,352,128]{2,1,0:T(8,128)(2,1)S(1)} %bitcast.38, bf16[352,352]{1,0:T(8,128)(2,1)} %get-tuple-element.360), kind=kOutput, calls=%fused_computation.35.clone.1 | convolution fusion | flops 253755392 | bytes 2410496 | tf_op jit(solution)/shard_map/while/body/eval_jaxpr/ij,cjb->cib/dot_general | solution.py:76
  46.0 1.1 %collective-permute-start.1 = (f32[144,128]{1,0:T(8,128)S(1)}, f32[144,128]{1,0:T(8,128)S(1)}, u32[]{:S(2)}, u32[]{:S(2)}) collective-permute-start(f32[144,128]{1,0:T(8,128)S(1)} %get-tuple-element.321), channel_id=1, source_target_pairs={{0,8},{8,16},{16,24},{24,0},{1,9},{9,17},{17,25},{25,1},{2,10},{10... | collective-permute-start | bytes 221192 | tf_op jit(solution)/shard_map/while/body/eval_jaxpr/ppermute | solution.py:16
  47.2 3.0 %fusion.97 = f32[1872,256]{1,0:T(8,128)S(1)} fusion(s32[2816]{0:T(1024)S(1)} %get-tuple-element.362, bf16[2816,128]{1,0:T(8,128)(2,1)S(1)} %get-tuple-element.318, bf16[2816,128]{1,0:T(8,128)(2,1)S(1)} %get-tuple-element.319), kind=kOutput, calls=%fused_computation.13.clone.1 | convolution fusion | flops 2712461312 | bytes 3369984 | tf_op jit(solution)/shard_map/while/body/eval_jaxpr/dot_general | solution.py:83
  52.0 1.3 %fusion.99 = f32[1872,128]{1,0:T(8,128)S(1)} fusion(f32[144,128]{1,0:T(8,128)S(1)} %slice_add_fusion.9, f32[1728,128]{1,0:T(8,128)S(1)} %fusion.98, f32[1872,128]{1,0:T(8,128)S(1)} %get-tuple-element.341, f32[1872,128]{1,0:T(8,128)S(1)} %get-tuple-element.342, f32[]{:T(128)S(6)} %select_n.45, f32[]{:T(128)S(6)} %mul.171, ...), kind=kLoop, calls=%fused_computation.28.clone.1 | loop fusion | flops 2156544 | bytes 3848840 | tf_op jit(solution)/shard_map/while/body/eval_jaxpr/sub | solution.py:96
  53.5 1.6 %collective-permute-start.5 = (bf16[1728,128]{1,0:T(8,128)(2,1)S(1)}, bf16[1728,128]{1,0:T(8,128)(2,1)S(1)}, u32[]{:S(2)}, u32[]{:S(2)}) collective-permute-start(bf16[1728,128]{1,0:T(8,128)(2,1)S(1)} %slice.138), channel_id=1, source_target_pairs={{0,2},{2,0},{1,3},{3,1},{4,6},{6,4},{5,7},{7,5},{8,10},{10,8},{9,1... | collective-permute-start | bytes 1327112 | tf_op jit(solution)/shard_map/ppermute | solution.py:26
  55.1 6.8 %collective-permute-done.5 = bf16[1728,128]{1,0:T(8,128)(2,1)S(1)} collective-permute-done((bf16[1728,128]{1,0:T(8,128)(2,1)S(1)}, bf16[1728,128]{1,0:T(8,128)(2,1)S(1)}, u32[]{:S(2)}, u32[]{:S(2)}) %collective-permute-start.5) | collective-permute-done | bytes 442400 | tf_op jit(solution)/shard_map/ppermute | solution.py:26
  61.9 1.8 %collective-permute-done.6 = bf16[1728,128]{1,0:T(8,128)(2,1)S(1)} collective-permute-done((bf16[1728,128]{1,0:T(8,128)(2,1)S(1)}, bf16[1728,128]{1,0:T(8,128)(2,1)S(1)}, u32[]{:S(2)}, u32[]{:S(2)}) %collective-permute-start.6) | collective-permute-done | bytes 442400 | tf_op jit(solution)/shard_map/ppermute | solution.py:26
  63.7 1.5 %fusion.44 = f32[1728,128]{1,0:T(8,128)} fusion(bf16[1728,128]{1,0:T(8,128)(2,1)S(1)} %collective-permute-done.6, bf16[1728,128]{1,0:T(8,128)(2,1)S(1)} %collective-permute-done.5, bf16[1728,128]{1,0:T(8,128)(2,1)S(1)} %collective-permute-done.4, bf16[1728,128]{1,0:T(8,128)(2,1)S(1)} %slice.138, bf16[128,128]{1,0:T(8,128)(2,1)S(1)} %get-tuple-element.245, ...), kind=kOutput, calls=%fused_computation.48 | convolution fusion | flops 234094592 | bytes 2785280 | tf_op jit(solution)/shard_map/dot_general | solution.py:110
  (77 shorter events, 16.5 us)
Async XLA Ops:
  0.0 11.8 %copy-start.3 = (f32[1728]{0:T(1024)S(1)}, f32[1728]{0:T(1024)}, u32[]{:S(2)}) copy-start(f32[1728]{0:T(1024)} %param.11) | copy-start | bytes 20740
  0.0 11.8 %copy-start.4 = (f32[1728]{0:T(1024)S(1)}, f32[1728]{0:T(1024)}, u32[]{:S(2)}) copy-start(f32[1728]{0:T(1024)} %param.10) | copy-start | bytes 20740
  0.0 10.6 %copy-start.5 = (s32[8,343]{1,0:T(8,128)S(1)}, s32[8,343]{1,0:T(8,128)}, u32[]{:S(2)}) copy-start(s32[8,343]{1,0:T(8,128)} %param.13) | copy-start | bytes 32932
  0.0 10.7 %copy-start = (bf16[343,343]{1,0:T(8,128)(2,1)S(1)}, bf16[343,343]{1,0:T(8,128)(2,1)}, u32[]{:S(2)}) copy-start(bf16[343,343]{1,0:T(8,128)(2,1)} %param.12) | copy-start | bytes 705898
  1.5 10.4 %collective-permute-start.2 = (f32[144,128]{1,0:T(8,128)S(1)}, f32[144,128]{1,0:T(8,128)S(1)}, u32[]{:S(2)}, u32[]{:S(2)}) collective-permute-start(f32[144,128]{1,0:T(8,128)S(1)} %fusion.54), channel_id=1, source_target_pairs={{0,24},{8,0},{16,8},{24,16},{1,25},{9,1},{17,9},{25,17},{2,26},{10... | collective-permute-start | bytes 221192 | tf_op jit(solution)/shard_map/ppermute | solution.py:16
  8.2 3.6 %collective-permute-start.3 = (f32[2,144]{1,0:T(2,128)S(1)}, f32[2,144]{1,0:T(2,128)S(1)}, u32[]{:S(2)}, u32[]{:S(2)}) collective-permute-start(f32[2,144]{1,0:T(2,128)S(1)} %fusion.52), channel_id=1, source_target_pairs={{0,24},{8,0},{16,8},{24,16},{1,25},{9,1},{17,9},{25,17},{2,26},{10... | collective-permute-start | bytes 3464 | tf_op jit(solution)/shard_map/ppermute | solution.py:16
  11.9 0.7 %copy-start.2 = (s32[144]{0:T(256)S(1)}, s32[144]{0:T(256)}, u32[]{:S(2)}) copy-start(s32[144]{0:T(256)} %param.14) | copy-start | bytes 1732
  12.6 49.3 %copy-start.1 = (bf16[512,128]{1,0:T(8,128)(2,1)S(1)}, bf16[512,128]{1,0:T(8,128)(2,1)}, u32[]{:S(2)}) copy-start(bf16[512,128]{1,0:T(8,128)(2,1)} %param.15) | copy-start | bytes 393220
  17.7 7.4 %collective-permute-start = (f32[144,128]{1,0:T(8,128)S(1)}, f32[144,128]{1,0:T(8,128)S(1)}, u32[]{:S(2)}, u32[]{:S(2)}) collective-permute-start(f32[144,128]{1,0:T(8,128)S(1)} %get-tuple-element.320), channel_id=1, source_target_pairs={{0,24},{8,0},{16,8},{24,16},{1,25},{9,1},{17,9},{25,17},{2,26},{10... | collective-permute-start | bytes 221192 | tf_op jit(solution)/shard_map/while/body/eval_jaxpr/ppermute | solution.py:16
  19.2 5.3 %collective-permute-start.1 = (f32[144,128]{1,0:T(8,128)S(1)}, f32[144,128]{1,0:T(8,128)S(1)}, u32[]{:S(2)}, u32[]{:S(2)}) collective-permute-start(f32[144,128]{1,0:T(8,128)S(1)} %get-tuple-element.321), channel_id=1, source_target_pairs={{0,8},{8,16},{16,24},{24,0},{1,9},{9,17},{17,25},{25,1},{2,10},{10... | collective-permute-start | bytes 221192 | tf_op jit(solution)/shard_map/while/body/eval_jaxpr/ppermute | solution.py:16
  31.7 6.8 %collective-permute-start = (f32[144,128]{1,0:T(8,128)S(1)}, f32[144,128]{1,0:T(8,128)S(1)}, u32[]{:S(2)}, u32[]{:S(2)}) collective-permute-start(f32[144,128]{1,0:T(8,128)S(1)} %get-tuple-element.320), channel_id=1, source_target_pairs={{0,24},{8,0},{16,8},{24,16},{1,25},{9,1},{17,9},{25,17},{2,26},{10... | collective-permute-start | bytes 221192 | tf_op jit(solution)/shard_map/while/body/eval_jaxpr/ppermute | solution.py:16
  32.6 5.3 %collective-permute-start.1 = (f32[144,128]{1,0:T(8,128)S(1)}, f32[144,128]{1,0:T(8,128)S(1)}, u32[]{:S(2)}, u32[]{:S(2)}) collective-permute-start(f32[144,128]{1,0:T(8,128)S(1)} %get-tuple-element.321), channel_id=1, source_target_pairs={{0,8},{8,16},{16,24},{24,0},{1,9},{9,17},{17,25},{25,1},{2,10},{10... | collective-permute-start | bytes 221192 | tf_op jit(solution)/shard_map/while/body/eval_jaxpr/ppermute | solution.py:16
  45.1 6.9 %collective-permute-start = (f32[144,128]{1,0:T(8,128)S(1)}, f32[144,128]{1,0:T(8,128)S(1)}, u32[]{:S(2)}, u32[]{:S(2)}) collective-permute-start(f32[144,128]{1,0:T(8,128)S(1)} %get-tuple-element.320), channel_id=1, source_target_pairs={{0,24},{8,0},{16,8},{24,16},{1,25},{9,1},{17,9},{25,17},{2,26},{10... | collective-permute-start | bytes 221192 | tf_op jit(solution)/shard_map/while/body/eval_jaxpr/ppermute | solution.py:16
  46.0 5.3 %collective-permute-start.1 = (f32[144,128]{1,0:T(8,128)S(1)}, f32[144,128]{1,0:T(8,128)S(1)}, u32[]{:S(2)}, u32[]{:S(2)}) collective-permute-start(f32[144,128]{1,0:T(8,128)S(1)} %get-tuple-element.321), channel_id=1, source_target_pairs={{0,8},{8,16},{16,24},{24,0},{1,9},{9,17},{17,25},{25,1},{2,10},{10... | collective-permute-start | bytes 221192 | tf_op jit(solution)/shard_map/while/body/eval_jaxpr/ppermute | solution.py:16
  53.5 8.4 %collective-permute-start.5 = (bf16[1728,128]{1,0:T(8,128)(2,1)S(1)}, bf16[1728,128]{1,0:T(8,128)(2,1)S(1)}, u32[]{:S(2)}, u32[]{:S(2)}) collective-permute-start(bf16[1728,128]{1,0:T(8,128)(2,1)S(1)} %slice.138), channel_id=1, source_target_pairs={{0,2},{2,0},{1,3},{3,1},{4,6},{6,4},{5,7},{7,5},{8,10},{10,8},{9,1... | collective-permute-start | bytes 1327112 | tf_op jit(solution)/shard_map/ppermute | solution.py:26
  55.1 6.8 %collective-permute-start.4 = (bf16[1728,128]{1,0:T(8,128)(2,1)S(1)}, bf16[1728,128]{1,0:T(8,128)(2,1)S(1)}, u32[]{:S(2)}, u32[]{:S(2)}) collective-permute-start(bf16[1728,128]{1,0:T(8,128)(2,1)S(1)} %slice.138), channel_id=1, source_target_pairs={{0,1},{1,0},{2,3},{3,2},{4,5},{5,4},{6,7},{7,6},{8,9},{9,8},{10,11... | collective-permute-start | bytes 1327112 | tf_op jit(solution)/shard_map/ppermute | solution.py:26
  61.9 1.8 %collective-permute-start.6 = (bf16[1728,128]{1,0:T(8,128)(2,1)S(1)}, bf16[1728,128]{1,0:T(8,128)(2,1)S(1)}, u32[]{:S(2)}, u32[]{:S(2)}) collective-permute-start(bf16[1728,128]{1,0:T(8,128)(2,1)S(1)} %collective-permute-done.5), channel_id=1, source_target_pairs={{0,1},{1,0},{2,3},{3,2},{4,5},{5,4},{6,7},{7,6},{8,9},{9,8},{10,11... | collective-permute-start | bytes 1327112 | tf_op jit(solution)/shard_map/ppermute | solution.py:26

commit v14 on v5

--- a/solution.py
+++ b/solution.py
@@ -78,11 +78,11 @@
         ).reshape(-1, state_count)
         both = high_low(products)
         rim = summed_halves(jnp.dot(rim_sel, both, preferred_element_type=jnp.float32))
-        from_prev = ring(rim[face_count:], "dom", 1)
+        from_prev = ring(high_low(rim[face_count:]), "dom", 1)
         from_next = ring(rim[:face_count], "dom", -1)
         main = summed_halves(jnp.dot(scatter_sel, both, preferred_element_type=jnp.float32))
         own = main[:node_count] + summed_halves(
-            jnp.dot(face_put, high_low(from_prev), preferred_element_type=jnp.float32)
+            jnp.dot(face_put, from_prev, preferred_element_type=jnp.float32)
         )
         summed = jnp.concatenate([own, main[node_count:] + from_next], 0)
         return wide_mass[:, None] * summed + wide_potential[:, None] * field_in

time: 65.2 us -> 65.4 us (level)
  no operation moved by 1% of the time
where the time goes in v14:
time: 65.4 us; the launch traced here: 65 us
  matrix products  28.6 us (44%)
  starting transfers between devices  12.5 us (19%)
  waiting for transfers between devices  11.5 us (18%)
  other arithmetic  7.55 us (12%)
  local copies, waits for them, and re-layouts  4.32 us (7%)
    ppermute x8, starting transfers between devices, ring(): return lax.ppermute(block, axis, route)  10.9 us
    dot_general x3, matrix products, operate(): jnp.dot(scatter_sel, both, preferred_element_type=jnp.float32)  9.06 us
    ppermute x3, waiting for transfers between devices, from_partner(): return lax.ppermute(block, axis, route)  7.76 us
    dot_general x3, matrix products, operate(): lax.dot_general(scatter_sel, weighted, (((0,), (0,)), ((), ())), preferre...  7.04 us
    dot_general x3, matrix products, operate(): jnp.einsum('ij,cjb->cib', padded_matrix, values, preferred_element_type=j...  4.46 us
    sub x3, other arithmetic, chebyshev_step(): return (current, gain * scaled - keep * previous)  3.86 us
    ppermute x8, waiting for transfers between devices, ring(): return lax.ppermute(block, axis, route)  3.79 us
    dot_general x3, matrix products, operate(): jnp.dot(rim_sel, both, preferred_element_type=jnp.float32)  1.89 us
  transfers between devices with their start and end apart: 11, of which 6 were waited for; matrix products, arithmetic and copies ran while one was open for 27% of the time, Pallas kernels for 0%

profile of v14, /device:TPU:0, one launch (start us, length us, event | category | flops | bytes accessed | tf_op | source)
XLA Modules:
  0.0 65.0 jit_solution(4574398895323282003)
XLA Ops:
  0.1 1.4 %fusion.42 = f32[144,128]{1,0:T(8,128)S(1)} fusion(bf16[1728,128]{1,0:T(8,128)(2,1)} %param.9, s32[1728]{0:T(1024)S(1)} %add_reduce_fusion, s32[144]{0:T(256)} %param.14), kind=kOutput, calls=%fused_computation.50 | convolution fusion | flops 63949824 | bytes 523584 | tf_op jit(solution)/shard_map/dot_general | solution.py:57
  1.5 4.0 %collective-permute-start.2 = (f32[144,128]{1,0:T(8,128)S(1)}, f32[144,128]{1,0:T(8,128)S(1)}, u32[]{:S(2)}, u32[]{:S(2)}) collective-permute-start(f32[144,128]{1,0:T(8,128)S(1)} %fusion.42), channel_id=1, source_target_pairs={{0,24},{8,0},{16,8},{24,16},{1,25},{9,1},{17,9},{25,17},{2,26},{10... | collective-permute-start | bytes 221192 | tf_op jit(solution)/shard_map/ppermute | solution.py:16
  6.9 1.4 %fusion.40 = f32[2,144]{1,0:T(2,128)S(1)} fusion(s32[144]{0:T(256)} %param.14, s32[1728]{0:T(1024)S(1)} %add_reduce_fusion, f32[1,1728]{1,0:T(1,128)S(1)} %stack.10, f32[1,1728]{1,0:T(1,128)S(1)} %stack.9), kind=kOutput, calls=%fused_computation.48 | convolution fusion | flops 6224256 | bytes 22464 | tf_op jit(solution)/shard_map/dot_general | solution.py:58
  12.6 41.0 %while.17 = (s32[]{:T(128)}, f32[1872,128]{1,0:T(8,128)S(1)}, f32[1872,128]{1,0:T(8,128)S(1)}, f32[1872]{0:T(1024)S(1)}, bf16[352,352]{1,0:T(8,128)(2,1)}, /*ind...) while((s32[]{:T(128)}, f32[1872,128]{1,0:T(8,128)S(1)}, ...), condition=%wide.region_1.2_spmd.clone.clone, body=%wide.region_0.1_spmd.clone.clone.sunk | while | flops 4879314944 | bytes 31196832 | solution.py:98
  12.6 2.4 %fusion.85 = bf16[2816,128]{0,1:T(8,128)(2,1)S(1)} fusion(s32[2816]{0:T(1024)S(1)} %get-tuple-element.355, f32[1872,128]{1,0:T(8,128)S(1)} %get-tuple-element.335, f32[1872]{0:T(1024)S(1)} %get-tuple-element.352), kind=kOutput, calls=%fused_computation.10.clone.1 | convolution fusion | flops 1360900096 | bytes 1698112 | tf_op jit(solution)/shard_map/while/body/eval_jaxpr/dot_general | solution.py:72
  15.3 1.5 %fusion.86 = f32[8,128,352]{1,2,0:T(8,128)S(1)} fusion(bf16[8,352,128]{2,1,0:T(8,128)(2,1)S(1)} %bitcast.44, bf16[352,352]{1,0:T(8,128)(2,1)} %get-tuple-element.353), kind=kOutput, calls=%fused_computation.35.clone.1 | convolution fusion | flops 253755392 | bytes 2410496 | tf_op jit(solution)/shard_map/while/body/eval_jaxpr/ij,cjb->cib/dot_general | solution.py:76
  17.7 1.5 %collective-permute-start = (f32[144,128]{1,0:T(8,128)S(1)}, f32[144,128]{1,0:T(8,128)S(1)}, u32[]{:S(2)}, u32[]{:S(2)}) collective-permute-start(f32[144,128]{1,0:T(8,128)S(1)} %get-tuple-element.314), channel_id=1, source_target_pairs={{0,24},{8,0},{16,8},{24,16},{1,25},{9,1},{17,9},{25,17},{2,26},{10... | collective-permute-start | bytes 221192 | tf_op jit(solution)/shard_map/while/body/eval_jaxpr/ppermute | solution.py:16
  19.9 3.0 %fusion.88 = f32[1872,256]{1,0:T(8,128)S(1)} fusion(s32[2816]{0:T(1024)S(1)} %get-tuple-element.355, bf16[2816,128]{1,0:T(8,128)(2,1)S(1)} %get-tuple-element.312, bf16[2816,128]{1,0:T(8,128)(2,1)S(1)} %get-tuple-element.313), kind=kOutput, calls=%fused_computation.13.clone.1 | convolution fusion | flops 2712461312 | bytes 3369984 | tf_op jit(solution)/shard_map/while/body/eval_jaxpr/dot_general | solution.py:83
  23.0 1.5 %collective-permute-done.1 = bf16[144,256]{1,0:T(8,128)(2,1)S(1)} collective-permute-done((bf16[144,256]{1,0:T(8,128)(2,1)S(1)}, bf16[144,256]{1,0:T(8,128)(2,1)S(1)}, u32[]{:S(2)}, u32[]{:S(2)}) %collective-permute-start.1) | collective-permute-done | bytes 73760 | tf_op jit(solution)/shard_map/while/body/eval_jaxpr/ppermute | solution.py:16
  25.2 1.3 %fusion.90 = f32[1872,128]{1,0:T(8,128)S(1)} fusion(f32[144,128]{1,0:T(8,128)S(1)} %slice_add_fusion.9, f32[1728,128]{1,0:T(8,128)S(1)} %fusion.89, f32[1872,128]{1,0:T(8,128)S(1)} %get-tuple-element.334, f32[1872,128]{1,0:T(8,128)S(1)} %get-tuple-element.335, f32[]{:T(128)S(6)} %select_n.45, f32[]{:T(128)S(6)} %mul.171, ...), kind=kLoop, calls=%fused_computation.28.clone.1 | loop fusion | flops 2156544 | bytes 3848840 | tf_op jit(solution)/shard_map/while/body/eval_jaxpr/sub | solution.py:96
  26.7 2.3 %fusion.85 = bf16[2816,128]{0,1:T(8,128)(2,1)S(1)} fusion(s32[2816]{0:T(1024)S(1)} %get-tuple-element.355, f32[1872,128]{1,0:T(8,128)S(1)} %get-tuple-element.335, f32[1872]{0:T(1024)S(1)} %get-tuple-element.352), kind=kOutput, calls=%fused_computation.10.clone.1 | convolution fusion | flops 1360900096 | bytes 1698112 | tf_op jit(solution)/shard_map/while/body/eval_jaxpr/dot_general | solution.py:72
  29.4 1.5 %fusion.86 = f32[8,128,352]{1,2,0:T(8,128)S(1)} fusion(bf16[8,352,128]{2,1,0:T(8,128)(2,1)S(1)} %bitcast.44, bf16[352,352]{1,0:T(8,128)(2,1)} %get-tuple-element.353), kind=kOutput, calls=%fused_computation.35.clone.1 | convolution fusion | flops 253755392 | bytes 2410496 | tf_op jit(solution)/shard_map/while/body/eval_jaxpr/ij,cjb->cib/dot_general | solution.py:76
  32.7 1.3 %collective-permute-start.1 = (bf16[144,256]{1,0:T(8,128)(2,1)S(1)}, bf16[144,256]{1,0:T(8,128)(2,1)S(1)}, u32[]{:S(2)}, u32[]{:S(2)}) collective-permute-start(bf16[144,256]{1,0:T(8,128)(2,1)S(1)} %pad_maximum_fusion.12), channel_id=1, source_target_pairs={{0,8},{8,16},{16,24},{24,0},{1,9},{9,17},{17,25},{25,1},{2,10},{10... | collective-permute-start | bytes 221192 | tf_op jit(solution)/shard_map/while/body/eval_jaxpr/ppermute | solution.py:16
  33.9 3.0 %fusion.88 = f32[1872,256]{1,0:T(8,128)S(1)} fusion(s32[2816]{0:T(1024)S(1)} %get-tuple-element.355, bf16[2816,128]{1,0:T(8,128)(2,1)S(1)} %get-tuple-element.312, bf16[2816,128]{1,0:T(8,128)(2,1)S(1)} %get-tuple-element.313), kind=kOutput, calls=%fused_computation.13.clone.1 | convolution fusion | flops 2712461312 | bytes 3369984 | tf_op jit(solution)/shard_map/while/body/eval_jaxpr/dot_general | solution.py:83
  38.6 1.3 %fusion.90 = f32[1872,128]{1,0:T(8,128)S(1)} fusion(f32[144,128]{1,0:T(8,128)S(1)} %slice_add_fusion.9, f32[1728,128]{1,0:T(8,128)S(1)} %fusion.89, f32[1872,128]{1,0:T(8,128)S(1)} %get-tuple-element.334, f32[1872,128]{1,0:T(8,128)S(1)} %get-tuple-element.335, f32[]{:T(128)S(6)} %select_n.45, f32[]{:T(128)S(6)} %mul.171, ...), kind=kLoop, calls=%fused_computation.28.clone.1 | loop fusion | flops 2156544 | bytes 3848840 | tf_op jit(solution)/shard_map/while/body/eval_jaxpr/sub | solution.py:96
  40.1 2.3 %fusion.85 = bf16[2816,128]{0,1:T(8,128)(2,1)S(1)} fusion(s32[2816]{0:T(1024)S(1)} %get-tuple-element.355, f32[1872,128]{1,0:T(8,128)S(1)} %get-tuple-element.335, f32[1872]{0:T(1024)S(1)} %get-tuple-element.352), kind=kOutput, calls=%fused_computation.10.clone.1 | convolution fusion | flops 1360900096 | bytes 1698112 | tf_op jit(solution)/shard_map/while/body/eval_jaxpr/dot_general | solution.py:72
  42.8 1.5 %fusion.86 = f32[8,128,352]{1,2,0:T(8,128)S(1)} fusion(bf16[8,352,128]{2,1,0:T(8,128)(2,1)S(1)} %bitcast.44, bf16[352,352]{1,0:T(8,128)(2,1)} %get-tuple-element.353), kind=kOutput, calls=%fused_computation.35.clone.1 | convolution fusion | flops 253755392 | bytes 2410496 | tf_op jit(solution)/shard_map/while/body/eval_jaxpr/ij,cjb->cib/dot_general | solution.py:76
  46.2 1.2 %collective-permute-start.1 = (bf16[144,256]{1,0:T(8,128)(2,1)S(1)}, bf16[144,256]{1,0:T(8,128)(2,1)S(1)}, u32[]{:S(2)}, u32[]{:S(2)}) collective-permute-start(bf16[144,256]{1,0:T(8,128)(2,1)S(1)} %pad_maximum_fusion.12), channel_id=1, source_target_pairs={{0,8},{8,16},{16,24},{24,0},{1,9},{9,17},{17,25},{25,1},{2,10},{10... | collective-permute-start | bytes 221192 | tf_op jit(solution)/shard_map/while/body/eval_jaxpr/ppermute | solution.py:16
  47.4 3.0 %fusion.88 = f32[1872,256]{1,0:T(8,128)S(1)} fusion(s32[2816]{0:T(1024)S(1)} %get-tuple-element.355, bf16[2816,128]{1,0:T(8,128)(2,1)S(1)} %get-tuple-element.312, bf16[2816,128]{1,0:T(8,128)(2,1)S(1)} %get-tuple-element.313), kind=kOutput, calls=%fused_computation.13.clone.1 | convolution fusion | flops 2712461312 | bytes 3369984 | tf_op jit(solution)/shard_map/while/body/eval_jaxpr/dot_general | solution.py:83
  52.1 1.3 %fusion.90 = f32[1872,128]{1,0:T(8,128)S(1)} fusion(f32[144,128]{1,0:T(8,128)S(1)} %slice_add_fusion.9, f32[1728,128]{1,0:T(8,128)S(1)} %fusion.89, f32[1872,128]{1,0:T(8,128)S(1)} %get-tuple-element.334, f32[1872,128]{1,0:T(8,128)S(1)} %get-tuple-element.335, f32[]{:T(128)S(6)} %select_n.45, f32[]{:T(128)S(6)} %mul.171, ...), kind=kLoop, calls=%fused_computation.28.clone.1 | loop fusion | flops 2156544 | bytes 3848840 | tf_op jit(solution)/shard_map/while/body/eval_jaxpr/sub | solution.py:96
  53.6 1.6 %collective-permute-start.5 = (bf16[1728,128]{1,0:T(8,128)(2,1)S(1)}, bf16[1728,128]{1,0:T(8,128)(2,1)S(1)}, u32[]{:S(2)}, u32[]{:S(2)}) collective-permute-start(bf16[1728,128]{1,0:T(8,128)(2,1)S(1)} %slice.140), channel_id=1, source_target_pairs={{0,2},{2,0},{1,3},{3,1},{4,6},{6,4},{5,7},{7,5},{8,10},{10,8},{9,1... | collective-permute-start | bytes 1327112 | tf_op jit(solution)/shard_map/ppermute | solution.py:26
  55.5 6.5 %collective-permute-done.5 = bf16[1728,128]{1,0:T(8,128)(2,1)S(1)} collective-permute-done((bf16[1728,128]{1,0:T(8,128)(2,1)S(1)}, bf16[1728,128]{1,0:T(8,128)(2,1)S(1)}, u32[]{:S(2)}, u32[]{:S(2)}) %collective-permute-start.5) | collective-permute-done | bytes 442400 | tf_op jit(solution)/shard_map/ppermute | solution.py:26
  62.6 1.3 %collective-permute-done.6 = bf16[1728,128]{1,0:T(8,128)(2,1)S(1)} collective-permute-done((bf16[1728,128]{1,0:T(8,128)(2,1)S(1)}, bf16[1728,128]{1,0:T(8,128)(2,1)S(1)}, u32[]{:S(2)}, u32[]{:S(2)}) %collective-permute-start.6) | collective-permute-done | bytes 442400 | tf_op jit(solution)/shard_map/ppermute | solution.py:26
  63.8 1.2 %convolution_add_fusion = f32[1728,128]{1,0:T(8,128)} fusion(f32[1728,128]{1,0:T(8,128)S(1)} %convolution_add_fusion.1, bf16[1728,128]{1,0:T(8,128)(2,1)S(1)} %collective-permute-done.6, bf16[512,128]{1,0:T(8,128)(2,1)S(1)} %copy-done, s32[]{:T(128)S(6)} %select_n.38), kind=kOutput, calls=%fused_computation.45 | convolution fusion | flops 56844288 | bytes 2244612 | tf_op jit(solution)/shard_map/dot_general | solution.py:111
  (79 shorter events, 17.3 us)
Async XLA Ops:
  0.0 55.3 %copy-start = (bf16[512,128]{1,0:T(8,128)(2,1)S(1)}, bf16[512,128]{1,0:T(8,128)(2,1)}, u32[]{:S(2)}) copy-start(bf16[512,128]{1,0:T(8,128)(2,1)} %param.15) | copy-start | bytes 393220
  0.0 11.8 %copy-start.3 = (f32[1728]{0:T(1024)S(1)}, f32[1728]{0:T(1024)}, u32[]{:S(2)}) copy-start(f32[1728]{0:T(1024)} %param.11) | copy-start | bytes 20740
  0.0 11.8 %copy-start.4 = (f32[1728]{0:T(1024)S(1)}, f32[1728]{0:T(1024)}, u32[]{:S(2)}) copy-start(f32[1728]{0:T(1024)} %param.10) | copy-start | bytes 20740
  0.0 10.6 %copy-start.5 = (s32[8,343]{1,0:T(8,128)S(1)}, s32[8,343]{1,0:T(8,128)}, u32[]{:S(2)}) copy-start(s32[8,343]{1,0:T(8,128)} %param.13) | copy-start | bytes 32932
  0.0 10.7 %copy-start.1 = (bf16[343,343]{1,0:T(8,128)(2,1)S(1)}, bf16[343,343]{1,0:T(8,128)(2,1)}, u32[]{:S(2)}) copy-start(bf16[343,343]{1,0:T(8,128)(2,1)} %param.12) | copy-start | bytes 705898
  1.5 10.4 %collective-permute-start.2 = (f32[144,128]{1,0:T(8,128)S(1)}, f32[144,128]{1,0:T(8,128)S(1)}, u32[]{:S(2)}, u32[]{:S(2)}) collective-permute-start(f32[144,128]{1,0:T(8,128)S(1)} %fusion.42), channel_id=1, source_target_pairs={{0,24},{8,0},{16,8},{24,16},{1,25},{9,1},{17,9},{25,17},{2,26},{10... | collective-permute-start | bytes 221192 | tf_op jit(solution)/shard_map/ppermute | solution.py:16
  8.2 3.6 %collective-permute-start.3 = (f32[2,144]{1,0:T(2,128)S(1)}, f32[2,144]{1,0:T(2,128)S(1)}, u32[]{:S(2)}, u32[]{:S(2)}) collective-permute-start(f32[2,144]{1,0:T(2,128)S(1)} %fusion.40), channel_id=1, source_target_pairs={{0,24},{8,0},{16,8},{24,16},{1,25},{9,1},{17,9},{25,17},{2,26},{10... | collective-permute-start | bytes 3464 | tf_op jit(solution)/shard_map/ppermute | solution.py:16
  11.9 0.7 %copy-start.2 = (s32[144]{0:T(256)S(1)}, s32[144]{0:T(256)}, u32[]{:S(2)}) copy-start(s32[144]{0:T(256)} %param.14) | copy-start | bytes 1732
  17.7 7.4 %collective-permute-start = (f32[144,128]{1,0:T(8,128)S(1)}, f32[144,128]{1,0:T(8,128)S(1)}, u32[]{:S(2)}, u32[]{:S(2)}) collective-permute-start(f32[144,128]{1,0:T(8,128)S(1)} %get-tuple-element.314), channel_id=1, source_target_pairs={{0,24},{8,0},{16,8},{24,16},{1,25},{9,1},{17,9},{25,17},{2,26},{10... | collective-permute-start | bytes 221192 | tf_op jit(solution)/shard_map/while/body/eval_jaxpr/ppermute | solution.py:16
  19.2 5.3 %collective-permute-start.1 = (bf16[144,256]{1,0:T(8,128)(2,1)S(1)}, bf16[144,256]{1,0:T(8,128)(2,1)S(1)}, u32[]{:S(2)}, u32[]{:S(2)}) collective-permute-start(bf16[144,256]{1,0:T(8,128)(2,1)S(1)} %pad_maximum_fusion.12), channel_id=1, source_target_pairs={{0,8},{8,16},{16,24},{24,0},{1,9},{9,17},{17,25},{25,1},{2,10},{10... | collective-permute-start | bytes 221192 | tf_op jit(solution)/shard_map/while/body/eval_jaxpr/ppermute | solution.py:16
  31.8 6.8 %collective-permute-start = (f32[144,128]{1,0:T(8,128)S(1)}, f32[144,128]{1,0:T(8,128)S(1)}, u32[]{:S(2)}, u32[]{:S(2)}) collective-permute-start(f32[144,128]{1,0:T(8,128)S(1)} %get-tuple-element.314), channel_id=1, source_target_pairs={{0,24},{8,0},{16,8},{24,16},{1,25},{9,1},{17,9},{25,17},{2,26},{10... | collective-permute-start | bytes 221192 | tf_op jit(solution)/shard_map/while/body/eval_jaxpr/ppermute | solution.py:16
  32.7 5.3 %collective-permute-start.1 = (bf16[144,256]{1,0:T(8,128)(2,1)S(1)}, bf16[144,256]{1,0:T(8,128)(2,1)S(1)}, u32[]{:S(2)}, u32[]{:S(2)}) collective-permute-start(bf16[144,256]{1,0:T(8,128)(2,1)S(1)} %pad_maximum_fusion.12), channel_id=1, source_target_pairs={{0,8},{8,16},{16,24},{24,0},{1,9},{9,17},{17,25},{25,1},{2,10},{10... | collective-permute-start | bytes 221192 | tf_op jit(solution)/shard_map/while/body/eval_jaxpr/ppermute | solution.py:16
  45.2 6.9 %collective-permute-start = (f32[144,128]{1,0:T(8,128)S(1)}, f32[144,128]{1,0:T(8,128)S(1)}, u32[]{:S(2)}, u32[]{:S(2)}) collective-permute-start(f32[144,128]{1,0:T(8,128)S(1)} %get-tuple-element.314), channel_id=1, source_target_pairs={{0,24},{8,0},{16,8},{24,16},{1,25},{9,1},{17,9},{25,17},{2,26},{10... | collective-permute-start | bytes 221192 | tf_op jit(solution)/shard_map/while/body/eval_jaxpr/ppermute | solution.py:16
  46.2 5.3 %collective-permute-start.1 = (bf16[144,256]{1,0:T(8,128)(2,1)S(1)}, bf16[144,256]{1,0:T(8,128)(2,1)S(1)}, u32[]{:S(2)}, u32[]{:S(2)}) collective-permute-start(bf16[144,256]{1,0:T(8,128)(2,1)S(1)} %pad_maximum_fusion.12), channel_id=1, source_target_pairs={{0,8},{8,16},{16,24},{24,0},{1,9},{9,17},{17,25},{25,1},{2,10},{10... | collective-permute-start | bytes 221192 | tf_op jit(solution)/shard_map/while/body/eval_jaxpr/ppermute | solution.py:16
  53.6 8.4 %collective-permute-start.5 = (bf16[1728,128]{1,0:T(8,128)(2,1)S(1)}, bf16[1728,128]{1,0:T(8,128)(2,1)S(1)}, u32[]{:S(2)}, u32[]{:S(2)}) collective-permute-start(bf16[1728,128]{1,0:T(8,128)(2,1)S(1)} %slice.140), channel_id=1, source_target_pairs={{0,2},{2,0},{1,3},{3,1},{4,6},{6,4},{5,7},{7,5},{8,10},{10,8},{9,1... | collective-permute-start | bytes 1327112 | tf_op jit(solution)/shard_map/ppermute | solution.py:26
  55.3 6.8 %collective-permute-start.4 = (bf16[1728,128]{1,0:T(8,128)(2,1)S(1)}, bf16[1728,128]{1,0:T(8,128)(2,1)S(1)}, u32[]{:S(2)}, u32[]{:S(2)}) collective-permute-start(bf16[1728,128]{1,0:T(8,128)(2,1)S(1)} %slice.140), channel_id=1, source_target_pairs={{0,1},{1,0},{2,3},{3,2},{4,5},{5,4},{6,7},{7,6},{8,9},{9,8},{10,11... | collective-permute-start | bytes 1327112 | tf_op jit(solution)/shard_map/ppermute | solution.py:26
  62.0 1.8 %collective-permute-start.6 = (bf16[1728,128]{1,0:T(8,128)(2,1)S(1)}, bf16[1728,128]{1,0:T(8,128)(2,1)S(1)}, u32[]{:S(2)}, u32[]{:S(2)}) collective-permute-start(bf16[1728,128]{1,0:T(8,128)(2,1)S(1)} %collective-permute-done.5), channel_id=1, source_target_pairs={{0,1},{1,0},{2,3},{3,2},{4,5},{5,4},{6,7},{7,6},{8,9},{9,8},{10,11... | collective-permute-start | bytes 1327112 | tf_op jit(solution)/shard_map/ppermute | solution.py:26

commit v15 on v5

--- a/solution.py
+++ b/solution.py
@@ -95,7 +95,33 @@
         keep = jnp.where(first, 0.0, 1.0).astype(jnp.float32)
         return current, gain * scaled - keep * previous
 
-    previous, current = lax.fori_loop(0, POLY, chebyshev_step, (field_start, field_start))
+    previous, current = lax.fori_loop(
+        0, POLY - 1, chebyshev_step, (field_start, field_start)
+    )
+
+    weighted = (wide_mass[:, None] * current).astype(jnp.bfloat16)
+    values = lax.dot_general(
+        scatter_sel, weighted, (((0,), (0,)), ((), ())), preferred_element_type=jnp.float32
+    )
+    values = values.astype(jnp.bfloat16).reshape(cell_count, padded_size, state_count)
+    products = jnp.einsum(
+        "ij,cjb->cib", padded_matrix, values, preferred_element_type=jnp.float32
+    ).reshape(-1, state_count)
+    both = high_low(products)
+    ghost_part = summed_halves(
+        jnp.dot(rim_sel[face_count:], both, preferred_element_type=jnp.float32)
+    )
+    from_prev = ring(ghost_part, "dom", 1)
+    main = summed_halves(
+        jnp.dot(scatter_sel[:node_count], both, preferred_element_type=jnp.float32)
+    )
+    own = main + summed_halves(
+        jnp.dot(face_put, high_low(from_prev), preferred_element_type=jnp.float32)
+    )
+    field = current[:node_count]
+    applied = wide_mass[:node_count, None] * own + wide_potential[:node_count, None] * field
+    scaled = (applied - centre * field) / half_span
+    current = 2.0 * scaled - previous[:node_count]
     filtered = current[:node_count].astype(jnp.bfloat16)
     position = lax.axis_index("st") % 4
 

time: 65.2 us -> 71.1 us (1.090)
  other arithmetic: 7.43 us -> 11.3 us
  matrix products: 28.6 us -> 30.9 us
  waiting for transfers between devices: 11.6 us -> 9.69 us
  local copies, waits for them, and re-layouts: 4.35 us -> 5.78 us
    dot_general x0 -> x5, matrix products: none -> 10.4 us  [the longest x1 6.11 us: body(): lax.dot_general(scatter_sel, weighted, (((0,), (0,)), ((), ())), preferre...]
    eq x0 -> x1, other arithmetic: none -> 5.91 us  [body(): scatter_sel = (wide_ids == cell_rows[None, :]).astype(jnp.bfloat16)]
    ppermute x8 -> x7, waiting for transfers between devices: 3.85 us -> 0.64 us  [ring(): return lax.ppermute(block, axis, route)]
    dot_general x3 -> x2, matrix products: 8.99 us -> 6.04 us  [operate(): jnp.dot(scatter_sel, both, preferred_element_type=jnp.float32)]
    dot_general x3 -> x2, matrix products: 7.05 us -> 4.69 us  [operate(): lax.dot_general(scatter_sel, weighted, (((0,), (0,)), ((), ())), preferre...]
    dot_general x3 -> x2, matrix products: 4.46 us -> 2.98 us  [operate(): jnp.einsum('ij,cjb->cib', padded_matrix, values, preferred_element_type=j...]
    ppermute x3, waiting for transfers between devices: 7.72 us -> 9.06 us  [from_partner(): return lax.ppermute(block, axis, route)]
    sub x3 -> x2, other arithmetic: 3.86 us -> 2.58 us  [chebyshev_step(): return (current, gain * scaled - keep * previous)]
  transfers between devices with their start and end apart: 11 -> 10, of which waited for: 6 -> 3; matrix products, arithmetic and copies ran while one was open for 27% -> 29% of each run, Pallas kernels for 0% -> 0%
where the time goes in v15:
time: 71.1 us; the launch traced here: 70.8 us
  matrix products  30.9 us (43%)
  starting transfers between devices  12.2 us (17%)
  other arithmetic  11.3 us (16%)
  waiting for transfers between devices  9.69 us (14%)
  local copies, waits for them, and re-layouts  5.78 us (8%)
    ppermute x7, starting transfers between devices, ring(): return lax.ppermute(block, axis, route)  10.6 us
    ppermute x3, waiting for transfers between devices, from_partner(): return lax.ppermute(block, axis, route)  9.06 us
    dot_general x1, matrix products, body(): lax.dot_general(scatter_sel, weighted, (((0,), (0,)), ((), ())), preferre...  6.11 us
    dot_general x2, matrix products, operate(): jnp.dot(scatter_sel, both, preferred_element_type=jnp.float32)  6.04 us
    eq x1, other arithmetic, body(): scatter_sel = (wide_ids == cell_rows[None, :]).astype(jnp.bfloat16)  5.91 us
    dot_general x2, matrix products, operate(): lax.dot_general(scatter_sel, weighted, (((0,), (0,)), ((), ())), preferre...  4.69 us
    dot_general x2, matrix products, operate(): jnp.einsum('ij,cjb->cib', padded_matrix, values, preferred_element_type=j...  2.98 us
    dot_general x1, matrix products, body(): jnp.dot(scatter_sel[:node_count], both, preferred_element_type=jnp.float32)  2.87 us
  transfers between devices with their start and end apart: 10, of which 3 were waited for; matrix products, arithmetic and copies ran while one was open for 29% of the time, Pallas kernels for 0%

profile of v15, /device:TPU:0, one launch (start us, length us, event | category | flops | bytes accessed | tf_op | source)
XLA Modules:
  0.0 70.8 jit_solution(7843550586467206246)
XLA Ops:
  1.5 1.4 %fusion.48 = f32[2,144]{1,0:T(2,128)S(1)} fusion(s32[144]{0:T(256)} %param.14, s32[1728]{0:T(1024)S(1)} %add_reduce_fusion, f32[1,1728]{1,0:T(1,128)S(1)} %stack.10, f32[1,1728]{1,0:T(1,128)S(1)} %stack.9), kind=kOutput, calls=%fused_computation.57 | convolution fusion | flops 6224256 | bytes 22464 | tf_op jit(solution)/shard_map/dot_general | solution.py:58
  2.8 3.9 %collective-permute-start.2 = (f32[2,144]{1,0:T(2,128)S(1)}, f32[2,144]{1,0:T(2,128)S(1)}, u32[]{:S(2)}, u32[]{:S(2)}) collective-permute-start(f32[2,144]{1,0:T(2,128)S(1)} %fusion.48), channel_id=1, source_target_pairs={{0,24},{8,0},{16,8},{24,16},{1,25},{9,1},{17,9},{25,17},{2,26},{10... | collective-permute-start | bytes 3464 | tf_op jit(solution)/shard_map/ppermute | solution.py:16
  6.7 1.4 %fusion.53 = f32[144,128]{1,0:T(8,128)S(1)} fusion(bf16[1728,128]{1,0:T(8,128)(2,1)} %param.9, s32[1728]{0:T(1024)S(1)} %add_reduce_fusion, s32[144]{0:T(256)} %param.14), kind=kOutput, calls=%fused_computation.65 | convolution fusion | flops 63949824 | bytes 523584 | tf_op jit(solution)/shard_map/dot_general | solution.py:57
  9.5 5.9 %iota_compare_fusion.1 = pred[1872,2816]{1,0:T(8,128)(4,1)} fusion(s32[2816]{0:T(1024)S(1)} %eq.68), kind=kLoop, calls=%fused_computation.48 | loop fusion | flops 5271552 | bytes 5282816 | tf_op jit(solution)/shard_map/eq | solution.py:51
  16.7 27.2 %while.17 = (s32[]{:T(128)}, f32[1872,128]{1,0:T(8,128)S(1)}, f32[1872,128]{1,0:T(8,128)S(1)}, f32[1872]{0:T(1024)S(1)}, bf16[352,352]{1,0:T(8,128)(2,1)}, /*ind...) while((s32[]{:T(128)}, f32[1872,128]{1,0:T(8,128)S(1)}, ...), condition=%wide.region_1.2_spmd.clone.clone, body=%wide.region_0.1_spmd.clone.clone.sunk | while | flops 4879314944 | bytes 31196824 | solution.py:98
  16.9 2.3 %fusion.121 = bf16[2816,128]{0,1:T(8,128)(2,1)S(1)} fusion(s32[2816]{0:T(1024)S(1)} %get-tuple-element.362, f32[1872,128]{1,0:T(8,128)S(1)} %get-tuple-element.342, f32[1872]{0:T(1024)S(1)} %get-tuple-element.359), kind=kOutput, calls=%fused_computation.10.clone.1 | convolution fusion | flops 1360900096 | bytes 1698112 | tf_op jit(solution)/shard_map/while/body/eval_jaxpr/dot_general | solution.py:72
  19.6 1.5 %fusion.122 = f32[8,128,352]{1,2,0:T(8,128)S(1)} fusion(bf16[8,352,128]{2,1,0:T(8,128)(2,1)S(1)} %bitcast.52, bf16[352,352]{1,0:T(8,128)(2,1)} %get-tuple-element.360), kind=kOutput, calls=%fused_computation.35.clone.1 | convolution fusion | flops 253755392 | bytes 2410496 | tf_op jit(solution)/shard_map/while/body/eval_jaxpr/ij,cjb->cib/dot_general | solution.py:76
  22.0 1.5 %collective-permute-start.1 = (f32[144,128]{1,0:T(8,128)S(1)}, f32[144,128]{1,0:T(8,128)S(1)}, u32[]{:S(2)}, u32[]{:S(2)}) collective-permute-start(f32[144,128]{1,0:T(8,128)S(1)} %get-tuple-element.321), channel_id=1, source_target_pairs={{0,8},{8,16},{16,24},{24,0},{1,9},{9,17},{17,25},{25,1},{2,10},{10... | collective-permute-start | bytes 221192 | tf_op jit(solution)/shard_map/while/body/eval_jaxpr/ppermute | solution.py:16
  23.5 1.4 %collective-permute-start = (f32[144,128]{1,0:T(8,128)S(1)}, f32[144,128]{1,0:T(8,128)S(1)}, u32[]{:S(2)}, u32[]{:S(2)}) collective-permute-start(f32[144,128]{1,0:T(8,128)S(1)} %get-tuple-element.320), channel_id=1, source_target_pairs={{0,24},{8,0},{16,8},{24,16},{1,25},{9,1},{17,9},{25,17},{2,26},{10... | collective-permute-start | bytes 221192 | tf_op jit(solution)/shard_map/while/body/eval_jaxpr/ppermute | solution.py:16
  25.0 3.0 %fusion.125 = f32[1872,256]{1,0:T(8,128)S(1)} fusion(s32[2816]{0:T(1024)S(1)} %get-tuple-element.362, bf16[2816,128]{1,0:T(8,128)(2,1)S(1)} %get-tuple-element.318, bf16[2816,128]{1,0:T(8,128)(2,1)S(1)} %get-tuple-element.319), kind=kOutput, calls=%fused_computation.13.clone.1 | convolution fusion | flops 2712461312 | bytes 3369984 | tf_op jit(solution)/shard_map/while/body/eval_jaxpr/dot_general | solution.py:83
  28.8 1.3 %fusion.127 = f32[1872,128]{1,0:T(8,128)S(1)} fusion(f32[144,128]{1,0:T(8,128)S(1)} %slice_add_fusion.12, f32[1728,128]{1,0:T(8,128)S(1)} %fusion.126, f32[1872,128]{1,0:T(8,128)S(1)} %get-tuple-element.341, f32[1872,128]{1,0:T(8,128)S(1)} %get-tuple-element.342, f32[]{:T(128)S(6)} %select_n.45, f32[]{:T(128)S(6)} %mul.240, ...), kind=kLoop, calls=%fused_computation.28.clone.1 | loop fusion | flops 2156544 | bytes 3848840 | tf_op jit(solution)/shard_map/while/body/eval_jaxpr/sub | solution.py:96
  30.3 2.3 %fusion.121 = bf16[2816,128]{0,1:T(8,128)(2,1)S(1)} fusion(s32[2816]{0:T(1024)S(1)} %get-tuple-element.362, f32[1872,128]{1,0:T(8,128)S(1)} %get-tuple-element.342, f32[1872]{0:T(1024)S(1)} %get-tuple-element.359), kind=kOutput, calls=%fused_computation.10.clone.1 | convolution fusion | flops 1360900096 | bytes 1698112 | tf_op jit(solution)/shard_map/while/body/eval_jaxpr/dot_general | solution.py:72
  33.0 1.5 %fusion.122 = f32[8,128,352]{1,2,0:T(8,128)S(1)} fusion(bf16[8,352,128]{2,1,0:T(8,128)(2,1)S(1)} %bitcast.52, bf16[352,352]{1,0:T(8,128)(2,1)} %get-tuple-element.360), kind=kOutput, calls=%fused_computation.35.clone.1 | convolution fusion | flops 253755392 | bytes 2410496 | tf_op jit(solution)/shard_map/while/body/eval_jaxpr/ij,cjb->cib/dot_general | solution.py:76
  36.0 2.3 %collective-permute-start = (f32[144,128]{1,0:T(8,128)S(1)}, f32[144,128]{1,0:T(8,128)S(1)}, u32[]{:S(2)}, u32[]{:S(2)}) collective-permute-start(f32[144,128]{1,0:T(8,128)S(1)} %get-tuple-element.320), channel_id=1, source_target_pairs={{0,24},{8,0},{16,8},{24,16},{1,25},{9,1},{17,9},{25,17},{2,26},{10... | collective-permute-start | bytes 221192 | tf_op jit(solution)/shard_map/while/body/eval_jaxpr/ppermute | solution.py:16
  38.4 3.0 %fusion.125 = f32[1872,256]{1,0:T(8,128)S(1)} fusion(s32[2816]{0:T(1024)S(1)} %get-tuple-element.362, bf16[2816,128]{1,0:T(8,128)(2,1)S(1)} %get-tuple-element.318, bf16[2816,128]{1,0:T(8,128)(2,1)S(1)} %get-tuple-element.319), kind=kOutput, calls=%fused_computation.13.clone.1 | convolution fusion | flops 2712461312 | bytes 3369984 | tf_op jit(solution)/shard_map/while/body/eval_jaxpr/dot_general | solution.py:83
  42.2 1.3 %fusion.127 = f32[1872,128]{1,0:T(8,128)S(1)} fusion(f32[144,128]{1,0:T(8,128)S(1)} %slice_add_fusion.12, f32[1728,128]{1,0:T(8,128)S(1)} %fusion.126, f32[1872,128]{1,0:T(8,128)S(1)} %get-tuple-element.341, f32[1872,128]{1,0:T(8,128)S(1)} %get-tuple-element.342, f32[]{:T(128)S(6)} %select_n.45, f32[]{:T(128)S(6)} %mul.240, ...), kind=kLoop, calls=%fused_computation.28.clone.1 | loop fusion | flops 2156544 | bytes 3848840 | tf_op jit(solution)/shard_map/while/body/eval_jaxpr/sub | solution.py:96
  43.9 6.1 %convolution_convert_fusion = bf16[2816,128]{1,0:T(8,128)(2,1)S(1)} fusion(s32[2816]{0:T(1024)S(1)} %get-tuple-element.388, f32[1872,128]{1,0:T(8,128)S(1)} %get-tuple-element.160, f32[1872]{0:T(1024)S(1)} %get-tuple-element.383), kind=kOutput, calls=%fused_computation.51 | convolution fusion | flops 1355628544 | bytes 1698112 | tf_op jit(solution)/shard_map/dot_general | solution.py:103
  51.4 1.7 %copy-done.1 = pred[1872,2816]{1,0:T(8,128)(4,1)S(1)} copy-done((pred[1872,2816]{1,0:T(8,128)(4,1)S(1)}, pred[1872,2816]{1,0:T(8,128)(4,1)}, u32[]{:S(2)}) %copy-start.1) | copy-done | bytes 5271576
  53.0 2.9 %fusion.44 = f32[1728,256]{1,0:T(8,128)S(1)} fusion(pred[1872,2816]{1,0:T(8,128)(4,1)S(1)} %copy-done.1, bf16[2816,128]{1,0:T(8,128)(2,1)S(1)} %get-tuple-element.246, bf16[2816,128]{1,0:T(8,128)(2,1)S(1)} %get-tuple-element.245), kind=kOutput, calls=%fused_computation.49 | convolution fusion | flops 2494300160 | bytes 8077312 | tf_op jit(solution)/shard_map/dot_general | solution.py:116
  57.0 1.1 %fusion.61 = bf16[1728,128]{1,0:T(8,128)(2,1)S(1)} fusion(f32[1728,256]{1,0:T(8,128)S(1)} %fusion.46, f32[1728,256]{1,0:T(8,128)S(1)} %fusion.44, f32[1872,128]{1,0:T(8,128)S(1)} %get-tuple-element.161, f32[1872,128]{1,0:T(8,128)S(1)} %get-tuple-element.160, f32[1728]{0:T(1024)S(1)} %copy-done.5, f32[1728]{0:T(1024)S(1)} %copy-done.6), kind=kLoop, calls=%fused_computation.76 | loop fusion | flops 2433024 | bytes 5764608 | tf_op jit(solution)/shard_map/convert_element_type | solution.py:125
  58.1 1.6 %collective-permute-start.6 = (bf16[1728,128]{1,0:T(8,128)(2,1)S(1)}, bf16[1728,128]{1,0:T(8,128)(2,1)S(1)}, u32[]{:S(2)}, u32[]{:S(2)}) collective-permute-start(bf16[1728,128]{1,0:T(8,128)(2,1)S(1)} %fusion.61), channel_id=1, source_target_pairs={{0,2},{2,0},{1,3},{3,1},{4,6},{6,4},{5,7},{7,5},{8,10},{10,8},{9,1... | collective-permute-start | bytes 1327112 | tf_op jit(solution)/shard_map/ppermute | solution.py:26
  60.0 7.8 %collective-permute-done.6 = bf16[1728,128]{1,0:T(8,128)(2,1)S(1)} collective-permute-done((bf16[1728,128]{1,0:T(8,128)(2,1)S(1)}, bf16[1728,128]{1,0:T(8,128)(2,1)S(1)}, u32[]{:S(2)}, u32[]{:S(2)}) %collective-permute-start.6) | collective-permute-done | bytes 442400 | tf_op jit(solution)/shard_map/ppermute | solution.py:26
  68.3 1.3 %collective-permute-done.7 = bf16[1728,128]{1,0:T(8,128)(2,1)S(1)} collective-permute-done((bf16[1728,128]{1,0:T(8,128)(2,1)S(1)}, bf16[1728,128]{1,0:T(8,128)(2,1)S(1)}, u32[]{:S(2)}, u32[]{:S(2)}) %collective-permute-start.7) | collective-permute-done | bytes 442400 | tf_op jit(solution)/shard_map/ppermute | solution.py:26
  69.6 1.2 %convolution_add_fusion = f32[1728,128]{1,0:T(8,128)} fusion(f32[1728,128]{1,0:T(8,128)S(1)} %convolution_add_fusion.1, bf16[1728,128]{1,0:T(8,128)(2,1)S(1)} %collective-permute-done.7, bf16[512,128]{1,0:T(8,128)(2,1)S(1)} %copy-done, s32[]{:T(128)S(6)} %select_n.38), kind=kOutput, calls=%fused_computation.52 | convolution fusion | flops 56844288 | bytes 2244612 | tf_op jit(solution)/shard_map/dot_general | solution.py:137
  (76 shorter events, 12.2 us)
Async XLA Ops:
  0.0 59.7 %copy-start = (bf16[512,128]{1,0:T(8,128)(2,1)S(1)}, bf16[512,128]{1,0:T(8,128)(2,1)}, u32[]{:S(2)}) copy-start(bf16[512,128]{1,0:T(8,128)(2,1)} %param.15) | copy-start | bytes 393220
  2.8 13.6 %collective-permute-start.2 = (f32[2,144]{1,0:T(2,128)S(1)}, f32[2,144]{1,0:T(2,128)S(1)}, u32[]{:S(2)}, u32[]{:S(2)}) collective-permute-start(f32[2,144]{1,0:T(2,128)S(1)} %fusion.48), channel_id=1, source_target_pairs={{0,24},{8,0},{16,8},{24,16},{1,25},{9,1},{17,9},{25,17},{2,26},{10... | collective-permute-start | bytes 3464 | tf_op jit(solution)/shard_map/ppermute | solution.py:16
  8.1 8.4 %collective-permute-start.3 = (f32[144,128]{1,0:T(8,128)S(1)}, f32[144,128]{1,0:T(8,128)S(1)}, u32[]{:S(2)}, u32[]{:S(2)}) collective-permute-start(f32[144,128]{1,0:T(8,128)S(1)} %fusion.53), channel_id=1, source_target_pairs={{0,24},{8,0},{16,8},{24,16},{1,25},{9,1},{17,9},{25,17},{2,26},{10... | collective-permute-start | bytes 221192 | tf_op jit(solution)/shard_map/ppermute | solution.py:16
  9.5 5.9 %copy-start.7 = (s32[144]{0:T(256)S(1)}, s32[144]{0:T(256)}, u32[]{:S(2)}) copy-start(s32[144]{0:T(256)} %param.14) | copy-start | bytes 1732
  9.5 6.0 %copy-start.4 = (bf16[1728,128]{1,0:T(8,128)(2,1)S(1)}, bf16[1728,128]{1,0:T(8,128)(2,1)}, u32[]{:S(2)}) copy-start(bf16[1728,128]{1,0:T(8,128)(2,1)} %param.9) | copy-start | bytes 1327108
  9.5 6.1 %copy-start.2 = (bf16[343,343]{1,0:T(8,128)(2,1)S(1)}, bf16[343,343]{1,0:T(8,128)(2,1)}, u32[]{:S(2)}) copy-start(bf16[343,343]{1,0:T(8,128)(2,1)} %param.12) | copy-start | bytes 705898
  15.4 1.0 %copy-start.6 = (f32[1728]{0:T(1024)S(1)}, f32[1728]{0:T(1024)}, u32[]{:S(2)}) copy-start(f32[1728]{0:T(1024)} %param.10) | copy-start | bytes 20740
  15.4 1.0 %copy-start.5 = (f32[1728]{0:T(1024)S(1)}, f32[1728]{0:T(1024)}, u32[]{:S(2)}) copy-start(f32[1728]{0:T(1024)} %param.11) | copy-start | bytes 20740
  22.0 6.1 %collective-permute-start.1 = (f32[144,128]{1,0:T(8,128)S(1)}, f32[144,128]{1,0:T(8,128)S(1)}, u32[]{:S(2)}, u32[]{:S(2)}) collective-permute-start(f32[144,128]{1,0:T(8,128)S(1)} %get-tuple-element.321), channel_id=1, source_target_pairs={{0,8},{8,16},{16,24},{24,0},{1,9},{9,17},{17,25},{25,1},{2,10},{10... | collective-permute-start | bytes 221192 | tf_op jit(solution)/shard_map/while/body/eval_jaxpr/ppermute | solution.py:16
  23.5 5.2 %collective-permute-start = (f32[144,128]{1,0:T(8,128)S(1)}, f32[144,128]{1,0:T(8,128)S(1)}, u32[]{:S(2)}, u32[]{:S(2)}) collective-permute-start(f32[144,128]{1,0:T(8,128)S(1)} %get-tuple-element.320), channel_id=1, source_target_pairs={{0,24},{8,0},{16,8},{24,16},{1,25},{9,1},{17,9},{25,17},{2,26},{10... | collective-permute-start | bytes 221192 | tf_op jit(solution)/shard_map/while/body/eval_jaxpr/ppermute | solution.py:16
  35.4 6.1 %collective-permute-start.1 = (f32[144,128]{1,0:T(8,128)S(1)}, f32[144,128]{1,0:T(8,128)S(1)}, u32[]{:S(2)}, u32[]{:S(2)}) collective-permute-start(f32[144,128]{1,0:T(8,128)S(1)} %get-tuple-element.321), channel_id=1, source_target_pairs={{0,8},{8,16},{16,24},{24,0},{1,9},{9,17},{17,25},{25,1},{2,10},{10... | collective-permute-start | bytes 221192 | tf_op jit(solution)/shard_map/while/body/eval_jaxpr/ppermute | solution.py:16
  36.0 6.1 %collective-permute-start = (f32[144,128]{1,0:T(8,128)S(1)}, f32[144,128]{1,0:T(8,128)S(1)}, u32[]{:S(2)}, u32[]{:S(2)}) collective-permute-start(f32[144,128]{1,0:T(8,128)S(1)} %get-tuple-element.320), channel_id=1, source_target_pairs={{0,24},{8,0},{16,8},{24,16},{1,25},{9,1},{17,9},{25,17},{2,26},{10... | collective-permute-start | bytes 221192 | tf_op jit(solution)/shard_map/while/body/eval_jaxpr/ppermute | solution.py:16
  43.9 6.1 %copy-start.3 = (bf16[343,343]{1,0:T(8,128)(2,1)S(1)}, bf16[343,343]{1,0:T(8,128)(2,1)}, u32[]{:S(2)}) copy-start(bf16[343,343]{1,0:T(8,128)(2,1)} %param.12) | copy-start | bytes 705898
  50.5 2.5 %copy-start.1 = (pred[1872,2816]{1,0:T(8,128)(4,1)S(1)}, pred[1872,2816]{1,0:T(8,128)(4,1)}, u32[]{:S(2)}) copy-start(pred[1872,2816]{1,0:T(8,128)(4,1)} %iota_compare_fusion.1) | copy-start | bytes 15814660
  51.2 5.3 %collective-permute-start.4 = (f32[144,128]{1,0:T(8,128)S(1)}, f32[144,128]{1,0:T(8,128)S(1)}, u32[]{:S(2)}, u32[]{:S(2)}) collective-permute-start(f32[144,128]{1,0:T(8,128)S(1)} %slice_add_fusion.6), channel_id=1, source_target_pairs={{0,8},{8,16},{16,24},{24,0},{1,9},{9,17},{17,25},{25,1},{2,10},{10... | collective-permute-start | bytes 221192 | tf_op jit(solution)/shard_map/ppermute | solution.py:16
  58.1 9.7 %collective-permute-start.6 = (bf16[1728,128]{1,0:T(8,128)(2,1)S(1)}, bf16[1728,128]{1,0:T(8,128)(2,1)S(1)}, u32[]{:S(2)}, u32[]{:S(2)}) collective-permute-start(bf16[1728,128]{1,0:T(8,128)(2,1)S(1)} %fusion.61), channel_id=1, source_target_pairs={{0,2},{2,0},{1,3},{3,1},{4,6},{6,4},{5,7},{7,5},{8,10},{10,8},{9,1... | collective-permute-start | bytes 1327112 | tf_op jit(solution)/shard_map/ppermute | solution.py:26
  59.7 8.1 %collective-permute-start.5 = (bf16[1728,128]{1,0:T(8,128)(2,1)S(1)}, bf16[1728,128]{1,0:T(8,128)(2,1)S(1)}, u32[]{:S(2)}, u32[]{:S(2)}) collective-permute-start(bf16[1728,128]{1,0:T(8,128)(2,1)S(1)} %fusion.61), channel_id=1, source_target_pairs={{0,1},{1,0},{2,3},{3,2},{4,5},{5,4},{6,7},{7,6},{8,9},{9,8},{10,11... | collective-permute-start | bytes 1327112 | tf_op jit(solution)/shard_map/ppermute | solution.py:26
  67.8 1.8 %collective-permute-start.7 = (bf16[1728,128]{1,0:T(8,128)(2,1)S(1)}, bf16[1728,128]{1,0:T(8,128)(2,1)S(1)}, u32[]{:S(2)}, u32[]{:S(2)}) collective-permute-start(bf16[1728,128]{1,0:T(8,128)(2,1)S(1)} %collective-permute-done.6), channel_id=1, source_target_pairs={{0,1},{1,0},{2,3},{3,2},{4,5},{5,4},{6,7},{7,6},{8,9},{9,8},{10,11... | collective-permute-start | bytes 1327112 | tf_op jit(solution)/shard_map/ppermute | solution.py:26

commit v16 on v5

--- a/solution.py
+++ b/solution.py
@@ -77,9 +77,16 @@
             "ij,cjb->cib", padded_matrix, values, preferred_element_type=jnp.float32
         ).reshape(-1, state_count)
         both = high_low(products)
-        rim = summed_halves(jnp.dot(rim_sel, both, preferred_element_type=jnp.float32))
-        from_prev = ring(rim[face_count:], "dom", 1)
-        from_next = ring(rim[:face_count], "dom", -1)
+        ghost_part = summed_halves(
+            jnp.dot(rim_sel[face_count:], both, preferred_element_type=jnp.float32)
+        )
+        from_prev = ring(ghost_part, "dom", 1)
+        ghost_part, both = lax.optimization_barrier((ghost_part, both))
+        face_part = summed_halves(
+            jnp.dot(rim_sel[:face_count], both, preferred_element_type=jnp.float32)
+        )
+        from_next = ring(face_part, "dom", -1)
+        rim = jnp.concatenate([face_part, ghost_part], 0)
         main = summed_halves(jnp.dot(scatter_sel, both, preferred_element_type=jnp.float32))
         own = main[:node_count] + summed_halves(
             jnp.dot(face_put, high_low(from_prev), preferred_element_type=jnp.float32)

time: 65.2 us -> 71.4 us (1.095)
  local copies, waits for them, and re-layouts: 4.35 us -> 8.57 us
  starting transfers between devices: 12.4 us -> 15.2 us
  waiting for transfers between devices: 11.6 us -> 9.08 us
  other arithmetic: 7.43 us -> 8.43 us
    ppermute x8, waiting for transfers between devices: 3.85 us -> 0.02 us  [ring(): return lax.ppermute(block, axis, route)]
    while x6 -> x12, local copies, waits for them, and re-layouts: 0.38 us -> 3.93 us
    ppermute x8, starting transfers between devices: 10.7 us -> 13.6 us  [ring(): return lax.ppermute(block, axis, route)]
    convert_element_type x0 -> x1, other arithmetic: none -> 1.54 us  [body(): rim_sel = (rim_ids[:, None] == cell_rows[None, :]).astype(jnp.bfloat16)]
    ppermute x3, waiting for transfers between devices: 7.72 us -> 9.06 us  [from_partner(): return lax.ppermute(block, axis, route)]
    convert_element_type x1, other arithmetic: 1.07 us -> 0.06 us  [body(): field_start = jnp.concatenate([states.astype(jnp.float32), ghost_states], 0)]
    dot_general x3 -> x6, matrix products: 1.89 us -> 2.31 us  [the longest x3 1.17 us: operate(): jnp.dot(rim_sel[:face_count], both, preferred_element_type=jnp.float32)]
  transfers between devices with their start and end apart: 11 -> 11, of which waited for: 6 -> 2; matrix products, arithmetic and copies ran while one was open for 27% -> 29% of each run, Pallas kernels for 0% -> 0%
where the time goes in v16:
time: 71.4 us; the launch traced here: 70.9 us
  matrix products  29 us (41%)
  starting transfers between devices  15.2 us (21%)
  waiting for transfers between devices  9.08 us (13%)
  local copies, waits for them, and re-layouts  8.57 us (12%)
  other arithmetic  8.43 us (12%)
    ppermute x8, starting transfers between devices, ring(): return lax.ppermute(block, axis, route)  13.6 us
    ppermute x3, waiting for transfers between devices, from_partner(): return lax.ppermute(block, axis, route)  9.06 us
    dot_general x3, matrix products, operate(): jnp.dot(scatter_sel, both, preferred_element_type=jnp.float32)  9 us
    dot_general x3, matrix products, operate(): lax.dot_general(scatter_sel, weighted, (((0,), (0,)), ((), ())), preferre...  7.05 us
    dot_general x3, matrix products, operate(): jnp.einsum('ij,cjb->cib', padded_matrix, values, preferred_element_type=j...  4.46 us
    while x12, local copies, waits for them, and re-layouts  3.93 us
    sub x3, other arithmetic, chebyshev_step(): return (current, gain * scaled - keep * previous)  3.86 us
    ppermute x3, starting transfers between devices, from_partner(): return lax.ppermute(block, axis, route)  1.65 us
  transfers between devices with their start and end apart: 11, of which 2 were waited for; matrix products, arithmetic and copies ran while one was open for 29% of the time, Pallas kernels for 0%

profile of v16, /device:TPU:0, one launch (start us, length us, event | category | flops | bytes accessed | tf_op | source)
XLA Modules:
  0.0 70.9 jit_solution(15501391761717891553)
XLA Ops:
  0.0 1.4 %fusion.40 = f32[144,128]{1,0:T(8,128)S(1)} fusion(bf16[1728,128]{1,0:T(8,128)(2,1)} %param.9, s32[1728]{0:T(1024)S(1)} %add_reduce_fusion, s32[144]{0:T(256)} %param.14), kind=kOutput, calls=%fused_computation.51 | convolution fusion | flops 63949824 | bytes 523584 | tf_op jit(solution)/shard_map/dot_general | solution.py:57
  1.5 3.9 %collective-permute-start.2 = (f32[144,128]{1,0:T(8,128)S(1)}, f32[144,128]{1,0:T(8,128)S(1)}, u32[]{:S(2)}, u32[]{:S(2)}) collective-permute-start(f32[144,128]{1,0:T(8,128)S(1)} %fusion.40), channel_id=1, source_target_pairs={{0,24},{8,0},{16,8},{24,16},{1,25},{9,1},{17,9},{25,17},{2,26},{10... | collective-permute-start | bytes 221192 | tf_op jit(solution)/shard_map/ppermute | solution.py:16
  6.8 1.4 %fusion.38 = f32[2,144]{1,0:T(2,128)S(1)} fusion(s32[144]{0:T(256)} %param.14, s32[1728]{0:T(1024)S(1)} %add_reduce_fusion, f32[1,1728]{1,0:T(1,128)S(1)} %stack.10, f32[1,1728]{1,0:T(1,128)S(1)} %stack.9), kind=kOutput, calls=%fused_computation.49 | convolution fusion | flops 6224256 | bytes 22464 | tf_op jit(solution)/shard_map/dot_general | solution.py:58
  10.3 1.5 %compare_convert_fusion.2 = bf16[288,2816]{1,0:T(8,128)(2,1)} fusion(s32[2816]{0:T(1024)S(1)} %eq.75, s32[288]{0:T(512)S(1)} %pad_add_fusion), kind=kLoop, calls=%fused_computation.45 | loop fusion | flops 1622016 | bytes 1634432 | tf_op jit(solution)/shard_map/convert_element_type | solution.py:53
  13.5 44.6 %while.16 = (s32[]{:T(128)}, f32[1872,128]{1,0:T(8,128)S(1)}, f32[1872,128]{1,0:T(8,128)S(1)}, f32[1872]{0:T(1024)S(1)}, bf16[352,352]{1,0:T(8,128)(2,1)}, /*ind...) while((s32[]{:T(128)}, f32[1872,128]{1,0:T(8,128)S(1)}, ...), condition=%wide.region_1.2_spmd.clone, body=%wide.region_0.1_spmd.clone.sunk | while | flops 4877692928 | bytes 43324988 | solution.py:105
  13.5 2.3 %fusion.91 = bf16[2816,128]{0,1:T(8,128)(2,1)S(1)} fusion(s32[2816]{0:T(1024)S(1)} %get-tuple-element.326, f32[1872,128]{1,0:T(8,128)S(1)} %get-tuple-element.305, f32[1872]{0:T(1024)S(1)} %get-tuple-element.322), kind=kOutput, calls=%fused_computation.9.clone.1 | convolution fusion | flops 1360900096 | bytes 1698112 | tf_op jit(solution)/shard_map/while/body/eval_jaxpr/dot_general | solution.py:72
  16.2 1.5 %fusion.92 = f32[8,128,352]{1,2,0:T(8,128)S(1)} fusion(bf16[8,352,128]{2,1,0:T(8,128)(2,1)S(1)} %bitcast.51, bf16[352,352]{1,0:T(8,128)(2,1)} %get-tuple-element.323), kind=kOutput, calls=%fused_computation.33.clone.1 | convolution fusion | flops 253755392 | bytes 2410496 | tf_op jit(solution)/shard_map/while/body/eval_jaxpr/ij,cjb->cib/dot_general | solution.py:76
  19.5 1.5 %collective-permute-start.1 = (f32[144,128]{1,0:T(8,128)S(1)}, f32[144,128]{1,0:T(8,128)S(1)}, u32[]{:S(2)}, u32[]{:S(2)}) collective-permute-start(f32[144,128]{1,0:T(8,128)S(1)} %slice_add_fusion.9), channel_id=1, source_target_pairs={{0,8},{8,16},{16,24},{24,0},{1,9},{9,17},{17,25},{25,1},{2,10},{10... | collective-permute-start | bytes 221192 | tf_op jit(solution)/shard_map/while/body/eval_jaxpr/ppermute | solution.py:16
  21.6 1.5 %collective-permute-start = (f32[144,128]{1,0:T(8,128)S(1)}, f32[144,128]{1,0:T(8,128)S(1)}, u32[]{:S(2)}, u32[]{:S(2)}) collective-permute-start(f32[144,128]{1,0:T(8,128)S(1)} %slice_add_fusion.10), channel_id=1, source_target_pairs={{0,24},{8,0},{16,8},{24,16},{1,25},{9,1},{17,9},{25,17},{2,26},{10... | collective-permute-start | bytes 221192 | tf_op jit(solution)/shard_map/while/body/eval_jaxpr/ppermute | solution.py:16
  23.1 3.0 %fusion.93 = f32[1872,256]{1,0:T(8,128)S(1)} fusion(bf16[2816,256]{1,0:T(8,128)(2,1)S(1)} %pad_maximum_fusion.8, s32[2816]{0:T(1024)S(1)} %get-tuple-element.326), kind=kOutput, calls=%fused_computation.11.clone.1 | convolution fusion | flops 2709577728 | bytes 3369984 | tf_op jit(solution)/shard_map/while/body/eval_jaxpr/dot_general | solution.py:90
  26.9 1.3 %fusion.95 = f32[1872,128]{1,0:T(8,128)S(1)} fusion(f32[144,128]{1,0:T(8,128)S(1)} %slice_add_fusion.12, f32[1728,128]{1,0:T(8,128)S(1)} %fusion.94, f32[1872,128]{1,0:T(8,128)S(1)} %get-tuple-element.304, f32[1872,128]{1,0:T(8,128)S(1)} %get-tuple-element.305, f32[]{:T(128)S(6)} %select_n.43, f32[]{:T(128)S(6)} %mul.160, ...), kind=kLoop, calls=%fused_computation.24.clone.1 | loop fusion | flops 2156544 | bytes 3848840 | tf_op jit(solution)/shard_map/while/body/eval_jaxpr/sub | solution.py:103
  28.4 2.4 %fusion.91 = bf16[2816,128]{0,1:T(8,128)(2,1)S(1)} fusion(s32[2816]{0:T(1024)S(1)} %get-tuple-element.326, f32[1872,128]{1,0:T(8,128)S(1)} %get-tuple-element.305, f32[1872]{0:T(1024)S(1)} %get-tuple-element.322), kind=kOutput, calls=%fused_computation.9.clone.1 | convolution fusion | flops 1360900096 | bytes 1698112 | tf_op jit(solution)/shard_map/while/body/eval_jaxpr/dot_general | solution.py:72
  31.1 1.5 %fusion.92 = f32[8,128,352]{1,2,0:T(8,128)S(1)} fusion(bf16[8,352,128]{2,1,0:T(8,128)(2,1)S(1)} %bitcast.51, bf16[352,352]{1,0:T(8,128)(2,1)} %get-tuple-element.323), kind=kOutput, calls=%fused_computation.33.clone.1 | convolution fusion | flops 253755392 | bytes 2410496 | tf_op jit(solution)/shard_map/while/body/eval_jaxpr/ij,cjb->cib/dot_general | solution.py:76
  35.6 2.4 %collective-permute-start = (f32[144,128]{1,0:T(8,128)S(1)}, f32[144,128]{1,0:T(8,128)S(1)}, u32[]{:S(2)}, u32[]{:S(2)}) collective-permute-start(f32[144,128]{1,0:T(8,128)S(1)} %slice_add_fusion.10), channel_id=1, source_target_pairs={{0,24},{8,0},{16,8},{24,16},{1,25},{9,1},{17,9},{25,17},{2,26},{10... | collective-permute-start | bytes 221192 | tf_op jit(solution)/shard_map/while/body/eval_jaxpr/ppermute | solution.py:16
  38.0 3.0 %fusion.93 = f32[1872,256]{1,0:T(8,128)S(1)} fusion(bf16[2816,256]{1,0:T(8,128)(2,1)S(1)} %pad_maximum_fusion.8, s32[2816]{0:T(1024)S(1)} %get-tuple-element.326), kind=kOutput, calls=%fused_computation.11.clone.1 | convolution fusion | flops 2709577728 | bytes 3369984 | tf_op jit(solution)/shard_map/while/body/eval_jaxpr/dot_general | solution.py:90
  41.8 1.3 %fusion.95 = f32[1872,128]{1,0:T(8,128)S(1)} fusion(f32[144,128]{1,0:T(8,128)S(1)} %slice_add_fusion.12, f32[1728,128]{1,0:T(8,128)S(1)} %fusion.94, f32[1872,128]{1,0:T(8,128)S(1)} %get-tuple-element.304, f32[1872,128]{1,0:T(8,128)S(1)} %get-tuple-element.305, f32[]{:T(128)S(6)} %select_n.43, f32[]{:T(128)S(6)} %mul.160, ...), kind=kLoop, calls=%fused_computation.24.clone.1 | loop fusion | flops 2156544 | bytes 3848840 | tf_op jit(solution)/shard_map/while/body/eval_jaxpr/sub | solution.py:103
  43.2 2.4 %fusion.91 = bf16[2816,128]{0,1:T(8,128)(2,1)S(1)} fusion(s32[2816]{0:T(1024)S(1)} %get-tuple-element.326, f32[1872,128]{1,0:T(8,128)S(1)} %get-tuple-element.305, f32[1872]{0:T(1024)S(1)} %get-tuple-element.322), kind=kOutput, calls=%fused_computation.9.clone.1 | convolution fusion | flops 1360900096 | bytes 1698112 | tf_op jit(solution)/shard_map/while/body/eval_jaxpr/dot_general | solution.py:72
  45.9 1.5 %fusion.92 = f32[8,128,352]{1,2,0:T(8,128)S(1)} fusion(bf16[8,352,128]{2,1,0:T(8,128)(2,1)S(1)} %bitcast.51, bf16[352,352]{1,0:T(8,128)(2,1)} %get-tuple-element.323), kind=kOutput, calls=%fused_computation.33.clone.1 | convolution fusion | flops 253755392 | bytes 2410496 | tf_op jit(solution)/shard_map/while/body/eval_jaxpr/ij,cjb->cib/dot_general | solution.py:76
  50.0 2.9 %collective-permute-start = (f32[144,128]{1,0:T(8,128)S(1)}, f32[144,128]{1,0:T(8,128)S(1)}, u32[]{:S(2)}, u32[]{:S(2)}) collective-permute-start(f32[144,128]{1,0:T(8,128)S(1)} %slice_add_fusion.10), channel_id=1, source_target_pairs={{0,24},{8,0},{16,8},{24,16},{1,25},{9,1},{17,9},{25,17},{2,26},{10... | collective-permute-start | bytes 221192 | tf_op jit(solution)/shard_map/while/body/eval_jaxpr/ppermute | solution.py:16
  52.9 3.0 %fusion.93 = f32[1872,256]{1,0:T(8,128)S(1)} fusion(bf16[2816,256]{1,0:T(8,128)(2,1)S(1)} %pad_maximum_fusion.8, s32[2816]{0:T(1024)S(1)} %get-tuple-element.326), kind=kOutput, calls=%fused_computation.11.clone.1 | convolution fusion | flops 2709577728 | bytes 3369984 | tf_op jit(solution)/shard_map/while/body/eval_jaxpr/dot_general | solution.py:90
  56.7 1.3 %fusion.95 = f32[1872,128]{1,0:T(8,128)S(1)} fusion(f32[144,128]{1,0:T(8,128)S(1)} %slice_add_fusion.12, f32[1728,128]{1,0:T(8,128)S(1)} %fusion.94, f32[1872,128]{1,0:T(8,128)S(1)} %get-tuple-element.304, f32[1872,128]{1,0:T(8,128)S(1)} %get-tuple-element.305, f32[]{:T(128)S(6)} %select_n.43, f32[]{:T(128)S(6)} %mul.160, ...), kind=kLoop, calls=%fused_computation.24.clone.1 | loop fusion | flops 2156544 | bytes 3848840 | tf_op jit(solution)/shard_map/while/body/eval_jaxpr/sub | solution.py:103
  58.2 1.6 %collective-permute-start.5 = (bf16[1728,128]{1,0:T(8,128)(2,1)S(1)}, bf16[1728,128]{1,0:T(8,128)(2,1)S(1)}, u32[]{:S(2)}, u32[]{:S(2)}) collective-permute-start(bf16[1728,128]{1,0:T(8,128)(2,1)S(1)} %slice.150), channel_id=1, source_target_pairs={{0,2},{2,0},{1,3},{3,1},{4,6},{6,4},{5,7},{7,5},{8,10},{10,8},{9,1... | collective-permute-start | bytes 1327112 | tf_op jit(solution)/shard_map/ppermute | solution.py:26
  60.1 7.8 %collective-permute-done.5 = bf16[1728,128]{1,0:T(8,128)(2,1)S(1)} collective-permute-done((bf16[1728,128]{1,0:T(8,128)(2,1)S(1)}, bf16[1728,128]{1,0:T(8,128)(2,1)S(1)}, u32[]{:S(2)}, u32[]{:S(2)}) %collective-permute-start.5) | collective-permute-done | bytes 442400 | tf_op jit(solution)/shard_map/ppermute | solution.py:26
  68.5 1.2 %collective-permute-done.6 = bf16[1728,128]{1,0:T(8,128)(2,1)S(1)} collective-permute-done((bf16[1728,128]{1,0:T(8,128)(2,1)S(1)}, bf16[1728,128]{1,0:T(8,128)(2,1)S(1)}, u32[]{:S(2)}, u32[]{:S(2)}) %collective-permute-start.6) | collective-permute-done | bytes 442400 | tf_op jit(solution)/shard_map/ppermute | solution.py:26
  (92 shorter events, 18.6 us)
Async XLA Ops:
  0.0 59.8 %copy-start = (bf16[512,128]{1,0:T(8,128)(2,1)S(1)}, bf16[512,128]{1,0:T(8,128)(2,1)}, u32[]{:S(2)}) copy-start(bf16[512,128]{1,0:T(8,128)(2,1)} %param.15) | copy-start | bytes 393220
  0.0 11.9 %copy-start.2 = (bf16[1728,128]{1,0:T(8,128)(2,1)S(1)}, bf16[1728,128]{1,0:T(8,128)(2,1)}, u32[]{:S(2)}) copy-start(bf16[1728,128]{1,0:T(8,128)(2,1)} %param.9) | copy-start | bytes 1327108
  1.5 11.3 %collective-permute-start.2 = (f32[144,128]{1,0:T(8,128)S(1)}, f32[144,128]{1,0:T(8,128)S(1)}, u32[]{:S(2)}, u32[]{:S(2)}) collective-permute-start(f32[144,128]{1,0:T(8,128)S(1)} %fusion.40), channel_id=1, source_target_pairs={{0,24},{8,0},{16,8},{24,16},{1,25},{9,1},{17,9},{25,17},{2,26},{10... | collective-permute-start | bytes 221192 | tf_op jit(solution)/shard_map/ppermute | solution.py:16
  6.8 5.1 %copy-start.3 = (bf16[343,343]{1,0:T(8,128)(2,1)S(1)}, bf16[343,343]{1,0:T(8,128)(2,1)}, u32[]{:S(2)}) copy-start(bf16[343,343]{1,0:T(8,128)(2,1)} %param.12) | copy-start | bytes 705898
  8.2 4.5 %collective-permute-start.3 = (f32[2,144]{1,0:T(2,128)S(1)}, f32[2,144]{1,0:T(2,128)S(1)}, u32[]{:S(2)}, u32[]{:S(2)}) collective-permute-start(f32[2,144]{1,0:T(2,128)S(1)} %fusion.38), channel_id=1, source_target_pairs={{0,24},{8,0},{16,8},{24,16},{1,25},{9,1},{17,9},{25,17},{2,26},{10... | collective-permute-start | bytes 3464 | tf_op jit(solution)/shard_map/ppermute | solution.py:16
  9.5 3.2 %copy-start.5 = (f32[1728]{0:T(1024)S(1)}, f32[1728]{0:T(1024)}, u32[]{:S(2)}) copy-start(f32[1728]{0:T(1024)} %param.11) | copy-start | bytes 20740
  9.5 3.2 %copy-start.6 = (f32[1728]{0:T(1024)S(1)}, f32[1728]{0:T(1024)}, u32[]{:S(2)}) copy-start(f32[1728]{0:T(1024)} %param.10) | copy-start | bytes 20740
  12.8 0.7 copy-start.4
  17.7 1.4 %copy-start.1 = (bf16[288,2816]{1,0:T(8,128)(2,1)S(1)}, bf16[288,2816]{1,0:T(8,128)(2,1)}, u32[]{:S(2)}) copy-start(bf16[288,2816]{1,0:T(8,128)(2,1)} %get-tuple-element.324) | copy-start | bytes 4866052 | tf_op jit(solution)/shard_map/while
  19.5 6.7 %collective-permute-start.1 = (f32[144,128]{1,0:T(8,128)S(1)}, f32[144,128]{1,0:T(8,128)S(1)}, u32[]{:S(2)}, u32[]{:S(2)}) collective-permute-start(f32[144,128]{1,0:T(8,128)S(1)} %slice_add_fusion.9), channel_id=1, source_target_pairs={{0,8},{8,16},{16,24},{24,0},{1,9},{9,17},{17,25},{25,1},{2,10},{10... | collective-permute-start | bytes 221192 | tf_op jit(solution)/shard_map/while/body/eval_jaxpr/ppermute | solution.py:16
  21.6 5.2 %collective-permute-start = (f32[144,128]{1,0:T(8,128)S(1)}, f32[144,128]{1,0:T(8,128)S(1)}, u32[]{:S(2)}, u32[]{:S(2)}) collective-permute-start(f32[144,128]{1,0:T(8,128)S(1)} %slice_add_fusion.10), channel_id=1, source_target_pairs={{0,24},{8,0},{16,8},{24,16},{1,25},{9,1},{17,9},{25,17},{2,26},{10... | collective-permute-start | bytes 221192 | tf_op jit(solution)/shard_map/while/body/eval_jaxpr/ppermute | solution.py:16
  32.6 1.4 %copy-start.1 = (bf16[288,2816]{1,0:T(8,128)(2,1)S(1)}, bf16[288,2816]{1,0:T(8,128)(2,1)}, u32[]{:S(2)}) copy-start(bf16[288,2816]{1,0:T(8,128)(2,1)} %get-tuple-element.324) | copy-start | bytes 4866052 | tf_op jit(solution)/shard_map/while
  34.4 6.7 %collective-permute-start.1 = (f32[144,128]{1,0:T(8,128)S(1)}, f32[144,128]{1,0:T(8,128)S(1)}, u32[]{:S(2)}, u32[]{:S(2)}) collective-permute-start(f32[144,128]{1,0:T(8,128)S(1)} %slice_add_fusion.9), channel_id=1, source_target_pairs={{0,8},{8,16},{16,24},{24,0},{1,9},{9,17},{17,25},{25,1},{2,10},{10... | collective-permute-start | bytes 221192 | tf_op jit(solution)/shard_map/while/body/eval_jaxpr/ppermute | solution.py:16
  35.6 6.1 %collective-permute-start = (f32[144,128]{1,0:T(8,128)S(1)}, f32[144,128]{1,0:T(8,128)S(1)}, u32[]{:S(2)}, u32[]{:S(2)}) collective-permute-start(f32[144,128]{1,0:T(8,128)S(1)} %slice_add_fusion.10), channel_id=1, source_target_pairs={{0,24},{8,0},{16,8},{24,16},{1,25},{9,1},{17,9},{25,17},{2,26},{10... | collective-permute-start | bytes 221192 | tf_op jit(solution)/shard_map/while/body/eval_jaxpr/ppermute | solution.py:16
  47.4 1.4 %copy-start.1 = (bf16[288,2816]{1,0:T(8,128)(2,1)S(1)}, bf16[288,2816]{1,0:T(8,128)(2,1)}, u32[]{:S(2)}) copy-start(bf16[288,2816]{1,0:T(8,128)(2,1)} %get-tuple-element.324) | copy-start | bytes 4866052 | tf_op jit(solution)/shard_map/while
  49.3 6.7 %collective-permute-start.1 = (f32[144,128]{1,0:T(8,128)S(1)}, f32[144,128]{1,0:T(8,128)S(1)}, u32[]{:S(2)}, u32[]{:S(2)}) collective-permute-start(f32[144,128]{1,0:T(8,128)S(1)} %slice_add_fusion.9), channel_id=1, source_target_pairs={{0,8},{8,16},{16,24},{24,0},{1,9},{9,17},{17,25},{25,1},{2,10},{10... | collective-permute-start | bytes 221192 | tf_op jit(solution)/shard_map/while/body/eval_jaxpr/ppermute | solution.py:16
  50.0 6.7 %collective-permute-start = (f32[144,128]{1,0:T(8,128)S(1)}, f32[144,128]{1,0:T(8,128)S(1)}, u32[]{:S(2)}, u32[]{:S(2)}) collective-permute-start(f32[144,128]{1,0:T(8,128)S(1)} %slice_add_fusion.10), channel_id=1, source_target_pairs={{0,24},{8,0},{16,8},{24,16},{1,25},{9,1},{17,9},{25,17},{2,26},{10... | collective-permute-start | bytes 221192 | tf_op jit(solution)/shard_map/while/body/eval_jaxpr/ppermute | solution.py:16
  58.2 9.7 %collective-permute-start.5 = (bf16[1728,128]{1,0:T(8,128)(2,1)S(1)}, bf16[1728,128]{1,0:T(8,128)(2,1)S(1)}, u32[]{:S(2)}, u32[]{:S(2)}) collective-permute-start(bf16[1728,128]{1,0:T(8,128)(2,1)S(1)} %slice.150), channel_id=1, source_target_pairs={{0,2},{2,0},{1,3},{3,1},{4,6},{6,4},{5,7},{7,5},{8,10},{10,8},{9,1... | collective-permute-start | bytes 1327112 | tf_op jit(solution)/shard_map/ppermute | solution.py:26
  59.8 8.1 %collective-permute-start.4 = (bf16[1728,128]{1,0:T(8,128)(2,1)S(1)}, bf16[1728,128]{1,0:T(8,128)(2,1)S(1)}, u32[]{:S(2)}, u32[]{:S(2)}) collective-permute-start(bf16[1728,128]{1,0:T(8,128)(2,1)S(1)} %slice.150), channel_id=1, source_target_pairs={{0,1},{1,0},{2,3},{3,2},{4,5},{5,4},{6,7},{7,6},{8,9},{9,8},{10,11... | collective-permute-start | bytes 1327112 | tf_op jit(solution)/shard_map/ppermute | solution.py:26
  67.9 1.8 %collective-permute-start.6 = (bf16[1728,128]{1,0:T(8,128)(2,1)S(1)}, bf16[1728,128]{1,0:T(8,128)(2,1)S(1)}, u32[]{:S(2)}, u32[]{:S(2)}) collective-permute-start(bf16[1728,128]{1,0:T(8,128)(2,1)S(1)} %collective-permute-done.5), channel_id=1, source_target_pairs={{0,1},{1,0},{2,3},{3,2},{4,5},{5,4},{6,7},{7,6},{8,9},{9,8},{10,11... | collective-permute-start | bytes 1327112 | tf_op jit(solution)/shard_map/ppermute | solution.py:26

commit v17 on v5

--- a/solution.py
+++ b/solution.py
@@ -77,9 +77,9 @@
             "ij,cjb->cib", padded_matrix, values, preferred_element_type=jnp.float32
         ).reshape(-1, state_count)
         both = high_low(products)
-        rim = summed_halves(jnp.dot(rim_sel, both, preferred_element_type=jnp.float32))
-        from_prev = ring(rim[face_count:], "dom", 1)
-        from_next = ring(rim[:face_count], "dom", -1)
+        rim = jnp.dot(rim_sel, both, preferred_element_type=jnp.float32)
+        from_prev = summed_halves(ring(rim[face_count:], "dom", 1))
+        from_next = summed_halves(ring(rim[:face_count], "dom", -1))
         main = summed_halves(jnp.dot(scatter_sel, both, preferred_element_type=jnp.float32))
         own = main[:node_count] + summed_halves(
             jnp.dot(face_put, high_low(from_prev), preferred_element_type=jnp.float32)

time: 65.2 us -> 71.8 us (1.10)
  waiting for transfers between devices: 11.6 us -> 16.4 us
  local copies, waits for them, and re-layouts: 4.35 us -> 6.35 us
    ppermute x8, waiting for transfers between devices: 3.85 us -> 8.53 us  [ring(): return lax.ppermute(block, axis, route)]
    slice x3, local copies, waits for them, and re-layouts: 0.04 us -> 2.04 us  [operate(): from_prev = summed_halves(ring(rim[face_count:], 'dom', 1))]
  transfers between devices with their start and end apart: 11 -> 11, of which waited for: 6 -> 6; matrix products, arithmetic and copies ran while one was open for 27% -> 24% of each run, Pallas kernels for 0% -> 0%
where the time goes in v17:
time: 71.8 us; the launch traced here: 71.4 us
  matrix products  28.5 us (40%)
  waiting for transfers between devices  16.4 us (23%)
  starting transfers between devices  12.2 us (17%)
  other arithmetic  7.42 us (10%)
  local copies, waits for them, and re-layouts  6.35 us (9%)
    ppermute x8, starting transfers between devices, ring(): return lax.ppermute(block, axis, route)  10.6 us
    dot_general x3, matrix products, operate(): jnp.dot(scatter_sel, both, preferred_element_type=jnp.float32)  8.98 us
    ppermute x8, waiting for transfers between devices, ring(): return lax.ppermute(block, axis, route)  8.53 us
    ppermute x3, waiting for transfers between devices, from_partner(): return lax.ppermute(block, axis, route)  7.91 us
    dot_general x3, matrix products, operate(): lax.dot_general(scatter_sel, weighted, (((0,), (0,)), ((), ())), preferre...  7.05 us
    dot_general x3, matrix products, operate(): jnp.einsum('ij,cjb->cib', padded_matrix, values, preferred_element_type=j...  4.46 us
    sub x3, other arithmetic, chebyshev_step(): return (current, gain * scaled - keep * previous)  3.86 us
    slice x3, local copies, waits for them, and re-layouts, operate(): from_prev = summed_halves(ring(rim[face_count:], 'dom', 1))  2.04 us
  transfers between devices with their start and end apart: 11, of which 6 were waited for; matrix products, arithmetic and copies ran while one was open for 24% of the time, Pallas kernels for 0%

profile of v17, /device:TPU:0, one launch (start us, length us, event | category | flops | bytes accessed | tf_op | source)
XLA Modules:
  0.0 71.4 jit_solution(3822245937682247892)
XLA Ops:
  0.1 1.4 %fusion.47 = f32[144,128]{1,0:T(8,128)S(1)} fusion(bf16[1728,128]{1,0:T(8,128)(2,1)} %param.9, s32[1728]{0:T(1024)S(1)} %add_reduce_fusion, s32[144]{0:T(256)} %param.14), kind=kOutput, calls=%fused_computation.54 | convolution fusion | flops 63949824 | bytes 523584 | tf_op jit(solution)/shard_map/dot_general | solution.py:57
  1.5 4.0 %collective-permute-start.2 = (f32[144,128]{1,0:T(8,128)S(1)}, f32[144,128]{1,0:T(8,128)S(1)}, u32[]{:S(2)}, u32[]{:S(2)}) collective-permute-start(f32[144,128]{1,0:T(8,128)S(1)} %fusion.47), channel_id=1, source_target_pairs={{0,24},{8,0},{16,8},{24,16},{1,25},{9,1},{17,9},{25,17},{2,26},{10... | collective-permute-start | bytes 221192 | tf_op jit(solution)/shard_map/ppermute | solution.py:16
  6.9 1.4 %fusion.45 = f32[2,144]{1,0:T(2,128)S(1)} fusion(s32[144]{0:T(256)} %param.14, s32[1728]{0:T(1024)S(1)} %add_reduce_fusion, f32[1,1728]{1,0:T(1,128)S(1)} %stack.10, f32[1,1728]{1,0:T(1,128)S(1)} %stack.9), kind=kOutput, calls=%fused_computation.52 | convolution fusion | flops 6224256 | bytes 22464 | tf_op jit(solution)/shard_map/dot_general | solution.py:58
  12.6 47.2 %while.17 = (s32[]{:T(128)}, f32[1872,128]{1,0:T(8,128)S(1)}, f32[1872,128]{1,0:T(8,128)S(1)}, f32[1872]{0:T(1024)S(1)}, bf16[352,352]{1,0:T(8,128)(2,1)}, /*ind...) while((s32[]{:T(128)}, f32[1872,128]{1,0:T(8,128)S(1)}, ...), condition=%wide.region_1.2_spmd.clone.clone, body=%wide.region_0.1_spmd.clone.clone.sunk | while | flops 4879314944 | bytes 31786656 | solution.py:98
  12.6 2.4 %fusion.92 = bf16[2816,128]{0,1:T(8,128)(2,1)S(1)} fusion(s32[2816]{0:T(1024)S(1)} %get-tuple-element.358, f32[1872,128]{1,0:T(8,128)S(1)} %get-tuple-element.338, f32[1872]{0:T(1024)S(1)} %get-tuple-element.355), kind=kOutput, calls=%fused_computation.10.clone.1 | convolution fusion | flops 1360900096 | bytes 1698112 | tf_op jit(solution)/shard_map/while/body/eval_jaxpr/dot_general | solution.py:72
  15.3 1.5 %fusion.93 = f32[8,128,352]{1,2,0:T(8,128)S(1)} fusion(bf16[8,352,128]{2,1,0:T(8,128)(2,1)S(1)} %bitcast.41, bf16[352,352]{1,0:T(8,128)(2,1)} %get-tuple-element.356), kind=kOutput, calls=%fused_computation.35.clone.1 | convolution fusion | flops 253755392 | bytes 2410496 | tf_op jit(solution)/shard_map/while/body/eval_jaxpr/ij,cjb->cib/dot_general | solution.py:76
  18.4 1.4 %collective-permute-start = (f32[144,256]{1,0:T(8,128)S(1)}, f32[144,256]{1,0:T(8,128)S(1)}, u32[]{:S(2)}, u32[]{:S(2)}) collective-permute-start(f32[144,256]{1,0:T(8,128)S(1)} %get-tuple-element.316), channel_id=1, source_target_pairs={{0,24},{8,0},{16,8},{24,16},{1,25},{9,1},{17,9},{25,17},{2,26},{10... | collective-permute-start | bytes 442376 | tf_op jit(solution)/shard_map/while/body/eval_jaxpr/ppermute | solution.py:16
  20.4 3.0 %fusion.96 = f32[1872,256]{1,0:T(8,128)S(1)} fusion(s32[2816]{0:T(1024)S(1)} %get-tuple-element.358, bf16[2816,128]{1,0:T(8,128)(2,1)S(1)} %get-tuple-element.314, bf16[2816,128]{1,0:T(8,128)(2,1)S(1)} %get-tuple-element.315), kind=kOutput, calls=%fused_computation.13.clone.1 | convolution fusion | flops 2712461312 | bytes 3369984 | tf_op jit(solution)/shard_map/while/body/eval_jaxpr/dot_general | solution.py:83
  23.5 3.1 %collective-permute-done.1 = f32[144,256]{1,0:T(8,128)S(1)} collective-permute-done((f32[144,256]{1,0:T(8,128)}, f32[144,256]{1,0:T(8,128)S(1)}, u32[]{:S(2)}, u32[]{:S(2)}) %collective-permute-start.1) | collective-permute-done | bytes 147488 | tf_op jit(solution)/shard_map/while/body/eval_jaxpr/ppermute | solution.py:16
  27.3 1.3 %fusion.99 = f32[1872,128]{1,0:T(8,128)S(1)} fusion(f32[144,128]{1,0:T(8,128)S(1)} %fusion.97, f32[1728,128]{1,0:T(8,128)S(1)} %fusion.98, f32[1872,128]{1,0:T(8,128)S(1)} %get-tuple-element.337, f32[1872,128]{1,0:T(8,128)S(1)} %get-tuple-element.338, f32[]{:T(128)S(6)} %select_n.45, f32[]{:T(128)S(6)} %mul.171, f32[1872]{0:T(1024)S(1)} %get-tuple-element.357, ...), kind=kLoop, calls=%fused_computation.28.clone.1 | loop fusion | flops 2156544 | bytes 3848840 | tf_op jit(solution)/shard_map/while/body/eval_jaxpr/sub | solution.py:96
  28.7 2.3 %fusion.92 = bf16[2816,128]{0,1:T(8,128)(2,1)S(1)} fusion(s32[2816]{0:T(1024)S(1)} %get-tuple-element.358, f32[1872,128]{1,0:T(8,128)S(1)} %get-tuple-element.338, f32[1872]{0:T(1024)S(1)} %get-tuple-element.355), kind=kOutput, calls=%fused_computation.10.clone.1 | convolution fusion | flops 1360900096 | bytes 1698112 | tf_op jit(solution)/shard_map/while/body/eval_jaxpr/dot_general | solution.py:72
  31.4 1.5 %fusion.93 = f32[8,128,352]{1,2,0:T(8,128)S(1)} fusion(bf16[8,352,128]{2,1,0:T(8,128)(2,1)S(1)} %bitcast.41, bf16[352,352]{1,0:T(8,128)(2,1)} %get-tuple-element.356), kind=kOutput, calls=%fused_computation.35.clone.1 | convolution fusion | flops 253755392 | bytes 2410496 | tf_op jit(solution)/shard_map/while/body/eval_jaxpr/ij,cjb->cib/dot_general | solution.py:76
  34.5 2.0 %collective-permute-start = (f32[144,256]{1,0:T(8,128)S(1)}, f32[144,256]{1,0:T(8,128)S(1)}, u32[]{:S(2)}, u32[]{:S(2)}) collective-permute-start(f32[144,256]{1,0:T(8,128)S(1)} %get-tuple-element.316), channel_id=1, source_target_pairs={{0,24},{8,0},{16,8},{24,16},{1,25},{9,1},{17,9},{25,17},{2,26},{10... | collective-permute-start | bytes 442376 | tf_op jit(solution)/shard_map/while/body/eval_jaxpr/ppermute | solution.py:16
  36.5 3.0 %fusion.96 = f32[1872,256]{1,0:T(8,128)S(1)} fusion(s32[2816]{0:T(1024)S(1)} %get-tuple-element.358, bf16[2816,128]{1,0:T(8,128)(2,1)S(1)} %get-tuple-element.314, bf16[2816,128]{1,0:T(8,128)(2,1)S(1)} %get-tuple-element.315), kind=kOutput, calls=%fused_computation.13.clone.1 | convolution fusion | flops 2712461312 | bytes 3369984 | tf_op jit(solution)/shard_map/while/body/eval_jaxpr/dot_general | solution.py:83
  39.6 3.5 %collective-permute-done.1 = f32[144,256]{1,0:T(8,128)S(1)} collective-permute-done((f32[144,256]{1,0:T(8,128)}, f32[144,256]{1,0:T(8,128)S(1)}, u32[]{:S(2)}, u32[]{:S(2)}) %collective-permute-start.1) | collective-permute-done | bytes 147488 | tf_op jit(solution)/shard_map/while/body/eval_jaxpr/ppermute | solution.py:16
  43.8 1.3 %fusion.99 = f32[1872,128]{1,0:T(8,128)S(1)} fusion(f32[144,128]{1,0:T(8,128)S(1)} %fusion.97, f32[1728,128]{1,0:T(8,128)S(1)} %fusion.98, f32[1872,128]{1,0:T(8,128)S(1)} %get-tuple-element.337, f32[1872,128]{1,0:T(8,128)S(1)} %get-tuple-element.338, f32[]{:T(128)S(6)} %select_n.45, f32[]{:T(128)S(6)} %mul.171, f32[1872]{0:T(1024)S(1)} %get-tuple-element.357, ...), kind=kLoop, calls=%fused_computation.28.clone.1 | loop fusion | flops 2156544 | bytes 3848840 | tf_op jit(solution)/shard_map/while/body/eval_jaxpr/sub | solution.py:96
  45.3 2.3 %fusion.92 = bf16[2816,128]{0,1:T(8,128)(2,1)S(1)} fusion(s32[2816]{0:T(1024)S(1)} %get-tuple-element.358, f32[1872,128]{1,0:T(8,128)S(1)} %get-tuple-element.338, f32[1872]{0:T(1024)S(1)} %get-tuple-element.355), kind=kOutput, calls=%fused_computation.10.clone.1 | convolution fusion | flops 1360900096 | bytes 1698112 | tf_op jit(solution)/shard_map/while/body/eval_jaxpr/dot_general | solution.py:72
  48.0 1.5 %fusion.93 = f32[8,128,352]{1,2,0:T(8,128)S(1)} fusion(bf16[8,352,128]{2,1,0:T(8,128)(2,1)S(1)} %bitcast.41, bf16[352,352]{1,0:T(8,128)(2,1)} %get-tuple-element.356), kind=kOutput, calls=%fused_computation.35.clone.1 | convolution fusion | flops 253755392 | bytes 2410496 | tf_op jit(solution)/shard_map/while/body/eval_jaxpr/ij,cjb->cib/dot_general | solution.py:76
  51.4 1.7 %collective-permute-start.1 = (f32[144,256]{1,0:T(8,128)}, f32[144,256]{1,0:T(8,128)S(1)}, u32[]{:S(2)}, u32[]{:S(2)}) collective-permute-start(f32[144,256]{1,0:T(8,128)} %get-tuple-element.317), channel_id=1, source_target_pairs={{0,8},{8,16},{16,24},{24,0},{1,9},{9,17},{17,25},{25,1},{2,10},{10... | collective-permute-start | bytes 442376 | tf_op jit(solution)/shard_map/while/body/eval_jaxpr/ppermute | solution.py:16
  53.0 3.0 %fusion.96 = f32[1872,256]{1,0:T(8,128)S(1)} fusion(s32[2816]{0:T(1024)S(1)} %get-tuple-element.358, bf16[2816,128]{1,0:T(8,128)(2,1)S(1)} %get-tuple-element.314, bf16[2816,128]{1,0:T(8,128)(2,1)S(1)} %get-tuple-element.315), kind=kOutput, calls=%fused_computation.13.clone.1 | convolution fusion | flops 2712461312 | bytes 3369984 | tf_op jit(solution)/shard_map/while/body/eval_jaxpr/dot_general | solution.py:83
  56.1 1.5 %collective-permute-done.1 = f32[144,256]{1,0:T(8,128)S(1)} collective-permute-done((f32[144,256]{1,0:T(8,128)}, f32[144,256]{1,0:T(8,128)S(1)}, u32[]{:S(2)}, u32[]{:S(2)}) %collective-permute-start.1) | collective-permute-done | bytes 147488 | tf_op jit(solution)/shard_map/while/body/eval_jaxpr/ppermute | solution.py:16
  58.3 1.3 %fusion.99 = f32[1872,128]{1,0:T(8,128)S(1)} fusion(f32[144,128]{1,0:T(8,128)S(1)} %fusion.97, f32[1728,128]{1,0:T(8,128)S(1)} %fusion.98, f32[1872,128]{1,0:T(8,128)S(1)} %get-tuple-element.337, f32[1872,128]{1,0:T(8,128)S(1)} %get-tuple-element.338, f32[]{:T(128)S(6)} %select_n.45, f32[]{:T(128)S(6)} %mul.171, f32[1872]{0:T(1024)S(1)} %get-tuple-element.357, ...), kind=kLoop, calls=%fused_computation.28.clone.1 | loop fusion | flops 2156544 | bytes 3848840 | tf_op jit(solution)/shard_map/while/body/eval_jaxpr/sub | solution.py:96
  59.8 1.6 %collective-permute-start.5 = (bf16[1728,128]{1,0:T(8,128)(2,1)S(1)}, bf16[1728,128]{1,0:T(8,128)(2,1)S(1)}, u32[]{:S(2)}, u32[]{:S(2)}) collective-permute-start(bf16[1728,128]{1,0:T(8,128)(2,1)S(1)} %slice.170), channel_id=1, source_target_pairs={{0,2},{2,0},{1,3},{3,1},{4,6},{6,4},{5,7},{7,5},{8,10},{10,8},{9,1... | collective-permute-start | bytes 1327112 | tf_op jit(solution)/shard_map/ppermute | solution.py:26
  61.7 6.7 %collective-permute-done.5 = bf16[1728,128]{1,0:T(8,128)(2,1)S(1)} collective-permute-done((bf16[1728,128]{1,0:T(8,128)(2,1)S(1)}, bf16[1728,128]{1,0:T(8,128)(2,1)S(1)}, u32[]{:S(2)}, u32[]{:S(2)}) %collective-permute-start.5) | collective-permute-done | bytes 442400 | tf_op jit(solution)/shard_map/ppermute | solution.py:26
  (76 shorter events, 18.3 us)
Async XLA Ops:
  0.0 61.5 %copy-start = (bf16[512,128]{1,0:T(8,128)(2,1)S(1)}, bf16[512,128]{1,0:T(8,128)(2,1)}, u32[]{:S(2)}) copy-start(bf16[512,128]{1,0:T(8,128)(2,1)} %param.15) | copy-start | bytes 393220
  0.0 11.8 %copy-start.3 = (f32[1728]{0:T(1024)S(1)}, f32[1728]{0:T(1024)}, u32[]{:S(2)}) copy-start(f32[1728]{0:T(1024)} %param.11) | copy-start | bytes 20740
  0.0 11.8 %copy-start.4 = (f32[1728]{0:T(1024)S(1)}, f32[1728]{0:T(1024)}, u32[]{:S(2)}) copy-start(f32[1728]{0:T(1024)} %param.10) | copy-start | bytes 20740
  0.0 10.6 %copy-start.5 = (s32[8,343]{1,0:T(8,128)S(1)}, s32[8,343]{1,0:T(8,128)}, u32[]{:S(2)}) copy-start(s32[8,343]{1,0:T(8,128)} %param.13) | copy-start | bytes 32932
  0.0 10.7 %copy-start.1 = (bf16[343,343]{1,0:T(8,128)(2,1)S(1)}, bf16[343,343]{1,0:T(8,128)(2,1)}, u32[]{:S(2)}) copy-start(bf16[343,343]{1,0:T(8,128)(2,1)} %param.12) | copy-start | bytes 705898
  1.5 10.4 %collective-permute-start.2 = (f32[144,128]{1,0:T(8,128)S(1)}, f32[144,128]{1,0:T(8,128)S(1)}, u32[]{:S(2)}, u32[]{:S(2)}) collective-permute-start(f32[144,128]{1,0:T(8,128)S(1)} %fusion.47), channel_id=1, source_target_pairs={{0,24},{8,0},{16,8},{24,16},{1,25},{9,1},{17,9},{25,17},{2,26},{10... | collective-permute-start | bytes 221192 | tf_op jit(solution)/shard_map/ppermute | solution.py:16
  8.2 3.6 %collective-permute-start.3 = (f32[2,144]{1,0:T(2,128)S(1)}, f32[2,144]{1,0:T(2,128)S(1)}, u32[]{:S(2)}, u32[]{:S(2)}) collective-permute-start(f32[2,144]{1,0:T(2,128)S(1)} %fusion.45), channel_id=1, source_target_pairs={{0,24},{8,0},{16,8},{24,16},{1,25},{9,1},{17,9},{25,17},{2,26},{10... | collective-permute-start | bytes 3464 | tf_op jit(solution)/shard_map/ppermute | solution.py:16
  11.9 0.7 copy-start.2
  18.4 8.9 %collective-permute-start = (f32[144,256]{1,0:T(8,128)S(1)}, f32[144,256]{1,0:T(8,128)S(1)}, u32[]{:S(2)}, u32[]{:S(2)}) collective-permute-start(f32[144,256]{1,0:T(8,128)S(1)} %get-tuple-element.316), channel_id=1, source_target_pairs={{0,24},{8,0},{16,8},{24,16},{1,25},{9,1},{17,9},{25,17},{2,26},{10... | collective-permute-start | bytes 442376 | tf_op jit(solution)/shard_map/while/body/eval_jaxpr/ppermute | solution.py:16
  19.8 6.8 %collective-permute-start.1 = (f32[144,256]{1,0:T(8,128)}, f32[144,256]{1,0:T(8,128)S(1)}, u32[]{:S(2)}, u32[]{:S(2)}) collective-permute-start(f32[144,256]{1,0:T(8,128)} %get-tuple-element.317), channel_id=1, source_target_pairs={{0,8},{8,16},{16,24},{24,0},{1,9},{9,17},{17,25},{25,1},{2,10},{10... | collective-permute-start | bytes 442376 | tf_op jit(solution)/shard_map/while/body/eval_jaxpr/ppermute | solution.py:16
  34.5 9.3 %collective-permute-start = (f32[144,256]{1,0:T(8,128)S(1)}, f32[144,256]{1,0:T(8,128)S(1)}, u32[]{:S(2)}, u32[]{:S(2)}) collective-permute-start(f32[144,256]{1,0:T(8,128)S(1)} %get-tuple-element.316), channel_id=1, source_target_pairs={{0,24},{8,0},{16,8},{24,16},{1,25},{9,1},{17,9},{25,17},{2,26},{10... | collective-permute-start | bytes 442376 | tf_op jit(solution)/shard_map/while/body/eval_jaxpr/ppermute | solution.py:16
  36.4 6.7 %collective-permute-start.1 = (f32[144,256]{1,0:T(8,128)}, f32[144,256]{1,0:T(8,128)S(1)}, u32[]{:S(2)}, u32[]{:S(2)}) collective-permute-start(f32[144,256]{1,0:T(8,128)} %get-tuple-element.317), channel_id=1, source_target_pairs={{0,8},{8,16},{16,24},{24,0},{1,9},{9,17},{17,25},{25,1},{2,10},{10... | collective-permute-start | bytes 442376 | tf_op jit(solution)/shard_map/while/body/eval_jaxpr/ppermute | solution.py:16
  51.0 7.3 %collective-permute-start = (f32[144,256]{1,0:T(8,128)S(1)}, f32[144,256]{1,0:T(8,128)S(1)}, u32[]{:S(2)}, u32[]{:S(2)}) collective-permute-start(f32[144,256]{1,0:T(8,128)S(1)} %get-tuple-element.316), channel_id=1, source_target_pairs={{0,24},{8,0},{16,8},{24,16},{1,25},{9,1},{17,9},{25,17},{2,26},{10... | collective-permute-start | bytes 442376 | tf_op jit(solution)/shard_map/while/body/eval_jaxpr/ppermute | solution.py:16
  51.4 6.3 %collective-permute-start.1 = (f32[144,256]{1,0:T(8,128)}, f32[144,256]{1,0:T(8,128)S(1)}, u32[]{:S(2)}, u32[]{:S(2)}) collective-permute-start(f32[144,256]{1,0:T(8,128)} %get-tuple-element.317), channel_id=1, source_target_pairs={{0,8},{8,16},{16,24},{24,0},{1,9},{9,17},{17,25},{25,1},{2,10},{10... | collective-permute-start | bytes 442376 | tf_op jit(solution)/shard_map/while/body/eval_jaxpr/ppermute | solution.py:16
  59.8 8.6 %collective-permute-start.5 = (bf16[1728,128]{1,0:T(8,128)(2,1)S(1)}, bf16[1728,128]{1,0:T(8,128)(2,1)S(1)}, u32[]{:S(2)}, u32[]{:S(2)}) collective-permute-start(bf16[1728,128]{1,0:T(8,128)(2,1)S(1)} %slice.170), channel_id=1, source_target_pairs={{0,2},{2,0},{1,3},{3,1},{4,6},{6,4},{5,7},{7,5},{8,10},{10,8},{9,1... | collective-permute-start | bytes 1327112 | tf_op jit(solution)/shard_map/ppermute | solution.py:26
  61.5 6.9 %collective-permute-start.4 = (bf16[1728,128]{1,0:T(8,128)(2,1)S(1)}, bf16[1728,128]{1,0:T(8,128)(2,1)S(1)}, u32[]{:S(2)}, u32[]{:S(2)}) collective-permute-start(bf16[1728,128]{1,0:T(8,128)(2,1)S(1)} %slice.170), channel_id=1, source_target_pairs={{0,1},{1,0},{2,3},{3,2},{4,5},{5,4},{6,7},{7,6},{8,9},{9,8},{10,11... | collective-permute-start | bytes 1327112 | tf_op jit(solution)/shard_map/ppermute | solution.py:26
  68.4 1.8 %collective-permute-start.6 = (bf16[1728,128]{1,0:T(8,128)(2,1)S(1)}, bf16[1728,128]{1,0:T(8,128)(2,1)S(1)}, u32[]{:S(2)}, u32[]{:S(2)}) collective-permute-start(bf16[1728,128]{1,0:T(8,128)(2,1)S(1)} %collective-permute-done.5), channel_id=1, source_target_pairs={{0,1},{1,0},{2,3},{3,2},{4,5},{5,4},{6,7},{7,6},{8,9},{9,8},{10,11... | collective-permute-start | bytes 1327112 | tf_op jit(solution)/shard_map/ppermute | solution.py:26

commit v18 on v5

--- a/solution.py
+++ b/solution.py
@@ -54,7 +54,7 @@
     face_put = (wide_ids[:node_count] == face_rows[None, :]).astype(jnp.bfloat16)
     face_take = (face_rows[:, None] == wide_ids[:node_count, 0][None, :]).astype(jnp.bfloat16)
 
-    face_states = jnp.dot(face_take, states, preferred_element_type=jnp.float32)
+    face_states = jnp.dot(face_take, states, preferred_element_type=jnp.bfloat16)
     face_mass_potential = lax.dot_general(
         jnp.stack([inv_mass, potential], 0),
         face_put.astype(jnp.float32),
@@ -63,7 +63,7 @@
         preferred_element_type=jnp.float32,
     )
     ghost_states, ghost_mass_potential = ring((face_states, face_mass_potential), "dom", -1)
-    field_start = jnp.concatenate([states.astype(jnp.float32), ghost_states], 0)
+    field_start = jnp.concatenate([states, ghost_states], 0).astype(jnp.float32)
     wide_mass = jnp.concatenate([inv_mass, ghost_mass_potential[0]], 0)
     wide_potential = jnp.concatenate([potential, ghost_mass_potential[1]], 0)
 

time: 65.2 us -> 65.7 us (level)
  local copies, waits for them, and re-layouts: 4.35 us -> 5.89 us
  other arithmetic: 7.43 us -> 6.36 us
    convert_element_type x1, other arithmetic: 1.07 us -> 0.06 us  [body(): field_start = jnp.concatenate([states, ghost_states], 0).astype(jnp.float32)]
    pad x1, local copies, waits for them, and re-layouts: 0.74 us -> 1.69 us  [body(): padded_matrix = jnp.pad(cell_matrix, ((0, pad), (0, pad)))]
    pad x1, local copies, waits for them, and re-layouts: 0.01 us -> 0.71 us  [body(): jnp.pad(connect, ((0, 0), (0, pad)), constant_values=-1).reshape(-1)]
  transfers between devices with their start and end apart: 11 -> 11, of which waited for: 6 -> 5; matrix products, arithmetic and copies ran while one was open for 27% -> 28% of each run, Pallas kernels for 0% -> 0%
where the time goes in v18:
time: 65.7 us; the launch traced here: 65.2 us
  matrix products  28.5 us (43%)
  starting transfers between devices  12.4 us (19%)
  waiting for transfers between devices  11.6 us (18%)
  other arithmetic  6.36 us (10%)
  local copies, waits for them, and re-layouts  5.89 us (9%)
    ppermute x8, starting transfers between devices, ring(): return lax.ppermute(block, axis, route)  10.7 us
    dot_general x3, matrix products, operate(): jnp.dot(scatter_sel, both, preferred_element_type=jnp.float32)  8.99 us
    ppermute x3, waiting for transfers between devices, from_partner(): return lax.ppermute(block, axis, route)  7.71 us
    dot_general x3, matrix products, operate(): lax.dot_general(scatter_sel, weighted, (((0,), (0,)), ((), ())), preferre...  7.05 us
    dot_general x3, matrix products, operate(): jnp.einsum('ij,cjb->cib', padded_matrix, values, preferred_element_type=j...  4.46 us
    sub x3, other arithmetic, chebyshev_step(): return (current, gain * scaled - keep * previous)  3.86 us
    ppermute x8, waiting for transfers between devices, ring(): return lax.ppermute(block, axis, route)  3.86 us
    dot_general x3, matrix products, operate(): jnp.dot(rim_sel, both, preferred_element_type=jnp.float32)  1.89 us
  transfers between devices with their start and end apart: 11, of which 5 were waited for; matrix products, arithmetic and copies ran while one was open for 28% of the time, Pallas kernels for 0%

profile of v18, /device:TPU:0, one launch (start us, length us, event | category | flops | bytes accessed | tf_op | source)
XLA Modules:
  0.0 65.2 jit_solution(10075445549640797694)
XLA Ops:
  0.1 1.4 %fusion.46 = bf16[144,128]{1,0:T(8,128)(2,1)S(1)} fusion(bf16[1728,128]{1,0:T(8,128)(2,1)} %param.9, s32[1728]{0:T(1024)S(1)} %add_reduce_fusion, s32[144]{0:T(256)} %param.14), kind=kOutput, calls=%fused_computation.53 | convolution fusion | flops 63949824 | bytes 486720 | tf_op jit(solution)/shard_map/dot_general | solution.py:57
  1.5 4.0 %collective-permute-start.2 = (bf16[144,128]{1,0:T(8,128)(2,1)S(1)}, bf16[144,128]{1,0:T(8,128)(2,1)S(1)}, u32[]{:S(2)}, u32[]{:S(2)}) collective-permute-start(bf16[144,128]{1,0:T(8,128)(2,1)S(1)} %fusion.46), channel_id=1, source_target_pairs={{0,24},{8,0},{16,8},{24,16},{1,25},{9,1},{17,9},{25,17},{2,26},{10... | collective-permute-start | bytes 110600 | tf_op jit(solution)/shard_map/ppermute | solution.py:16
  6.9 1.4 %fusion.44 = f32[2,144]{1,0:T(2,128)S(1)} fusion(s32[144]{0:T(256)} %param.14, s32[1728]{0:T(1024)S(1)} %add_reduce_fusion, f32[1,1728]{1,0:T(1,128)S(1)} %stack.10, f32[1,1728]{1,0:T(1,128)S(1)} %stack.9), kind=kOutput, calls=%fused_computation.51 | convolution fusion | flops 6224256 | bytes 22464 | tf_op jit(solution)/shard_map/dot_general | solution.py:58
  10.3 1.7 %pad.9 = bf16[352,352]{1,0:T(8,128)(2,1)} pad(bf16[343,343]{1,0:T(8,128)(2,1)} %param.12, bf16[]{:T(256)} %constant.67.clone.1), padding=0_9x0_9 | pad | bytes 483108 | tf_op jit(solution)/shard_map/jit(_pad)/pad | solution.py:48
  12.7 41.1 %while.17 = (s32[]{:T(128)}, f32[1872,128]{1,0:T(8,128)S(1)}, f32[1872,128]{1,0:T(8,128)S(1)}, f32[1872]{0:T(1024)S(1)}, bf16[352,352]{1,0:T(8,128)(2,1)}, /*ind...) while((s32[]{:T(128)}, f32[1872,128]{1,0:T(8,128)S(1)}, ...), condition=%wide.region_1.2_spmd.clone.clone, body=%wide.region_0.1_spmd.clone.clone.sunk | while | flops 4879314944 | bytes 31196832 | solution.py:98
  12.7 2.3 %fusion.90 = bf16[2816,128]{0,1:T(8,128)(2,1)S(1)} fusion(s32[2816]{0:T(1024)S(1)} %get-tuple-element.358, f32[1872,128]{1,0:T(8,128)S(1)} %get-tuple-element.338, f32[1872]{0:T(1024)S(1)} %get-tuple-element.355), kind=kOutput, calls=%fused_computation.10.clone.1 | convolution fusion | flops 1360900096 | bytes 1698112 | tf_op jit(solution)/shard_map/while/body/eval_jaxpr/dot_general | solution.py:72
  15.4 1.5 %fusion.91 = f32[8,128,352]{1,2,0:T(8,128)S(1)} fusion(bf16[8,352,128]{2,1,0:T(8,128)(2,1)S(1)} %bitcast.41, bf16[352,352]{1,0:T(8,128)(2,1)} %get-tuple-element.356), kind=kOutput, calls=%fused_computation.35.clone.1 | convolution fusion | flops 253755392 | bytes 2410496 | tf_op jit(solution)/shard_map/while/body/eval_jaxpr/ij,cjb->cib/dot_general | solution.py:76
  17.8 1.5 %collective-permute-start = (f32[144,128]{1,0:T(8,128)S(1)}, f32[144,128]{1,0:T(8,128)S(1)}, u32[]{:S(2)}, u32[]{:S(2)}) collective-permute-start(f32[144,128]{1,0:T(8,128)S(1)} %get-tuple-element.316), channel_id=1, source_target_pairs={{0,24},{8,0},{16,8},{24,16},{1,25},{9,1},{17,9},{25,17},{2,26},{10... | collective-permute-start | bytes 221192 | tf_op jit(solution)/shard_map/while/body/eval_jaxpr/ppermute | solution.py:16
  19.9 3.0 %fusion.94 = f32[1872,256]{1,0:T(8,128)S(1)} fusion(s32[2816]{0:T(1024)S(1)} %get-tuple-element.358, bf16[2816,128]{1,0:T(8,128)(2,1)S(1)} %get-tuple-element.314, bf16[2816,128]{1,0:T(8,128)(2,1)S(1)} %get-tuple-element.315), kind=kOutput, calls=%fused_computation.13.clone.1 | convolution fusion | flops 2712461312 | bytes 3369984 | tf_op jit(solution)/shard_map/while/body/eval_jaxpr/dot_general | solution.py:83
  23.0 1.5 %collective-permute-done.1 = f32[144,128]{1,0:T(8,128)S(1)} collective-permute-done((f32[144,128]{1,0:T(8,128)S(1)}, f32[144,128]{1,0:T(8,128)S(1)}, u32[]{:S(2)}, u32[]{:S(2)}) %collective-permute-start.1) | collective-permute-done | bytes 73760 | tf_op jit(solution)/shard_map/while/body/eval_jaxpr/ppermute | solution.py:16
  25.2 1.3 %fusion.96 = f32[1872,128]{1,0:T(8,128)S(1)} fusion(f32[144,128]{1,0:T(8,128)S(1)} %slice_add_fusion.9, f32[1728,128]{1,0:T(8,128)S(1)} %fusion.95, f32[1872,128]{1,0:T(8,128)S(1)} %get-tuple-element.337, f32[1872,128]{1,0:T(8,128)S(1)} %get-tuple-element.338, f32[]{:T(128)S(6)} %select_n.45, f32[]{:T(128)S(6)} %mul.171, ...), kind=kLoop, calls=%fused_computation.28.clone.1 | loop fusion | flops 2156544 | bytes 3848840 | tf_op jit(solution)/shard_map/while/body/eval_jaxpr/sub | solution.py:96
  26.7 2.4 %fusion.90 = bf16[2816,128]{0,1:T(8,128)(2,1)S(1)} fusion(s32[2816]{0:T(1024)S(1)} %get-tuple-element.358, f32[1872,128]{1,0:T(8,128)S(1)} %get-tuple-element.338, f32[1872]{0:T(1024)S(1)} %get-tuple-element.355), kind=kOutput, calls=%fused_computation.10.clone.1 | convolution fusion | flops 1360900096 | bytes 1698112 | tf_op jit(solution)/shard_map/while/body/eval_jaxpr/dot_general | solution.py:72
  29.4 1.5 %fusion.91 = f32[8,128,352]{1,2,0:T(8,128)S(1)} fusion(bf16[8,352,128]{2,1,0:T(8,128)(2,1)S(1)} %bitcast.41, bf16[352,352]{1,0:T(8,128)(2,1)} %get-tuple-element.356), kind=kOutput, calls=%fused_computation.35.clone.1 | convolution fusion | flops 253755392 | bytes 2410496 | tf_op jit(solution)/shard_map/while/body/eval_jaxpr/ij,cjb->cib/dot_general | solution.py:76
  33.9 3.0 %fusion.94 = f32[1872,256]{1,0:T(8,128)S(1)} fusion(s32[2816]{0:T(1024)S(1)} %get-tuple-element.358, bf16[2816,128]{1,0:T(8,128)(2,1)S(1)} %get-tuple-element.314, bf16[2816,128]{1,0:T(8,128)(2,1)S(1)} %get-tuple-element.315), kind=kOutput, calls=%fused_computation.13.clone.1 | convolution fusion | flops 2712461312 | bytes 3369984 | tf_op jit(solution)/shard_map/while/body/eval_jaxpr/dot_general | solution.py:83
  38.6 1.3 %fusion.96 = f32[1872,128]{1,0:T(8,128)S(1)} fusion(f32[144,128]{1,0:T(8,128)S(1)} %slice_add_fusion.9, f32[1728,128]{1,0:T(8,128)S(1)} %fusion.95, f32[1872,128]{1,0:T(8,128)S(1)} %get-tuple-element.337, f32[1872,128]{1,0:T(8,128)S(1)} %get-tuple-element.338, f32[]{:T(128)S(6)} %select_n.45, f32[]{:T(128)S(6)} %mul.171, ...), kind=kLoop, calls=%fused_computation.28.clone.1 | loop fusion | flops 2156544 | bytes 3848840 | tf_op jit(solution)/shard_map/while/body/eval_jaxpr/sub | solution.py:96
  40.0 2.4 %fusion.90 = bf16[2816,128]{0,1:T(8,128)(2,1)S(1)} fusion(s32[2816]{0:T(1024)S(1)} %get-tuple-element.358, f32[1872,128]{1,0:T(8,128)S(1)} %get-tuple-element.338, f32[1872]{0:T(1024)S(1)} %get-tuple-element.355), kind=kOutput, calls=%fused_computation.10.clone.1 | convolution fusion | flops 1360900096 | bytes 1698112 | tf_op jit(solution)/shard_map/while/body/eval_jaxpr/dot_general | solution.py:72
  42.8 1.5 %fusion.91 = f32[8,128,352]{1,2,0:T(8,128)S(1)} fusion(bf16[8,352,128]{2,1,0:T(8,128)(2,1)S(1)} %bitcast.41, bf16[352,352]{1,0:T(8,128)(2,1)} %get-tuple-element.356), kind=kOutput, calls=%fused_computation.35.clone.1 | convolution fusion | flops 253755392 | bytes 2410496 | tf_op jit(solution)/shard_map/while/body/eval_jaxpr/ij,cjb->cib/dot_general | solution.py:76
  45.2 1.3 %collective-permute-start = (f32[144,128]{1,0:T(8,128)S(1)}, f32[144,128]{1,0:T(8,128)S(1)}, u32[]{:S(2)}, u32[]{:S(2)}) collective-permute-start(f32[144,128]{1,0:T(8,128)S(1)} %get-tuple-element.316), channel_id=1, source_target_pairs={{0,24},{8,0},{16,8},{24,16},{1,25},{9,1},{17,9},{25,17},{2,26},{10... | collective-permute-start | bytes 221192 | tf_op jit(solution)/shard_map/while/body/eval_jaxpr/ppermute | solution.py:16
  47.2 3.0 %fusion.94 = f32[1872,256]{1,0:T(8,128)S(1)} fusion(s32[2816]{0:T(1024)S(1)} %get-tuple-element.358, bf16[2816,128]{1,0:T(8,128)(2,1)S(1)} %get-tuple-element.314, bf16[2816,128]{1,0:T(8,128)(2,1)S(1)} %get-tuple-element.315), kind=kOutput, calls=%fused_computation.13.clone.1 | convolution fusion | flops 2712461312 | bytes 3369984 | tf_op jit(solution)/shard_map/while/body/eval_jaxpr/dot_general | solution.py:83
  50.4 1.3 %collective-permute-done.1 = f32[144,128]{1,0:T(8,128)S(1)} collective-permute-done((f32[144,128]{1,0:T(8,128)S(1)}, f32[144,128]{1,0:T(8,128)S(1)}, u32[]{:S(2)}, u32[]{:S(2)}) %collective-permute-start.1) | collective-permute-done | bytes 73760 | tf_op jit(solution)/shard_map/while/body/eval_jaxpr/ppermute | solution.py:16
  52.4 1.3 %fusion.96 = f32[1872,128]{1,0:T(8,128)S(1)} fusion(f32[144,128]{1,0:T(8,128)S(1)} %slice_add_fusion.9, f32[1728,128]{1,0:T(8,128)S(1)} %fusion.95, f32[1872,128]{1,0:T(8,128)S(1)} %get-tuple-element.337, f32[1872,128]{1,0:T(8,128)S(1)} %get-tuple-element.338, f32[]{:T(128)S(6)} %select_n.45, f32[]{:T(128)S(6)} %mul.171, ...), kind=kLoop, calls=%fused_computation.28.clone.1 | loop fusion | flops 2156544 | bytes 3848840 | tf_op jit(solution)/shard_map/while/body/eval_jaxpr/sub | solution.py:96
  53.9 1.6 %collective-permute-start.5 = (bf16[1728,128]{1,0:T(8,128)(2,1)S(1)}, bf16[1728,128]{1,0:T(8,128)(2,1)S(1)}, u32[]{:S(2)}, u32[]{:S(2)}) collective-permute-start(bf16[1728,128]{1,0:T(8,128)(2,1)S(1)} %slice.138), channel_id=1, source_target_pairs={{0,2},{2,0},{1,3},{3,1},{4,6},{6,4},{5,7},{7,5},{8,10},{10,8},{9,1... | collective-permute-start | bytes 1327112 | tf_op jit(solution)/shard_map/ppermute | solution.py:26
  55.8 6.5 %collective-permute-done.5 = bf16[1728,128]{1,0:T(8,128)(2,1)S(1)} collective-permute-done((bf16[1728,128]{1,0:T(8,128)(2,1)S(1)}, bf16[1728,128]{1,0:T(8,128)(2,1)S(1)}, u32[]{:S(2)}, u32[]{:S(2)}) %collective-permute-start.5) | collective-permute-done | bytes 442400 | tf_op jit(solution)/shard_map/ppermute | solution.py:26
  62.8 1.2 %collective-permute-done.6 = bf16[1728,128]{1,0:T(8,128)(2,1)S(1)} collective-permute-done((bf16[1728,128]{1,0:T(8,128)(2,1)S(1)}, bf16[1728,128]{1,0:T(8,128)(2,1)S(1)}, u32[]{:S(2)}, u32[]{:S(2)}) %collective-permute-start.6) | collective-permute-done | bytes 442400 | tf_op jit(solution)/shard_map/ppermute | solution.py:26
  (76 shorter events, 16.9 us)
Async XLA Ops:
  0.0 55.5 %copy-start = (bf16[512,128]{1,0:T(8,128)(2,1)S(1)}, bf16[512,128]{1,0:T(8,128)(2,1)}, u32[]{:S(2)}) copy-start(bf16[512,128]{1,0:T(8,128)(2,1)} %param.15) | copy-start | bytes 393220
  0.0 12.1 %copy-start.1 = (bf16[1728,128]{1,0:T(8,128)(2,1)S(1)}, bf16[1728,128]{1,0:T(8,128)(2,1)}, u32[]{:S(2)}) copy-start(bf16[1728,128]{1,0:T(8,128)(2,1)} %param.9) | copy-start | bytes 1327108
  0.0 12.0 %copy-start.3 = (f32[1728]{0:T(1024)S(1)}, f32[1728]{0:T(1024)}, u32[]{:S(2)}) copy-start(f32[1728]{0:T(1024)} %param.11) | copy-start | bytes 20740
  0.0 12.0 %copy-start.4 = (f32[1728]{0:T(1024)S(1)}, f32[1728]{0:T(1024)}, u32[]{:S(2)}) copy-start(f32[1728]{0:T(1024)} %param.10) | copy-start | bytes 20740
  1.5 10.6 %collective-permute-start.2 = (bf16[144,128]{1,0:T(8,128)(2,1)S(1)}, bf16[144,128]{1,0:T(8,128)(2,1)S(1)}, u32[]{:S(2)}, u32[]{:S(2)}) collective-permute-start(bf16[144,128]{1,0:T(8,128)(2,1)S(1)} %fusion.46), channel_id=1, source_target_pairs={{0,24},{8,0},{16,8},{24,16},{1,25},{9,1},{17,9},{25,17},{2,26},{10... | collective-permute-start | bytes 110600 | tf_op jit(solution)/shard_map/ppermute | solution.py:16
  8.2 3.8 %collective-permute-start.3 = (f32[2,144]{1,0:T(2,128)S(1)}, f32[2,144]{1,0:T(2,128)S(1)}, u32[]{:S(2)}, u32[]{:S(2)}) collective-permute-start(f32[2,144]{1,0:T(2,128)S(1)} %fusion.44), channel_id=1, source_target_pairs={{0,24},{8,0},{16,8},{24,16},{1,25},{9,1},{17,9},{25,17},{2,26},{10... | collective-permute-start | bytes 3464 | tf_op jit(solution)/shard_map/ppermute | solution.py:16
  12.0 0.7 %copy-start.2 = (s32[144]{0:T(256)S(1)}, s32[144]{0:T(256)}, u32[]{:S(2)}) copy-start(s32[144]{0:T(256)} %param.14) | copy-start | bytes 1732
  17.8 7.4 %collective-permute-start = (f32[144,128]{1,0:T(8,128)S(1)}, f32[144,128]{1,0:T(8,128)S(1)}, u32[]{:S(2)}, u32[]{:S(2)}) collective-permute-start(f32[144,128]{1,0:T(8,128)S(1)} %get-tuple-element.316), channel_id=1, source_target_pairs={{0,24},{8,0},{16,8},{24,16},{1,25},{9,1},{17,9},{25,17},{2,26},{10... | collective-permute-start | bytes 221192 | tf_op jit(solution)/shard_map/while/body/eval_jaxpr/ppermute | solution.py:16
  19.3 5.3 %collective-permute-start.1 = (f32[144,128]{1,0:T(8,128)S(1)}, f32[144,128]{1,0:T(8,128)S(1)}, u32[]{:S(2)}, u32[]{:S(2)}) collective-permute-start(f32[144,128]{1,0:T(8,128)S(1)} %get-tuple-element.317), channel_id=1, source_target_pairs={{0,8},{8,16},{16,24},{24,0},{1,9},{9,17},{17,25},{25,1},{2,10},{10... | collective-permute-start | bytes 221192 | tf_op jit(solution)/shard_map/while/body/eval_jaxpr/ppermute | solution.py:16
  31.8 6.8 %collective-permute-start = (f32[144,128]{1,0:T(8,128)S(1)}, f32[144,128]{1,0:T(8,128)S(1)}, u32[]{:S(2)}, u32[]{:S(2)}) collective-permute-start(f32[144,128]{1,0:T(8,128)S(1)} %get-tuple-element.316), channel_id=1, source_target_pairs={{0,24},{8,0},{16,8},{24,16},{1,25},{9,1},{17,9},{25,17},{2,26},{10... | collective-permute-start | bytes 221192 | tf_op jit(solution)/shard_map/while/body/eval_jaxpr/ppermute | solution.py:16
  32.7 5.3 %collective-permute-start.1 = (f32[144,128]{1,0:T(8,128)S(1)}, f32[144,128]{1,0:T(8,128)S(1)}, u32[]{:S(2)}, u32[]{:S(2)}) collective-permute-start(f32[144,128]{1,0:T(8,128)S(1)} %get-tuple-element.317), channel_id=1, source_target_pairs={{0,8},{8,16},{16,24},{24,0},{1,9},{9,17},{17,25},{25,1},{2,10},{10... | collective-permute-start | bytes 221192 | tf_op jit(solution)/shard_map/while/body/eval_jaxpr/ppermute | solution.py:16
  45.2 7.2 %collective-permute-start = (f32[144,128]{1,0:T(8,128)S(1)}, f32[144,128]{1,0:T(8,128)S(1)}, u32[]{:S(2)}, u32[]{:S(2)}) collective-permute-start(f32[144,128]{1,0:T(8,128)S(1)} %get-tuple-element.316), channel_id=1, source_target_pairs={{0,24},{8,0},{16,8},{24,16},{1,25},{9,1},{17,9},{25,17},{2,26},{10... | collective-permute-start | bytes 221192 | tf_op jit(solution)/shard_map/while/body/eval_jaxpr/ppermute | solution.py:16
  46.4 5.3 %collective-permute-start.1 = (f32[144,128]{1,0:T(8,128)S(1)}, f32[144,128]{1,0:T(8,128)S(1)}, u32[]{:S(2)}, u32[]{:S(2)}) collective-permute-start(f32[144,128]{1,0:T(8,128)S(1)} %get-tuple-element.317), channel_id=1, source_target_pairs={{0,8},{8,16},{16,24},{24,0},{1,9},{9,17},{17,25},{25,1},{2,10},{10... | collective-permute-start | bytes 221192 | tf_op jit(solution)/shard_map/while/body/eval_jaxpr/ppermute | solution.py:16
  53.9 8.4 %collective-permute-start.5 = (bf16[1728,128]{1,0:T(8,128)(2,1)S(1)}, bf16[1728,128]{1,0:T(8,128)(2,1)S(1)}, u32[]{:S(2)}, u32[]{:S(2)}) collective-permute-start(bf16[1728,128]{1,0:T(8,128)(2,1)S(1)} %slice.138), channel_id=1, source_target_pairs={{0,2},{2,0},{1,3},{3,1},{4,6},{6,4},{5,7},{7,5},{8,10},{10,8},{9,1... | collective-permute-start | bytes 1327112 | tf_op jit(solution)/shard_map/ppermute | solution.py:26
  55.5 6.7 %collective-permute-start.4 = (bf16[1728,128]{1,0:T(8,128)(2,1)S(1)}, bf16[1728,128]{1,0:T(8,128)(2,1)S(1)}, u32[]{:S(2)}, u32[]{:S(2)}) collective-permute-start(bf16[1728,128]{1,0:T(8,128)(2,1)S(1)} %slice.138), channel_id=1, source_target_pairs={{0,1},{1,0},{2,3},{3,2},{4,5},{5,4},{6,7},{7,6},{8,9},{9,8},{10,11... | collective-permute-start | bytes 1327112 | tf_op jit(solution)/shard_map/ppermute | solution.py:26
  62.2 1.8 %collective-permute-start.6 = (bf16[1728,128]{1,0:T(8,128)(2,1)S(1)}, bf16[1728,128]{1,0:T(8,128)(2,1)S(1)}, u32[]{:S(2)}, u32[]{:S(2)}) collective-permute-start(bf16[1728,128]{1,0:T(8,128)(2,1)S(1)} %collective-permute-done.5), channel_id=1, source_target_pairs={{0,1},{1,0},{2,3},{3,2},{4,5},{5,4},{6,7},{7,6},{8,9},{9,8},{10,11... | collective-permute-start | bytes 1327112 | tf_op jit(solution)/shard_map/ppermute | solution.py:26
